TPU v7x, 32 devices: a whole 2x2x4 slice. The times are simulated.
32 devices in a mesh: dp: 4 (over z), vocab: 8 (over y, x, core).
Axes of the slice: x: 2, y: 2, z: 4, core: 2. Of those that a mesh axis runs over, the one named last changes fastest.
Arguments:
- hidden: bfloat16 [512, 8192], P('dp', 'vocab'), may hold values from -8 to 8
- out_weight: bfloat16 [19456, 8192], P('vocab', 'dp'), may hold values from -0.397747564 to 0.397747564
- token_blocks: int32 [8, 4, 16], P('vocab'), may hold values from 0 to 18, as said below
- counts: int32 [8, 4], P('vocab'), may hold values from 4 to 16, as said below
Outputs:
- allowed_logprob: float32 [8, 4, 16, 128, 128], P('vocab', 'dp')
- expected: float32 [512, 8192], P('vocab', 'dp')
Inputs may be any that keep to these rules, and one draw needn't show every extreme that they name: token_blocks[j, b, s] names one of the 19 token blocks of shard j; the entries of one list are distinct; slots at or past counts[j, b] carry no meaning. `counts`: for every beam block, some shard allows exactly 16 slots.
All inputs are finite; a program needn't handle non-finite values.
Results may differ from a plain program's by a relative error of at most 0.0021.
Values may be sent and summed in bfloat16 or wider, within the bound.
No kernel may reach another device: no remote copies, remote signals or barrier semaphores. Data moves between devices by JAX's collectives and lax.ppermute only.
A program may use at most 128 MiB of HBM per device.

v0:
```python
import jax
import jax.numpy as jnp
from jax import lax
from jax.sharding import PartitionSpec as P

D = 8192
TB = 128
BB = 128
MOST = 16


def per_device(hidden, out_weight, token_blocks, counts):
    beams_here = hidden.shape[0]
    vocab_here, columns_here = out_weight.shape
    own_blocks = beams_here // BB
    block_lists = token_blocks[0]
    block_counts = counts[0]
    weight_blocks = out_weight.reshape(vocab_here // TB, TB, columns_here)
    first_block = lax.axis_index("dp") * own_blocks
    own_counts = lax.dynamic_slice_in_dim(block_counts, first_block, own_blocks, 0)
    beam_rows = lax.all_gather(hidden, "vocab", axis=1, tiled=True)
    beam_columns = lax.all_to_all(beam_rows, "dp", split_axis=1, concat_axis=0, tiled=True)
    column_blocks = beam_columns.reshape(-1, BB, columns_here)
    pick_part = block_lists

    def partial_one_block(pair_in):
        return jnp.einsum(
            "rd,std->srt", pair_in[0], weight_blocks[pair_in[1]], preferred_element_type=jnp.float32
        )

    logits = lax.psum_scatter(
        lax.map(partial_one_block, (column_blocks, pick_part)),
        "dp",
        scatter_dimension=0,
        tiled=True,
    )
    live = jnp.arange(MOST, dtype=jnp.int32)[None, :] < own_counts[:, None]
    live_mask = live[:, :, None, None]
    masked = jnp.where(live_mask, logits, -jnp.inf)
    local_max = jnp.max(masked, axis=(1, 3))
    beam_max = lax.pmax(local_max, "vocab")
    local_total = jnp.sum(jnp.exp(masked - beam_max[:, None, :, None]), axis=(1, 3))
    beam_total = lax.psum(local_total, "vocab")
    shifted = logits - beam_max[:, None, :, None] - jnp.log(beam_total)[:, None, :, None]
    allowed_logprob = jnp.where(live_mask, shifted, 0.0)
    probabilities = jnp.where(live_mask, jnp.exp(shifted), 0.0).astype(jnp.bfloat16)
    prob_part = lax.all_gather(probabilities, "dp", axis=0, tiled=True)
    block_count = prob_part.shape[0]
    pick_part = block_lists

    def expected_one_block(pair_in):
        return jnp.einsum(
            "srt,std->rd", pair_in[0], weight_blocks[pair_in[1]], preferred_element_type=jnp.float32
        )

    embedding_part = lax.map(expected_one_block, (prob_part, pick_part)).reshape(
        block_count * BB, columns_here
    )
    summed = lax.psum_scatter(embedding_part, "vocab", scatter_dimension=0, tiled=True)
    squares = lax.psum(jnp.sum(summed * summed, axis=1), "dp")
    expected = summed * lax.rsqrt(squares / D + 1e-06)[:, None]
    return (allowed_logprob[None], expected)


def solution(mesh):
    in_specs = (P("dp", "vocab"), P("vocab", "dp"), P("vocab", None, None), P("vocab", None))
    out_specs = (P("vocab", "dp", None, None, None), P("vocab", "dp"))
    return jax.shard_map(
        per_device, mesh=mesh, in_specs=in_specs, out_specs=out_specs, check_vma=False
    )
```

profile of v0, /device:TPU:0, one launch (start us, length us, event | category | flops | bytes accessed | tf_op | source)
XLA Modules:
  0.0 437.9 jit_solution(15092039008348145845)
XLA Ops:
  7.2 0.0 copy-start
  7.2 0.0 copy-start.1
  7.2 0.0 all-gather.3.cloned.1.call-start
  7.2 1.8 copy.10
  9.0 0.0 all-gather.3.cloned.1.call-update
  9.1 31.9 %all-gather.3.cloned.1.call-done = bf16[128,8192]{0,1:T(8,128)(2,1)} async-done(((bf16[128,1024]{0,1:T(8,128)(2,1)}), bf16[128,8192]{0,1:T(8,128)(2,1)}) %all-gather.3.cloned.1.call-update) | async-done | bytes 2097168 | tf_op jit(solution)/shard_map/all_gather | solution.py:21
  41.0 4.6 %all-to-all-start = ((bf16[128,4,2048]{0,2,1:T(8,128)(2,1)}), bf16[128,4,2048]{0,2,1:T(8,128)(2,1)}, u32[]{:S(2)}, u32[]{:S(2)}) async-start(bf16[128,4,2048]{0,2,1:T(8,128)(2,1)} %bitcast.68), calls=%async_computation | async-start | bytes 4194304 | tf_op jit(solution)/shard_map/all_to_all | solution.py:22
  45.6 0.0 reduce-scatter.3.cloned.1.call-start
  45.6 48.8 %all-to-all-done = bf16[128,4,2048]{0,2,1:T(8,128)(2,1)} async-done(((bf16[128,4,2048]{0,2,1:T(8,128)(2,1)}), bf16[128,4,2048]{0,2,1:T(8,128)(2,1)}, u32[]{:S(2)}, u32[]{:S(2)}) %all-to-all-start) | async-done | bytes 2097184 | tf_op jit(solution)/shard_map/all_to_all | solution.py:22
  94.4 0.0 copy-done.1
  94.4 63.4 %while.20 = (s32[]{:T(128)}, f32[4,16,128,128]{3,2,1,0:T(8,128)}, s32[4,16]{1,0:T(4,128)S(1)}, bf16[19,128,2048]{2,1,0:T(8,128)(2,1)}, bf16[4,128,2048]{1,2,0:T(8,128)(2,1)}, /*index=5*/s32[]{:T(128)}) while((s32[]{:T(128)}, f32[4,16,128,128]{3,2,1,0:T(8,128)}, s32[4,16]{1,0:T(4,128)S(1)}, bf16[19,128,2048]{2,1,0:T(8,128)(2,1)}, ...), condition=%wide.region_1.2_spmd, body=%wide.region_0.1_spmd.sunk | while | flops 1073742848 | bytes 30938440 | solution.py:32
  94.4 8.6 %gather_fusion = bf16[16,128,2048]{2,1,0:T(8,128)(2,1)} fusion(bf16[19,128,2048]{2,1,0:T(8,128)(2,1)} %get-tuple-element.167, s32[1024]{0:T(1024)S(1)} %pad_clamp_fusion.4), kind=kCustom, calls=%fused_computation.clone.1 | custom fusion | bytes 16777280 | tf_op jit(solution)/shard_map/while/body/eval_jaxpr/gather | solution.py:28
  103.0 5.8 %convolution_bitcast_fusion.3 = f32[1,16,128,128]{2,3,1,0:T(8,128)S(1)} fusion(bf16[16,128,2048]{2,1,0:T(8,128)(2,1)} %gather_fusion, bf16[4,128,2048]{1,2,0:T(8,128)(2,1)} %get-tuple-element.168, s32[]{:T(128)} %get-tuple-element.158), kind=kOutput, calls=%fused_computation.2.clone.1 | convolution fusion | flops 1073741824 | bytes 9961984 | tf_op jit(solution)/shard_map/while/body/eval_jaxpr/rd,std->srt/dot_general | solution.py:27
  108.9 0.3 copy.19
  109.2 1.1 constant_dynamic-update-slice_fusion.2
  110.4 8.6 %gather_fusion = bf16[16,128,2048]{2,1,0:T(8,128)(2,1)} fusion(bf16[19,128,2048]{2,1,0:T(8,128)(2,1)} %get-tuple-element.167, s32[1024]{0:T(1024)S(1)} %pad_clamp_fusion.4), kind=kCustom, calls=%fused_computation.clone.1 | custom fusion | bytes 16777280 | tf_op jit(solution)/shard_map/while/body/eval_jaxpr/gather | solution.py:28
  119.0 5.8 %convolution_bitcast_fusion.3 = f32[1,16,128,128]{2,3,1,0:T(8,128)S(1)} fusion(bf16[16,128,2048]{2,1,0:T(8,128)(2,1)} %gather_fusion, bf16[4,128,2048]{1,2,0:T(8,128)(2,1)} %get-tuple-element.168, s32[]{:T(128)} %get-tuple-element.158), kind=kOutput, calls=%fused_computation.2.clone.1 | convolution fusion | flops 1073741824 | bytes 9961984 | tf_op jit(solution)/shard_map/while/body/eval_jaxpr/rd,std->srt/dot_general | solution.py:27
  124.8 0.3 copy.19
  125.1 1.1 constant_dynamic-update-slice_fusion.2
  126.2 8.6 %gather_fusion = bf16[16,128,2048]{2,1,0:T(8,128)(2,1)} fusion(bf16[19,128,2048]{2,1,0:T(8,128)(2,1)} %get-tuple-element.167, s32[1024]{0:T(1024)S(1)} %pad_clamp_fusion.4), kind=kCustom, calls=%fused_computation.clone.1 | custom fusion | bytes 16777280 | tf_op jit(solution)/shard_map/while/body/eval_jaxpr/gather | solution.py:28
  134.8 5.8 %convolution_bitcast_fusion.3 = f32[1,16,128,128]{2,3,1,0:T(8,128)S(1)} fusion(bf16[16,128,2048]{2,1,0:T(8,128)(2,1)} %gather_fusion, bf16[4,128,2048]{1,2,0:T(8,128)(2,1)} %get-tuple-element.168, s32[]{:T(128)} %get-tuple-element.158), kind=kOutput, calls=%fused_computation.2.clone.1 | convolution fusion | flops 1073741824 | bytes 9961984 | tf_op jit(solution)/shard_map/while/body/eval_jaxpr/rd,std->srt/dot_general | solution.py:27
  140.6 0.3 copy.19
  140.9 1.1 constant_dynamic-update-slice_fusion.2
  142.0 8.6 %gather_fusion = bf16[16,128,2048]{2,1,0:T(8,128)(2,1)} fusion(bf16[19,128,2048]{2,1,0:T(8,128)(2,1)} %get-tuple-element.167, s32[1024]{0:T(1024)S(1)} %pad_clamp_fusion.4), kind=kCustom, calls=%fused_computation.clone.1 | custom fusion | bytes 16777280 | tf_op jit(solution)/shard_map/while/body/eval_jaxpr/gather | solution.py:28
  150.6 5.8 %convolution_bitcast_fusion.3 = f32[1,16,128,128]{2,3,1,0:T(8,128)S(1)} fusion(bf16[16,128,2048]{2,1,0:T(8,128)(2,1)} %gather_fusion, bf16[4,128,2048]{1,2,0:T(8,128)(2,1)} %get-tuple-element.168, s32[]{:T(128)} %get-tuple-element.158), kind=kOutput, calls=%fused_computation.2.clone.1 | convolution fusion | flops 1073741824 | bytes 9961984 | tf_op jit(solution)/shard_map/while/body/eval_jaxpr/rd,std->srt/dot_general | solution.py:27
  156.4 0.3 copy.19
  156.8 1.1 constant_dynamic-update-slice_fusion.2
  157.8 0.0 reduce-scatter.3.cloned.1.call-update
  157.8 0.0 all-gather.5.cloned.1.call-start
  157.9 0.0 copy-done
  157.9 0.6 constant_dynamic-slice_fusion.2
  158.5 0.6 iota_compare_fusion
  159.2 73.7 %reduce-scatter.3.cloned.1.call-done = f32[1,16,128,128]{3,2,1,0:T(8,128)} async-done(((f32[4,16,128,128]{3,2,1,0:T(8,128)}), f32[1,16,128,128]{3,2,1,0:T(8,128)}) %reduce-scatter.3.cloned.1.call-update) | async-done | bytes 1048592 | tf_op jit(solution)/shard_map/reduce_scatter | solution.py:31
  232.9 1.4 select_reduce_fusion
  234.3 13.3 %pmax.7 = f32[128]{0:T(128)S(1)} all-reduce(f32[128]{0:T(128)S(1)} %select_reduce_fusion), channel_id=1, replica_groups=mesh['dp'=4,'vocab'=8] {'vocab'}, use_global_device_ids=true, to_apply=%region_4.5 | all-reduce | flops 128 | bytes 1024 | tf_op jit(solution)/shard_map/pmax | solution.py:41
  247.6 1.6 exponential_reduce_fusion
  249.2 11.8 %psum.14 = f32[1,128]{1,0:T(1,128)S(1)} all-reduce(f32[1,128]{1,0:T(1,128)S(1)} %bitcast.69), channel_id=1, replica_groups=mesh['dp'=4,'vocab'=8] {'vocab'}, use_global_device_ids=true, to_apply=%region_6.7 | all-reduce | flops 128 | bytes 1024 | tf_op jit(solution)/shard_map/psum | solution.py:43
  261.0 2.8 select_convert_fusion
  263.8 0.0 all-gather.5.cloned.1.call-update
  263.8 0.0 reduce-scatter.5.cloned.1.call-start
  263.9 44.7 %all-gather.5.cloned.1.call-done = bf16[4,16,128,128]{3,2,1,0:T(8,128)(2,1)} async-done(((bf16[1,16,128,128]{3,2,1,0:T(8,128)(2,1)}), bf16[4,16,128,128]{3,2,1,0:T(8,128)(2,1)}) %all-gather.5.cloned.1.call-update) | async-done | bytes 2097168 | tf_op jit(solution)/shard_map/all_gather | solution.py:47
  308.6 57.7 %while.21 = (s32[]{:T(128)}, f32[4,128,2048]{2,1,0:T(8,128)}, bf16[4,16,128,128]{3,2,1,0:T(8,128)(2,1)}, s32[4,16]{1,0:T(4,128)S(1)}, bf16[19,128,2048]{2,1,0:T(8,128)(2,1)}, /*index=5*/s32[]{:T(128)}) while((s32[]{:T(128)}, f32[4,128,2048]{2,1,0:T(8,128)}, bf16[4,16,128,128]{3,2,1,0:T(8,128)(2,1)}, s32[4,16]{1,0:T(4,128)S(1)}, ...), condition=%wide.region_8.9_spmd, body=%wide.region_7.8_spmd.sunk | while | flops 1073742848 | bytes 26744136 | solution.py:56
  308.7 8.6 %gather_fusion.1 = bf16[16,128,2048]{2,1,0:T(8,128)(2,1)} fusion(bf16[19,128,2048]{2,1,0:T(8,128)(2,1)} %get-tuple-element.186, s32[1024]{0:T(1024)S(1)} %pad_clamp_fusion.5), kind=kCustom, calls=%fused_computation.1.clone.1 | custom fusion | bytes 16777280 | tf_op jit(solution)/shard_map/while/body/eval_jaxpr/gather | solution.py:53
  317.3 5.9 %fusion.26 = f32[4,128,2048]{2,1,0:T(8,128)} fusion(f32[4,128,2048]{2,1,0:T(8,128)} %get-tuple-element.177, s32[]{:T(128)} %get-tuple-element.176, bf16[16,128,2048]{2,1,0:T(8,128)(2,1)} %gather_fusion.1, bf16[4,16,128,128]{3,2,1,0:T(8,128)(2,1)} %get-tuple-element.184), kind=kOutput, calls=%fused_computation.13.clone.1 | convolution fusion | flops 1073741824 | bytes 9962496 | tf_op jit(solution)/shard_map/while/body/eval_jaxpr/srt,std->rd/dot_general | solution.py:52
  323.2 8.6 %gather_fusion.1 = bf16[16,128,2048]{2,1,0:T(8,128)(2,1)} fusion(bf16[19,128,2048]{2,1,0:T(8,128)(2,1)} %get-tuple-element.186, s32[1024]{0:T(1024)S(1)} %pad_clamp_fusion.5), kind=kCustom, calls=%fused_computation.1.clone.1 | custom fusion | bytes 16777280 | tf_op jit(solution)/shard_map/while/body/eval_jaxpr/gather | solution.py:53
  331.8 5.8 %fusion.26 = f32[4,128,2048]{2,1,0:T(8,128)} fusion(f32[4,128,2048]{2,1,0:T(8,128)} %get-tuple-element.177, s32[]{:T(128)} %get-tuple-element.176, bf16[16,128,2048]{2,1,0:T(8,128)(2,1)} %gather_fusion.1, bf16[4,16,128,128]{3,2,1,0:T(8,128)(2,1)} %get-tuple-element.184), kind=kOutput, calls=%fused_computation.13.clone.1 | convolution fusion | flops 1073741824 | bytes 9962496 | tf_op jit(solution)/shard_map/while/body/eval_jaxpr/srt,std->rd/dot_general | solution.py:52
  337.6 8.6 %gather_fusion.1 = bf16[16,128,2048]{2,1,0:T(8,128)(2,1)} fusion(bf16[19,128,2048]{2,1,0:T(8,128)(2,1)} %get-tuple-element.186, s32[1024]{0:T(1024)S(1)} %pad_clamp_fusion.5), kind=kCustom, calls=%fused_computation.1.clone.1 | custom fusion | bytes 16777280 | tf_op jit(solution)/shard_map/while/body/eval_jaxpr/gather | solution.py:53
  346.2 5.8 %fusion.26 = f32[4,128,2048]{2,1,0:T(8,128)} fusion(f32[4,128,2048]{2,1,0:T(8,128)} %get-tuple-element.177, s32[]{:T(128)} %get-tuple-element.176, bf16[16,128,2048]{2,1,0:T(8,128)(2,1)} %gather_fusion.1, bf16[4,16,128,128]{3,2,1,0:T(8,128)(2,1)} %get-tuple-element.184), kind=kOutput, calls=%fused_computation.13.clone.1 | convolution fusion | flops 1073741824 | bytes 9962496 | tf_op jit(solution)/shard_map/while/body/eval_jaxpr/srt,std->rd/dot_general | solution.py:52
  352.0 8.6 %gather_fusion.1 = bf16[16,128,2048]{2,1,0:T(8,128)(2,1)} fusion(bf16[19,128,2048]{2,1,0:T(8,128)(2,1)} %get-tuple-element.186, s32[1024]{0:T(1024)S(1)} %pad_clamp_fusion.5), kind=kCustom, calls=%fused_computation.1.clone.1 | custom fusion | bytes 16777280 | tf_op jit(solution)/shard_map/while/body/eval_jaxpr/gather | solution.py:53
  360.6 5.8 %fusion.26 = f32[4,128,2048]{2,1,0:T(8,128)} fusion(f32[4,128,2048]{2,1,0:T(8,128)} %get-tuple-element.177, s32[]{:T(128)} %get-tuple-element.176, bf16[16,128,2048]{2,1,0:T(8,128)(2,1)} %gather_fusion.1, bf16[4,16,128,128]{3,2,1,0:T(8,128)(2,1)} %get-tuple-element.184), kind=kOutput, calls=%fused_computation.13.clone.1 | convolution fusion | flops 1073741824 | bytes 9962496 | tf_op jit(solution)/shard_map/while/body/eval_jaxpr/srt,std->rd/dot_general | solution.py:52
  366.4 0.0 reduce-scatter.5.cloned.1.call-update
  366.4 50.1 %reduce-scatter.5.cloned.1.call-done = f32[64,2048]{1,0:T(8,128)} async-done(((f32[512,2048]{1,0:T(8,128)}), f32[64,2048]{1,0:T(8,128)}) %reduce-scatter.5.cloned.1.call-update) | async-done | bytes 524304 | tf_op jit(solution)/shard_map/reduce_scatter | solution.py:59
  416.5 1.2 multiply_reduce_fusion
  417.7 11.7 %psum.15 = f32[64]{0:T(128)S(1)} all-reduce(f32[64]{0:T(128)S(1)} %multiply_reduce_fusion), channel_id=1, replica_groups=mesh['dp'=4,'vocab'=8] {'dp'}, use_global_device_ids=true, to_apply=%region_11.12 | all-reduce | flops 64 | bytes 512 | tf_op jit(solution)/shard_map/psum | solution.py:60
  429.4 1.9 broadcast_multiply_fusion
  (20 shorter events, 0.1 us)
Async XLA Ops:
  7.2 150.7 %copy-start = (s32[1,4]{1,0:T(1,128)S(1)}, s32[1,4]{1,0:T(1,128)}, u32[]{:S(2)}) copy-start(s32[1,4]{1,0:T(1,128)} %param.11) | copy-start | bytes 52
  7.2 87.2 %copy-start.1 = (s32[1,4,16]{2,1,0:T(4,128)S(1)}, s32[1,4,16]{2,1,0:T(4,128)}, u32[]{:S(2)}) copy-start(s32[1,4,16]{2,1,0:T(4,128)} %param.10) | copy-start | bytes 772
  7.2 33.8 %all-gather.3.cloned.1.call-start = ((), (), s32[]{:S(2)}) async-start(), calls=%async_computation.3 | async-start | bytes 2359296 | tf_op jit(solution)/shard_map/all_gather | solution.py:21
  41.0 53.4 %all-to-all-start = ((bf16[128,4,2048]{0,2,1:T(8,128)(2,1)}), bf16[128,4,2048]{0,2,1:T(8,128)(2,1)}, u32[]{:S(2)}, u32[]{:S(2)}) async-start(bf16[128,4,2048]{0,2,1:T(8,128)(2,1)} %bitcast.68), calls=%async_computation | async-start | bytes 4194304 | tf_op jit(solution)/shard_map/all_to_all | solution.py:22
  45.6 187.3 %reduce-scatter.3.cloned.1.call-start = ((), (), s32[]{:S(2)}) async-start(), calls=%async_computation.4 | async-start | bytes 5242880 | tf_op jit(solution)/shard_map/reduce_scatter | solution.py:31
  157.8 150.8 %all-gather.5.cloned.1.call-start = ((), (), s32[]{:S(2)}) async-start(), calls=%async_computation.5 | async-start | bytes 2621440 | tf_op jit(solution)/shard_map/all_gather | solution.py:47
  263.8 152.7 %reduce-scatter.5.cloned.1.call-start = ((), (), s32[]{:S(2)}) async-start(), calls=%async_computation.6 | async-start | bytes 4718592 | tf_op jit(solution)/shard_map/reduce_scatter | solution.py:59
Sparse Core Ops, SparseCore 0:
  10.5 30.4 all-gather.2
  158.0 74.8 reduce-scatter.2
  264.0 44.6 all-gather.4
  366.5 49.9 reduce-scatter.4
where the time goes:
time: 439 us; the launch traced here: 438 us
  waiting for transfers between devices  249 us (57%)
  local copies, waits for them, and re-layouts  76.8 us (17%)
  matrix products  46.6 us (11%)
  blocking collectives  36.8 us (8%)
  between operations  13.8 us (3%)
  other arithmetic  9.7 us (2%)
  starting transfers between devices  4.72 us (1%)
    reduce_scatter x1, waiting for transfers between devices, per_device(): lax.psum_scatter(lax.map(partial_one_block, (column_blocks, pick_part)),...  73.7 us
    reduce_scatter x1, waiting for transfers between devices, per_device(): lax.psum_scatter(embedding_part, 'vocab', scatter_dimension=0, tiled=True)  50.1 us
    all_to_all x1, waiting for transfers between devices, per_device(): lax.all_to_all(beam_rows, 'dp', split_axis=1, concat_axis=0, tiled=True)  48.8 us
    all_gather x1, waiting for transfers between devices, per_device(): prob_part = lax.all_gather(probabilities, 'dp', axis=0, tiled=True)  44.7 us
    gather x4, local copies, waits for them, and re-layouts, partial_one_block(): weight_blocks[pair_in[1]]  34.4 us
    gather x4, local copies, waits for them, and re-layouts, expected_one_block(): weight_blocks[pair_in[1]]  34.4 us
    all_gather x1, waiting for transfers between devices, per_device(): beam_rows = lax.all_gather(hidden, 'vocab', axis=1, tiled=True)  31.9 us
    dot_general x4, matrix products, expected_one_block(): jnp.einsum('srt,std->rd', pair_in[0], weight_blocks[pair_in[1]], preferre...  23.3 us
  transfers between devices with their start and end apart: 5, of which 5 were waited for; matrix products, arithmetic and copies ran while one was open for 0% of the time, Pallas kernels for 0%

commit v1 on v0

v1 whole, which is shorter than its diff:
```python
import jax
import jax.numpy as jnp
from jax import lax
from jax.sharding import PartitionSpec as P

TB = 128
BB = 128
MOST = 16


def per_device(hidden, out_weight, token_blocks, counts):
    vocab_here, columns_here = out_weight.shape
    width = hidden.shape[1] * lax.psum(1, "vocab")
    n_tb = vocab_here // TB
    block_lists = token_blocks[0]
    block_counts = counts[0]
    n_blk = block_lists.shape[0]
    own_blocks = hidden.shape[0] // BB
    first_block = lax.axis_index("dp") * own_blocks
    own_counts = lax.dynamic_slice_in_dim(block_counts, first_block, own_blocks, 0)

    beam_rows = lax.all_gather(hidden, "vocab", axis=1, tiled=True)
    beam_columns = lax.all_to_all(beam_rows, "dp", split_axis=1, concat_axis=0, tiled=True)

    with jax.named_scope("dense_logits"):
        full = jnp.einsum(
            "bd,vd->bv", beam_columns, out_weight, preferred_element_type=jnp.float32
        )
        full4 = full.reshape(n_blk, BB, n_tb, TB)
        rows = jnp.arange(n_blk, dtype=jnp.int32)[:, None]
        picked = full4[rows, :, block_lists, :]

    logits = lax.psum_scatter(picked, "dp", scatter_dimension=0, tiled=True)

    with jax.named_scope("softmax_stats"):
        live = jnp.arange(MOST, dtype=jnp.int32)[None, :] < own_counts[:, None]
        live_mask = live[:, :, None, None]
        masked = jnp.where(live_mask, logits, -jnp.inf)
        local_max = jnp.max(masked, axis=(1, 3))
        local_total = jnp.sum(jnp.exp(masked - local_max[:, None, :, None]), axis=(1, 3))
        stats = lax.all_gather(jnp.stack([local_max, local_total]), "vocab", axis=0)
        beam_max = jnp.max(stats[:, 0], axis=0)
        beam_total = jnp.sum(stats[:, 1] * jnp.exp(stats[:, 0] - beam_max[None]), axis=0)
        shifted = logits - beam_max[:, None, :, None] - jnp.log(beam_total)[:, None, :, None]
        allowed_logprob = jnp.where(live_mask, shifted, 0.0)
        probabilities = jnp.where(live_mask, jnp.exp(shifted), 0.0).astype(jnp.bfloat16)

    prob_part = lax.all_gather(probabilities, "dp", axis=0, tiled=True)

    with jax.named_scope("dense_expected"):
        onehot = (
            block_lists[:, :, None] == jnp.arange(n_tb, dtype=jnp.int32)[None, None, :]
        ).astype(jnp.bfloat16)
        spread = jnp.einsum(
            "bsk,bsrt->brkt", onehot, prob_part, preferred_element_type=jnp.float32
        ).astype(jnp.bfloat16)
        embedding_part = jnp.einsum(
            "bv,vd->bd",
            spread.reshape(n_blk * BB, n_tb * TB),
            out_weight,
            preferred_element_type=jnp.float32,
        )
    summed = lax.psum_scatter(embedding_part, "vocab", scatter_dimension=0, tiled=True)
    squares = lax.psum(jnp.sum(summed * summed, axis=1), "dp")
    expected = summed * lax.rsqrt(squares / width + 1e-06)[:, None]
    return (allowed_logprob[None], expected)


def solution(mesh):
    in_specs = (P("dp", "vocab"), P("vocab", "dp"), P("vocab", None, None), P("vocab", None))
    out_specs = (P("vocab", "dp", None, None, None), P("vocab", "dp"))
    return jax.shard_map(
        per_device, mesh=mesh, in_specs=in_specs, out_specs=out_specs, check_vma=False
    )
```

time: 439 us -> 334 us (0.76)
  local copies, waits for them, and re-layouts: 76.8 us -> 11.8 us
  matrix products: 46.6 us -> 22.7 us
  blocking collectives: 36.8 us -> 20.6 us
    gather x8 -> x1, local copies, waits for them, and re-layouts: 68.8 us -> 5.26 us  [per_device(): picked = full4[rows, :, block_lists, :]]
    dot_general x8 -> x3, matrix products: 46.6 us -> 22.7 us  [the longest x1 9.91 us: per_device(): jnp.einsum('bd,vd->bv', beam_columns, out_weight, preferred_element_type=...]
    pmax x1 -> x0, blocking collectives: 13.3 us -> none  [per_device(): beam_max = lax.pmax(local_max, 'vocab')]
    psum x1 -> x0, blocking collectives: 11.8 us -> none  [per_device(): beam_total = lax.psum(local_total, 'vocab')]
    all_gather x0 -> x1, blocking collectives: none -> 8.9 us  [per_device(): stats = lax.all_gather(jnp.stack([local_max, local_total]), 'vocab', axis=0)]
    dynamic_update_slice x8 -> x0, local copies, waits for them, and re-layouts: 5.64 us -> none  [per_device(): lax.map(partial_one_block, (column_blocks, pick_part))]
where the time goes in v1:
time: 334 us; the launch traced here: 333 us
  waiting for transfers between devices  250 us (75%)
  matrix products  22.7 us (7%)
  blocking collectives  20.6 us (6%)
  between operations  13.8 us (4%)
  local copies, waits for them, and re-layouts  11.8 us (4%)
  other arithmetic  9.65 us (3%)
  starting transfers between devices  4.72 us (1%)
    reduce_scatter x1, waiting for transfers between devices, per_device(): logits = lax.psum_scatter(picked, 'dp', scatter_dimension=0, tiled=True)  73.8 us
    reduce_scatter x1, waiting for transfers between devices, per_device(): lax.psum_scatter(embedding_part, 'vocab', scatter_dimension=0, tiled=True)  50.1 us
    all_to_all x1, waiting for transfers between devices, per_device(): lax.all_to_all(beam_rows, 'dp', split_axis=1, concat_axis=0, tiled=True)  48.5 us
    all_gather x1, waiting for transfers between devices, per_device(): prob_part = lax.all_gather(probabilities, 'dp', axis=0, tiled=True)  45.4 us
    all_gather x1, waiting for transfers between devices, per_device(): beam_rows = lax.all_gather(hidden, 'vocab', axis=1, tiled=True)  31.9 us
    psum x1, blocking collectives, per_device(): squares = lax.psum(jnp.sum(summed * summed, axis=1), 'dp')  11.7 us
    dot_general x1, matrix products, per_device(): jnp.einsum('bd,vd->bv', beam_columns, out_weight, preferred_element_type=...  9.91 us
    dot_general x1, matrix products, per_device(): jnp.einsum('bv,vd->bd', spread.reshape(n_blk * BB, n_tb * TB), out_weight...  9.53 us
  transfers between devices with their start and end apart: 5, of which 5 were waited for; matrix products, arithmetic and copies ran while one was open for 0% of the time, Pallas kernels for 0%

profile of v1, /device:TPU:0, one launch (start us, length us, event | category | flops | bytes accessed | tf_op | source)
XLA Modules:
  0.0 333.0 jit_solution(18080191292290261255)
XLA Ops:
  7.2 0.0 copy-start
  7.2 0.0 all-gather.4.cloned.1.call-start
  7.2 1.8 copy.15
  9.0 0.0 all-gather.4.cloned.1.call-update
  9.0 31.9 %all-gather.4.cloned.1.call-done = bf16[128,8192]{0,1:T(8,128)(2,1)} async-done(((bf16[128,1024]{0,1:T(8,128)(2,1)}), bf16[128,8192]{0,1:T(8,128)(2,1)}) %all-gather.4.cloned.1.call-update) | async-done | bytes 2097168 | tf_op jit(solution)/shard_map/all_gather | solution.py:22
  41.0 0.0 copy-start.1
  41.0 4.0 %copy.16 = bf16[128,4,2048]{2,0,1:T(8,128)(2,1)} copy(bf16[128,4,2048]{0,2,1:T(8,128)(2,1)} %bitcast.42) | data formatting | bytes 4194304 | tf_op jit(solution)/shard_map/all_to_all | solution.py:23
  45.0 4.6 %all-to-all-start = ((bf16[128,4,2048]{2,0,1:T(8,128)(2,1)}), bf16[128,4,2048]{2,0,1:T(8,128)(2,1)S(1)}, u32[]{:S(2)}, u32[]{:S(2)}) async-start(bf16[128,4,2048]{2,0,1:T(8,128)(2,1)} %copy.16), calls=%async_computation | async-start | bytes 4194304 | tf_op jit(solution)/shard_map/all_to_all | solution.py:23
  49.6 0.0 reduce-scatter.3.cloned.1.call-start
  49.6 0.0 copy-done.1
  49.6 0.1 reshape.130
  49.7 48.5 %all-to-all-done = bf16[128,4,2048]{2,0,1:T(8,128)(2,1)S(1)} async-done(((bf16[128,4,2048]{2,0,1:T(8,128)(2,1)}), bf16[128,4,2048]{2,0,1:T(8,128)(2,1)S(1)}, u32[]{:S(2)}, u32[]{:S(2)}) %all-to-all-start) | async-done | bytes 2097184 | tf_op jit(solution)/shard_map/all_to_all | solution.py:23
  98.2 9.9 %fusion.3 = f32[4,128,19,128]{3,1,2,0:T(8,128)} fusion(bf16[19,128,2048,1]{2,1,0,3:T(8,128)(2,1)} %bitcast.50, bf16[128,4,2048]{2,0,1:T(8,128)(2,1)S(1)} %all-to-all-done), kind=kOutput, calls=%fused_computation.5 | convolution fusion | flops 5100273664 | bytes 17039360 | tf_op jit(solution)/shard_map/dense_logits/bd,vd->bv/dot_general | solution.py:26
  108.1 5.3 %gather_fusion = f32[64,128,128]{2,1,0:T(8,128)} fusion(f32[4,128,19,128]{3,1,2,0:T(8,128)} %fusion.3, s32[64]{0:T(128)S(1)} %reshape.130), kind=kCustom, calls=%fused_computation | custom fusion | bytes 8389120 | tf_op jit(solution)/shard_map/dense_logits/gather | solution.py:31
  113.4 0.0 reduce-scatter.3.cloned.1.call-update
  113.4 0.0 all-gather.6.cloned.1.call-start
  113.4 0.0 copy-done
  113.4 0.6 constant_dynamic-slice_fusion
  114.0 0.6 iota_compare_fusion.1
  114.7 73.8 %reduce-scatter.3.cloned.1.call-done = f32[1,16,128,128]{3,2,1,0:T(8,128)} async-done(((f32[4,16,128,128]{3,2,1,0:T(8,128)}), f32[1,16,128,128]{3,2,1,0:T(8,128)}) %reduce-scatter.3.cloned.1.call-update) | async-done | bytes 1048592 | tf_op jit(solution)/shard_map/reduce_scatter | solution.py:33
  188.5 1.4 select_reduce_fusion
  189.9 1.6 exponential_reduce_fusion
  191.5 8.9 %all-gather = f32[16,1,128]{2,1,0:T(1,128)S(1)} all-gather(f32[2,1,128]{2,1,0:T(1,128)S(1)} %pad_maximum_fusion), channel_id=2, replica_groups=mesh['dp'=4,'vocab'=8] {'vocab'}, dimensions={0}, use_global_device_ids=true | all-gather | bytes 9216 | tf_op jit(solution)/shard_map/softmax_stats/all_gather | solution.py:41
  200.4 2.8 select_convert_fusion
  203.2 0.0 all-gather.6.cloned.1.call-update
  203.3 0.0 reduce-scatter.5.cloned.1.call-start
  203.3 45.4 %all-gather.6.cloned.1.call-done = bf16[4,16,128,128]{3,2,1,0:T(8,128)(2,1)} async-done(((bf16[1,16,128,128]{3,2,1,0:T(8,128)(2,1)}), bf16[4,16,128,128]{3,2,1,0:T(8,128)(2,1)}) %all-gather.6.cloned.1.call-update) | async-done | bytes 2097168 | tf_op jit(solution)/shard_map/all_gather | solution.py:48
  248.7 3.3 convolution_convert_fusion
  251.9 9.5 %fusion = f32[512,2048]{1,0:T(8,128)} fusion(bf16[2432,2048]{1,0:T(8,128)(2,1)} %param.5, bf16[64,8,19,128]{3,2,1,0:T(8,128)(2,1)S(1)} %bitcast.41), kind=kOutput, calls=%fused_computation.1 | convolution fusion | flops 5100273664 | bytes 16646144 | tf_op jit(solution)/shard_map/dense_expected/bv,vd->bd/dot_general | solution.py:57
  261.5 0.0 reduce-scatter.5.cloned.1.call-update
  261.5 50.1 %reduce-scatter.5.cloned.1.call-done = f32[64,2048]{1,0:T(8,128)} async-done(((f32[512,2048]{1,0:T(8,128)}), f32[64,2048]{1,0:T(8,128)}) %reduce-scatter.5.cloned.1.call-update) | async-done | bytes 524304 | tf_op jit(solution)/shard_map/reduce_scatter | solution.py:63
  311.6 1.2 multiply_reduce_fusion
  312.8 11.7 %psum.7 = f32[64]{0:T(128)S(1)} all-reduce(f32[64]{0:T(128)S(1)} %multiply_reduce_fusion), channel_id=1, replica_groups=mesh['dp'=4,'vocab'=8] {'dp'}, use_global_device_ids=true, to_apply=%region_7.8 | all-reduce | flops 64 | bytes 512 | tf_op jit(solution)/shard_map/psum | solution.py:64
  324.5 1.9 broadcast_multiply_fusion
  (7 shorter events, 0.1 us)
Async XLA Ops:
  7.2 106.3 %copy-start = (s32[1,4]{1,0:T(1,128)S(1)}, s32[1,4]{1,0:T(1,128)}, u32[]{:S(2)}) copy-start(s32[1,4]{1,0:T(1,128)} %param.7) | copy-start | bytes 52
  7.2 33.8 %all-gather.4.cloned.1.call-start = ((), (), s32[]{:S(2)}) async-start(), calls=%async_computation.3 | async-start | bytes 2359296 | tf_op jit(solution)/shard_map/all_gather | solution.py:22
  41.0 8.6 %copy-start.1 = (s32[1,4,16]{2,1,0:T(4,128)S(1)}, s32[1,4,16]{2,1,0:T(4,128)}, u32[]{:S(2)}) copy-start(s32[1,4,16]{2,1,0:T(4,128)} %param.6) | copy-start | bytes 772
  45.0 53.2 %all-to-all-start = ((bf16[128,4,2048]{2,0,1:T(8,128)(2,1)}), bf16[128,4,2048]{2,0,1:T(8,128)(2,1)S(1)}, u32[]{:S(2)}, u32[]{:S(2)}) async-start(bf16[128,4,2048]{2,0,1:T(8,128)(2,1)} %copy.16), calls=%async_computation | async-start | bytes 4194304 | tf_op jit(solution)/shard_map/all_to_all | solution.py:23
  49.6 138.9 %reduce-scatter.3.cloned.1.call-start = ((), (), s32[]{:S(2)}) async-start(), calls=%async_computation.4 | async-start | bytes 5242880 | tf_op jit(solution)/shard_map/reduce_scatter | solution.py:33
  113.4 135.3 %all-gather.6.cloned.1.call-start = ((), (), s32[]{:S(2)}) async-start(), calls=%async_computation.5 | async-start | bytes 2621440 | tf_op jit(solution)/shard_map/all_gather | solution.py:48
  203.3 108.3 %reduce-scatter.5.cloned.1.call-start = ((), (), s32[]{:S(2)}) async-start(), calls=%async_computation.6 | async-start | bytes 4718592 | tf_op jit(solution)/shard_map/reduce_scatter | solution.py:63
Sparse Core Ops, SparseCore 0:
  10.4 30.4 all-gather.3
  113.5 74.9 reduce-scatter.2
  203.4 45.2 all-gather.5
  261.6 49.9 reduce-scatter.4

commit v2 on v1

--- a/solution.py
+++ b/solution.py
@@ -10,7 +10,6 @@
 
 def per_device(hidden, out_weight, token_blocks, counts):
     vocab_here, columns_here = out_weight.shape
-    width = hidden.shape[1] * lax.psum(1, "vocab")
     n_tb = vocab_here // TB
     block_lists = token_blocks[0]
     block_counts = counts[0]
@@ -19,8 +18,18 @@
     first_block = lax.axis_index("dp") * own_blocks
     own_counts = lax.dynamic_slice_in_dim(block_counts, first_block, own_blocks, 0)
 
-    beam_rows = lax.all_gather(hidden, "vocab", axis=1, tiled=True)
-    beam_columns = lax.all_to_all(beam_rows, "dp", split_axis=1, concat_axis=0, tiled=True)
+    n_vocab = lax.psum(1, "vocab")
+    n_dp = lax.psum(1, "dp")
+    with jax.named_scope("hidden_spread"):
+        row_slices = lax.all_to_all(hidden, "vocab", split_axis=0, concat_axis=1, tiled=True)
+        plane_rows = lax.all_to_all(row_slices, "dp", split_axis=1, concat_axis=0, tiled=True)
+        gathered = lax.all_gather(plane_rows, "vocab", axis=0, tiled=True)
+        group = hidden.shape[0] // n_vocab
+        beam_columns = (
+            gathered.reshape(n_vocab, n_dp, group, columns_here)
+            .transpose(1, 0, 2, 3)
+            .reshape(n_dp * n_vocab * group, columns_here)
+        )
 
     with jax.named_scope("dense_logits"):
         full = jnp.einsum(
@@ -62,6 +71,7 @@
         )
     summed = lax.psum_scatter(embedding_part, "vocab", scatter_dimension=0, tiled=True)
     squares = lax.psum(jnp.sum(summed * summed, axis=1), "dp")
+    width = hidden.shape[1] * n_vocab
     expected = summed * lax.rsqrt(squares / width + 1e-06)[:, None]
     return (allowed_logprob[None], expected)
 

time: 334 us -> 298 us (0.89)
  waiting for transfers between devices: 250 us -> 196 us
  blocking collectives: 20.6 us -> 45.8 us
  starting transfers between devices: 4.72 us -> 0.16 us
  local copies, waits for them, and re-layouts: 11.8 us -> 8.29 us
    all_to_all x1 -> x0, waiting for transfers between devices: 48.5 us -> none  [per_device(): lax.all_to_all(beam_rows, 'dp', split_axis=1, concat_axis=0, tiled=True)]
    all_to_all x0 -> x2, blocking collectives: none -> 25.2 us  [the longest x1 13.1 us: per_device(): lax.all_to_all(row_slices, 'dp', split_axis=1, concat_axis=0, tiled=True)]
    all_gather x1, waiting for transfers between devices: 31.9 us -> 24.9 us  [per_device(): gathered = lax.all_gather(plane_rows, 'vocab', axis=0, tiled=True)]
    all_to_all x1 -> x0, starting transfers between devices: 4.6 us -> none  [per_device(): lax.all_to_all(beam_rows, 'dp', split_axis=1, concat_axis=0, tiled=True)]
    all_to_all x1 -> x3, local copies, waits for them, and re-layouts: 4.01 us -> 0.51 us  [the longest x2 0.36 us: per_device(): lax.all_to_all(row_slices, 'dp', split_axis=1, concat_axis=0, tiled=True)]
  transfers between devices with their start and end apart: 5 -> 4, of which waited for: 5 -> 4; matrix products, arithmetic and copies ran while one was open for 0% -> 1% of each run, Pallas kernels for 0% -> 0%
where the time goes in v2:
time: 298 us; the launch traced here: 297 us
  waiting for transfers between devices  196 us (66%)
  blocking collectives  45.8 us (15%)
  matrix products  22.5 us (8%)
  between operations  13.8 us (5%)
  other arithmetic  10.3 us (3%)
  local copies, waits for them, and re-layouts  8.29 us (3%)
    reduce_scatter x1, waiting for transfers between devices, per_device(): logits = lax.psum_scatter(picked, 'dp', scatter_dimension=0, tiled=True)  75.6 us
    reduce_scatter x1, waiting for transfers between devices, per_device(): lax.psum_scatter(embedding_part, 'vocab', scatter_dimension=0, tiled=True)  50.1 us
    all_gather x1, waiting for transfers between devices, per_device(): prob_part = lax.all_gather(probabilities, 'dp', axis=0, tiled=True)  45.4 us
    all_gather x1, waiting for transfers between devices, per_device(): gathered = lax.all_gather(plane_rows, 'vocab', axis=0, tiled=True)  24.9 us
    all_to_all x1, blocking collectives, per_device(): lax.all_to_all(row_slices, 'dp', split_axis=1, concat_axis=0, tiled=True)  13.1 us
    all_to_all x1, blocking collectives, per_device(): lax.all_to_all(hidden, 'vocab', split_axis=0, concat_axis=1, tiled=True)  12.1 us
    psum x1, blocking collectives, per_device(): squares = lax.psum(jnp.sum(summed * summed, axis=1), 'dp')  11.7 us
    dot_general x1, matrix products, per_device(): jnp.einsum('bd,vd->bv', beam_columns, out_weight, preferred_element_type=...  9.76 us
  transfers between devices with their start and end apart: 4, of which 4 were waited for; matrix products, arithmetic and copies ran while one was open for 1% of the time, Pallas kernels for 0%

profile of v2, /device:TPU:0, one launch (start us, length us, event | category | flops | bytes accessed | tf_op | source)
XLA Modules:
  0.0 297.1 jit_solution(613679004408229539)
XLA Ops:
  7.2 0.0 copy-start
  7.2 0.0 all-gather.4.cloned.1.call-start
  7.2 12.1 %all_to_all.35 = bf16[8,16,1024]{2,1,0:T(8,128)(2,1)S(1)} all-to-all(bf16[8,16,1024]{2,1,0:T(8,128)(2,1)} %bitcast.52), channel_id=1, replica_groups=mesh['dp'=4,'vocab'=8] {'vocab'}, dimensions={0} | all-to-all | bytes 524288 | tf_op jit(solution)/shard_map/hidden_spread/all_to_all | solution.py:24
  19.3 0.1 copy.16
  19.5 0.2 all_to_all.29
  19.7 0.2 copy.17
  19.9 13.1 %all_to_all.36 = bf16[16,4,2048]{2,0,1:T(8,128)(2,1)} all-to-all(bf16[16,4,2048]{2,0,1:T(8,128)(2,1)S(1)} %copy.17), channel_id=1, replica_groups=mesh['dp'=4,'vocab'=8] {'dp'}, dimensions={1} | all-to-all | bytes 524288 | tf_op jit(solution)/shard_map/hidden_spread/all_to_all | solution.py:25
  33.0 0.0 all-gather.4.cloned.1.call-update
  33.0 0.0 reduce-scatter.3.cloned.1.call-start
  33.0 0.7 fusion.9
  33.7 0.1 reshape.139
  33.8 24.9 %all-gather.4.cloned.1.call-done = bf16[512,2048]{1,0:T(8,128)(2,1)} async-done(((bf16[64,2048]{1,0:T(8,128)(2,1)}), bf16[512,2048]{1,0:T(8,128)(2,1)}) %all-gather.4.cloned.1.call-update) | async-done | bytes 2097168 | tf_op jit(solution)/shard_map/hidden_spread/all_gather | solution.py:26
  58.7 1.8 copy.18
  60.6 9.8 %fusion.11 = f32[4,128,19,128]{3,1,2,0:T(8,128)} fusion(bf16[4,128,2048,1]{2,1,3,0:T(8,128)(2,1)S(1)} %bitcast.49, bf16[19,128,2048,1]{2,1,0,3:T(8,128)(2,1)} %bitcast.60), kind=kOutput, calls=%fused_computation.26 | convolution fusion | flops 5100273664 | bytes 17039360 | tf_op jit(solution)/shard_map/dense_logits/bd,vd->bv/dot_general | solution.py:35
  70.3 5.3 %gather_fusion = f32[64,128,128]{2,1,0:T(8,128)} fusion(f32[4,128,19,128]{3,1,2,0:T(8,128)} %fusion.11, s32[64]{0:T(128)S(1)} %reshape.139), kind=kCustom, calls=%fused_computation | custom fusion | bytes 8389120 | tf_op jit(solution)/shard_map/dense_logits/gather | solution.py:40
  75.6 0.0 copy-start.1
  75.6 0.0 reduce-scatter.3.cloned.1.call-update
  75.6 0.0 all-gather.6.cloned.1.call-start
  75.7 0.0 copy-done
  75.7 0.6 constant_dynamic-slice_fusion
  76.3 0.6 iota_compare_fusion.1
  76.9 75.6 %reduce-scatter.3.cloned.1.call-done = f32[1,16,128,128]{3,2,1,0:T(8,128)} async-done(((f32[4,16,128,128]{3,2,1,0:T(8,128)}), f32[1,16,128,128]{3,2,1,0:T(8,128)}) %reduce-scatter.3.cloned.1.call-update) | async-done | bytes 1048592 | tf_op jit(solution)/shard_map/reduce_scatter | solution.py:42
  152.6 1.4 select_reduce_fusion
  154.0 1.6 exponential_reduce_fusion
  155.6 8.9 %all-gather = f32[16,1,128]{2,1,0:T(1,128)S(1)} all-gather(f32[2,1,128]{2,1,0:T(1,128)S(1)} %pad_maximum_fusion), channel_id=2, replica_groups=mesh['dp'=4,'vocab'=8] {'vocab'}, dimensions={0}, use_global_device_ids=true | all-gather | bytes 9216 | tf_op jit(solution)/shard_map/softmax_stats/all_gather | solution.py:50
  164.5 2.8 select_convert_fusion
  167.4 0.0 all-gather.6.cloned.1.call-update
  167.4 0.0 reduce-scatter.5.cloned.1.call-start
  167.4 45.4 %all-gather.6.cloned.1.call-done = bf16[4,16,128,128]{3,2,1,0:T(8,128)(2,1)} async-done(((bf16[1,16,128,128]{3,2,1,0:T(8,128)(2,1)}), bf16[4,16,128,128]{3,2,1,0:T(8,128)(2,1)}) %all-gather.6.cloned.1.call-update) | async-done | bytes 2097168 | tf_op jit(solution)/shard_map/all_gather | solution.py:57
  212.8 0.0 copy-done.1
  212.8 3.3 %convolution_convert_fusion = bf16[4,128,128,19]{2,3,1,0:T(8,128)(2,1)S(1)} fusion(bf16[4,16,128,128]{3,2,1,0:T(8,128)(2,1)} %all-gather.6.cloned.1.call-done, s32[4,16]{1,0:T(4,128)S(1)} %bitcast.57), kind=kOutput, calls=%fused_computation.4 | convolution fusion | flops 41092288 | bytes 4587776 | tf_op jit(solution)/shard_map/dense_expected/bsk,bsrt->brkt/dot_general | solution.py:63
  216.1 9.5 %fusion = f32[512,2048]{1,0:T(8,128)} fusion(bf16[2432,2048]{1,0:T(8,128)(2,1)} %param.5, bf16[64,8,19,128]{3,2,1,0:T(8,128)(2,1)S(1)} %bitcast.47), kind=kOutput, calls=%fused_computation.1 | convolution fusion | flops 5100273664 | bytes 16646144 | tf_op jit(solution)/shard_map/dense_expected/bv,vd->bd/dot_general | solution.py:66
  225.6 0.0 reduce-scatter.5.cloned.1.call-update
  225.6 50.1 %reduce-scatter.5.cloned.1.call-done = f32[64,2048]{1,0:T(8,128)} async-done(((f32[512,2048]{1,0:T(8,128)}), f32[64,2048]{1,0:T(8,128)}) %reduce-scatter.5.cloned.1.call-update) | async-done | bytes 524304 | tf_op jit(solution)/shard_map/reduce_scatter | solution.py:72
  275.7 1.2 multiply_reduce_fusion
  276.9 11.7 %psum.7 = f32[64]{0:T(128)S(1)} all-reduce(f32[64]{0:T(128)S(1)} %multiply_reduce_fusion), channel_id=1, replica_groups=mesh['dp'=4,'vocab'=8] {'dp'}, use_global_device_ids=true, to_apply=%region_7.8 | all-reduce | flops 64 | bytes 512 | tf_op jit(solution)/shard_map/psum | solution.py:73
  288.6 1.9 broadcast_multiply_fusion
  (6 shorter events, 0.1 us)
Async XLA Ops:
  7.2 68.5 %copy-start = (s32[1,4]{1,0:T(1,128)S(1)}, s32[1,4]{1,0:T(1,128)}, u32[]{:S(2)}) copy-start(s32[1,4]{1,0:T(1,128)} %param.7) | copy-start | bytes 52
  7.2 51.6 %all-gather.4.cloned.1.call-start = ((), (), s32[]{:S(2)}) async-start(), calls=%async_computation.4 | async-start | bytes 2359296 | tf_op jit(solution)/shard_map/hidden_spread/all_gather | solution.py:26
  33.0 119.6 %reduce-scatter.3.cloned.1.call-start = ((), (), s32[]{:S(2)}) async-start(), calls=%async_computation.5 | async-start | bytes 5242880 | tf_op jit(solution)/shard_map/reduce_scatter | solution.py:42
  75.6 137.2 %copy-start.1 = (s32[1,4,16]{2,1,0:T(4,128)S(1)}, s32[1,4,16]{2,1,0:T(4,128)}, u32[]{:S(2)}) copy-start(s32[1,4,16]{2,1,0:T(4,128)} %param.6) | copy-start | bytes 772
  75.6 137.2 %all-gather.6.cloned.1.call-start = ((), (), s32[]{:S(2)}) async-start(), calls=%async_computation.6 | async-start | bytes 2621440 | tf_op jit(solution)/shard_map/all_gather | solution.py:57
  167.4 108.4 %reduce-scatter.5.cloned.1.call-start = ((), (), s32[]{:S(2)}) async-start(), calls=%async_computation.7 | async-start | bytes 4718592 | tf_op jit(solution)/shard_map/reduce_scatter | solution.py:72
Sparse Core Ops, SparseCore 0:
  33.1 25.5 all-gather.3
  75.7 76.7 reduce-scatter.2
  167.5 45.2 all-gather.5
  225.7 49.9 reduce-scatter.4

commit v3 on v2

--- a/solution.py
+++ b/solution.py
@@ -6,6 +6,37 @@
 TB = 128
 BB = 128
 MOST = 16
+
+
+def exchange_stage(x, remaining, bit, n):
+    me = lax.axis_index("vocab")
+    axis = remaining.index(bit)
+    mine = (me // (1 << bit)) % 2
+    keep = lax.dynamic_index_in_dim(x, mine, axis=axis, keepdims=False)
+    send = lax.dynamic_index_in_dim(x, 1 - mine, axis=axis, keepdims=False)
+    perm = [(s, s ^ (1 << bit)) for s in range(n)]
+    got = lax.ppermute(send, "vocab", perm=perm)
+    return keep + got, [b for b in remaining if b != bit]
+
+
+def halving_reduce_scatter(part, n):
+    levels = n.bit_length() - 1
+    rows, cols = part.shape
+    group = rows // n
+    remaining = list(range(levels - 1, -1, -1))
+    x = part.reshape([2] * levels + [group, cols])
+    with jax.named_scope("summed_core_stage"):
+        x, remaining = exchange_stage(x, remaining, 0, n)
+    half = cols // 2
+    first, second = x[..., :half], x[..., half:]
+    rest_a, rest_b = list(remaining), list(remaining)
+    order_a = sorted(remaining)
+    order_b = sorted(remaining, reverse=True)
+    for step in range(len(order_a)):
+        with jax.named_scope("summed_chip_stage"):
+            first, rest_a = exchange_stage(first, rest_a, order_a[step], n)
+            second, rest_b = exchange_stage(second, rest_b, order_b[step], n)
+    return jnp.concatenate([first, second], axis=-1)
 
 
 def per_device(hidden, out_weight, token_blocks, counts):
@@ -69,7 +100,7 @@
             out_weight,
             preferred_element_type=jnp.float32,
         )
-    summed = lax.psum_scatter(embedding_part, "vocab", scatter_dimension=0, tiled=True)
+    summed = halving_reduce_scatter(embedding_part, n_vocab)
     squares = lax.psum(jnp.sum(summed * summed, axis=1), "dp")
     width = hidden.shape[1] * n_vocab
     expected = summed * lax.rsqrt(squares / width + 1e-06)[:, None]

time: 298 us -> 279 us (0.936)
  waiting for transfers between devices: 196 us -> 168 us
  local copies, waits for them, and re-layouts: 8.29 us -> 16.3 us
  starting transfers between devices: 0.16 us -> 5.77 us
    reduce_scatter x1 -> x0, waiting for transfers between devices: 50.1 us -> none  [per_device(): lax.psum_scatter(embedding_part, 'vocab', scatter_dimension=0, tiled=True)]
    ppermute x0 -> x5, waiting for transfers between devices: none -> 21.2 us  [exchange_stage(): got = lax.ppermute(send, 'vocab', perm=perm)]
    ppermute x0 -> x5, starting transfers between devices: none -> 5.65 us  [exchange_stage(): got = lax.ppermute(send, 'vocab', perm=perm)]
    squeeze x0 -> x5, local copies, waits for them, and re-layouts: none -> 3.18 us  [exchange_stage(): send = lax.dynamic_index_in_dim(x, 1 - mine, axis=axis, keepdims=False)]
  transfers between devices with their start and end apart: 4 -> 8, of which waited for: 4 -> 8; matrix products, arithmetic and copies ran while one was open for 1% -> 1% of each run, Pallas kernels for 0% -> 0%
where the time goes in v3:
time: 279 us; the launch traced here: 278 us
  waiting for transfers between devices  168 us (60%)
  blocking collectives  43.6 us (16%)
  matrix products  22 us (8%)
  local copies, waits for them, and re-layouts  16.3 us (6%)
  between operations  13.9 us (5%)
  other arithmetic  8.65 us (3%)
  starting transfers between devices  5.77 us (2%)
    reduce_scatter x1, waiting for transfers between devices, per_device(): logits = lax.psum_scatter(picked, 'dp', scatter_dimension=0, tiled=True)  75.6 us
    all_gather x1, waiting for transfers between devices, per_device(): prob_part = lax.all_gather(probabilities, 'dp', axis=0, tiled=True)  45.4 us
    all_gather x1, waiting for transfers between devices, per_device(): gathered = lax.all_gather(plane_rows, 'vocab', axis=0, tiled=True)  25.6 us
    ppermute x5, waiting for transfers between devices, exchange_stage(): got = lax.ppermute(send, 'vocab', perm=perm)  21.2 us
    all_to_all x1, blocking collectives, per_device(): lax.all_to_all(row_slices, 'dp', split_axis=1, concat_axis=0, tiled=True)  13.1 us
    all_to_all x1, blocking collectives, per_device(): lax.all_to_all(hidden, 'vocab', split_axis=0, concat_axis=1, tiled=True)  12.1 us
    dot_general x1, matrix products, per_device(): jnp.einsum('bd,vd->bv', beam_columns, out_weight, preferred_element_type=...  9.78 us
    psum x1, blocking collectives, per_device(): squares = lax.psum(jnp.sum(summed * summed, axis=1), 'dp')  9.51 us
  transfers between devices with their start and end apart: 8, of which 8 were waited for; matrix products, arithmetic and copies ran while one was open for 1% of the time, Pallas kernels for 0%

profile of v3, /device:TPU:0, one launch (start us, length us, event | category | flops | bytes accessed | tf_op | source)
XLA Modules:
  0.0 278.1 jit_solution(7276035777309197173)
XLA Ops:
  7.2 0.0 copy-start
  7.2 0.0 copy-start.3
  7.2 0.0 all-gather.4.cloned.1.call-start
  7.2 12.1 %all_to_all.35 = bf16[8,16,1024]{2,1,0:T(8,128)(2,1)S(1)} all-to-all(bf16[8,16,1024]{2,1,0:T(8,128)(2,1)} %bitcast.72), channel_id=1, replica_groups=mesh['dp'=4,'vocab'=8] {'vocab'}, dimensions={0} | all-to-all | bytes 524288 | tf_op jit(solution)/shard_map/hidden_spread/all_to_all | solution.py:55
  19.3 0.1 copy.15
  19.5 0.2 all_to_all.29
  19.7 0.2 copy.16
  19.9 13.1 %all_to_all.36 = bf16[16,4,2048]{2,0,1:T(8,128)(2,1)} all-to-all(bf16[16,4,2048]{2,0,1:T(8,128)(2,1)S(1)} %copy.16), channel_id=1, replica_groups=mesh['dp'=4,'vocab'=8] {'dp'}, dimensions={1} | all-to-all | bytes 524288 | tf_op jit(solution)/shard_map/hidden_spread/all_to_all | solution.py:56
  33.0 0.0 all-gather.4.cloned.1.call-update
  33.0 0.0 reduce-scatter.2.cloned.1.call-start
  33.0 0.0 copy-done.3
  33.1 0.1 reshape.139
  33.1 25.6 %all-gather.4.cloned.1.call-done = bf16[512,2048]{1,0:T(8,128)(2,1)} async-done(((bf16[64,2048]{1,0:T(8,128)(2,1)}), bf16[512,2048]{1,0:T(8,128)(2,1)}) %all-gather.4.cloned.1.call-update) | async-done | bytes 2097168 | tf_op jit(solution)/shard_map/hidden_spread/all_gather | solution.py:57
  58.8 1.8 copy.17
  60.6 9.8 %fusion.12 = f32[4,128,19,128]{3,1,2,0:T(8,128)} fusion(bf16[4,128,2048,1]{2,1,3,0:T(8,128)(2,1)S(1)} %bitcast.69, bf16[19,128,2048,1]{2,1,0,3:T(8,128)(2,1)} %bitcast.80), kind=kOutput, calls=%fused_computation.37 | convolution fusion | flops 5100273664 | bytes 17039360 | tf_op jit(solution)/shard_map/dense_logits/bd,vd->bv/dot_general | solution.py:66
  70.4 5.3 %gather_fusion = f32[64,128,128]{2,1,0:T(8,128)} fusion(f32[4,128,19,128]{3,1,2,0:T(8,128)} %fusion.12, s32[64]{0:T(128)S(1)} %reshape.139), kind=kCustom, calls=%fused_computation | custom fusion | bytes 8389120 | tf_op jit(solution)/shard_map/dense_logits/gather | solution.py:71
  75.6 0.0 reduce-scatter.2.cloned.1.call-update
  75.6 0.0 all-gather.6.cloned.1.call-start
  75.7 0.0 copy-done
  75.7 0.6 constant_dynamic-slice_fusion
  76.3 0.6 iota_compare_fusion.1
  76.9 75.6 %reduce-scatter.2.cloned.1.call-done = f32[1,16,128,128]{3,2,1,0:T(8,128)} async-done(((f32[4,16,128,128]{3,2,1,0:T(8,128)}), f32[1,16,128,128]{3,2,1,0:T(8,128)}) %reduce-scatter.2.cloned.1.call-update) | async-done | bytes 1048592 | tf_op jit(solution)/shard_map/reduce_scatter | solution.py:73
  152.6 0.0 copy-start.1
  152.6 1.5 select_reduce_fusion
  154.1 1.6 exponential_reduce_fusion
  155.7 8.9 %all-gather = f32[16,1,128]{2,1,0:T(1,128)S(1)} all-gather(f32[2,1,128]{2,1,0:T(1,128)S(1)} %pad_maximum_fusion.1), channel_id=2, replica_groups=mesh['dp'=4,'vocab'=8] {'vocab'}, dimensions={0}, use_global_device_ids=true | all-gather | bytes 9216 | tf_op jit(solution)/shard_map/softmax_stats/all_gather | solution.py:81
  164.6 0.0 copy-done.1
  164.6 1.6 select_convert_fusion
  166.2 0.0 all-gather.6.cloned.1.call-update
  166.3 45.4 %all-gather.6.cloned.1.call-done = bf16[4,16,128,128]{3,2,1,0:T(8,128)(2,1)} async-done(((bf16[1,16,128,128]{3,2,1,0:T(8,128)(2,1)}), bf16[4,16,128,128]{3,2,1,0:T(8,128)(2,1)}) %all-gather.6.cloned.1.call-update) | async-done | bytes 2097168 | tf_op jit(solution)/shard_map/all_gather | solution.py:88
  211.7 3.3 %convert_bitcast_fusion = bf16[4,128,19,128]{3,2,1,0:T(8,128)(2,1)S(1)} fusion(bf16[4,16,128,128]{3,2,1,0:T(8,128)(2,1)} %all-gather.6.cloned.1.call-done, s32[4,16]{1,0:T(4,128)S(1)} %bitcast.77), kind=kOutput, calls=%fused_computation.3 | convolution fusion | flops 41092288 | bytes 4587776 | tf_op jit(solution)/shard_map/dense_expected/bsk,bsrt->brkt/dot_general | solution.py:94
  214.9 2.7 dot_general.19
  217.7 9.0 %fusion = f32[2,2,2,64,2048]{4,3,2,1,0:T(8,128)S(1)} fusion(bf16[2,2,2,64,2432]{4,3,2,1,0:T(8,128)(2,1)} %dot_general.19, bf16[2432,2048]{1,0:T(8,128)(2,1)} %param.5), kind=kOutput, calls=%fused_computation.1 | convolution fusion | flops 5100273664 | bytes 16646144 | tf_op jit(solution)/shard_map/dense_expected/bv,vd->bd/dot_general | solution.py:97
  226.7 0.0 copy-start.2
  226.7 1.9 copy-done.2
  228.6 1.5 dynamic-slice_bitcast_fusion
  230.1 0.0 collective-permute-start
  230.1 4.4 %collective-permute-done = f32[2,2,64,2048]{3,2,1,0:T(8,128)S(1)} collective-permute-done((f32[2,2,64,2048]{3,2,1,0:T(8,128)}, f32[2,2,64,2048]{3,2,1,0:T(8,128)S(1)}, u32[]{:S(2)}, u32[]{:S(2)}) %collective-permute-start) | collective-permute-done | bytes 2097184 | tf_op jit(solution)/shard_map/summed_core_stage/ppermute | solution.py:18
  234.5 2.0 bitcast_add_fusion
  236.5 0.1 fusion.10
  236.6 0.8 dynamic-slice_bitcast_fusion.1
  237.4 1.5 collective-permute-start.3
  238.9 0.8 dynamic-slice_bitcast_fusion.2
  239.7 1.5 collective-permute-start.1
  241.2 10.4 %collective-permute-done.3 = f32[2,64,1024]{2,1,0:T(8,128)S(1)} collective-permute-done((f32[2,64,1024]{2,1,0:T(8,128)}, f32[2,64,1024]{2,1,0:T(8,128)S(1)}, u32[]{:S(2)}, u32[]{:S(2)}) %collective-permute-start.3) | collective-permute-done | bytes 524320 | tf_op jit(solution)/shard_map/summed_chip_stage/ppermute | solution.py:18
  251.6 0.1 bitcast_add_fusion.1
  251.7 1.5 collective-permute-start.4
  253.3 0.4 collective-permute-done.1
  253.6 0.1 bitcast_add_fusion.2
  253.7 1.2 collective-permute-start.2
  254.9 4.4 %collective-permute-done.4 = f32[64,1024]{1,0:T(8,128)S(1)} collective-permute-done((f32[64,1024]{1,0:T(8,128)S(1)}, f32[64,1024]{1,0:T(8,128)S(1)}, u32[]{:S(2)}, u32[]{:S(2)}) %collective-permute-start.4) | collective-permute-done | bytes 262176 | tf_op jit(solution)/shard_map/summed_chip_stage/ppermute | solution.py:18
  259.3 1.7 collective-permute-done.2
  261.1 0.1 multiply_reduce_fusion
  261.2 9.5 %psum.7 = f32[64]{0:T(128)S(1)} all-reduce(f32[64]{0:T(128)S(1)} %multiply_reduce_fusion), channel_id=1, replica_groups=mesh['dp'=4,'vocab'=8] {'dp'}, use_global_device_ids=true, to_apply=%region_6.7 | all-reduce | flops 64 | bytes 512 | tf_op jit(solution)/shard_map/psum | solution.py:104
  270.7 0.9 fusion.3
  (11 shorter events, 0.2 us)
Async XLA Ops:
  7.2 68.5 %copy-start = (s32[1,4]{1,0:T(1,128)S(1)}, s32[1,4]{1,0:T(1,128)}, u32[]{:S(2)}) copy-start(s32[1,4]{1,0:T(1,128)} %param.7) | copy-start | bytes 52
  7.2 25.9 %copy-start.3 = (s32[1,4,16]{2,1,0:T(4,128)S(1)}, s32[1,4,16]{2,1,0:T(4,128)}, u32[]{:S(2)}) copy-start(s32[1,4,16]{2,1,0:T(4,128)} %param.6) | copy-start | bytes 772
  7.2 51.6 %all-gather.4.cloned.1.call-start = ((), (), s32[]{:S(2)}) async-start(), calls=%async_computation.3 | async-start | bytes 2359296 | tf_op jit(solution)/shard_map/hidden_spread/all_gather | solution.py:57
  33.0 119.6 %reduce-scatter.2.cloned.1.call-start = ((), (), s32[]{:S(2)}) async-start(), calls=%async_computation.4 | async-start | bytes 5242880 | tf_op jit(solution)/shard_map/reduce_scatter | solution.py:73
  75.6 136.0 %all-gather.6.cloned.1.call-start = ((), (), s32[]{:S(2)}) async-start(), calls=%async_computation.5 | async-start | bytes 2621440 | tf_op jit(solution)/shard_map/all_gather | solution.py:88
  152.6 12.1 %copy-start.1 = (f32[1,16,128,128]{3,2,1,0:T(8,128)S(1)}, f32[1,16,128,128]{3,2,1,0:T(8,128)}, u32[]{:S(2)}) copy-start(f32[1,16,128,128]{3,2,1,0:T(8,128)} %reduce-scatter.2.cloned.1.call-done) | copy-start | bytes 3145732
  226.7 1.9 copy-start.2
  230.1 4.4 %collective-permute-start = (f32[2,2,64,2048]{3,2,1,0:T(8,128)}, f32[2,2,64,2048]{3,2,1,0:T(8,128)S(1)}, u32[]{:S(2)}, u32[]{:S(2)}) collective-permute-start(f32[2,2,64,2048]{3,2,1,0:T(8,128)} %dynamic-slice_bitcast_fusion), channel_id=1, source_target_pairs={{0,1},{1,0},{2,3},{3,2},{4,5},{5,4},{6,7},{7,6},{8,9},{9,8},{10,11... | collective-permute-start | bytes 6291464 | tf_op jit(solution)/shard_map/summed_core_stage/ppermute | solution.py:18
  237.4 14.2 %collective-permute-start.3 = (f32[2,64,1024]{2,1,0:T(8,128)}, f32[2,64,1024]{2,1,0:T(8,128)S(1)}, u32[]{:S(2)}, u32[]{:S(2)}) collective-permute-start(f32[2,64,1024]{2,1,0:T(8,128)} %dynamic-slice_bitcast_fusion.1), channel_id=1, source_target_pairs={{0,4},{1,5},{2,6},{3,7},{4,0},{5,1},{6,2},{7,3},{8,12},{9,13},{10,... | collective-permute-start | bytes 1572872 | tf_op jit(solution)/shard_map/summed_chip_stage/ppermute | solution.py:18
  239.7 13.9 %collective-permute-start.1 = (f32[2,64,1024]{2,1,0:T(8,128)}, f32[2,64,1024]{2,1,0:T(8,128)S(1)}, u32[]{:S(2)}, u32[]{:S(2)}) collective-permute-start(f32[2,64,1024]{2,1,0:T(8,128)} %dynamic-slice_bitcast_fusion.2), channel_id=1, source_target_pairs={{0,2},{1,3},{2,0},{3,1},{4,6},{5,7},{6,4},{7,5},{8,10},{9,11},{10,... | collective-permute-start | bytes 1572872 | tf_op jit(solution)/shard_map/summed_chip_stage/ppermute | solution.py:18
  251.7 7.6 %collective-permute-start.4 = (f32[64,1024]{1,0:T(8,128)S(1)}, f32[64,1024]{1,0:T(8,128)S(1)}, u32[]{:S(2)}, u32[]{:S(2)}) collective-permute-start(f32[64,1024]{1,0:T(8,128)S(1)} %dynamic-slice_bitcast_fusion.3), channel_id=1, source_target_pairs={{0,2},{1,3},{2,0},{3,1},{4,6},{5,7},{6,4},{7,5},{8,10},{9,11},{10,... | collective-permute-start | bytes 786440 | tf_op jit(solution)/shard_map/summed_chip_stage/ppermute | solution.py:18
  253.7 7.3 %collective-permute-start.2 = (f32[64,1024]{1,0:T(8,128)S(1)}, f32[64,1024]{1,0:T(8,128)S(1)}, u32[]{:S(2)}, u32[]{:S(2)}) collective-permute-start(f32[64,1024]{1,0:T(8,128)S(1)} %dynamic-slice_bitcast_fusion.4), channel_id=1, source_target_pairs={{0,4},{1,5},{2,6},{3,7},{4,0},{5,1},{6,2},{7,3},{8,12},{9,13},{10,... | collective-permute-start | bytes 786440 | tf_op jit(solution)/shard_map/summed_chip_stage/ppermute | solution.py:18
Sparse Core Ops, SparseCore 0:
  33.1 25.5 all-gather.3
  75.8 76.7 reduce-scatter.1
  166.4 45.2 all-gather.5

commit v4 on v3

--- a/solution.py
+++ b/solution.py
@@ -39,6 +39,47 @@
     return jnp.concatenate([first, second], axis=-1)
 
 
+def permute_all_to_all(x, axis_name, n, split_axis, concat_axis):
+    me = lax.axis_index(axis_name)
+    pieces = jnp.stack(jnp.split(x, n, axis=split_axis))
+    got = [lax.dynamic_index_in_dim(pieces, me, axis=0, keepdims=False)]
+    for shift in range(1, n):
+        send = lax.dynamic_index_in_dim(pieces, (me + shift) % n, axis=0, keepdims=False)
+        perm = [(s, (s + shift) % n) for s in range(n)]
+        got.append(lax.ppermute(send, axis_name, perm=perm))
+    received = jnp.stack(got)
+    order = (me - jnp.arange(n, dtype=jnp.int32)) % n
+    by_source = jnp.take(received, order, axis=0)
+    return jnp.concatenate([by_source[k] for k in range(n)], axis=concat_axis)
+
+
+def gather_stage(x, have, bit, n):
+    me = lax.axis_index("vocab")
+    mine = (me // (1 << bit)) % 2
+    perm = [(s, s ^ (1 << bit)) for s in range(n)]
+    got = lax.ppermute(x, "vocab", perm=perm)
+    pos = len([b for b in have if b > bit])
+    low = jnp.stack([x, got], axis=pos)
+    high = jnp.stack([got, x], axis=pos)
+    return jnp.where(mine == 0, low, high), sorted(have + [bit], reverse=True)
+
+
+def doubling_all_gather(x, n):
+    levels = n.bit_length() - 1
+    rows, cols = x.shape
+    half = cols // 2
+    first, second = x[:, :half], x[:, half:]
+    have_a, have_b = [], []
+    order_a = list(range(1, levels)) + [0]
+    order_b = list(range(levels - 1, 0, -1)) + [0]
+    for step in range(levels):
+        with jax.named_scope("hidden_gather_stage"):
+            first, have_a = gather_stage(first, have_a, order_a[step], n)
+            second, have_b = gather_stage(second, have_b, order_b[step], n)
+    joined = jnp.concatenate([first, second], axis=-1)
+    return joined.reshape(n * rows, cols)
+
+
 def per_device(hidden, out_weight, token_blocks, counts):
     vocab_here, columns_here = out_weight.shape
     n_tb = vocab_here // TB
@@ -52,9 +93,9 @@
     n_vocab = lax.psum(1, "vocab")
     n_dp = lax.psum(1, "dp")
     with jax.named_scope("hidden_spread"):
-        row_slices = lax.all_to_all(hidden, "vocab", split_axis=0, concat_axis=1, tiled=True)
-        plane_rows = lax.all_to_all(row_slices, "dp", split_axis=1, concat_axis=0, tiled=True)
-        gathered = lax.all_gather(plane_rows, "vocab", axis=0, tiled=True)
+        row_slices = permute_all_to_all(hidden, "vocab", n_vocab, split_axis=0, concat_axis=1)
+        plane_rows = permute_all_to_all(row_slices, "dp", n_dp, split_axis=1, concat_axis=0)
+        gathered = doubling_all_gather(plane_rows, n_vocab)
         group = hidden.shape[0] // n_vocab
         beam_columns = (
             gathered.reshape(n_vocab, n_dp, group, columns_here)

time: 279 us -> 271 us (0.971)
  blocking collectives: 43.6 us -> 18.6 us
  starting transfers between devices: 5.77 us -> 23.4 us
  waiting for transfers between devices: 168 us -> 161 us
  local copies, waits for them, and re-layouts: 16.3 us -> 22.8 us
    all_gather x1 -> x0, waiting for transfers between devices: 25.6 us -> none  [per_device(): gathered = lax.all_gather(plane_rows, 'vocab', axis=0, tiled=True)]
    all_to_all x2 -> x0, blocking collectives: 25.2 us -> none  [the longest x1 13.1 us: per_device(): lax.all_to_all(row_slices, 'dp', split_axis=1, concat_axis=0, tiled=True)]
    ppermute x0 -> x16, waiting for transfers between devices: none -> 19.8 us  [the longest x6 12 us: gather_stage(): got = lax.ppermute(x, 'vocab', perm=perm)]
    ppermute x0 -> x16, starting transfers between devices: none -> 17.7 us  [the longest x10 14.5 us: permute_all_to_all(): got.append(lax.ppermute(send, axis_name, perm=perm))]
    unnamed x8 -> x27, local copies, waits for them, and re-layouts: 1.95 us -> 8.34 us
  transfers between devices with their start and end apart: 8 -> 23, of which waited for: 8 -> 16; matrix products, arithmetic and copies ran while one was open for 1% -> 1% of each run, Pallas kernels for 0% -> 0%
where the time goes in v4:
time: 271 us; the launch traced here: 270 us
  waiting for transfers between devices  161 us (59%)
  starting transfers between devices  23.4 us (9%)
  local copies, waits for them, and re-layouts  22.8 us (8%)
  matrix products  19.6 us (7%)
  blocking collectives  18.6 us (7%)
  between operations  14.7 us (5%)
  other arithmetic  9.94 us (4%)
    reduce_scatter x1, waiting for transfers between devices, per_device(): logits = lax.psum_scatter(picked, 'dp', scatter_dimension=0, tiled=True)  74.4 us
    all_gather x1, waiting for transfers between devices, per_device(): prob_part = lax.all_gather(probabilities, 'dp', axis=0, tiled=True)  45.4 us
    ppermute x5, waiting for transfers between devices, exchange_stage(): got = lax.ppermute(send, 'vocab', perm=perm)  21.2 us
    ppermute x10, starting transfers between devices, permute_all_to_all(): got.append(lax.ppermute(send, axis_name, perm=perm))  14.5 us
    ppermute x6, waiting for transfers between devices, gather_stage(): got = lax.ppermute(x, 'vocab', perm=perm)  12 us
    psum x1, blocking collectives, per_device(): squares = lax.psum(jnp.sum(summed * summed, axis=1), 'dp')  9.51 us
    all_gather x1, blocking collectives, per_device(): stats = lax.all_gather(jnp.stack([local_max, local_total]), 'vocab', axis=0)  9.08 us
    dot_general x1, matrix products, per_device(): jnp.einsum('bv,vd->bd', spread.reshape(n_blk * BB, n_tb * TB), out_weight...  8.98 us
  transfers between devices with their start and end apart: 23, of which 16 were waited for; matrix products, arithmetic and copies ran while one was open for 1% of the time, Pallas kernels for 0%

profile of v4, /device:TPU:0, one launch (start us, length us, event | category | flops | bytes accessed | tf_op | source)
XLA Modules:
  0.0 270.0 jit_solution(8672514940731182547)
XLA Ops:
  7.3 0.8 constant_dynamic-update-slice_fusion.7
  8.1 0.8 constant_dynamic-update-slice_fusion.6
  8.8 0.8 constant_dynamic-update-slice_fusion.5
  9.6 0.8 constant_dynamic-update-slice_fusion.4
  10.4 0.8 constant_dynamic-update-slice_fusion.3
  11.1 0.8 constant_dynamic-update-slice_fusion.2
  11.9 0.8 constant_dynamic-update-slice_fusion.1
  12.6 0.8 constant_dynamic-update-slice_fusion
  13.4 0.5 collective-permute-start
  14.0 2.5 collective-permute-start.1
  16.5 2.4 collective-permute-start.2
  18.9 0.5 collective-permute-start.3
  19.6 1.5 collective-permute-start.5
  21.1 2.3 collective-permute-start.6
  23.5 0.2 collective-permute-done.5
  23.7 1.3 collective-permute-done.6
  25.0 0.6 gather_fusion
  25.9 3.7 %collective-permute-start.9 = (bf16[16,2048]{1,0:T(8,128)(2,1)S(1)}, bf16[16,2048]{1,0:T(8,128)(2,1)S(1)}, u32[]{:S(2)}, u32[]{:S(2)}) collective-permute-start(bf16[16,2048]{1,0:T(8,128)(2,1)S(1)} %get-tuple-element.21), channel_id=1, source_target_pairs={{0,24},{8,0},{16,8},{24,16},{1,25},{9,1},{17,9},{25,17},{2,26},{10... | collective-permute-start | bytes 196616 | tf_op jit(solution)/shard_map/hidden_spread/ppermute | solution.py:49
  29.5 1.0 collective-permute-start.7
  30.5 1.5 collective-permute-done.9
  32.0 4.8 %collective-permute-done.8 = bf16[16,2048]{1,0:T(8,128)(2,1)S(1)} collective-permute-done((bf16[16,2048]{1,0:T(8,128)(2,1)S(1)}, bf16[16,2048]{1,0:T(8,128)(2,1)S(1)}, u32[]{:S(2)}, u32[]{:S(2)}) %collective-permute-start.8) | collective-permute-done | bytes 65568 | tf_op jit(solution)/shard_map/hidden_spread/ppermute | solution.py:49
  36.9 0.6 gather_fusion.1
  37.7 0.6 collective-permute-start.13
  38.3 0.7 collective-permute-start.10
  39.2 4.1 %collective-permute-done.13 = bf16[64,1024]{1,0:T(8,128)(2,1)S(1)} collective-permute-done((bf16[64,1024]{1,0:T(8,128)(2,1)S(1)}, bf16[64,1024]{1,0:T(8,128)(2,1)S(1)}, u32[]{:S(2)}, u32[]{:S(2)}) %collective-permute-start.13) | collective-permute-done | bytes 131104 | tf_op jit(solution)/shard_map/hidden_spread/hidden_gather_stage/ppermute | solution.py:60
  43.3 1.3 collective-permute-start.14
  44.6 0.5 collective-permute-start.11
  45.2 5.6 %collective-permute-done.14 = bf16[2,64,1024]{2,1,0:T(8,128)(2,1)S(1)} collective-permute-done((bf16[2,64,1024]{2,1,0:T(8,128)(2,1)S(1)}, bf16[2,64,1024]{2,1,0:T(8,128)(2,1)S(1)}, u32[]{:S(2)}, u32[]{:S(2)}) %collective-permute-start.14) | collective-permute-done | bytes 262176 | tf_op jit(solution)/shard_map/hidden_spread/hidden_gather_stage/ppermute | solution.py:60
  50.9 0.9 collective-permute-done.11
  52.2 0.6 collective-permute-done.15
  52.8 0.2 maximum_select_fusion.1
  53.1 0.8 collective-permute-done.12
  54.0 0.2 maximum_bitcast_fusion
  54.2 0.2 copy.25
  54.5 1.0 slice-done.2
  55.5 7.4 %fusion.19 = f32[4,128,19,128]{3,1,2,0:T(8,128)} fusion(bf16[4,128,2048,1]{2,1,3,0:T(8,128)(2,1)S(1)} %bitcast.185, bf16[19,128,2048,1]{2,1,0,3:T(8,128)(2,1)S(1)} %bitcast.210), kind=kOutput, calls=%fused_computation.130 | convolution fusion | flops 5100273664 | bytes 17039360 | tf_op jit(solution)/shard_map/dense_logits/bd,vd->bv/dot_general | solution.py:107
  62.9 5.3 %gather_fusion.2 = f32[64,128,128]{2,1,0:T(8,128)} fusion(f32[4,128,19,128]{3,1,2,0:T(8,128)} %fusion.19, s32[64]{0:T(128)S(1)} %reshape.615), kind=kCustom, calls=%fused_computation.2 | custom fusion | bytes 8389120 | tf_op jit(solution)/shard_map/dense_logits/gather | solution.py:112
  68.2 0.6 constant_dynamic-slice_fusion.1
  68.8 0.6 iota_compare_fusion.1
  69.4 74.4 %reduce-scatter.2.cloned.1.call-done = f32[1,16,128,128]{3,2,1,0:T(8,128)} async-done(((f32[4,16,128,128]{3,2,1,0:T(8,128)}), f32[1,16,128,128]{3,2,1,0:T(8,128)}) %reduce-scatter.2.cloned.1.call-update) | async-done | bytes 1048592 | tf_op jit(solution)/shard_map/reduce_scatter | solution.py:114
  143.8 1.5 select_reduce_fusion
  145.4 1.6 exponential_reduce_fusion
  146.9 9.1 %all-gather = f32[16,1,128]{2,1,0:T(1,128)S(1)} all-gather(f32[2,1,128]{2,1,0:T(1,128)S(1)} %pad_maximum_fusion.4), channel_id=2, replica_groups=mesh['dp'=4,'vocab'=8] {'vocab'}, dimensions={0}, use_global_device_ids=true | all-gather | bytes 9216 | tf_op jit(solution)/shard_map/softmax_stats/all_gather | solution.py:122
  156.1 1.6 select_convert_fusion
  157.7 45.4 %all-gather.3.cloned.1.call-done = bf16[4,16,128,128]{3,2,1,0:T(8,128)(2,1)} async-done(((bf16[1,16,128,128]{3,2,1,0:T(8,128)(2,1)}), bf16[4,16,128,128]{3,2,1,0:T(8,128)(2,1)}) %all-gather.3.cloned.1.call-update) | async-done | bytes 2097168 | tf_op jit(solution)/shard_map/all_gather | solution.py:129
  203.1 3.3 %convert_bitcast_fusion = bf16[4,128,19,128]{3,2,1,0:T(8,128)(2,1)S(1)} fusion(bf16[4,16,128,128]{3,2,1,0:T(8,128)(2,1)} %all-gather.3.cloned.1.call-done, s32[4,16]{1,0:T(4,128)S(1)} %bitcast.205), kind=kOutput, calls=%fused_computation.5 | convolution fusion | flops 41092288 | bytes 4587776 | tf_op jit(solution)/shard_map/dense_expected/bsk,bsrt->brkt/dot_general | solution.py:135
  206.4 2.8 %dot_general.19 = bf16[2,2,2,64,2432]{4,3,2,1,0:T(8,128)(2,1)} reshape(bf16[4,128,19,128]{3,2,1,0:T(8,128)(2,1)S(1)} %convert_bitcast_fusion) | data formatting | bytes 4980736 | tf_op jit(solution)/shard_map/dense_expected/bv,vd->bd/dot_general | solution.py:138
  209.2 9.0 %fusion = f32[2,2,2,64,2048]{4,3,2,1,0:T(8,128)S(1)} fusion(bf16[2,2,2,64,2432]{4,3,2,1,0:T(8,128)(2,1)} %dot_general.19, bf16[2432,2048]{1,0:T(8,128)(2,1)} %param.5), kind=kOutput, calls=%fused_computation.3 | convolution fusion | flops 5100273664 | bytes 16646144 | tf_op jit(solution)/shard_map/dense_expected/bv,vd->bd/dot_general | solution.py:138
  218.2 1.9 copy-done.2
  220.1 1.5 dynamic-slice_bitcast_fusion
  221.6 4.4 %collective-permute-done.16 = f32[2,2,64,2048]{3,2,1,0:T(8,128)S(1)} collective-permute-done((f32[2,2,64,2048]{3,2,1,0:T(8,128)}, f32[2,2,64,2048]{3,2,1,0:T(8,128)S(1)}, u32[]{:S(2)}, u32[]{:S(2)}) %collective-permute-start.16) | collective-permute-done | bytes 2097184 | tf_op jit(solution)/shard_map/summed_core_stage/ppermute | solution.py:18
  226.0 2.0 bitcast_add_fusion
  228.1 0.8 dynamic-slice_bitcast_fusion.1
  228.9 1.5 collective-permute-start.19
  230.4 0.8 dynamic-slice_bitcast_fusion.2
  231.3 1.5 collective-permute-start.17
  232.7 10.4 %collective-permute-done.19 = f32[2,64,1024]{2,1,0:T(8,128)S(1)} collective-permute-done((f32[2,64,1024]{2,1,0:T(8,128)}, f32[2,64,1024]{2,1,0:T(8,128)S(1)}, u32[]{:S(2)}, u32[]{:S(2)}) %collective-permute-start.19) | collective-permute-done | bytes 524320 | tf_op jit(solution)/shard_map/summed_chip_stage/ppermute | solution.py:18
  243.2 1.5 collective-permute-start.20
  244.8 0.4 collective-permute-done.17
  245.3 1.2 collective-permute-start.18
  246.4 4.4 %collective-permute-done.20 = f32[64,1024]{1,0:T(8,128)S(1)} collective-permute-done((f32[64,1024]{1,0:T(8,128)S(1)}, f32[64,1024]{1,0:T(8,128)S(1)}, u32[]{:S(2)}, u32[]{:S(2)}) %collective-permute-start.20) | collective-permute-done | bytes 262176 | tf_op jit(solution)/shard_map/summed_chip_stage/ppermute | solution.py:18
  250.8 1.7 collective-permute-done.18
  252.7 9.5 %psum.7 = f32[64]{0:T(128)S(1)} all-reduce(f32[64]{0:T(128)S(1)} %multiply_reduce_fusion), channel_id=1, replica_groups=mesh['dp'=4,'vocab'=8] {'dp'}, use_global_device_ids=true, to_apply=%region_6.7 | all-reduce | flops 64 | bytes 512 | tf_op jit(solution)/shard_map/psum | solution.py:145
  262.2 0.9 fusion.4
  (82 shorter events, 2.4 us)
Async XLA Ops:
  7.2 61.0 %copy-start = (s32[1,4]{1,0:T(1,128)S(1)}, s32[1,4]{1,0:T(1,128)}, u32[]{:S(2)}) copy-start(s32[1,4]{1,0:T(1,128)} %param.7) | copy-start | bytes 52
  7.2 136.7 %reduce-scatter.2.cloned.1.call-start = ((), (), s32[]{:S(2)}) async-start(), calls=%async_computation.1 | async-start | bytes 5242880 | tf_op jit(solution)/shard_map/reduce_scatter | solution.py:114
  13.4 6.2 %collective-permute-start = (bf16[16,1024]{1,0:T(8,128)(2,1)S(1)}, bf16[16,1024]{1,0:T(8,128)(2,1)S(1)}, u32[]{:S(2)}, u32[]{:S(2)}) collective-permute-start(bf16[16,1024]{1,0:T(8,128)(2,1)S(1)} %get-tuple-element.38), channel_id=1, source_target_pairs={{0,1},{1,2},{2,3},{3,4},{4,5},{5,6},{6,7},{7,0},{8,9},{9,10},{10,1... | collective-permute-start | bytes 98312 | tf_op jit(solution)/shard_map/hidden_spread/ppermute | solution.py:49
  14.0 7.2 %collective-permute-start.1 = (bf16[16,1024]{1,0:T(8,128)(2,1)S(1)}, bf16[16,1024]{1,0:T(8,128)(2,1)S(1)}, u32[]{:S(2)}, u32[]{:S(2)}) collective-permute-start(bf16[16,1024]{1,0:T(8,128)(2,1)S(1)} %get-tuple-element.37), channel_id=1, source_target_pairs={{0,2},{1,3},{2,4},{3,5},{4,6},{5,7},{6,0},{7,1},{8,10},{9,11},{10,... | collective-permute-start | bytes 98312 | tf_op jit(solution)/shard_map/hidden_spread/ppermute | solution.py:49
  16.5 6.9 %collective-permute-start.2 = (bf16[16,1024]{1,0:T(8,128)(2,1)S(1)}, bf16[16,1024]{1,0:T(8,128)(2,1)S(1)}, u32[]{:S(2)}, u32[]{:S(2)}) collective-permute-start(bf16[16,1024]{1,0:T(8,128)(2,1)S(1)} %get-tuple-element.36), channel_id=1, source_target_pairs={{0,3},{1,4},{2,5},{3,6},{4,7},{5,0},{6,1},{7,2},{8,11},{9,12},{10,... | collective-permute-start | bytes 98312 | tf_op jit(solution)/shard_map/hidden_spread/ppermute | solution.py:49
  18.9 4.6 %collective-permute-start.3 = (bf16[16,1024]{1,0:T(8,128)(2,1)S(1)}, bf16[16,1024]{1,0:T(8,128)(2,1)S(1)}, u32[]{:S(2)}, u32[]{:S(2)}) collective-permute-start(bf16[16,1024]{1,0:T(8,128)(2,1)S(1)} %get-tuple-element.35), channel_id=1, source_target_pairs={{0,4},{1,5},{2,6},{3,7},{4,0},{5,1},{6,2},{7,3},{8,12},{9,13},{10,... | collective-permute-start | bytes 98312 | tf_op jit(solution)/shard_map/hidden_spread/ppermute | solution.py:49
  19.4 4.1 %collective-permute-start.4 = (bf16[16,1024]{1,0:T(8,128)(2,1)S(1)}, bf16[16,1024]{1,0:T(8,128)(2,1)S(1)}, u32[]{:S(2)}, u32[]{:S(2)}) collective-permute-start(bf16[16,1024]{1,0:T(8,128)(2,1)S(1)} %get-tuple-element.34), channel_id=1, source_target_pairs={{0,5},{1,6},{2,7},{3,0},{4,1},{5,2},{6,3},{7,4},{8,13},{9,14},{10,... | collective-permute-start | bytes 98312 | tf_op jit(solution)/shard_map/hidden_spread/ppermute | solution.py:49
  19.6 4.1 %collective-permute-start.5 = (bf16[16,1024]{1,0:T(8,128)(2,1)S(1)}, bf16[16,1024]{1,0:T(8,128)(2,1)S(1)}, u32[]{:S(2)}, u32[]{:S(2)}) collective-permute-start(bf16[16,1024]{1,0:T(8,128)(2,1)S(1)} %get-tuple-element.33), channel_id=1, source_target_pairs={{0,6},{1,7},{2,0},{3,1},{4,2},{5,3},{6,4},{7,5},{8,14},{9,15},{10,... | collective-permute-start | bytes 98312 | tf_op jit(solution)/shard_map/hidden_spread/ppermute | solution.py:49
  21.1 3.9 %collective-permute-start.6 = (bf16[16,1024]{1,0:T(8,128)(2,1)S(1)}, bf16[16,1024]{1,0:T(8,128)(2,1)S(1)}, u32[]{:S(2)}, u32[]{:S(2)}) collective-permute-start(bf16[16,1024]{1,0:T(8,128)(2,1)S(1)} %get-tuple-element.32), channel_id=1, source_target_pairs={{0,7},{1,0},{2,1},{3,2},{4,3},{5,4},{6,5},{7,6},{8,15},{9,8},{10,9... | collective-permute-start | bytes 98312 | tf_op jit(solution)/shard_map/hidden_spread/ppermute | solution.py:49
  25.7 13.3 %copy-start.3 = (s32[1,4,16]{2,1,0:T(4,128)S(1)}, s32[1,4,16]{2,1,0:T(4,128)}, u32[]{:S(2)}) copy-start(s32[1,4,16]{2,1,0:T(4,128)} %param.6) | copy-start | bytes 772
  25.9 6.2 %collective-permute-start.9 = (bf16[16,2048]{1,0:T(8,128)(2,1)S(1)}, bf16[16,2048]{1,0:T(8,128)(2,1)S(1)}, u32[]{:S(2)}, u32[]{:S(2)}) collective-permute-start(bf16[16,2048]{1,0:T(8,128)(2,1)S(1)} %get-tuple-element.21), channel_id=1, source_target_pairs={{0,24},{8,0},{16,8},{24,16},{1,25},{9,1},{17,9},{25,17},{2,26},{10... | collective-permute-start | bytes 196616 | tf_op jit(solution)/shard_map/hidden_spread/ppermute | solution.py:49
  29.5 7.3 %collective-permute-start.8 = (bf16[16,2048]{1,0:T(8,128)(2,1)S(1)}, bf16[16,2048]{1,0:T(8,128)(2,1)S(1)}, u32[]{:S(2)}, u32[]{:S(2)}) collective-permute-start(bf16[16,2048]{1,0:T(8,128)(2,1)S(1)} %get-tuple-element.22), channel_id=1, source_target_pairs={{0,16},{8,24},{16,0},{24,8},{1,17},{9,25},{17,1},{25,9},{2,18},{10... | collective-permute-start | bytes 196616 | tf_op jit(solution)/shard_map/hidden_spread/ppermute | solution.py:49
  29.5 7.3 %collective-permute-start.7 = (bf16[16,2048]{1,0:T(8,128)(2,1)S(1)}, bf16[16,2048]{1,0:T(8,128)(2,1)S(1)}, u32[]{:S(2)}, u32[]{:S(2)}) collective-permute-start(bf16[16,2048]{1,0:T(8,128)(2,1)S(1)} %get-tuple-element.23), channel_id=1, source_target_pairs={{0,8},{8,16},{16,24},{24,0},{1,9},{9,17},{17,25},{25,1},{2,10},{10... | collective-permute-start | bytes 196616 | tf_op jit(solution)/shard_map/hidden_spread/ppermute | solution.py:49
  37.7 5.5 %collective-permute-start.13 = (bf16[64,1024]{1,0:T(8,128)(2,1)S(1)}, bf16[64,1024]{1,0:T(8,128)(2,1)S(1)}, u32[]{:S(2)}, u32[]{:S(2)}) collective-permute-start(bf16[64,1024]{1,0:T(8,128)(2,1)S(1)} %get-tuple-element.14), channel_id=1, source_target_pairs={{0,4},{1,5},{2,6},{3,7},{4,0},{5,1},{6,2},{7,3},{8,12},{9,13},{10,... | collective-permute-start | bytes 393224 | tf_op jit(solution)/shard_map/hidden_spread/hidden_gather_stage/ppermute | solution.py:60
  38.3 6.3 %collective-permute-start.10 = (bf16[64,1024]{1,0:T(8,128)(2,1)S(1)}, bf16[64,1024]{1,0:T(8,128)(2,1)S(1)}, u32[]{:S(2)}, u32[]{:S(2)}) collective-permute-start(bf16[64,1024]{1,0:T(8,128)(2,1)S(1)} %get-tuple-element.15), channel_id=1, source_target_pairs={{0,2},{1,3},{2,0},{3,1},{4,6},{5,7},{6,4},{7,5},{8,10},{9,11},{10,... | collective-permute-start | bytes 393224 | tf_op jit(solution)/shard_map/hidden_spread/hidden_gather_stage/ppermute | solution.py:60
  43.2 11.2 %slice-start = ((s8[9961472]{0:T(1024)(128)(4,1)}), s8[4194304]{0:T(1024)(128)(4,1)S(1)}, s32[]{:S(2)}) async-start(s8[9961472]{0:T(1024)(128)(4,1)} %bitcast.208), calls=%async_computation.3 | async-start | bytes 8388608
  43.3 7.5 %collective-permute-start.14 = (bf16[2,64,1024]{2,1,0:T(8,128)(2,1)S(1)}, bf16[2,64,1024]{2,1,0:T(8,128)(2,1)S(1)}, u32[]{:S(2)}, u32[]{:S(2)}) collective-permute-start(bf16[2,64,1024]{2,1,0:T(8,128)(2,1)S(1)} %maximum_select_fusion.8), channel_id=1, source_target_pairs={{0,2},{1,3},{2,0},{3,1},{4,6},{5,7},{6,4},{7,5},{8,10},{9,11},{10,... | collective-permute-start | bytes 786440 | tf_op jit(solution)/shard_map/hidden_spread/hidden_gather_stage/ppermute | solution.py:60
  44.6 7.3 %collective-permute-start.11 = (bf16[2,64,1024]{2,1,0:T(8,128)(2,1)S(1)}, bf16[2,64,1024]{2,1,0:T(8,128)(2,1)S(1)}, u32[]{:S(2)}, u32[]{:S(2)}) collective-permute-start(bf16[2,64,1024]{2,1,0:T(8,128)(2,1)S(1)} %maximum_select_fusion.6), channel_id=1, source_target_pairs={{0,4},{1,5},{2,6},{3,7},{4,0},{5,1},{6,2},{7,3},{8,12},{9,13},{10,... | collective-permute-start | bytes 786440 | tf_op jit(solution)/shard_map/hidden_spread/hidden_gather_stage/ppermute | solution.py:60
  50.8 2.0 collective-permute-start.15
  51.9 2.0 collective-permute-start.12
  52.1 2.3 slice-start.1
  54.0 1.5 slice-start.2
  68.1 135.0 %all-gather.3.cloned.1.call-start = ((), (), s32[]{:S(2)}) async-start(), calls=%async_computation.2 | async-start | bytes 2621440 | tf_op jit(solution)/shard_map/all_gather | solution.py:129
  143.8 12.2 %copy-start.1 = (f32[1,16,128,128]{3,2,1,0:T(8,128)S(1)}, f32[1,16,128,128]{3,2,1,0:T(8,128)}, u32[]{:S(2)}) copy-start(f32[1,16,128,128]{3,2,1,0:T(8,128)} %reduce-scatter.2.cloned.1.call-done) | copy-start | bytes 3145732
  218.2 1.9 copy-start.2
  221.6 4.4 %collective-permute-start.16 = (f32[2,2,64,2048]{3,2,1,0:T(8,128)}, f32[2,2,64,2048]{3,2,1,0:T(8,128)S(1)}, u32[]{:S(2)}, u32[]{:S(2)}) collective-permute-start(f32[2,2,64,2048]{3,2,1,0:T(8,128)} %dynamic-slice_bitcast_fusion), channel_id=1, source_target_pairs={{0,1},{1,0},{2,3},{3,2},{4,5},{5,4},{6,7},{7,6},{8,9},{9,8},{10,11... | collective-permute-start | bytes 6291464 | tf_op jit(solution)/shard_map/summed_core_stage/ppermute | solution.py:18
  228.9 14.2 %collective-permute-start.19 = (f32[2,64,1024]{2,1,0:T(8,128)}, f32[2,64,1024]{2,1,0:T(8,128)S(1)}, u32[]{:S(2)}, u32[]{:S(2)}) collective-permute-start(f32[2,64,1024]{2,1,0:T(8,128)} %dynamic-slice_bitcast_fusion.1), channel_id=1, source_target_pairs={{0,4},{1,5},{2,6},{3,7},{4,0},{5,1},{6,2},{7,3},{8,12},{9,13},{10,... | collective-permute-start | bytes 1572872 | tf_op jit(solution)/shard_map/summed_chip_stage/ppermute | solution.py:18
  231.3 13.9 %collective-permute-start.17 = (f32[2,64,1024]{2,1,0:T(8,128)}, f32[2,64,1024]{2,1,0:T(8,128)S(1)}, u32[]{:S(2)}, u32[]{:S(2)}) collective-permute-start(f32[2,64,1024]{2,1,0:T(8,128)} %dynamic-slice_bitcast_fusion.2), channel_id=1, source_target_pairs={{0,2},{1,3},{2,0},{3,1},{4,6},{5,7},{6,4},{7,5},{8,10},{9,11},{10,... | collective-permute-start | bytes 1572872 | tf_op jit(solution)/shard_map/summed_chip_stage/ppermute | solution.py:18
  243.2 7.6 %collective-permute-start.20 = (f32[64,1024]{1,0:T(8,128)S(1)}, f32[64,1024]{1,0:T(8,128)S(1)}, u32[]{:S(2)}, u32[]{:S(2)}) collective-permute-start(f32[64,1024]{1,0:T(8,128)S(1)} %dynamic-slice_bitcast_fusion.3), channel_id=1, source_target_pairs={{0,2},{1,3},{2,0},{3,1},{4,6},{5,7},{6,4},{7,5},{8,10},{9,11},{10,... | collective-permute-start | bytes 786440 | tf_op jit(solution)/shard_map/summed_chip_stage/ppermute | solution.py:18
  245.3 7.3 %collective-permute-start.18 = (f32[64,1024]{1,0:T(8,128)S(1)}, f32[64,1024]{1,0:T(8,128)S(1)}, u32[]{:S(2)}, u32[]{:S(2)}) collective-permute-start(f32[64,1024]{1,0:T(8,128)S(1)} %dynamic-slice_bitcast_fusion.4), channel_id=1, source_target_pairs={{0,4},{1,5},{2,6},{3,7},{4,0},{5,1},{6,2},{7,3},{8,12},{9,13},{10,... | collective-permute-start | bytes 786440 | tf_op jit(solution)/shard_map/summed_chip_stage/ppermute | solution.py:18
Sparse Core Ops, SparseCore 0:
  68.3 75.5 reduce-scatter.1
  157.8 45.2 all-gather.2

commit v5 on v4

--- a/solution.py
+++ b/solution.py
@@ -41,7 +41,9 @@
 
 def permute_all_to_all(x, axis_name, n, split_axis, concat_axis):
     me = lax.axis_index(axis_name)
-    pieces = jnp.stack(jnp.split(x, n, axis=split_axis))
+    shape = list(x.shape)
+    shape[split_axis : split_axis + 1] = [n, x.shape[split_axis] // n]
+    pieces = jnp.moveaxis(x.reshape(shape), split_axis, 0)
     got = [lax.dynamic_index_in_dim(pieces, me, axis=0, keepdims=False)]
     for shift in range(1, n):
         send = lax.dynamic_index_in_dim(pieces, (me + shift) % n, axis=0, keepdims=False)
@@ -80,6 +82,60 @@
     return joined.reshape(n * rows, cols)
 
 
+def small_all_gather(x, n):
+    levels = n.bit_length() - 1
+    have = []
+    y = x
+    for bit in range(levels):
+        y, have = gather_stage(y, have, bit, n)
+    return y.reshape((n,) + x.shape)
+
+
+def butterfly_sum(x, axis_name, n):
+    levels = n.bit_length() - 1
+    for bit in range(levels):
+        perm = [(s, s ^ (1 << bit)) for s in range(n)]
+        x = x + lax.ppermute(x, axis_name, perm=perm)
+    return x
+
+
+def spread_block(probs_block, tokens, n_tb):
+    onehot = (tokens[:, None] == jnp.arange(n_tb, dtype=jnp.int32)[None, :]).astype(
+        jnp.bfloat16
+    )
+    spread = jnp.einsum(
+        "sk,srt->rkt", onehot, probs_block, preferred_element_type=jnp.float32
+    ).astype(jnp.bfloat16)
+    return spread.reshape(spread.shape[0], -1)
+
+
+def ring_expected(own_probs, block_lists, out_weight, n, n_blk, n_tb):
+    me = lax.axis_index("dp")
+    columns = out_weight.shape[1]
+    rows_per = own_probs.shape[1]
+    acc = jnp.zeros((n_blk, rows_per, columns), jnp.float32)
+
+    def add_piece(acc, piece, block):
+        block = jnp.clip(block, 0, n - 1)
+        tokens = lax.dynamic_index_in_dim(block_lists, block, axis=0, keepdims=False)
+        term = jnp.dot(
+            spread_block(piece, tokens, n_tb), out_weight, preferred_element_type=jnp.float32
+        )
+        old = lax.dynamic_index_in_dim(acc, block, axis=0, keepdims=False)
+        return lax.dynamic_update_index_in_dim(acc, old + term, block, axis=0)
+
+    acc = add_piece(acc, own_probs, me)
+    from_left, from_right = own_probs, own_probs
+    for step in range(1, n):
+        rightward = [(s, s + 1) for s in range(step - 1, n - 1)]
+        leftward = [(s, s - 1) for s in range(1, n - step + 1)]
+        from_left = lax.ppermute(from_left, "dp", perm=rightward)
+        from_right = lax.ppermute(from_right, "dp", perm=leftward)
+        acc = add_piece(acc, from_left, me - step)
+        acc = add_piece(acc, from_right, me + step)
+    return acc.reshape(n_blk * rows_per, columns)
+
+
 def per_device(hidden, out_weight, token_blocks, counts):
     vocab_here, columns_here = out_weight.shape
     n_tb = vocab_here // TB
@@ -89,6 +145,7 @@
     own_blocks = hidden.shape[0] // BB
     first_block = lax.axis_index("dp") * own_blocks
     own_counts = lax.dynamic_slice_in_dim(block_counts, first_block, own_blocks, 0)
+    assert own_blocks == 1 and n_blk == lax.psum(1, "dp")
 
     n_vocab = lax.psum(1, "vocab")
     n_dp = lax.psum(1, "dp")
@@ -119,30 +176,19 @@
         masked = jnp.where(live_mask, logits, -jnp.inf)
         local_max = jnp.max(masked, axis=(1, 3))
         local_total = jnp.sum(jnp.exp(masked - local_max[:, None, :, None]), axis=(1, 3))
-        stats = lax.all_gather(jnp.stack([local_max, local_total]), "vocab", axis=0)
+        stats = small_all_gather(jnp.stack([local_max, local_total]), n_vocab)
         beam_max = jnp.max(stats[:, 0], axis=0)
         beam_total = jnp.sum(stats[:, 1] * jnp.exp(stats[:, 0] - beam_max[None]), axis=0)
         shifted = logits - beam_max[:, None, :, None] - jnp.log(beam_total)[:, None, :, None]
         allowed_logprob = jnp.where(live_mask, shifted, 0.0)
         probabilities = jnp.where(live_mask, jnp.exp(shifted), 0.0).astype(jnp.bfloat16)
 
-    prob_part = lax.all_gather(probabilities, "dp", axis=0, tiled=True)
-
-    with jax.named_scope("dense_expected"):
-        onehot = (
-            block_lists[:, :, None] == jnp.arange(n_tb, dtype=jnp.int32)[None, None, :]
-        ).astype(jnp.bfloat16)
-        spread = jnp.einsum(
-            "bsk,bsrt->brkt", onehot, prob_part, preferred_element_type=jnp.float32
-        ).astype(jnp.bfloat16)
-        embedding_part = jnp.einsum(
-            "bv,vd->bd",
-            spread.reshape(n_blk * BB, n_tb * TB),
-            out_weight,
-            preferred_element_type=jnp.float32,
+    with jax.named_scope("expected_ring"):
+        embedding_part = ring_expected(
+            probabilities[0], block_lists, out_weight, n_dp, n_blk, n_tb
         )
     summed = halving_reduce_scatter(embedding_part, n_vocab)
-    squares = lax.psum(jnp.sum(summed * summed, axis=1), "dp")
+    squares = butterfly_sum(jnp.sum(summed * summed, axis=1), "dp", n_dp)
     width = hidden.shape[1] * n_vocab
     expected = summed * lax.rsqrt(squares / width + 1e-06)[:, None]
     return (allowed_logprob[None], expected)

time: 271 us -> 305 us (1.13)
  matrix products: 19.6 us -> 51.6 us
  waiting for transfers between devices: 161 us -> 138 us
  local copies, waits for them, and re-layouts: 22.8 us -> 45.7 us
  blocking collectives: 18.6 us -> 0 us
  starting transfers between devices: 23.4 us -> 38 us
  other arithmetic: 9.94 us -> 15.1 us
    all_gather x1 -> x0, waiting for transfers between devices: 45.4 us -> none  [per_device(): prob_part = lax.all_gather(probabilities, 'dp', axis=0, tiled=True)]
    dot_general x2 -> x14, matrix products: 12.2 us -> 44.3 us  [the longest x7 33.7 us: add_piece(): jnp.dot(spread_block(piece, tokens, n_tb), out_weight, preferred_element_...]
    ppermute x0 -> x8, waiting for transfers between devices: none -> 18.7 us  [the longest x3 12.8 us: ring_expected(): from_right = lax.ppermute(from_right, 'dp', perm=leftward)]
    ppermute x0 -> x8, starting transfers between devices: none -> 10.9 us  [the longest x3 5.59 us: ring_expected(): from_left = lax.ppermute(from_left, 'dp', perm=rightward)]
    dynamic_slice x1 -> x6, local copies, waits for them, and re-layouts: 0.03 us -> 9.56 us  [add_piece(): old = lax.dynamic_index_in_dim(acc, block, axis=0, keepdims=False)]
    psum x1 -> x0, blocking collectives: 9.51 us -> none  [per_device(): squares = lax.psum(jnp.sum(summed * summed, axis=1), 'dp')]
    all_gather x1 -> x0, blocking collectives: 9.08 us -> none  [per_device(): stats = lax.all_gather(jnp.stack([local_max, local_total]), 'vocab', axis=0)]
    convert_element_type x0 -> x7, local copies, waits for them, and re-layouts: none -> 8.94 us  [spread_block(): spread = jnp.einsum('sk,srt->rkt', onehot, probs_block, preferred_element...]
  transfers between devices with their start and end apart: 23 -> 33, of which waited for: 16 -> 21; matrix products, arithmetic and copies ran while one was open for 1% -> 10% of each run, Pallas kernels for 0% -> 0%
where the time goes in v5:
time: 305 us; the launch traced here: 304 us
  waiting for transfers between devices  138 us (45%)
  matrix products  51.6 us (17%)
  local copies, waits for them, and re-layouts  45.7 us (15%)
  starting transfers between devices  38 us (12%)
  other arithmetic  15.1 us (5%)
  between operations  15.1 us (5%)
    reduce_scatter x1, waiting for transfers between devices, per_device(): logits = lax.psum_scatter(picked, 'dp', scatter_dimension=0, tiled=True)  74.4 us
    dot_general x7, matrix products, add_piece(): jnp.dot(spread_block(piece, tokens, n_tb), out_weight, preferred_element_...  33.7 us
    ppermute x5, waiting for transfers between devices, exchange_stage(): got = lax.ppermute(send, 'vocab', perm=perm)  20.5 us
    ppermute x9, waiting for transfers between devices, gather_stage(): got = lax.ppermute(x, 'vocab', perm=perm)  17.4 us
    ppermute x10, starting transfers between devices, permute_all_to_all(): got.append(lax.ppermute(send, axis_name, perm=perm))  14.8 us
    ppermute x3, waiting for transfers between devices, ring_expected(): from_right = lax.ppermute(from_right, 'dp', perm=leftward)  12.8 us
    gather x2, local copies, waits for them, and re-layouts, per_device(): picked = full4[rows, :, block_lists, :]  11.8 us
    dot_general x7, matrix products, spread_block(): jnp.einsum('sk,srt->rkt', onehot, probs_block, preferred_element_type=jnp...  10.6 us
  transfers between devices with their start and end apart: 33, of which 21 were waited for; matrix products, arithmetic and copies ran while one was open for 10% of the time, Pallas kernels for 0%

profile of v5, /device:TPU:0, one launch (start us, length us, event | category | flops | bytes accessed | tf_op | source)
XLA Modules:
  0.0 303.9 jit_solution(686454529903983623)
XLA Ops:
  8.8 2.5 collective-permute-start.1
  11.3 2.4 collective-permute-start.2
  14.5 1.5 collective-permute-start.5
  16.0 2.3 collective-permute-start.6
  18.6 1.3 collective-permute-done.6
  21.5 3.7 %collective-permute-start.9 = (bf16[16,2048]{1,0:T(8,128)(2,1)S(1)}, bf16[16,2048]{1,0:T(8,128)(2,1)S(1)}, u32[]{:S(2)}, u32[]{:S(2)}) collective-permute-start(bf16[16,2048]{1,0:T(8,128)(2,1)S(1)} %bitcast.339), channel_id=1, source_target_pairs={{0,24},{8,0},{16,8},{24,16},{1,25},{9,1},{17,9},{25,17},{2,26},{10... | collective-permute-start | bytes 196616 | tf_op jit(solution)/shard_map/hidden_spread/ppermute | solution.py:51
  25.3 1.2 collective-permute-start.7
  27.7 4.8 %collective-permute-done.8 = bf16[16,2048]{1,0:T(8,128)(2,1)S(1)} collective-permute-done((bf16[16,2048]{1,0:T(8,128)(2,1)S(1)}, bf16[16,2048]{1,0:T(8,128)(2,1)S(1)}, u32[]{:S(2)}, u32[]{:S(2)}) %collective-permute-start.8) | collective-permute-done | bytes 65568 | tf_op jit(solution)/shard_map/hidden_spread/ppermute | solution.py:51
  34.7 4.2 %collective-permute-done.13 = bf16[64,1024]{1,0:T(8,128)(2,1)S(1)} collective-permute-done((bf16[64,1024]{1,0:T(8,128)(2,1)S(1)}, bf16[64,1024]{1,0:T(8,128)(2,1)S(1)}, u32[]{:S(2)}, u32[]{:S(2)}) %collective-permute-start.13) | collective-permute-done | bytes 131104 | tf_op jit(solution)/shard_map/hidden_spread/hidden_gather_stage/ppermute | solution.py:62
  38.9 1.3 collective-permute-start.14
  40.9 5.5 %collective-permute-done.14 = bf16[2,64,1024]{2,1,0:T(8,128)(2,1)S(1)} collective-permute-done((bf16[2,64,1024]{2,1,0:T(8,128)(2,1)S(1)}, bf16[2,64,1024]{2,1,0:T(8,128)(2,1)S(1)}, u32[]{:S(2)}, u32[]{:S(2)}) %collective-permute-start.14) | collective-permute-done | bytes 262176 | tf_op jit(solution)/shard_map/hidden_spread/hidden_gather_stage/ppermute | solution.py:62
  51.6 7.3 %fusion.72 = f32[4,128,19,128]{3,1,2,0:T(8,128)} fusion(bf16[4,128,2048,1]{2,1,3,0:T(8,128)(2,1)S(1)} %bitcast.324, bf16[19,128,2048,1]{2,1,0,3:T(8,128)(2,1)S(1)} %bitcast.305), kind=kOutput, calls=%fused_computation.207 | convolution fusion | flops 5100273664 | bytes 17039360 | tf_op jit(solution)/shard_map/dense_logits/bd,vd->bv/dot_general | solution.py:164
  58.9 5.2 %gather_fusion.2 = f32[64,128,128]{2,1,0:T(8,128)} fusion(f32[4,128,19,128]{3,1,2,0:T(8,128)} %fusion.72, s32[64]{0:T(128)S(1)} %reshape.1128), kind=kCustom, calls=%fused_computation.2 | custom fusion | bytes 8389120 | tf_op jit(solution)/shard_map/dense_logits/gather | solution.py:169
  64.1 6.6 %copy.39 = f32[4,16,128,128]{3,1,2,0:T(8,128)} copy(f32[4,16,128,128]{3,2,1,0:T(8,128)} %bitcast.314) | data formatting | bytes 8388608 | tf_op jit(solution)/shard_map/dense_logits/gather | solution.py:169
  72.0 74.4 %reduce-scatter.2.cloned.1.call-done = f32[1,16,128,128]{3,1,2,0:T(8,128)} async-done(((f32[4,16,128,128]{3,1,2,0:T(8,128)}), f32[1,16,128,128]{3,1,2,0:T(8,128)}) %reduce-scatter.2.cloned.1.call-update) | async-done | bytes 1048592 | tf_op jit(solution)/shard_map/reduce_scatter | solution.py:171
  146.4 2.3 select_reduce_fusion
  148.7 3.1 %exponential_reduce_fusion = f32[128]{0:T(128)S(1)} fusion(f32[1,16,128,128]{3,1,2,0:T(8,128)} %reduce-scatter.2.cloned.1.call-done, f32[128]{0:T(128)S(1)} %select_reduce_fusion, pred[16]{0:T(512)(128)(4,1)S(1)} %iota_compare_fusion.7), kind=kLoop, calls=%fused_computation.45 | loop fusion | flops 786304 | bytes 1049616 | tf_op jit(solution)/shard_map/softmax_stats/reduce_sum | solution.py:178
  153.0 1.5 collective-permute-start.17
  154.5 2.1 collective-permute-done.17
  156.6 1.5 collective-permute-start.18
  158.1 2.1 collective-permute-done.18
  160.3 1.7 fusion.20
  162.0 4.2 %collective-permute-start.19 = (bf16[16,128,128]{2,0,1:T(8,128)(2,1)S(1)}, bf16[16,128,128]{2,0,1:T(8,128)(2,1)}, u32[]{:S(2)}, u32[]{:S(2)}) collective-permute-start(bf16[16,128,128]{2,0,1:T(8,128)(2,1)S(1)} %get-tuple-element.10), channel_id=1, source_target_pairs={{0,8},{8,16},{16,24},{1,9},{9,17},{17,25},{2,10},{10,18},{18,26},{... | collective-permute-start | bytes 1572872 | tf_op jit(solution)/shard_map/expected_ring/ppermute | solution.py:132
  166.2 1.5 collective-permute-start.20
  169.2 5.4 %fusion = f32[4,128,2048]{2,1,0:T(8,128)S(1)} fusion(f32[4,128,2048]{2,1,0:T(8,128)S(1)} %broadcast_in_dim.108, s32[]{:T(128)S(6)} %min.22, bf16[128,2432]{0,1:T(8,128)(2,1)S(1)} %bitcast.317, bf16[2432,2048]{1,0:T(8,128)(2,1)} %param.5), kind=kOutput, calls=%fused_computation.4 | convolution fusion | flops 1275068416 | bytes 11632644 | tf_op jit(solution)/shard_map/expected_ring/dot_general | solution.py:121
  174.6 2.0 copy-done.2
  177.6 1.5 fusion.14
  179.1 1.3 copy.43
  180.4 2.5 fusion.15
  182.9 1.5 copy.44
  184.5 7.0 %fusion.12 = f32[4,128,2048]{2,1,0:T(8,128)} fusion(f32[4,128,2048]{2,1,0:T(8,128)} %copy-done.2, s32[]{:T(128)S(6)} %min.23, bf16[128,2432]{0,1:T(8,128)(2,1)} %bitcast.321, bf16[2432,2048]{1,0:T(8,128)(2,1)} %param.5, f32[1,128,2048]{2,1,0:T(8,128)} %constant_dynamic-slice_fusion.11), kind=kOutput, calls=%fused_computation.22 | convolution fusion | flops 1275330560 | bytes 12681220 | tf_op jit(solution)/shard_map/expected_ring/dot_general | solution.py:121
  191.5 1.3 constant_dynamic-slice_fusion.9
  193.5 1.3 collective-permute-start.22
  194.8 2.5 fusion.10
  197.4 2.3 constant_dynamic-slice_fusion.7
  200.9 1.3 copy.45
  202.2 7.7 %collective-permute-done.22 = bf16[16,128,128]{2,0,1:T(8,128)(2,1)} collective-permute-done((bf16[16,128,128]{2,0,1:T(8,128)(2,1)}, bf16[16,128,128]{2,0,1:T(8,128)(2,1)}, u32[]{:S(2)}, u32[]{:S(2)}) %collective-permute-start.22) | collective-permute-done | bytes 524320 | tf_op jit(solution)/shard_map/expected_ring/ppermute | solution.py:133
  209.9 2.5 fusion.17
  212.5 1.5 copy.46
  214.0 7.0 %fusion.8 = f32[4,128,2048]{2,1,0:T(8,128)} fusion(f32[4,128,2048]{2,1,0:T(8,128)} %fusion.10, s32[]{:T(128)S(6)} %min.25, bf16[128,2432]{0,1:T(8,128)(2,1)} %bitcast.322, bf16[2432,2048]{1,0:T(8,128)(2,1)} %param.5, f32[1,128,2048]{2,1,0:T(8,128)} %constant_dynamic-slice_fusion.7), kind=kOutput, calls=%fused_computation.16 | convolution fusion | flops 1275330560 | bytes 12681220 | tf_op jit(solution)/shard_map/expected_ring/dot_general | solution.py:121
  221.0 1.3 constant_dynamic-slice_fusion.5
  223.0 1.6 collective-permute-start.24
  224.6 2.5 fusion.6
  227.2 2.3 constant_dynamic-slice_fusion.3
  230.4 5.1 %collective-permute-done.24 = bf16[16,128,128]{2,0,1:T(8,128)(2,1)} collective-permute-done((bf16[16,128,128]{2,0,1:T(8,128)(2,1)}, bf16[16,128,128]{2,0,1:T(8,128)(2,1)}, u32[]{:S(2)}, u32[]{:S(2)}) %collective-permute-start.24) | collective-permute-done | bytes 524320 | tf_op jit(solution)/shard_map/expected_ring/ppermute | solution.py:133
  235.5 2.5 fusion.19
  238.1 2.3 copy.48
  240.4 6.8 %fusion.4 = f32[4,128,2048]{2,1,0:T(8,128)} fusion(f32[4,128,2048]{2,1,0:T(8,128)} %fusion.6, s32[]{:T(128)S(6)} %min.27, bf16[128,2432]{0,1:T(8,128)(2,1)S(1)} %bitcast.320, bf16[2432,2048]{1,0:T(8,128)(2,1)} %param.5, f32[1,128,2048]{2,1,0:T(8,128)} %constant_dynamic-slice_fusion.3), kind=kOutput, calls=%fused_computation.10 | convolution fusion | flops 1275330560 | bytes 12681220 | tf_op jit(solution)/shard_map/expected_ring/dot_general | solution.py:121
  247.2 1.3 constant_dynamic-slice_fusion.1
  248.6 2.5 fusion.2
  251.1 3.2 %dynamic-slice_bitcast_fusion = f32[2,2,64,2048]{3,2,1,0:T(8,128)} fusion(f32[2,2,2,64,2048]{4,3,2,1,0:T(8,128)} %bitcast.312, s32[]{:T(128)S(6)} %select_n.561), kind=kLoop, calls=%fused_computation.25 | loop fusion | bytes 4194308 | tf_op jit(solution)/shard_map/summed_core_stage/jit(dynamic_index_in_dim)/squeeze | solution.py:16
  254.3 4.5 %collective-permute-done.25 = f32[2,2,64,2048]{3,2,1,0:T(8,128)} collective-permute-done((f32[2,2,64,2048]{3,2,1,0:T(8,128)}, f32[2,2,64,2048]{3,2,1,0:T(8,128)}, u32[]{:S(2)}, u32[]{:S(2)}) %collective-permute-start.25) | collective-permute-done | bytes 2097184 | tf_op jit(solution)/shard_map/summed_core_stage/ppermute | solution.py:18
  258.8 2.5 bitcast_add_fusion
  262.5 1.5 collective-permute-start.28
  264.9 1.5 collective-permute-start.26
  266.4 10.2 %collective-permute-done.28 = f32[2,64,1024]{2,1,0:T(8,128)S(1)} collective-permute-done((f32[2,64,1024]{2,1,0:T(8,128)S(1)}, f32[2,64,1024]{2,1,0:T(8,128)S(1)}, u32[]{:S(2)}, u32[]{:S(2)}) %collective-permute-start.28) | collective-permute-done | bytes 524320 | tf_op jit(solution)/shard_map/summed_chip_stage/ppermute | solution.py:18
  276.6 1.2 bitcast_add_fusion.1
  277.7 1.5 collective-permute-start.29
  280.4 1.6 collective-permute-start.27
  282.0 3.4 %collective-permute-done.29 = f32[64,1024]{1,0:T(8,128)S(1)} collective-permute-done((f32[64,1024]{1,0:T(8,128)S(1)}, f32[64,1024]{1,0:T(8,128)S(1)}, u32[]{:S(2)}, u32[]{:S(2)}) %collective-permute-start.29) | collective-permute-done | bytes 262176 | tf_op jit(solution)/shard_map/summed_chip_stage/ppermute | solution.py:18
  285.4 2.4 collective-permute-done.27
  288.1 3.6 %collective-permute-done.30 = f32[64]{0:T(128)S(1)} collective-permute-done((f32[64]{0:T(128)S(1)}, f32[64]{0:T(128)S(1)}, u32[]{:S(2)}, u32[]{:S(2)}) %collective-permute-start.30) | collective-permute-done | bytes 288 | tf_op jit(solution)/shard_map/ppermute | solution.py:98
  292.5 1.3 copy.49
  293.8 2.3 collective-permute-done.31
  (165 shorter events, 27.1 us)
Async XLA Ops:
  7.2 63.6 %copy-start = (s32[1,4]{1,0:T(1,128)S(1)}, s32[1,4]{1,0:T(1,128)}, u32[]{:S(2)}) copy-start(s32[1,4]{1,0:T(1,128)} %param.7) | copy-start | bytes 52
  7.2 139.2 %reduce-scatter.2.cloned.1.call-start = ((), (), s32[]{:S(2)}) async-start(), calls=%async_computation.1 | async-start | bytes 5242880 | tf_op jit(solution)/shard_map/reduce_scatter | solution.py:171
  8.2 25.7 %copy-start.7 = (s32[1,4,16]{2,1,0:T(4,128)S(1)}, s32[1,4,16]{2,1,0:T(4,128)}, u32[]{:S(2)}) copy-start(s32[1,4,16]{2,1,0:T(4,128)} %param.6) | copy-start | bytes 772
  8.2 6.3 %collective-permute-start = (bf16[16,1024]{1,0:T(8,128)(2,1)S(1)}, bf16[16,1024]{1,0:T(8,128)(2,1)S(1)}, u32[]{:S(2)}, u32[]{:S(2)}) collective-permute-start(bf16[16,1024]{1,0:T(8,128)(2,1)S(1)} %get-tuple-element.34), channel_id=1, source_target_pairs={{0,1},{1,2},{2,3},{3,4},{4,5},{5,6},{6,7},{7,0},{8,9},{9,10},{10,1... | collective-permute-start | bytes 98312 | tf_op jit(solution)/shard_map/hidden_spread/ppermute | solution.py:51
  8.8 7.2 %collective-permute-start.1 = (bf16[16,1024]{1,0:T(8,128)(2,1)S(1)}, bf16[16,1024]{1,0:T(8,128)(2,1)S(1)}, u32[]{:S(2)}, u32[]{:S(2)}) collective-permute-start(bf16[16,1024]{1,0:T(8,128)(2,1)S(1)} %get-tuple-element.33), channel_id=1, source_target_pairs={{0,2},{1,3},{2,4},{3,5},{4,6},{5,7},{6,0},{7,1},{8,10},{9,11},{10,... | collective-permute-start | bytes 98312 | tf_op jit(solution)/shard_map/hidden_spread/ppermute | solution.py:51
  11.3 7.0 %collective-permute-start.2 = (bf16[16,1024]{1,0:T(8,128)(2,1)S(1)}, bf16[16,1024]{1,0:T(8,128)(2,1)S(1)}, u32[]{:S(2)}, u32[]{:S(2)}) collective-permute-start(bf16[16,1024]{1,0:T(8,128)(2,1)S(1)} %get-tuple-element.32), channel_id=1, source_target_pairs={{0,3},{1,4},{2,5},{3,6},{4,7},{5,0},{6,1},{7,2},{8,11},{9,12},{10,... | collective-permute-start | bytes 98312 | tf_op jit(solution)/shard_map/hidden_spread/ppermute | solution.py:51
  13.7 4.6 %collective-permute-start.3 = (bf16[16,1024]{1,0:T(8,128)(2,1)S(1)}, bf16[16,1024]{1,0:T(8,128)(2,1)S(1)}, u32[]{:S(2)}, u32[]{:S(2)}) collective-permute-start(bf16[16,1024]{1,0:T(8,128)(2,1)S(1)} %get-tuple-element.31), channel_id=1, source_target_pairs={{0,4},{1,5},{2,6},{3,7},{4,0},{5,1},{6,2},{7,3},{8,12},{9,13},{10,... | collective-permute-start | bytes 98312 | tf_op jit(solution)/shard_map/hidden_spread/ppermute | solution.py:51
  14.2 4.2 %collective-permute-start.4 = (bf16[16,1024]{1,0:T(8,128)(2,1)S(1)}, bf16[16,1024]{1,0:T(8,128)(2,1)S(1)}, u32[]{:S(2)}, u32[]{:S(2)}) collective-permute-start(bf16[16,1024]{1,0:T(8,128)(2,1)S(1)} %get-tuple-element.30), channel_id=1, source_target_pairs={{0,5},{1,6},{2,7},{3,0},{4,1},{5,2},{6,3},{7,4},{8,13},{9,14},{10,... | collective-permute-start | bytes 98312 | tf_op jit(solution)/shard_map/hidden_spread/ppermute | solution.py:51
  14.5 4.1 %collective-permute-start.5 = (bf16[16,1024]{1,0:T(8,128)(2,1)S(1)}, bf16[16,1024]{1,0:T(8,128)(2,1)S(1)}, u32[]{:S(2)}, u32[]{:S(2)}) collective-permute-start(bf16[16,1024]{1,0:T(8,128)(2,1)S(1)} %get-tuple-element.29), channel_id=1, source_target_pairs={{0,6},{1,7},{2,0},{3,1},{4,2},{5,3},{6,4},{7,5},{8,14},{9,15},{10,... | collective-permute-start | bytes 98312 | tf_op jit(solution)/shard_map/hidden_spread/ppermute | solution.py:51
  16.0 3.9 %collective-permute-start.6 = (bf16[16,1024]{1,0:T(8,128)(2,1)S(1)}, bf16[16,1024]{1,0:T(8,128)(2,1)S(1)}, u32[]{:S(2)}, u32[]{:S(2)}) collective-permute-start(bf16[16,1024]{1,0:T(8,128)(2,1)S(1)} %get-tuple-element.28), channel_id=1, source_target_pairs={{0,7},{1,0},{2,1},{3,2},{4,3},{5,4},{6,5},{7,6},{8,15},{9,8},{10,9... | collective-permute-start | bytes 98312 | tf_op jit(solution)/shard_map/hidden_spread/ppermute | solution.py:51
  21.5 6.2 %collective-permute-start.9 = (bf16[16,2048]{1,0:T(8,128)(2,1)S(1)}, bf16[16,2048]{1,0:T(8,128)(2,1)S(1)}, u32[]{:S(2)}, u32[]{:S(2)}) collective-permute-start(bf16[16,2048]{1,0:T(8,128)(2,1)S(1)} %bitcast.339), channel_id=1, source_target_pairs={{0,24},{8,0},{16,8},{24,16},{1,25},{9,1},{17,9},{25,17},{2,26},{10... | collective-permute-start | bytes 196616 | tf_op jit(solution)/shard_map/hidden_spread/ppermute | solution.py:51
  25.2 7.3 %collective-permute-start.8 = (bf16[16,2048]{1,0:T(8,128)(2,1)S(1)}, bf16[16,2048]{1,0:T(8,128)(2,1)S(1)}, u32[]{:S(2)}, u32[]{:S(2)}) collective-permute-start(bf16[16,2048]{1,0:T(8,128)(2,1)S(1)} %bitcast.340), channel_id=1, source_target_pairs={{0,16},{8,24},{16,0},{24,8},{1,17},{9,25},{17,1},{25,9},{2,18},{10... | collective-permute-start | bytes 196616 | tf_op jit(solution)/shard_map/hidden_spread/ppermute | solution.py:51
  25.3 7.2 %collective-permute-start.7 = (bf16[16,2048]{1,0:T(8,128)(2,1)S(1)}, bf16[16,2048]{1,0:T(8,128)(2,1)S(1)}, u32[]{:S(2)}, u32[]{:S(2)}) collective-permute-start(bf16[16,2048]{1,0:T(8,128)(2,1)S(1)} %bitcast.341), channel_id=1, source_target_pairs={{0,8},{8,16},{16,24},{24,0},{1,9},{9,17},{17,25},{25,1},{2,10},{10... | collective-permute-start | bytes 196616 | tf_op jit(solution)/shard_map/hidden_spread/ppermute | solution.py:51
  33.3 5.5 %collective-permute-start.13 = (bf16[64,1024]{1,0:T(8,128)(2,1)S(1)}, bf16[64,1024]{1,0:T(8,128)(2,1)S(1)}, u32[]{:S(2)}, u32[]{:S(2)}) collective-permute-start(bf16[64,1024]{1,0:T(8,128)(2,1)S(1)} %get-tuple-element.18), channel_id=1, source_target_pairs={{0,4},{1,5},{2,6},{3,7},{4,0},{5,1},{6,2},{7,3},{8,12},{9,13},{10,... | collective-permute-start | bytes 393224 | tf_op jit(solution)/shard_map/hidden_spread/hidden_gather_stage/ppermute | solution.py:62
  34.0 6.2 %collective-permute-start.10 = (bf16[64,1024]{1,0:T(8,128)(2,1)S(1)}, bf16[64,1024]{1,0:T(8,128)(2,1)S(1)}, u32[]{:S(2)}, u32[]{:S(2)}) collective-permute-start(bf16[64,1024]{1,0:T(8,128)(2,1)S(1)} %get-tuple-element.19), channel_id=1, source_target_pairs={{0,2},{1,3},{2,0},{3,1},{4,6},{5,7},{6,4},{7,5},{8,10},{9,11},{10,... | collective-permute-start | bytes 393224 | tf_op jit(solution)/shard_map/hidden_spread/hidden_gather_stage/ppermute | solution.py:62
  38.9 7.5 %collective-permute-start.14 = (bf16[2,64,1024]{2,1,0:T(8,128)(2,1)S(1)}, bf16[2,64,1024]{2,1,0:T(8,128)(2,1)S(1)}, u32[]{:S(2)}, u32[]{:S(2)}) collective-permute-start(bf16[2,64,1024]{2,1,0:T(8,128)(2,1)S(1)} %maximum_select_fusion.7), channel_id=1, source_target_pairs={{0,2},{1,3},{2,0},{3,1},{4,6},{5,7},{6,4},{7,5},{8,10},{9,11},{10,... | collective-permute-start | bytes 786440 | tf_op jit(solution)/shard_map/hidden_spread/hidden_gather_stage/ppermute | solution.py:62
  40.3 7.3 %collective-permute-start.11 = (bf16[2,64,1024]{2,1,0:T(8,128)(2,1)S(1)}, bf16[2,64,1024]{2,1,0:T(8,128)(2,1)S(1)}, u32[]{:S(2)}, u32[]{:S(2)}) collective-permute-start(bf16[2,64,1024]{2,1,0:T(8,128)(2,1)S(1)} %maximum_select_fusion.5), channel_id=1, source_target_pairs={{0,4},{1,5},{2,6},{3,7},{4,0},{5,1},{6,2},{7,3},{8,12},{9,13},{10,... | collective-permute-start | bytes 786440 | tf_op jit(solution)/shard_map/hidden_spread/hidden_gather_stage/ppermute | solution.py:62
  46.5 2.0 collective-permute-start.15
  47.5 2.7 slice-start
  47.6 2.0 collective-permute-start.12
  48.4 2.8 slice-start.1
  49.8 1.8 slice-start.2
  151.8 1.2 collective-permute-start.16
  153.0 3.6 %collective-permute-start.17 = (f32[2,2,1,128]{3,1,2,0:T(2,128)S(1)}, f32[2,2,1,128]{3,1,2,0:T(2,128)S(1)}, u32[]{:S(2)}, u32[]{:S(2)}) collective-permute-start(f32[2,2,1,128]{3,1,2,0:T(2,128)S(1)} %maximum_select_fusion.12), channel_id=1, source_target_pairs={{0,2},{1,3},{2,0},{3,1},{4,6},{5,7},{6,4},{7,5},{8,10},{9,11},{10,... | collective-permute-start | bytes 6152 | tf_op jit(solution)/shard_map/softmax_stats/ppermute | solution.py:62
  156.6 3.6 %collective-permute-start.18 = (f32[2,2,2,1,128]{4,2,1,3,0:T(2,128)S(1)}, f32[2,2,2,1,128]{4,2,1,3,0:T(2,128)S(1)}, u32[]{:S(2)}, u32[]{:S(2)}) collective-permute-start(f32[2,2,2,1,128]{4,2,1,3,0:T(2,128)S(1)} %maximum_select_fusion.10), channel_id=1, source_target_pairs={{0,4},{1,5},{2,6},{3,7},{4,0},{5,1},{6,2},{7,3},{8,12},{9,13},{10,... | collective-permute-start | bytes 12296 | tf_op jit(solution)/shard_map/softmax_stats/ppermute | solution.py:62
  162.0 15.6 %collective-permute-start.19 = (bf16[16,128,128]{2,0,1:T(8,128)(2,1)S(1)}, bf16[16,128,128]{2,0,1:T(8,128)(2,1)}, u32[]{:S(2)}, u32[]{:S(2)}) collective-permute-start(bf16[16,128,128]{2,0,1:T(8,128)(2,1)S(1)} %get-tuple-element.10), channel_id=1, source_target_pairs={{0,8},{8,16},{16,24},{1,9},{9,17},{17,25},{2,10},{10,18},{18,26},{... | collective-permute-start | bytes 1572872 | tf_op jit(solution)/shard_map/expected_ring/ppermute | solution.py:132
  166.2 14.2 %collective-permute-start.20 = (bf16[16,128,128]{2,0,1:T(8,128)(2,1)S(1)}, bf16[16,128,128]{2,0,1:T(8,128)(2,1)}, u32[]{:S(2)}, u32[]{:S(2)}) collective-permute-start(bf16[16,128,128]{2,0,1:T(8,128)(2,1)S(1)} %get-tuple-element.10), channel_id=1, source_target_pairs={{8,0},{16,8},{24,16},{9,1},{17,9},{25,17},{10,2},{18,10},{26,18},{... | collective-permute-start | bytes 1572872 | tf_op jit(solution)/shard_map/expected_ring/ppermute | solution.py:133
  174.6 2.0 copy-start.2
  180.4 14.4 %slice-start.3 = ((s8[9961472]{0:T(1024)(128)(4,1)}), s8[1572864]{0:T(1024)(128)(4,1)S(1)}, s32[]{:S(2)}) async-start(s8[9961472]{0:T(1024)(128)(4,1)} %bitcast.306), calls=%async_computation.5 | async-start | bytes 3145728
  184.5 10.3 %slice-start.4 = ((s8[9961472]{0:T(1024)(128)(4,1)}), s8[4194304]{0:T(1024)(128)(4,1)S(1)}, s32[]{:S(2)}) async-start(s8[9961472]{0:T(1024)(128)(4,1)} %bitcast.306), calls=%async_computation.6 | async-start | bytes 8388608
  184.5 10.3 %slice-start.5 = ((s8[9961472]{0:T(1024)(128)(4,1)}), s8[4194304]{0:T(1024)(128)(4,1)S(1)}, s32[]{:S(2)}) async-start(s8[9961472]{0:T(1024)(128)(4,1)} %bitcast.306), calls=%async_computation.7 | async-start | bytes 8388608
  192.8 6.9 %collective-permute-start.21 = (bf16[16,128,128]{2,0,1:T(8,128)(2,1)}, bf16[16,128,128]{2,0,1:T(8,128)(2,1)S(1)}, u32[]{:S(2)}, u32[]{:S(2)}) collective-permute-start(bf16[16,128,128]{2,0,1:T(8,128)(2,1)} %collective-permute-done.19), channel_id=1, source_target_pairs={{8,16},{16,24},{9,17},{17,25},{10,18},{18,26},{11,19},{19,27},{12,... | collective-permute-start | bytes 1572872 | tf_op jit(solution)/shard_map/expected_ring/ppermute | solution.py:132
  193.5 16.4 %collective-permute-start.22 = (bf16[16,128,128]{2,0,1:T(8,128)(2,1)}, bf16[16,128,128]{2,0,1:T(8,128)(2,1)}, u32[]{:S(2)}, u32[]{:S(2)}) collective-permute-start(bf16[16,128,128]{2,0,1:T(8,128)(2,1)} %collective-permute-done.20), channel_id=1, source_target_pairs={{8,0},{16,8},{9,1},{17,9},{10,2},{18,10},{11,3},{19,11},{12,4},{20... | collective-permute-start | bytes 1572872 | tf_op jit(solution)/shard_map/expected_ring/ppermute | solution.py:133
  199.7 0.8 copy-start.5
  209.9 14.7 %slice-start.6 = ((s8[9961472]{0:T(1024)(128)(4,1)}), s8[1572864]{0:T(1024)(128)(4,1)S(1)}, s32[]{:S(2)}) async-start(s8[9961472]{0:T(1024)(128)(4,1)} %bitcast.308), calls=%async_computation.8 | async-start | bytes 3145728
  214.0 8.3 %copy-start.6 = (bf16[16,128,128]{2,0,1:T(8,128)(2,1)S(1)}, bf16[16,128,128]{2,0,1:T(8,128)(2,1)}, u32[]{:S(2)}) copy-start(bf16[16,128,128]{2,0,1:T(8,128)(2,1)} %copy-done.5) | copy-start | bytes 1572868
  214.0 10.6 %slice-start.7 = ((s8[9961472]{0:T(1024)(128)(4,1)}), s8[4194304]{0:T(1024)(128)(4,1)S(1)}, s32[]{:S(2)}) async-start(s8[9961472]{0:T(1024)(128)(4,1)} %bitcast.308), calls=%async_computation.9 | async-start | bytes 8388608
  214.0 10.6 %slice-start.8 = ((s8[9961472]{0:T(1024)(128)(4,1)}), s8[4194304]{0:T(1024)(128)(4,1)S(1)}, s32[]{:S(2)}) async-start(s8[9961472]{0:T(1024)(128)(4,1)} %bitcast.308), calls=%async_computation.10 | async-start | bytes 8388608
  222.3 7.1 %collective-permute-start.23 = (bf16[16,128,128]{2,0,1:T(8,128)(2,1)S(1)}, bf16[16,128,128]{2,0,1:T(8,128)(2,1)S(1)}, u32[]{:S(2)}, u32[]{:S(2)}) collective-permute-start(bf16[16,128,128]{2,0,1:T(8,128)(2,1)S(1)} %copy-done.6), channel_id=1, source_target_pairs={{16,24},{17,25},{18,26},{19,27},{20,28},{21,29},{22,30},{23,31}} | collective-permute-start | bytes 1572872 | tf_op jit(solution)/shard_map/expected_ring/ppermute | solution.py:132
  223.0 12.5 %collective-permute-start.24 = (bf16[16,128,128]{2,0,1:T(8,128)(2,1)}, bf16[16,128,128]{2,0,1:T(8,128)(2,1)}, u32[]{:S(2)}, u32[]{:S(2)}) collective-permute-start(bf16[16,128,128]{2,0,1:T(8,128)(2,1)} %collective-permute-done.22), channel_id=1, source_target_pairs={{8,0},{9,1},{10,2},{11,3},{12,4},{13,5},{14,6},{15,7}} | collective-permute-start | bytes 1572872 | tf_op jit(solution)/shard_map/expected_ring/ppermute | solution.py:133
  235.5 13.0 %slice-start.9 = ((s8[9961472]{0:T(1024)(128)(4,1)}), s8[1572864]{0:T(1024)(128)(4,1)S(1)}, s32[]{:S(2)}) async-start(s8[9961472]{0:T(1024)(128)(4,1)} %bitcast.310), calls=%async_computation.11 | async-start | bytes 3145728
  240.4 8.1 %slice-start.10 = ((s8[9961472]{0:T(1024)(128)(4,1)}), s8[4194304]{0:T(1024)(128)(4,1)S(1)}, s32[]{:S(2)}) async-start(s8[9961472]{0:T(1024)(128)(4,1)} %bitcast.310), calls=%async_computation.12 | async-start | bytes 8388608
  240.4 8.1 %slice-start.11 = ((s8[9961472]{0:T(1024)(128)(4,1)}), s8[4194304]{0:T(1024)(128)(4,1)S(1)}, s32[]{:S(2)}) async-start(s8[9961472]{0:T(1024)(128)(4,1)} %bitcast.310), calls=%async_computation.13 | async-start | bytes 8388608
  240.4 8.1 %copy-start.4 = (bf16[128,19,128]{0,2,1:T(8,128)(2,1)S(1)}, bf16[128,19,128]{0,2,1:T(8,128)(2,1)}, u32[]{:S(2)}) copy-start(bf16[128,19,128]{0,2,1:T(8,128)(2,1)} %copy.48) | copy-start | bytes 1867780
  254.3 4.5 %collective-permute-start.25 = (f32[2,2,64,2048]{3,2,1,0:T(8,128)}, f32[2,2,64,2048]{3,2,1,0:T(8,128)}, u32[]{:S(2)}, u32[]{:S(2)}) collective-permute-start(f32[2,2,64,2048]{3,2,1,0:T(8,128)} %dynamic-slice_bitcast_fusion), channel_id=1, source_target_pairs={{0,1},{1,0},{2,3},{3,2},{4,5},{5,4},{6,7},{7,6},{8,9},{9,8},{10,11... | collective-permute-start | bytes 6291464 | tf_op jit(solution)/shard_map/summed_core_stage/ppermute | solution.py:18
  261.5 1.0 copy-start.3
  262.5 14.0 %collective-permute-start.28 = (f32[2,64,1024]{2,1,0:T(8,128)S(1)}, f32[2,64,1024]{2,1,0:T(8,128)S(1)}, u32[]{:S(2)}, u32[]{:S(2)}) collective-permute-start(f32[2,64,1024]{2,1,0:T(8,128)S(1)} %dynamic-slice_bitcast_fusion.1), channel_id=1, source_target_pairs={{0,4},{1,5},{2,6},{3,7},{4,0},{5,1},{6,2},{7,3},{8,12},{9,13},{10,... | collective-permute-start | bytes 1572872 | tf_op jit(solution)/shard_map/summed_chip_stage/ppermute | solution.py:18
  264.9 14.4 %collective-permute-start.26 = (f32[2,64,1024]{2,1,0:T(8,128)}, f32[2,64,1024]{2,1,0:T(8,128)}, u32[]{:S(2)}, u32[]{:S(2)}) collective-permute-start(f32[2,64,1024]{2,1,0:T(8,128)} %dynamic-slice_bitcast_fusion.2), channel_id=1, source_target_pairs={{0,2},{1,3},{2,0},{3,1},{4,6},{5,7},{6,4},{7,5},{8,10},{9,11},{10,... | collective-permute-start | bytes 1572872 | tf_op jit(solution)/shard_map/summed_chip_stage/ppermute | solution.py:18
  276.6 20.5 %copy-start.1 = (s32[1,4]{1,0:T(1,128)S(1)}, s32[1,4]{1,0:T(1,128)}, u32[]{:S(2)}) copy-start(s32[1,4]{1,0:T(1,128)} %param.7) | copy-start | bytes 52
  277.7 7.7 %collective-permute-start.29 = (f32[64,1024]{1,0:T(8,128)S(1)}, f32[64,1024]{1,0:T(8,128)S(1)}, u32[]{:S(2)}, u32[]{:S(2)}) collective-permute-start(f32[64,1024]{1,0:T(8,128)S(1)} %dynamic-slice_bitcast_fusion.3), channel_id=1, source_target_pairs={{0,2},{1,3},{2,0},{3,1},{4,6},{5,7},{6,4},{7,5},{8,10},{9,11},{10,... | collective-permute-start | bytes 786440 | tf_op jit(solution)/shard_map/summed_chip_stage/ppermute | solution.py:18
  280.4 7.4 %collective-permute-start.27 = (f32[64,1024]{1,0:T(8,128)S(1)}, f32[64,1024]{1,0:T(8,128)S(1)}, u32[]{:S(2)}, u32[]{:S(2)}) collective-permute-start(f32[64,1024]{1,0:T(8,128)S(1)} %dynamic-slice_bitcast_fusion.4), channel_id=1, source_target_pairs={{0,4},{1,5},{2,6},{3,7},{4,0},{5,1},{6,2},{7,3},{8,12},{9,13},{10,... | collective-permute-start | bytes 786440 | tf_op jit(solution)/shard_map/summed_chip_stage/ppermute | solution.py:18
  288.0 3.6 %collective-permute-start.30 = (f32[64]{0:T(128)S(1)}, f32[64]{0:T(128)S(1)}, u32[]{:S(2)}, u32[]{:S(2)}) collective-permute-start(f32[64]{0:T(128)S(1)} %multiply_reduce_fusion), channel_id=1, source_target_pairs={{0,8},{8,0},{16,24},{24,16},{1,9},{9,1},{17,25},{25,17},{2,10},{10... | collective-permute-start | bytes 776 | tf_op jit(solution)/shard_map/ppermute | solution.py:98
  291.6 4.5 %collective-permute-start.31 = (f32[64]{0:T(128)S(1)}, f32[64]{0:T(128)S(1)}, u32[]{:S(2)}, u32[]{:S(2)}) collective-permute-start(f32[64]{0:T(128)S(1)} %add.370), channel_id=1, source_target_pairs={{0,16},{8,24},{16,0},{24,8},{1,17},{9,25},{17,1},{25,9},{2,18},{10... | collective-permute-start | bytes 776 | tf_op jit(solution)/shard_map/ppermute | solution.py:98
Sparse Core Ops, SparseCore 0:
  70.9 75.4 reduce-scatter.1

commit v6 on v5

--- a/solution.py
+++ b/solution.py
@@ -138,17 +138,20 @@
 
 def per_device(hidden, out_weight, token_blocks, counts):
     vocab_here, columns_here = out_weight.shape
+    n_vocab = lax.psum(1, "vocab")
+    n_dp = lax.psum(1, "dp")
     n_tb = vocab_here // TB
     block_lists = token_blocks[0]
     block_counts = counts[0]
     n_blk = block_lists.shape[0]
     own_blocks = hidden.shape[0] // BB
-    first_block = lax.axis_index("dp") * own_blocks
-    own_counts = lax.dynamic_slice_in_dim(block_counts, first_block, own_blocks, 0)
-    assert own_blocks == 1 and n_blk == lax.psum(1, "dp")
-
-    n_vocab = lax.psum(1, "vocab")
-    n_dp = lax.psum(1, "dp")
+    assert own_blocks == 1 and n_blk == n_dp
+    me_dp = lax.axis_index("dp")
+    own_counts = lax.dynamic_slice_in_dim(block_counts, me_dp, 1, 0)
+    rows_per_dev = n_blk * BB // n_vocab
+    devs_per_block = BB // rows_per_dev
+    half_rows = rows_per_dev // 2
+
     with jax.named_scope("hidden_spread"):
         row_slices = permute_all_to_all(hidden, "vocab", n_vocab, split_axis=0, concat_axis=1)
         plane_rows = permute_all_to_all(row_slices, "dp", n_dp, split_axis=1, concat_axis=0)
@@ -157,37 +160,59 @@
         beam_columns = (
             gathered.reshape(n_vocab, n_dp, group, columns_here)
             .transpose(1, 0, 2, 3)
-            .reshape(n_dp * n_vocab * group, columns_here)
+            .reshape(n_blk, devs_per_block, 2, half_rows, columns_here)
         )
 
-    with jax.named_scope("dense_logits"):
-        full = jnp.einsum(
-            "bd,vd->bv", beam_columns, out_weight, preferred_element_type=jnp.float32
-        )
-        full4 = full.reshape(n_blk, BB, n_tb, TB)
-        rows = jnp.arange(n_blk, dtype=jnp.int32)[:, None]
-        picked = full4[rows, :, block_lists, :]
-
-    logits = lax.psum_scatter(picked, "dp", scatter_dimension=0, tiled=True)
-
-    with jax.named_scope("softmax_stats"):
-        live = jnp.arange(MOST, dtype=jnp.int32)[None, :] < own_counts[:, None]
-        live_mask = live[:, :, None, None]
-        masked = jnp.where(live_mask, logits, -jnp.inf)
-        local_max = jnp.max(masked, axis=(1, 3))
-        local_total = jnp.sum(jnp.exp(masked - local_max[:, None, :, None]), axis=(1, 3))
-        stats = small_all_gather(jnp.stack([local_max, local_total]), n_vocab)
-        beam_max = jnp.max(stats[:, 0], axis=0)
-        beam_total = jnp.sum(stats[:, 1] * jnp.exp(stats[:, 0] - beam_max[None]), axis=0)
-        shifted = logits - beam_max[:, None, :, None] - jnp.log(beam_total)[:, None, :, None]
-        allowed_logprob = jnp.where(live_mask, shifted, 0.0)
-        probabilities = jnp.where(live_mask, jnp.exp(shifted), 0.0).astype(jnp.bfloat16)
-
-    with jax.named_scope("expected_ring"):
-        embedding_part = ring_expected(
-            probabilities[0], block_lists, out_weight, n_dp, n_blk, n_tb
-        )
-    summed = halving_reduce_scatter(embedding_part, n_vocab)
+    live = jnp.arange(MOST, dtype=jnp.int32)[None, :] < own_counts[:, None]
+    live_mask = live[:, :, None, None]
+    block_ids = jnp.arange(n_blk, dtype=jnp.int32)[:, None]
+    onehot = (
+        block_lists[:, :, None] == jnp.arange(n_tb, dtype=jnp.int32)[None, None, :]
+    ).astype(jnp.bfloat16)
+
+    logprob_parts, summed_parts = [], []
+    for part in range(2):
+        with jax.named_scope("dense_logits"):
+            beams = beam_columns[:, :, part].reshape(n_blk * BB // 2, columns_here)
+            full = jnp.einsum(
+                "bd,vd->bv", beams, out_weight, preferred_element_type=jnp.float32
+            )
+            full4 = full.reshape(n_blk, BB // 2, n_tb, TB)
+            picked = full4[block_ids, :, block_lists, :]
+        logits = lax.psum_scatter(picked, "dp", scatter_dimension=0, tiled=True)
+
+        with jax.named_scope("softmax_stats"):
+            masked = jnp.where(live_mask, logits, -jnp.inf)
+            local_max = jnp.max(masked, axis=(1, 3))
+            local_total = jnp.sum(jnp.exp(masked - local_max[:, None, :, None]), axis=(1, 3))
+            stats = lax.all_gather(jnp.stack([local_max, local_total]), "vocab", axis=0)
+            beam_max = jnp.max(stats[:, 0], axis=0)
+            beam_total = jnp.sum(stats[:, 1] * jnp.exp(stats[:, 0] - beam_max[None]), axis=0)
+            shifted = logits - beam_max[:, None, :, None] - jnp.log(beam_total)[:, None, :, None]
+            logprob_parts.append(jnp.where(live_mask, shifted, 0.0))
+            probabilities = jnp.where(live_mask, jnp.exp(shifted), 0.0).astype(jnp.bfloat16)
+
+        prob_part = lax.all_gather(probabilities, "dp", axis=0, tiled=True)
+
+        with jax.named_scope("dense_expected"):
+            spread = jnp.einsum(
+                "bsk,bsrt->brkt", onehot, prob_part, preferred_element_type=jnp.float32
+            ).astype(jnp.bfloat16)
+            embedding_part = jnp.einsum(
+                "bv,vd->bd",
+                spread.reshape(n_blk * BB // 2, n_tb * TB),
+                out_weight,
+                preferred_element_type=jnp.float32,
+            )
+        summed_parts.append(halving_reduce_scatter(embedding_part, n_vocab))
+
+    def interleave(a, b, axis):
+        shape = a.shape[:axis] + (devs_per_block, half_rows) + a.shape[axis + 1 :]
+        joined = jnp.stack([a.reshape(shape), b.reshape(shape)], axis=axis + 1)
+        return joined.reshape(a.shape[:axis] + (2 * a.shape[axis],) + a.shape[axis + 1 :])
+
+    allowed_logprob = interleave(logprob_parts[0], logprob_parts[1], 2)
+    summed = jnp.concatenate(summed_parts, axis=0)
     squares = butterfly_sum(jnp.sum(summed * summed, axis=1), "dp", n_dp)
     width = hidden.shape[1] * n_vocab
     expected = summed * lax.rsqrt(squares / width + 1e-06)[:, None]

time: 305 us -> 274 us (0.90)
  local copies, waits for them, and re-layouts: 45.7 us -> 18.5 us
  matrix products: 51.6 us -> 24.9 us
  blocking collectives: 0 us -> 17.8 us
  waiting for transfers between devices: 138 us -> 152 us
  starting transfers between devices: 38 us -> 32.8 us
    all_gather x0 -> x2, waiting for transfers between devices: none -> 43.2 us  [per_device(): prob_part = lax.all_gather(probabilities, 'dp', axis=0, tiled=True)]
    dot_general x15 -> x6, matrix products: 51.6 us -> 24.9 us  [the longest x2 11.7 us: per_device(): jnp.einsum('bv,vd->bd', spread.reshape(n_blk * BB // 2, n_tb * TB), out_w...]
    all_gather x0 -> x2, blocking collectives: none -> 17.8 us  [per_device(): stats = lax.all_gather(jnp.stack([local_max, local_total]), 'vocab', axis=0)]
    ppermute x6 -> x0, waiting for transfers between devices: 12.8 us -> none  [the longest x3 12.8 us: ring_expected(): from_right = lax.ppermute(from_right, 'dp', perm=leftward)]
    ppermute x5 -> x10, waiting for transfers between devices: 20.5 us -> 9.2 us  [exchange_stage(): got = lax.ppermute(send, 'vocab', perm=perm)]
    ppermute x6 -> x0, starting transfers between devices: 9.93 us -> none  [the longest x3 5.59 us: ring_expected(): from_left = lax.ppermute(from_left, 'dp', perm=rightward)]
    dynamic_slice x7 -> x1, local copies, waits for them, and re-layouts: 10.1 us -> 0.59 us  [per_device(): own_counts = lax.dynamic_slice_in_dim(block_counts, me_dp, 1, 0)]
    convert_element_type x7 -> x0, local copies, waits for them, and re-layouts: 8.94 us -> none  [spread_block(): spread = jnp.einsum('sk,srt->rkt', onehot, probs_block, preferred_element...]
  transfers between devices with their start and end apart: 33 -> 32, of which waited for: 21 -> 22; matrix products, arithmetic and copies ran while one was open for 10% -> 14% of each run, Pallas kernels for 0% -> 0%
where the time goes in v6:
time: 274 us; the launch traced here: 273 us
  waiting for transfers between devices  152 us (55%)
  starting transfers between devices  32.8 us (12%)
  matrix products  24.9 us (9%)
  local copies, waits for them, and re-layouts  18.5 us (7%)
  blocking collectives  17.8 us (6%)
  between operations  14.6 us (5%)
  other arithmetic  12.9 us (5%)
    reduce_scatter x2, waiting for transfers between devices, per_device(): logits = lax.psum_scatter(picked, 'dp', scatter_dimension=0, tiled=True)  78.4 us
    all_gather x2, waiting for transfers between devices, per_device(): prob_part = lax.all_gather(probabilities, 'dp', axis=0, tiled=True)  43.2 us
    all_gather x2, blocking collectives, per_device(): stats = lax.all_gather(jnp.stack([local_max, local_total]), 'vocab', axis=0)  17.8 us
    ppermute x10, starting transfers between devices, permute_all_to_all(): got.append(lax.ppermute(send, axis_name, perm=perm))  15.5 us
    dot_general x2, matrix products, per_device(): jnp.einsum('bv,vd->bd', spread.reshape(n_blk * BB // 2, n_tb * TB), out_w...  11.7 us
    ppermute x6, waiting for transfers between devices, gather_stage(): got = lax.ppermute(x, 'vocab', perm=perm)  11.3 us
    ppermute x10, starting transfers between devices, exchange_stage(): got = lax.ppermute(send, 'vocab', perm=perm)  10.5 us
    ppermute x10, waiting for transfers between devices, exchange_stage(): got = lax.ppermute(send, 'vocab', perm=perm)  9.2 us
  transfers between devices with their start and end apart: 32, of which 22 were waited for; matrix products, arithmetic and copies ran while one was open for 14% of the time, Pallas kernels for 0%

profile of v6, /device:TPU:0, one launch (start us, length us, event | category | flops | bytes accessed | tf_op | source)
XLA Modules:
  0.0 273.3 jit_solution(13985944233673856768)
XLA Ops:
  7.3 0.9 dynamic-slice_bitcast_fusion.10
  8.8 2.5 collective-permute-start.1
  11.3 2.4 collective-permute-start.2
  14.5 1.5 collective-permute-start.5
  16.0 2.3 collective-permute-start.6
  18.6 1.3 collective-permute-done.6
  21.5 1.6 collective-permute-start.7
  23.1 2.7 collective-permute-start.8
  25.8 1.4 collective-permute-start.9
  27.3 0.9 collective-permute-done.7
  28.2 2.8 %collective-permute-done.8 = bf16[16,2048]{1,0:T(8,128)(2,1)S(1)} collective-permute-done((bf16[16,2048]{1,0:T(8,128)(2,1)S(1)}, bf16[16,2048]{1,0:T(8,128)(2,1)S(1)}, u32[]{:S(2)}, u32[]{:S(2)}) %collective-permute-start.8) | collective-permute-done | bytes 65568 | tf_op jit(solution)/shard_map/hidden_spread/ppermute | solution.py:51
  32.2 1.2 collective-permute-start.10
  33.5 3.8 %collective-permute-done.10 = bf16[64,1024]{1,0:T(8,128)(2,1)S(1)} collective-permute-done((bf16[64,1024]{1,0:T(8,128)(2,1)S(1)}, bf16[64,1024]{1,0:T(8,128)(2,1)S(1)}, u32[]{:S(2)}, u32[]{:S(2)}) %collective-permute-start.10) | collective-permute-done | bytes 131104 | tf_op jit(solution)/shard_map/hidden_spread/hidden_gather_stage/ppermute | solution.py:62
  37.3 0.6 collective-permute-start.11
  38.5 1.2 collective-permute-start.14
  39.7 4.6 %collective-permute-done.11 = bf16[2,64,1024]{2,1,0:T(8,128)(2,1)S(1)} collective-permute-done((bf16[2,64,1024]{2,1,0:T(8,128)(2,1)S(1)}, bf16[2,64,1024]{2,1,0:T(8,128)(2,1)S(1)}, u32[]{:S(2)}, u32[]{:S(2)}) %collective-permute-start.11) | collective-permute-done | bytes 262176 | tf_op jit(solution)/shard_map/hidden_spread/hidden_gather_stage/ppermute | solution.py:62
  44.5 1.0 collective-permute-done.14
  46.6 0.9 collective-permute-done.15
  48.5 1.4 slice-done.1
  50.3 2.9 %fusion.39 = f32[4,64,19,128]{3,1,2,0:T(8,128)S(1)} fusion(bf16[4,64,2048,1]{2,1,3,0:T(8,128)(2,1)S(1)} %bitcast.243, bf16[19,128,2048,1]{2,1,0,3:T(8,128)(2,1)S(1)} %bitcast.275), kind=kOutput, calls=%fused_computation.160 | convolution fusion | flops 2550136832 | bytes 13500416 | tf_op jit(solution)/shard_map/dense_logits/bd,vd->bv/dot_general | solution.py:177
  53.2 2.2 gather_fusion.2
  55.4 6.0 %fusion.40 = f32[4,64,19,128]{3,1,2,0:T(8,128)S(1)} fusion(bf16[4,64,2048,1]{2,1,3,0:T(8,128)(2,1)S(1)} %bitcast.242, bf16[19,128,2048,1]{2,1,0,3:T(8,128)(2,1)} %bitcast.272), kind=kOutput, calls=%fused_computation.161 | convolution fusion | flops 2550136832 | bytes 13500416 | tf_op jit(solution)/shard_map/dense_logits/bd,vd->bv/dot_general | solution.py:177
  61.4 2.1 gather_fusion.3
  63.6 0.6 constant_dynamic-slice_fusion.4
  64.2 0.6 iota_compare_fusion.1
  64.9 34.6 %reduce-scatter.3.cloned.1.call-done = f32[1,16,64,128]{3,2,1,0:T(8,128)} async-done(((f32[4,16,64,128]{3,2,1,0:T(8,128)}), f32[1,16,64,128]{3,2,1,0:T(8,128)}) %reduce-scatter.3.cloned.1.call-update) | async-done | bytes 524304 | tf_op jit(solution)/shard_map/reduce_scatter | solution.py:182
  99.5 1.3 select_reduce_fusion.1
  100.8 43.8 %reduce-scatter.5.cloned.1.call-done = f32[1,16,64,128]{3,2,1,0:T(8,128)} async-done(((f32[4,16,64,128]{3,2,1,0:T(8,128)}), f32[1,16,64,128]{3,2,1,0:T(8,128)}) %reduce-scatter.5.cloned.1.call-update) | async-done | bytes 524304 | tf_op jit(solution)/shard_map/reduce_scatter | solution.py:182
  144.6 1.5 exponential_reduce_fusion.1
  146.1 1.3 exponential_reduce_fusion
  147.5 8.9 %all-gather.1 = f32[16,1,64]{2,1,0:T(1,128)S(1)} all-gather(f32[2,1,64]{2,1,0:T(1,128)S(1)} %pad_maximum_fusion.6), channel_id=3, replica_groups=mesh['dp'=4,'vocab'=8] {'vocab'}, dimensions={0}, use_global_device_ids=true | all-gather | bytes 4608 | tf_op jit(solution)/shard_map/softmax_stats/all_gather | solution.py:188
  156.4 8.9 %all-gather = f32[16,1,64]{2,1,0:T(1,128)S(1)} all-gather(f32[2,1,64]{2,1,0:T(1,128)S(1)} %pad_maximum_fusion.5), channel_id=2, replica_groups=mesh['dp'=4,'vocab'=8] {'vocab'}, dimensions={0}, use_global_device_ids=true | all-gather | bytes 4608 | tf_op jit(solution)/shard_map/softmax_stats/all_gather | solution.py:188
  165.4 2.3 select_convert_fusion.1
  168.3 25.8 %all-gather.5.cloned.1.call-done = bf16[4,16,64,128]{3,2,1,0:T(8,128)(2,1)} async-done(((bf16[1,16,64,128]{3,2,1,0:T(8,128)(2,1)}), bf16[4,16,64,128]{3,2,1,0:T(8,128)(2,1)}) %all-gather.5.cloned.1.call-update) | async-done | bytes 1048592 | tf_op jit(solution)/shard_map/all_gather | solution.py:195
  194.2 2.2 fusion.4
  196.3 1.6 dot_general.34
  197.9 5.9 %fusion.2 = f32[2,2,2,32,2048]{4,3,2,1,0:T(8,128)S(1)} fusion(bf16[2,2,2,32,2432]{4,3,2,1,0:T(8,128)(2,1)} %dot_general.34, bf16[2432,2048]{1,0:T(8,128)(2,1)} %param.5), kind=kOutput, calls=%fused_computation.6 | convolution fusion | flops 2550136832 | bytes 13303808 | tf_op jit(solution)/shard_map/dense_expected/bv,vd->bd/dot_general | solution.py:201
  203.8 1.3 copy-done.3
  205.1 1.1 dynamic-slice_bitcast_fusion.1
  206.2 17.3 %all-gather.7.cloned.1.call-done = bf16[4,16,64,128]{3,2,1,0:T(8,128)(2,1)} async-done(((bf16[1,16,64,128]{3,2,1,0:T(8,128)(2,1)}), bf16[4,16,64,128]{3,2,1,0:T(8,128)(2,1)}) %all-gather.7.cloned.1.call-update) | async-done | bytes 1048592 | tf_op jit(solution)/shard_map/all_gather | solution.py:195
  223.5 2.2 fusion.5
  225.7 1.6 dot_general.37
  227.3 5.9 %fusion = f32[2,2,2,32,2048]{4,3,2,1,0:T(8,128)S(1)} fusion(bf16[2,2,2,32,2432]{4,3,2,1,0:T(8,128)(2,1)} %dot_general.37, bf16[2432,2048]{1,0:T(8,128)(2,1)} %param.5), kind=kOutput, calls=%fused_computation.4 | convolution fusion | flops 2550136832 | bytes 13303808 | tf_op jit(solution)/shard_map/dense_expected/bv,vd->bd/dot_general | solution.py:201
  233.1 1.0 dynamic-slice_bitcast_fusion
  234.2 1.7 bitcast_add_fusion.1
  236.0 1.5 collective-permute-start.17
  237.5 1.5 collective-permute-start.19
  239.1 1.4 bitcast_add_fusion
  240.6 0.6 collective-permute-start.22
  241.3 0.6 collective-permute-start.24
  241.9 3.4 %collective-permute-done.17 = f32[2,32,1024]{2,1,0:T(8,128)S(1)} collective-permute-done((f32[2,32,1024]{2,1,0:T(8,128)S(1)}, f32[2,32,1024]{2,1,0:T(8,128)S(1)}, u32[]{:S(2)}, u32[]{:S(2)}) %collective-permute-start.17) | collective-permute-done | bytes 262176 | tf_op jit(solution)/shard_map/summed_chip_stage/ppermute | solution.py:18
  245.3 1.5 collective-permute-start.18
  246.9 1.5 collective-permute-start.20
  248.4 2.4 collective-permute-done.22
  250.9 1.5 collective-permute-start.23
  252.5 1.5 collective-permute-start.25
  254.1 1.2 collective-permute-done.18
  255.3 2.0 collective-permute-done.23
  257.7 1.5 collective-permute-start.26
  259.2 2.1 collective-permute-done.26
  261.3 1.8 collective-permute-start.27
  263.2 1.1 copy.48
  264.3 1.5 collective-permute-done.27
  265.8 0.9 fusion.10
  (133 shorter events, 9.3 us)
Async XLA Ops:
  7.2 56.5 %copy-start = (s32[1,4]{1,0:T(1,128)S(1)}, s32[1,4]{1,0:T(1,128)}, u32[]{:S(2)}) copy-start(s32[1,4]{1,0:T(1,128)} %param.7) | copy-start | bytes 52
  7.2 92.3 %reduce-scatter.3.cloned.1.call-start = ((), (), s32[]{:S(2)}) async-start(), calls=%async_computation.2 | async-start | bytes 2621440 | tf_op jit(solution)/shard_map/reduce_scatter | solution.py:182
  8.2 6.3 %collective-permute-start = (bf16[16,1024]{1,0:T(8,128)(2,1)S(1)}, bf16[16,1024]{1,0:T(8,128)(2,1)S(1)}, u32[]{:S(2)}, u32[]{:S(2)}) collective-permute-start(bf16[16,1024]{1,0:T(8,128)(2,1)S(1)} %get-tuple-element.36), channel_id=1, source_target_pairs={{0,1},{1,2},{2,3},{3,4},{4,5},{5,6},{6,7},{7,0},{8,9},{9,10},{10,1... | collective-permute-start | bytes 98312 | tf_op jit(solution)/shard_map/hidden_spread/ppermute | solution.py:51
  8.8 7.2 %collective-permute-start.1 = (bf16[16,1024]{1,0:T(8,128)(2,1)S(1)}, bf16[16,1024]{1,0:T(8,128)(2,1)S(1)}, u32[]{:S(2)}, u32[]{:S(2)}) collective-permute-start(bf16[16,1024]{1,0:T(8,128)(2,1)S(1)} %get-tuple-element.35), channel_id=1, source_target_pairs={{0,2},{1,3},{2,4},{3,5},{4,6},{5,7},{6,0},{7,1},{8,10},{9,11},{10,... | collective-permute-start | bytes 98312 | tf_op jit(solution)/shard_map/hidden_spread/ppermute | solution.py:51
  11.3 7.0 %collective-permute-start.2 = (bf16[16,1024]{1,0:T(8,128)(2,1)S(1)}, bf16[16,1024]{1,0:T(8,128)(2,1)S(1)}, u32[]{:S(2)}, u32[]{:S(2)}) collective-permute-start(bf16[16,1024]{1,0:T(8,128)(2,1)S(1)} %get-tuple-element.34), channel_id=1, source_target_pairs={{0,3},{1,4},{2,5},{3,6},{4,7},{5,0},{6,1},{7,2},{8,11},{9,12},{10,... | collective-permute-start | bytes 98312 | tf_op jit(solution)/shard_map/hidden_spread/ppermute | solution.py:51
  13.7 4.6 %collective-permute-start.3 = (bf16[16,1024]{1,0:T(8,128)(2,1)S(1)}, bf16[16,1024]{1,0:T(8,128)(2,1)S(1)}, u32[]{:S(2)}, u32[]{:S(2)}) collective-permute-start(bf16[16,1024]{1,0:T(8,128)(2,1)S(1)} %get-tuple-element.33), channel_id=1, source_target_pairs={{0,4},{1,5},{2,6},{3,7},{4,0},{5,1},{6,2},{7,3},{8,12},{9,13},{10,... | collective-permute-start | bytes 98312 | tf_op jit(solution)/shard_map/hidden_spread/ppermute | solution.py:51
  14.2 4.2 %collective-permute-start.4 = (bf16[16,1024]{1,0:T(8,128)(2,1)S(1)}, bf16[16,1024]{1,0:T(8,128)(2,1)S(1)}, u32[]{:S(2)}, u32[]{:S(2)}) collective-permute-start(bf16[16,1024]{1,0:T(8,128)(2,1)S(1)} %get-tuple-element.32), channel_id=1, source_target_pairs={{0,5},{1,6},{2,7},{3,0},{4,1},{5,2},{6,3},{7,4},{8,13},{9,14},{10,... | collective-permute-start | bytes 98312 | tf_op jit(solution)/shard_map/hidden_spread/ppermute | solution.py:51
  14.5 4.1 %collective-permute-start.5 = (bf16[16,1024]{1,0:T(8,128)(2,1)S(1)}, bf16[16,1024]{1,0:T(8,128)(2,1)S(1)}, u32[]{:S(2)}, u32[]{:S(2)}) collective-permute-start(bf16[16,1024]{1,0:T(8,128)(2,1)S(1)} %get-tuple-element.31), channel_id=1, source_target_pairs={{0,6},{1,7},{2,0},{3,1},{4,2},{5,3},{6,4},{7,5},{8,14},{9,15},{10,... | collective-permute-start | bytes 98312 | tf_op jit(solution)/shard_map/hidden_spread/ppermute | solution.py:51
  16.0 3.9 %collective-permute-start.6 = (bf16[16,1024]{1,0:T(8,128)(2,1)S(1)}, bf16[16,1024]{1,0:T(8,128)(2,1)S(1)}, u32[]{:S(2)}, u32[]{:S(2)}) collective-permute-start(bf16[16,1024]{1,0:T(8,128)(2,1)S(1)} %get-tuple-element.30), channel_id=1, source_target_pairs={{0,7},{1,0},{2,1},{3,2},{4,3},{5,4},{6,5},{7,6},{8,15},{9,8},{10,9... | collective-permute-start | bytes 98312 | tf_op jit(solution)/shard_map/hidden_spread/ppermute | solution.py:51
  21.5 6.7 %collective-permute-start.7 = (bf16[16,2048]{1,0:T(8,128)(2,1)S(1)}, bf16[16,2048]{1,0:T(8,128)(2,1)S(1)}, u32[]{:S(2)}, u32[]{:S(2)}) collective-permute-start(bf16[16,2048]{1,0:T(8,128)(2,1)S(1)} %bitcast.252), channel_id=1, source_target_pairs={{0,8},{8,16},{16,24},{24,0},{1,9},{9,17},{17,25},{25,1},{2,10},{10... | collective-permute-start | bytes 196616 | tf_op jit(solution)/shard_map/hidden_spread/ppermute | solution.py:51
  23.1 10.3 %copy-start.4 = (s32[1,4,16]{2,1,0:T(4,128)S(1)}, s32[1,4,16]{2,1,0:T(4,128)}, u32[]{:S(2)}) copy-start(s32[1,4,16]{2,1,0:T(4,128)} %param.6) | copy-start | bytes 772
  23.1 7.8 %collective-permute-start.8 = (bf16[16,2048]{1,0:T(8,128)(2,1)S(1)}, bf16[16,2048]{1,0:T(8,128)(2,1)S(1)}, u32[]{:S(2)}, u32[]{:S(2)}) collective-permute-start(bf16[16,2048]{1,0:T(8,128)(2,1)S(1)} %bitcast.253), channel_id=1, source_target_pairs={{0,16},{8,24},{16,0},{24,8},{1,17},{9,25},{17,1},{25,9},{2,18},{10... | collective-permute-start | bytes 196616 | tf_op jit(solution)/shard_map/hidden_spread/ppermute | solution.py:51
  25.8 5.5 %collective-permute-start.9 = (bf16[16,2048]{1,0:T(8,128)(2,1)S(1)}, bf16[16,2048]{1,0:T(8,128)(2,1)S(1)}, u32[]{:S(2)}, u32[]{:S(2)}) collective-permute-start(bf16[16,2048]{1,0:T(8,128)(2,1)S(1)} %bitcast.254), channel_id=1, source_target_pairs={{0,24},{8,0},{16,8},{24,16},{1,25},{9,1},{17,9},{25,17},{2,26},{10... | collective-permute-start | bytes 196616 | tf_op jit(solution)/shard_map/hidden_spread/ppermute | solution.py:51
  32.2 5.1 %collective-permute-start.10 = (bf16[64,1024]{1,0:T(8,128)(2,1)S(1)}, bf16[64,1024]{1,0:T(8,128)(2,1)S(1)}, u32[]{:S(2)}, u32[]{:S(2)}) collective-permute-start(bf16[64,1024]{1,0:T(8,128)(2,1)S(1)} %get-tuple-element.21), channel_id=1, source_target_pairs={{0,2},{1,3},{2,0},{3,1},{4,6},{5,7},{6,4},{7,5},{8,10},{9,11},{10,... | collective-permute-start | bytes 393224 | tf_op jit(solution)/shard_map/hidden_spread/hidden_gather_stage/ppermute | solution.py:62
  33.5 5.0 %collective-permute-start.13 = (bf16[64,1024]{1,0:T(8,128)(2,1)S(1)}, bf16[64,1024]{1,0:T(8,128)(2,1)S(1)}, u32[]{:S(2)}, u32[]{:S(2)}) collective-permute-start(bf16[64,1024]{1,0:T(8,128)(2,1)S(1)} %get-tuple-element.20), channel_id=1, source_target_pairs={{0,4},{1,5},{2,6},{3,7},{4,0},{5,1},{6,2},{7,3},{8,12},{9,13},{10,... | collective-permute-start | bytes 393224 | tf_op jit(solution)/shard_map/hidden_spread/hidden_gather_stage/ppermute | solution.py:62
  37.3 7.0 %collective-permute-start.11 = (bf16[2,64,1024]{2,1,0:T(8,128)(2,1)S(1)}, bf16[2,64,1024]{2,1,0:T(8,128)(2,1)S(1)}, u32[]{:S(2)}, u32[]{:S(2)}) collective-permute-start(bf16[2,64,1024]{2,1,0:T(8,128)(2,1)S(1)} %maximum_select_fusion.5), channel_id=1, source_target_pairs={{0,4},{1,5},{2,6},{3,7},{4,0},{5,1},{6,2},{7,3},{8,12},{9,13},{10,... | collective-permute-start | bytes 786440 | tf_op jit(solution)/shard_map/hidden_spread/hidden_gather_stage/ppermute | solution.py:62
  38.5 7.0 %collective-permute-start.14 = (bf16[2,64,1024]{2,1,0:T(8,128)(2,1)S(1)}, bf16[2,64,1024]{2,1,0:T(8,128)(2,1)S(1)}, u32[]{:S(2)}, u32[]{:S(2)}) collective-permute-start(bf16[2,64,1024]{2,1,0:T(8,128)(2,1)S(1)} %maximum_select_fusion.7), channel_id=1, source_target_pairs={{0,2},{1,3},{2,0},{3,1},{4,6},{5,7},{6,4},{7,5},{8,10},{9,11},{10,... | collective-permute-start | bytes 786440 | tf_op jit(solution)/shard_map/hidden_spread/hidden_gather_stage/ppermute | solution.py:62
  44.4 2.0 collective-permute-start.12
  45.6 2.0 collective-permute-start.15
  45.9 2.6 slice-start
  47.6 2.3 slice-start.1
  48.0 2.2 slice-start.2
  55.4 89.3 %reduce-scatter.5.cloned.1.call-start = ((), (), s32[]{:S(2)}) async-start(), calls=%async_computation.3 | async-start | bytes 2621440 | tf_op jit(solution)/shard_map/reduce_scatter | solution.py:182
  63.6 130.6 %all-gather.5.cloned.1.call-start = ((), (), s32[]{:S(2)}) async-start(), calls=%async_computation.4 | async-start | bytes 1310720 | tf_op jit(solution)/shard_map/all_gather | solution.py:195
  99.5 65.9 %copy-start.2 = (f32[1,16,64,128]{3,2,1,0:T(8,128)S(1)}, f32[1,16,64,128]{3,2,1,0:T(8,128)}, u32[]{:S(2)}) copy-start(f32[1,16,64,128]{3,2,1,0:T(8,128)} %reduce-scatter.3.cloned.1.call-done) | copy-start | bytes 1572868
  167.7 55.8 %all-gather.7.cloned.1.call-start = ((), (), s32[]{:S(2)}) async-start(), calls=%async_computation.5 | async-start | bytes 1310720 | tf_op jit(solution)/shard_map/all_gather | solution.py:195
  203.8 1.4 copy-start.3
  206.2 28.0 %collective-permute-start.16 = (f32[2,2,32,2048]{3,2,1,0:T(8,128)}, f32[2,2,32,2048]{3,2,1,0:T(8,128)}, u32[]{:S(2)}, u32[]{:S(2)}) collective-permute-start(f32[2,2,32,2048]{3,2,1,0:T(8,128)} %dynamic-slice_bitcast_fusion.1), channel_id=1, source_target_pairs={{0,1},{1,0},{2,3},{3,2},{4,5},{5,4},{6,7},{7,6},{8,9},{9,8},{10,11... | collective-permute-start | bytes 3145736 | tf_op jit(solution)/shard_map/summed_core_stage/ppermute | solution.py:18
  234.2 4.9 %collective-permute-start.21 = (f32[2,2,32,2048]{3,2,1,0:T(8,128)}, f32[2,2,32,2048]{3,2,1,0:T(8,128)}, u32[]{:S(2)}, u32[]{:S(2)}) collective-permute-start(f32[2,2,32,2048]{3,2,1,0:T(8,128)} %dynamic-slice_bitcast_fusion), channel_id=1, source_target_pairs={{0,1},{1,0},{2,3},{3,2},{4,5},{5,4},{6,7},{7,6},{8,9},{9,8},{10,11... | collective-permute-start | bytes 3145736 | tf_op jit(solution)/shard_map/summed_core_stage/ppermute | solution.py:18
  236.0 9.2 %collective-permute-start.17 = (f32[2,32,1024]{2,1,0:T(8,128)S(1)}, f32[2,32,1024]{2,1,0:T(8,128)S(1)}, u32[]{:S(2)}, u32[]{:S(2)}) collective-permute-start(f32[2,32,1024]{2,1,0:T(8,128)S(1)} %dynamic-slice_bitcast_fusion.5), channel_id=1, source_target_pairs={{0,2},{1,3},{2,0},{3,1},{4,6},{5,7},{6,4},{7,5},{8,10},{9,11},{10,... | collective-permute-start | bytes 786440 | tf_op jit(solution)/shard_map/summed_chip_stage/ppermute | solution.py:18
  237.5 9.3 %collective-permute-start.19 = (f32[2,32,1024]{2,1,0:T(8,128)S(1)}, f32[2,32,1024]{2,1,0:T(8,128)S(1)}, u32[]{:S(2)}, u32[]{:S(2)}) collective-permute-start(f32[2,32,1024]{2,1,0:T(8,128)S(1)} %dynamic-slice_bitcast_fusion.4), channel_id=1, source_target_pairs={{0,4},{1,5},{2,6},{3,7},{4,0},{5,1},{6,2},{7,3},{8,12},{9,13},{10,... | collective-permute-start | bytes 786440 | tf_op jit(solution)/shard_map/summed_chip_stage/ppermute | solution.py:18
  240.6 10.2 %collective-permute-start.22 = (f32[2,32,1024]{2,1,0:T(8,128)S(1)}, f32[2,32,1024]{2,1,0:T(8,128)S(1)}, u32[]{:S(2)}, u32[]{:S(2)}) collective-permute-start(f32[2,32,1024]{2,1,0:T(8,128)S(1)} %dynamic-slice_bitcast_fusion.3), channel_id=1, source_target_pairs={{0,2},{1,3},{2,0},{3,1},{4,6},{5,7},{6,4},{7,5},{8,10},{9,11},{10,... | collective-permute-start | bytes 786440 | tf_op jit(solution)/shard_map/summed_chip_stage/ppermute | solution.py:18
  241.3 11.2 %collective-permute-start.24 = (f32[2,32,1024]{2,1,0:T(8,128)S(1)}, f32[2,32,1024]{2,1,0:T(8,128)S(1)}, u32[]{:S(2)}, u32[]{:S(2)}) collective-permute-start(f32[2,32,1024]{2,1,0:T(8,128)S(1)} %dynamic-slice_bitcast_fusion.2), channel_id=1, source_target_pairs={{0,4},{1,5},{2,6},{3,7},{4,0},{5,1},{6,2},{7,3},{8,12},{9,13},{10,... | collective-permute-start | bytes 786440 | tf_op jit(solution)/shard_map/summed_chip_stage/ppermute | solution.py:18
  245.3 9.9 %collective-permute-start.18 = (f32[32,1024]{1,0:T(8,128)S(1)}, f32[32,1024]{1,0:T(8,128)S(1)}, u32[]{:S(2)}, u32[]{:S(2)}) collective-permute-start(f32[32,1024]{1,0:T(8,128)S(1)} %dynamic-slice_bitcast_fusion.9), channel_id=1, source_target_pairs={{0,4},{1,5},{2,6},{3,7},{4,0},{5,1},{6,2},{7,3},{8,12},{9,13},{10,... | collective-permute-start | bytes 393224 | tf_op jit(solution)/shard_map/summed_chip_stage/ppermute | solution.py:18
  246.9 8.3 %collective-permute-start.20 = (f32[32,1024]{1,0:T(8,128)S(1)}, f32[32,1024]{1,0:T(8,128)S(1)}, u32[]{:S(2)}, u32[]{:S(2)}) collective-permute-start(f32[32,1024]{1,0:T(8,128)S(1)} %dynamic-slice_bitcast_fusion.8), channel_id=1, source_target_pairs={{0,2},{1,3},{2,0},{3,1},{4,6},{5,7},{6,4},{7,5},{8,10},{9,11},{10,... | collective-permute-start | bytes 393224 | tf_op jit(solution)/shard_map/summed_chip_stage/ppermute | solution.py:18
  250.9 6.4 %collective-permute-start.23 = (f32[32,1024]{1,0:T(8,128)S(1)}, f32[32,1024]{1,0:T(8,128)S(1)}, u32[]{:S(2)}, u32[]{:S(2)}) collective-permute-start(f32[32,1024]{1,0:T(8,128)S(1)} %dynamic-slice_bitcast_fusion.7), channel_id=1, source_target_pairs={{0,4},{1,5},{2,6},{3,7},{4,0},{5,1},{6,2},{7,3},{8,12},{9,13},{10,... | collective-permute-start | bytes 393224 | tf_op jit(solution)/shard_map/summed_chip_stage/ppermute | solution.py:18
  252.5 5.0 %collective-permute-start.25 = (f32[32,1024]{1,0:T(8,128)S(1)}, f32[32,1024]{1,0:T(8,128)S(1)}, u32[]{:S(2)}, u32[]{:S(2)}) collective-permute-start(f32[32,1024]{1,0:T(8,128)S(1)} %dynamic-slice_bitcast_fusion.6), channel_id=1, source_target_pairs={{0,2},{1,3},{2,0},{3,1},{4,6},{5,7},{6,4},{7,5},{8,10},{9,11},{10,... | collective-permute-start | bytes 393224 | tf_op jit(solution)/shard_map/summed_chip_stage/ppermute | solution.py:18
  257.7 3.6 %collective-permute-start.26 = (f32[64]{0:T(128)S(1)}, f32[64]{0:T(128)S(1)}, u32[]{:S(2)}, u32[]{:S(2)}) collective-permute-start(f32[64]{0:T(128)S(1)} %multiply_reduce_fusion), channel_id=1, source_target_pairs={{0,8},{8,0},{16,24},{24,16},{1,9},{9,1},{17,25},{25,17},{2,10},{10... | collective-permute-start | bytes 776 | tf_op jit(solution)/shard_map/ppermute | solution.py:98
  261.3 4.5 %collective-permute-start.27 = (f32[64]{0:T(128)S(1)}, f32[64]{0:T(128)S(1)}, u32[]{:S(2)}, u32[]{:S(2)}) collective-permute-start(f32[64]{0:T(128)S(1)} %add.347), channel_id=1, source_target_pairs={{0,16},{8,24},{16,0},{24,8},{1,17},{9,25},{17,1},{25,9},{2,18},{10... | collective-permute-start | bytes 776 | tf_op jit(solution)/shard_map/ppermute | solution.py:98
  263.1 3.6 %copy-start.1 = (s32[1,4]{1,0:T(1,128)S(1)}, s32[1,4]{1,0:T(1,128)}, u32[]{:S(2)}) copy-start(s32[1,4]{1,0:T(1,128)} %param.7) | copy-start | bytes 52
Sparse Core Ops, SparseCore 0:
  55.5 43.9 reduce-scatter.2
  101.8 42.8 reduce-scatter.4
  167.9 26.2 all-gather.4
  196.2 27.3 all-gather.6

commit v7 on v4

--- a/solution.py
+++ b/solution.py
@@ -41,7 +41,9 @@
 
 def permute_all_to_all(x, axis_name, n, split_axis, concat_axis):
     me = lax.axis_index(axis_name)
-    pieces = jnp.stack(jnp.split(x, n, axis=split_axis))
+    shape = list(x.shape)
+    shape[split_axis : split_axis + 1] = [n, x.shape[split_axis] // n]
+    pieces = jnp.moveaxis(x.reshape(shape), split_axis, 0)
     got = [lax.dynamic_index_in_dim(pieces, me, axis=0, keepdims=False)]
     for shift in range(1, n):
         send = lax.dynamic_index_in_dim(pieces, (me + shift) % n, axis=0, keepdims=False)
@@ -80,18 +82,57 @@
     return joined.reshape(n * rows, cols)
 
 
+def small_all_gather(x, n):
+    levels = n.bit_length() - 1
+    have = []
+    y = x
+    for bit in range(levels):
+        y, have = gather_stage(y, have, bit, n)
+    return y.reshape((n,) + x.shape)
+
+
+def butterfly_sum(x, axis_name, n):
+    levels = n.bit_length() - 1
+    for bit in range(levels):
+        perm = [(s, s ^ (1 << bit)) for s in range(n)]
+        x = x + lax.ppermute(x, axis_name, perm=perm)
+    return x
+
+
+def line_reduce_scatter(partials, n):
+    me = lax.axis_index("dp")
+    own = lambda block: lax.dynamic_index_in_dim(
+        partials, jnp.clip(block, 0, n - 1), axis=0, keepdims=False
+    )
+    from_left = None
+    from_right = None
+    for step in range(1, n):
+        send_up = own(me + n - step)
+        if from_left is not None:
+            send_up = send_up + from_left
+        send_down = own(me - n + step)
+        if from_right is not None:
+            send_down = send_down + from_right
+        upward = [(s, s + 1) for s in range(0, step)]
+        downward = [(s, s - 1) for s in range(n - step, n)]
+        from_left = lax.ppermute(send_up, "dp", perm=upward)
+        from_right = lax.ppermute(send_down, "dp", perm=downward)
+    return (own(me) + from_left + from_right)[None]
+
+
 def per_device(hidden, out_weight, token_blocks, counts):
     vocab_here, columns_here = out_weight.shape
+    n_vocab = lax.psum(1, "vocab")
+    n_dp = lax.psum(1, "dp")
     n_tb = vocab_here // TB
     block_lists = token_blocks[0]
     block_counts = counts[0]
     n_blk = block_lists.shape[0]
     own_blocks = hidden.shape[0] // BB
-    first_block = lax.axis_index("dp") * own_blocks
-    own_counts = lax.dynamic_slice_in_dim(block_counts, first_block, own_blocks, 0)
+    assert own_blocks == 1 and n_blk == n_dp
+    me_dp = lax.axis_index("dp")
+    own_counts = lax.dynamic_slice_in_dim(block_counts, me_dp, 1, 0)
 
-    n_vocab = lax.psum(1, "vocab")
-    n_dp = lax.psum(1, "dp")
     with jax.named_scope("hidden_spread"):
         row_slices = permute_all_to_all(hidden, "vocab", n_vocab, split_axis=0, concat_axis=1)
         plane_rows = permute_all_to_all(row_slices, "dp", n_dp, split_axis=1, concat_axis=0)
@@ -111,7 +152,8 @@
         rows = jnp.arange(n_blk, dtype=jnp.int32)[:, None]
         picked = full4[rows, :, block_lists, :]
 
-    logits = lax.psum_scatter(picked, "dp", scatter_dimension=0, tiled=True)
+    with jax.named_scope("logits_line_reduce"):
+        logits = line_reduce_scatter(picked, n_dp)
 
     with jax.named_scope("softmax_stats"):
         live = jnp.arange(MOST, dtype=jnp.int32)[None, :] < own_counts[:, None]
@@ -142,7 +184,7 @@
             preferred_element_type=jnp.float32,
         )
     summed = halving_reduce_scatter(embedding_part, n_vocab)
-    squares = lax.psum(jnp.sum(summed * summed, axis=1), "dp")
+    squares = butterfly_sum(jnp.sum(summed * summed, axis=1), "dp", n_dp)
     width = hidden.shape[1] * n_vocab
     expected = summed * lax.rsqrt(squares / width + 1e-06)[:, None]
     return (allowed_logprob[None], expected)

time: 271 us -> 296 us (1.092)
  starting transfers between devices: 23.4 us -> 40.1 us
  waiting for transfers between devices: 161 us -> 176 us
  blocking collectives: 18.6 us -> 9.25 us
  other arithmetic: 9.94 us -> 14.8 us
    ppermute x0 -> x8, waiting for transfers between devices: none -> 91 us  [the longest x3 59.5 us: line_reduce_scatter(): from_left = lax.ppermute(send_up, 'dp', perm=upward)]
    reduce_scatter x1 -> x0, waiting for transfers between devices: 74.4 us -> none  [per_device(): logits = lax.psum_scatter(picked, 'dp', scatter_dimension=0, tiled=True)]
    ppermute x0 -> x8, starting transfers between devices: none -> 16.6 us  [the longest x3 11.5 us: line_reduce_scatter(): from_left = lax.ppermute(send_up, 'dp', perm=upward)]
    psum x1 -> x0, blocking collectives: 9.51 us -> none  [per_device(): squares = lax.psum(jnp.sum(summed * summed, axis=1), 'dp')]
    add x0 -> x4, other arithmetic: none -> 6.04 us  [the longest x2 4.62 us: line_reduce_scatter(): send_up = send_up + from_left]
    unnamed x27 -> x29, local copies, waits for them, and re-layouts: 8.34 us -> 3.52 us
  transfers between devices with their start and end apart: 23 -> 30, of which waited for: 16 -> 21; matrix products, arithmetic and copies ran while one was open for 1% -> 2% of each run, Pallas kernels for 0% -> 0%
where the time goes in v7:
time: 296 us
  waiting for transfers between devices  176 us (59%)
  starting transfers between devices  40.1 us (14%)
  local copies, waits for them, and re-layouts  20.6 us (7%)
  matrix products  19.6 us (7%)
  other arithmetic  14.8 us (5%)
  between operations  14.8 us (5%)
  blocking collectives  9.25 us (3%)
    ppermute x3, waiting for transfers between devices, line_reduce_scatter(): from_left = lax.ppermute(send_up, 'dp', perm=upward)  59.5 us
    all_gather x1, waiting for transfers between devices, per_device(): prob_part = lax.all_gather(probabilities, 'dp', axis=0, tiled=True)  44.5 us
    ppermute x3, waiting for transfers between devices, line_reduce_scatter(): from_right = lax.ppermute(send_down, 'dp', perm=downward)  24.9 us
    ppermute x5, waiting for transfers between devices, exchange_stage(): got = lax.ppermute(send, 'vocab', perm=perm)  21.2 us
    ppermute x10, starting transfers between devices, permute_all_to_all(): got.append(lax.ppermute(send, axis_name, perm=perm))  14.6 us
    ppermute x6, waiting for transfers between devices, gather_stage(): got = lax.ppermute(x, 'vocab', perm=perm)  12.1 us
    ppermute x3, starting transfers between devices, line_reduce_scatter(): from_left = lax.ppermute(send_up, 'dp', perm=upward)  11.5 us
    all_gather x1, blocking collectives, per_device(): stats = lax.all_gather(jnp.stack([local_max, local_total]), 'vocab', axis=0)  9.25 us
  transfers between devices with their start and end apart: 30, of which 21 were waited for; matrix products, arithmetic and copies ran while one was open for 2% of the time, Pallas kernels for 0%

profile of v7, /device:TPU:0, one launch (start us, length us, event | category | flops | bytes accessed | tf_op | source)
XLA Modules:
  0.0 295.5 jit_solution(9907900643980951691)
XLA Ops:
  7.3 0.9 dynamic-slice_bitcast_fusion.7
  8.2 0.5 collective-permute-start
  8.8 2.5 collective-permute-start.1
  11.3 2.4 collective-permute-start.2
  14.5 1.5 collective-permute-start.5
  16.0 2.3 collective-permute-start.6
  18.6 1.3 collective-permute-done.6
  19.9 0.6 gather_fusion
  20.9 0.6 constant_dynamic-slice_fusion.3
  21.5 3.7 %collective-permute-start.9 = (bf16[16,2048]{1,0:T(8,128)(2,1)S(1)}, bf16[16,2048]{1,0:T(8,128)(2,1)S(1)}, u32[]{:S(2)}, u32[]{:S(2)}) collective-permute-start(bf16[16,2048]{1,0:T(8,128)(2,1)S(1)} %bitcast.226), channel_id=1, source_target_pairs={{0,24},{8,0},{16,8},{24,16},{1,25},{9,1},{17,9},{25,17},{2,26},{10... | collective-permute-start | bytes 196616 | tf_op jit(solution)/shard_map/hidden_spread/ppermute | solution.py:51
  25.3 1.0 collective-permute-start.7
  26.4 1.2 collective-permute-done.9
  27.7 4.8 %collective-permute-done.8 = bf16[16,2048]{1,0:T(8,128)(2,1)S(1)} collective-permute-done((bf16[16,2048]{1,0:T(8,128)(2,1)S(1)}, bf16[16,2048]{1,0:T(8,128)(2,1)S(1)}, u32[]{:S(2)}, u32[]{:S(2)}) %collective-permute-start.8) | collective-permute-done | bytes 65568 | tf_op jit(solution)/shard_map/hidden_spread/ppermute | solution.py:51
  32.5 0.6 gather_fusion.1
  33.3 0.6 collective-permute-start.13
  34.0 0.7 collective-permute-start.10
  34.7 4.2 %collective-permute-done.13 = bf16[64,1024]{1,0:T(8,128)(2,1)S(1)} collective-permute-done((bf16[64,1024]{1,0:T(8,128)(2,1)S(1)}, bf16[64,1024]{1,0:T(8,128)(2,1)S(1)}, u32[]{:S(2)}, u32[]{:S(2)}) %collective-permute-start.13) | collective-permute-done | bytes 131104 | tf_op jit(solution)/shard_map/hidden_spread/hidden_gather_stage/ppermute | solution.py:62
  38.9 1.3 collective-permute-start.14
  40.9 5.5 %collective-permute-done.14 = bf16[2,64,1024]{2,1,0:T(8,128)(2,1)S(1)} collective-permute-done((bf16[2,64,1024]{2,1,0:T(8,128)(2,1)S(1)}, bf16[2,64,1024]{2,1,0:T(8,128)(2,1)S(1)}, u32[]{:S(2)}, u32[]{:S(2)}) %collective-permute-start.14) | collective-permute-done | bytes 262176 | tf_op jit(solution)/shard_map/hidden_spread/hidden_gather_stage/ppermute | solution.py:62
  46.5 1.0 collective-permute-done.11
  48.7 0.9 collective-permute-done.12
  50.3 0.9 slice-done.1
  51.6 7.4 %fusion.29 = f32[4,128,19,128]{3,1,2,0:T(8,128)} fusion(bf16[4,128,2048,1]{2,1,3,0:T(8,128)(2,1)S(1)} %bitcast.211, bf16[19,128,2048,1]{2,1,0,3:T(8,128)(2,1)S(1)} %bitcast.241), kind=kOutput, calls=%fused_computation.139 | convolution fusion | flops 5100273664 | bytes 17039360 | tf_op jit(solution)/shard_map/dense_logits/bd,vd->bv/dot_general | solution.py:148
  58.9 5.3 %gather_fusion.2 = f32[64,128,128]{2,1,0:T(8,128)} fusion(f32[4,128,19,128]{3,1,2,0:T(8,128)} %fusion.29, s32[64]{0:T(128)S(1)} %reshape.640), kind=kCustom, calls=%fused_computation.2 | custom fusion | bytes 8389120 | tf_op jit(solution)/shard_map/dense_logits/gather | solution.py:153
  64.2 1.7 dynamic-slice_bitcast_fusion.2
  65.9 2.0 collective-permute-start.16
  67.9 1.6 collective-permute-start.19
  69.5 20.8 %collective-permute-done.16 = f32[16,128,128]{2,1,0:T(8,128)S(1)} collective-permute-done((f32[16,128,128]{2,1,0:T(8,128)S(1)}, f32[16,128,128]{2,1,0:T(8,128)S(1)}, u32[]{:S(2)}, u32[]{:S(2)}) %collective-permute-start.16) | collective-permute-done | bytes 1048608 | tf_op jit(solution)/shard_map/logits_line_reduce/ppermute | solution.py:118
  90.4 1.4 bitcast_add_fusion.3
  91.8 4.4 %collective-permute-start.17 = (f32[16,128,128]{2,1,0:T(8,128)S(1)}, f32[16,128,128]{2,1,0:T(8,128)S(1)}, u32[]{:S(2)}, u32[]{:S(2)}) collective-permute-start(f32[16,128,128]{2,1,0:T(8,128)S(1)} %bitcast_add_fusion.3), channel_id=1, source_target_pairs={{0,8},{8,16},{1,9},{9,17},{2,10},{10,18},{3,11},{11,19},{4,12},{12... | collective-permute-start | bytes 3145736 | tf_op jit(solution)/shard_map/logits_line_reduce/ppermute | solution.py:118
  96.3 21.6 %collective-permute-done.17 = f32[16,128,128]{2,1,0:T(8,128)S(1)} collective-permute-done((f32[16,128,128]{2,1,0:T(8,128)S(1)}, f32[16,128,128]{2,1,0:T(8,128)S(1)}, u32[]{:S(2)}, u32[]{:S(2)}) %collective-permute-start.17) | collective-permute-done | bytes 1048608 | tf_op jit(solution)/shard_map/logits_line_reduce/ppermute | solution.py:118
  117.8 3.2 %bitcast_add_fusion.4 = (f32[16,128,128]{2,1,0:T(8,128)}, f32[16,128,128]{2,1,0:T(8,128)S(1)}) fusion(f32[16,128,128]{2,1,0:T(8,128)S(1)} %collective-permute-done.17, f32[4,16,128,128]{3,2,1,0:T(8,128)} %bitcast.205, s32[]{:T(128)S(6)} %min.23, f32[16,128,128]{2,1,0:T(8,128)} %collective-permute-done.19, s32[]{:T(128)S(6)} %min.27), kind=kLoop, calls=%fused_computation.15 | loop fusion | flops 524288 | bytes 6291464 | tf_op jit(solution)/shard_map/logits_line_reduce/add | solution.py:112
  121.0 0.7 collective-permute-start.20
  121.8 5.0 %collective-permute-start.18 = (f32[16,128,128]{2,1,0:T(8,128)}, f32[16,128,128]{2,1,0:T(8,128)S(1)}, u32[]{:S(2)}, u32[]{:S(2)}) collective-permute-start(f32[16,128,128]{2,1,0:T(8,128)} %get-tuple-element.4), channel_id=1, source_target_pairs={{0,8},{8,16},{16,24},{1,9},{9,17},{17,25},{2,10},{10,18},{18,26},{... | collective-permute-start | bytes 3145736 | tf_op jit(solution)/shard_map/logits_line_reduce/ppermute | solution.py:118
  126.8 1.4 bitcast_add_fusion.2
  128.2 1.3 collective-permute-start.21
  129.5 0.6 constant_dynamic-slice_fusion.4
  130.1 0.6 iota_compare_fusion.1
  130.8 17.1 %collective-permute-done.18 = f32[16,128,128]{2,1,0:T(8,128)S(1)} collective-permute-done((f32[16,128,128]{2,1,0:T(8,128)}, f32[16,128,128]{2,1,0:T(8,128)S(1)}, u32[]{:S(2)}, u32[]{:S(2)}) %collective-permute-start.18) | collective-permute-done | bytes 1048608 | tf_op jit(solution)/shard_map/logits_line_reduce/ppermute | solution.py:118
  147.9 24.9 %collective-permute-done.21 = f32[16,128,128]{2,1,0:T(8,128)S(1)} collective-permute-done((f32[16,128,128]{2,1,0:T(8,128)S(1)}, f32[16,128,128]{2,1,0:T(8,128)S(1)}, u32[]{:S(2)}, u32[]{:S(2)}) %collective-permute-start.21) | collective-permute-done | bytes 1048608 | tf_op jit(solution)/shard_map/logits_line_reduce/ppermute | solution.py:119
  172.8 1.5 select_reduce_fusion
  174.6 9.2 %all-gather = f32[16,1,128]{2,1,0:T(1,128)S(1)} all-gather(f32[2,1,128]{2,1,0:T(1,128)S(1)} %pad_maximum_fusion.5), channel_id=2, replica_groups=mesh['dp'=4,'vocab'=8] {'vocab'}, dimensions={0}, use_global_device_ids=true | all-gather | bytes 9216 | tf_op jit(solution)/shard_map/softmax_stats/all_gather | solution.py:164
  183.9 1.6 select_convert_fusion
  185.6 44.5 %all-gather.4.cloned.1.call-done = bf16[64,128,128]{2,1,0:T(8,128)(2,1)} async-done(((bf16[16,128,128]{2,1,0:T(8,128)(2,1)}), bf16[64,128,128]{2,1,0:T(8,128)(2,1)}) %all-gather.4.cloned.1.call-update) | async-done | bytes 2097168 | tf_op jit(solution)/shard_map/all_gather | solution.py:171
  230.0 3.3 %convert_bitcast_fusion = bf16[4,128,19,128]{3,2,1,0:T(8,128)(2,1)S(1)} fusion(bf16[4,16,128,128]{3,2,1,0:T(8,128)(2,1)} %bitcast.210, s32[4,16]{1,0:T(4,128)S(1)} %bitcast.236), kind=kOutput, calls=%fused_computation.5 | convolution fusion | flops 41092288 | bytes 4587776 | tf_op jit(solution)/shard_map/dense_expected/bsk,bsrt->brkt/dot_general | solution.py:177
  233.3 2.8 dot_general.19
  236.1 9.0 %fusion = f32[2,2,2,64,2048]{4,3,2,1,0:T(8,128)S(1)} fusion(bf16[2,2,2,64,2432]{4,3,2,1,0:T(8,128)(2,1)} %dot_general.19, bf16[2432,2048]{1,0:T(8,128)(2,1)} %param.5), kind=kOutput, calls=%fused_computation.3 | convolution fusion | flops 5100273664 | bytes 16646144 | tf_op jit(solution)/shard_map/dense_expected/bv,vd->bd/dot_general | solution.py:180
  245.1 2.0 copy-done.1
  247.0 1.5 dynamic-slice_bitcast_fusion
  248.6 4.4 %collective-permute-done.22 = f32[2,2,64,2048]{3,2,1,0:T(8,128)S(1)} collective-permute-done((f32[2,2,64,2048]{3,2,1,0:T(8,128)}, f32[2,2,64,2048]{3,2,1,0:T(8,128)S(1)}, u32[]{:S(2)}, u32[]{:S(2)}) %collective-permute-start.22) | collective-permute-done | bytes 2097184 | tf_op jit(solution)/shard_map/summed_core_stage/ppermute | solution.py:18
  252.9 2.0 bitcast_add_fusion
  255.1 0.8 dynamic-slice_bitcast_fusion.3
  255.9 1.5 collective-permute-start.25
  257.4 0.8 dynamic-slice_bitcast_fusion.4
  258.2 1.5 collective-permute-start.23
  259.7 10.4 %collective-permute-done.25 = f32[2,64,1024]{2,1,0:T(8,128)S(1)} collective-permute-done((f32[2,64,1024]{2,1,0:T(8,128)}, f32[2,64,1024]{2,1,0:T(8,128)S(1)}, u32[]{:S(2)}, u32[]{:S(2)}) %collective-permute-start.25) | collective-permute-done | bytes 524320 | tf_op jit(solution)/shard_map/summed_chip_stage/ppermute | solution.py:18
  270.2 1.5 collective-permute-start.26
  272.2 1.2 collective-permute-start.24
  273.4 4.4 %collective-permute-done.26 = f32[64,1024]{1,0:T(8,128)S(1)} collective-permute-done((f32[64,1024]{1,0:T(8,128)S(1)}, f32[64,1024]{1,0:T(8,128)S(1)}, u32[]{:S(2)}, u32[]{:S(2)}) %collective-permute-start.26) | collective-permute-done | bytes 262176 | tf_op jit(solution)/shard_map/summed_chip_stage/ppermute | solution.py:18
  277.8 1.7 collective-permute-done.24
  279.9 3.4 %collective-permute-done.27 = f32[64]{0:T(128)S(1)} collective-permute-done((f32[64]{0:T(128)S(1)}, f32[64]{0:T(128)S(1)}, u32[]{:S(2)}, u32[]{:S(2)}) %collective-permute-start.27) | collective-permute-done | bytes 288 | tf_op jit(solution)/shard_map/ppermute | solution.py:98
  283.3 1.2 collective-permute-start.28
  284.5 3.2 %collective-permute-done.28 = f32[64]{0:T(128)S(1)} collective-permute-done((f32[64]{0:T(128)S(1)}, f32[64]{0:T(128)S(1)}, u32[]{:S(2)}, u32[]{:S(2)}) %collective-permute-start.28) | collective-permute-done | bytes 288 | tf_op jit(solution)/shard_map/ppermute | solution.py:98
  287.8 0.9 fusion.4
  (100 shorter events, 6.5 us)
Async XLA Ops:
  7.2 122.4 %copy-start = (s32[1,4]{1,0:T(1,128)S(1)}, s32[1,4]{1,0:T(1,128)}, u32[]{:S(2)}) copy-start(s32[1,4]{1,0:T(1,128)} %param.7) | copy-start | bytes 52
  7.2 222.9 %all-gather.4.cloned.1.call-start = ((), (), s32[]{:S(2)}) async-start(), calls=%async_computation | async-start | bytes 2621440 | tf_op jit(solution)/shard_map/all_gather | solution.py:171
  8.2 25.7 %copy-start.2 = (s32[1,4,16]{2,1,0:T(4,128)S(1)}, s32[1,4,16]{2,1,0:T(4,128)}, u32[]{:S(2)}) copy-start(s32[1,4,16]{2,1,0:T(4,128)} %param.6) | copy-start | bytes 772
  8.2 6.3 %collective-permute-start = (bf16[16,1024]{1,0:T(8,128)(2,1)S(1)}, bf16[16,1024]{1,0:T(8,128)(2,1)S(1)}, u32[]{:S(2)}, u32[]{:S(2)}) collective-permute-start(bf16[16,1024]{1,0:T(8,128)(2,1)S(1)} %get-tuple-element.34), channel_id=1, source_target_pairs={{0,1},{1,2},{2,3},{3,4},{4,5},{5,6},{6,7},{7,0},{8,9},{9,10},{10,1... | collective-permute-start | bytes 98312 | tf_op jit(solution)/shard_map/hidden_spread/ppermute | solution.py:51
  8.8 7.2 %collective-permute-start.1 = (bf16[16,1024]{1,0:T(8,128)(2,1)S(1)}, bf16[16,1024]{1,0:T(8,128)(2,1)S(1)}, u32[]{:S(2)}, u32[]{:S(2)}) collective-permute-start(bf16[16,1024]{1,0:T(8,128)(2,1)S(1)} %get-tuple-element.33), channel_id=1, source_target_pairs={{0,2},{1,3},{2,4},{3,5},{4,6},{5,7},{6,0},{7,1},{8,10},{9,11},{10,... | collective-permute-start | bytes 98312 | tf_op jit(solution)/shard_map/hidden_spread/ppermute | solution.py:51
  11.3 7.0 %collective-permute-start.2 = (bf16[16,1024]{1,0:T(8,128)(2,1)S(1)}, bf16[16,1024]{1,0:T(8,128)(2,1)S(1)}, u32[]{:S(2)}, u32[]{:S(2)}) collective-permute-start(bf16[16,1024]{1,0:T(8,128)(2,1)S(1)} %get-tuple-element.32), channel_id=1, source_target_pairs={{0,3},{1,4},{2,5},{3,6},{4,7},{5,0},{6,1},{7,2},{8,11},{9,12},{10,... | collective-permute-start | bytes 98312 | tf_op jit(solution)/shard_map/hidden_spread/ppermute | solution.py:51
  13.7 4.6 %collective-permute-start.3 = (bf16[16,1024]{1,0:T(8,128)(2,1)S(1)}, bf16[16,1024]{1,0:T(8,128)(2,1)S(1)}, u32[]{:S(2)}, u32[]{:S(2)}) collective-permute-start(bf16[16,1024]{1,0:T(8,128)(2,1)S(1)} %get-tuple-element.31), channel_id=1, source_target_pairs={{0,4},{1,5},{2,6},{3,7},{4,0},{5,1},{6,2},{7,3},{8,12},{9,13},{10,... | collective-permute-start | bytes 98312 | tf_op jit(solution)/shard_map/hidden_spread/ppermute | solution.py:51
  14.2 4.2 %collective-permute-start.4 = (bf16[16,1024]{1,0:T(8,128)(2,1)S(1)}, bf16[16,1024]{1,0:T(8,128)(2,1)S(1)}, u32[]{:S(2)}, u32[]{:S(2)}) collective-permute-start(bf16[16,1024]{1,0:T(8,128)(2,1)S(1)} %get-tuple-element.30), channel_id=1, source_target_pairs={{0,5},{1,6},{2,7},{3,0},{4,1},{5,2},{6,3},{7,4},{8,13},{9,14},{10,... | collective-permute-start | bytes 98312 | tf_op jit(solution)/shard_map/hidden_spread/ppermute | solution.py:51
  14.5 4.1 %collective-permute-start.5 = (bf16[16,1024]{1,0:T(8,128)(2,1)S(1)}, bf16[16,1024]{1,0:T(8,128)(2,1)S(1)}, u32[]{:S(2)}, u32[]{:S(2)}) collective-permute-start(bf16[16,1024]{1,0:T(8,128)(2,1)S(1)} %get-tuple-element.29), channel_id=1, source_target_pairs={{0,6},{1,7},{2,0},{3,1},{4,2},{5,3},{6,4},{7,5},{8,14},{9,15},{10,... | collective-permute-start | bytes 98312 | tf_op jit(solution)/shard_map/hidden_spread/ppermute | solution.py:51
  16.0 3.9 %collective-permute-start.6 = (bf16[16,1024]{1,0:T(8,128)(2,1)S(1)}, bf16[16,1024]{1,0:T(8,128)(2,1)S(1)}, u32[]{:S(2)}, u32[]{:S(2)}) collective-permute-start(bf16[16,1024]{1,0:T(8,128)(2,1)S(1)} %get-tuple-element.28), channel_id=1, source_target_pairs={{0,7},{1,0},{2,1},{3,2},{4,3},{5,4},{6,5},{7,6},{8,15},{9,8},{10,9... | collective-permute-start | bytes 98312 | tf_op jit(solution)/shard_map/hidden_spread/ppermute | solution.py:51
  21.5 6.2 %collective-permute-start.9 = (bf16[16,2048]{1,0:T(8,128)(2,1)S(1)}, bf16[16,2048]{1,0:T(8,128)(2,1)S(1)}, u32[]{:S(2)}, u32[]{:S(2)}) collective-permute-start(bf16[16,2048]{1,0:T(8,128)(2,1)S(1)} %bitcast.226), channel_id=1, source_target_pairs={{0,24},{8,0},{16,8},{24,16},{1,25},{9,1},{17,9},{25,17},{2,26},{10... | collective-permute-start | bytes 196616 | tf_op jit(solution)/shard_map/hidden_spread/ppermute | solution.py:51
  25.2 7.3 %collective-permute-start.8 = (bf16[16,2048]{1,0:T(8,128)(2,1)S(1)}, bf16[16,2048]{1,0:T(8,128)(2,1)S(1)}, u32[]{:S(2)}, u32[]{:S(2)}) collective-permute-start(bf16[16,2048]{1,0:T(8,128)(2,1)S(1)} %bitcast.227), channel_id=1, source_target_pairs={{0,16},{8,24},{16,0},{24,8},{1,17},{9,25},{17,1},{25,9},{2,18},{10... | collective-permute-start | bytes 196616 | tf_op jit(solution)/shard_map/hidden_spread/ppermute | solution.py:51
  25.3 7.2 %collective-permute-start.7 = (bf16[16,2048]{1,0:T(8,128)(2,1)S(1)}, bf16[16,2048]{1,0:T(8,128)(2,1)S(1)}, u32[]{:S(2)}, u32[]{:S(2)}) collective-permute-start(bf16[16,2048]{1,0:T(8,128)(2,1)S(1)} %bitcast.228), channel_id=1, source_target_pairs={{0,8},{8,16},{16,24},{24,0},{1,9},{9,17},{17,25},{25,1},{2,10},{10... | collective-permute-start | bytes 196616 | tf_op jit(solution)/shard_map/hidden_spread/ppermute | solution.py:51
  33.3 5.5 %collective-permute-start.13 = (bf16[64,1024]{1,0:T(8,128)(2,1)S(1)}, bf16[64,1024]{1,0:T(8,128)(2,1)S(1)}, u32[]{:S(2)}, u32[]{:S(2)}) collective-permute-start(bf16[64,1024]{1,0:T(8,128)(2,1)S(1)} %get-tuple-element.18), channel_id=1, source_target_pairs={{0,4},{1,5},{2,6},{3,7},{4,0},{5,1},{6,2},{7,3},{8,12},{9,13},{10,... | collective-permute-start | bytes 393224 | tf_op jit(solution)/shard_map/hidden_spread/hidden_gather_stage/ppermute | solution.py:62
  34.0 6.2 %collective-permute-start.10 = (bf16[64,1024]{1,0:T(8,128)(2,1)S(1)}, bf16[64,1024]{1,0:T(8,128)(2,1)S(1)}, u32[]{:S(2)}, u32[]{:S(2)}) collective-permute-start(bf16[64,1024]{1,0:T(8,128)(2,1)S(1)} %get-tuple-element.19), channel_id=1, source_target_pairs={{0,2},{1,3},{2,0},{3,1},{4,6},{5,7},{6,4},{7,5},{8,10},{9,11},{10,... | collective-permute-start | bytes 393224 | tf_op jit(solution)/shard_map/hidden_spread/hidden_gather_stage/ppermute | solution.py:62
  38.9 7.5 %collective-permute-start.14 = (bf16[2,64,1024]{2,1,0:T(8,128)(2,1)S(1)}, bf16[2,64,1024]{2,1,0:T(8,128)(2,1)S(1)}, u32[]{:S(2)}, u32[]{:S(2)}) collective-permute-start(bf16[2,64,1024]{2,1,0:T(8,128)(2,1)S(1)} %maximum_select_fusion.7), channel_id=1, source_target_pairs={{0,2},{1,3},{2,0},{3,1},{4,6},{5,7},{6,4},{7,5},{8,10},{9,11},{10,... | collective-permute-start | bytes 786440 | tf_op jit(solution)/shard_map/hidden_spread/hidden_gather_stage/ppermute | solution.py:62
  40.3 7.3 %collective-permute-start.11 = (bf16[2,64,1024]{2,1,0:T(8,128)(2,1)S(1)}, bf16[2,64,1024]{2,1,0:T(8,128)(2,1)S(1)}, u32[]{:S(2)}, u32[]{:S(2)}) collective-permute-start(bf16[2,64,1024]{2,1,0:T(8,128)(2,1)S(1)} %maximum_select_fusion.5), channel_id=1, source_target_pairs={{0,4},{1,5},{2,6},{3,7},{4,0},{5,1},{6,2},{7,3},{8,12},{9,13},{10,... | collective-permute-start | bytes 786440 | tf_op jit(solution)/shard_map/hidden_spread/hidden_gather_stage/ppermute | solution.py:62
  46.5 2.0 collective-permute-start.15
  47.5 2.7 slice-start
  47.6 2.0 collective-permute-start.12
  48.4 2.8 slice-start.1
  49.8 1.8 slice-start.2
  65.9 24.5 %collective-permute-start.16 = (f32[16,128,128]{2,1,0:T(8,128)S(1)}, f32[16,128,128]{2,1,0:T(8,128)S(1)}, u32[]{:S(2)}, u32[]{:S(2)}) collective-permute-start(f32[16,128,128]{2,1,0:T(8,128)S(1)} %get-tuple-element.6), channel_id=1, source_target_pairs={{0,8},{1,9},{2,10},{3,11},{4,12},{5,13},{6,14},{7,15}} | collective-permute-start | bytes 3145736 | tf_op jit(solution)/shard_map/logits_line_reduce/ppermute | solution.py:118
  67.9 28.3 %collective-permute-start.19 = (f32[16,128,128]{2,1,0:T(8,128)S(1)}, f32[16,128,128]{2,1,0:T(8,128)}, u32[]{:S(2)}, u32[]{:S(2)}) collective-permute-start(f32[16,128,128]{2,1,0:T(8,128)S(1)} %get-tuple-element.7), channel_id=1, source_target_pairs={{24,16},{25,17},{26,18},{27,19},{28,20},{29,21},{30,22},{31,23}} | collective-permute-start | bytes 3145736 | tf_op jit(solution)/shard_map/logits_line_reduce/ppermute | solution.py:119
  91.8 26.1 %collective-permute-start.17 = (f32[16,128,128]{2,1,0:T(8,128)S(1)}, f32[16,128,128]{2,1,0:T(8,128)S(1)}, u32[]{:S(2)}, u32[]{:S(2)}) collective-permute-start(f32[16,128,128]{2,1,0:T(8,128)S(1)} %bitcast_add_fusion.3), channel_id=1, source_target_pairs={{0,8},{8,16},{1,9},{9,17},{2,10},{10,18},{3,11},{11,19},{4,12},{12... | collective-permute-start | bytes 3145736 | tf_op jit(solution)/shard_map/logits_line_reduce/ppermute | solution.py:118
  121.0 5.8 %collective-permute-start.20 = (f32[16,128,128]{2,1,0:T(8,128)S(1)}, f32[16,128,128]{2,1,0:T(8,128)S(1)}, u32[]{:S(2)}, u32[]{:S(2)}) collective-permute-start(f32[16,128,128]{2,1,0:T(8,128)S(1)} %get-tuple-element.5), channel_id=1, source_target_pairs={{16,8},{24,16},{17,9},{25,17},{18,10},{26,18},{19,11},{27,19},{20,... | collective-permute-start | bytes 3145736 | tf_op jit(solution)/shard_map/logits_line_reduce/ppermute | solution.py:119
  121.8 26.1 %collective-permute-start.18 = (f32[16,128,128]{2,1,0:T(8,128)}, f32[16,128,128]{2,1,0:T(8,128)S(1)}, u32[]{:S(2)}, u32[]{:S(2)}) collective-permute-start(f32[16,128,128]{2,1,0:T(8,128)} %get-tuple-element.4), channel_id=1, source_target_pairs={{0,8},{8,16},{16,24},{1,9},{9,17},{17,25},{2,10},{10,18},{18,26},{... | collective-permute-start | bytes 3145736 | tf_op jit(solution)/shard_map/logits_line_reduce/ppermute | solution.py:118
  128.2 44.5 %collective-permute-start.21 = (f32[16,128,128]{2,1,0:T(8,128)S(1)}, f32[16,128,128]{2,1,0:T(8,128)S(1)}, u32[]{:S(2)}, u32[]{:S(2)}) collective-permute-start(f32[16,128,128]{2,1,0:T(8,128)S(1)} %bitcast_add_fusion.2), channel_id=1, source_target_pairs={{8,0},{16,8},{24,16},{9,1},{17,9},{25,17},{10,2},{18,10},{26,18},{... | collective-permute-start | bytes 3145736 | tf_op jit(solution)/shard_map/logits_line_reduce/ppermute | solution.py:119
  245.1 2.0 copy-start.1
  248.6 4.4 %collective-permute-start.22 = (f32[2,2,64,2048]{3,2,1,0:T(8,128)}, f32[2,2,64,2048]{3,2,1,0:T(8,128)S(1)}, u32[]{:S(2)}, u32[]{:S(2)}) collective-permute-start(f32[2,2,64,2048]{3,2,1,0:T(8,128)} %dynamic-slice_bitcast_fusion), channel_id=1, source_target_pairs={{0,1},{1,0},{2,3},{3,2},{4,5},{5,4},{6,7},{7,6},{8,9},{9,8},{10,11... | collective-permute-start | bytes 6291464 | tf_op jit(solution)/shard_map/summed_core_stage/ppermute | solution.py:18
  255.9 14.2 %collective-permute-start.25 = (f32[2,64,1024]{2,1,0:T(8,128)}, f32[2,64,1024]{2,1,0:T(8,128)S(1)}, u32[]{:S(2)}, u32[]{:S(2)}) collective-permute-start(f32[2,64,1024]{2,1,0:T(8,128)} %dynamic-slice_bitcast_fusion.3), channel_id=1, source_target_pairs={{0,4},{1,5},{2,6},{3,7},{4,0},{5,1},{6,2},{7,3},{8,12},{9,13},{10,... | collective-permute-start | bytes 1572872 | tf_op jit(solution)/shard_map/summed_chip_stage/ppermute | solution.py:18
  258.2 13.9 %collective-permute-start.23 = (f32[2,64,1024]{2,1,0:T(8,128)}, f32[2,64,1024]{2,1,0:T(8,128)S(1)}, u32[]{:S(2)}, u32[]{:S(2)}) collective-permute-start(f32[2,64,1024]{2,1,0:T(8,128)} %dynamic-slice_bitcast_fusion.4), channel_id=1, source_target_pairs={{0,2},{1,3},{2,0},{3,1},{4,6},{5,7},{6,4},{7,5},{8,10},{9,11},{10,... | collective-permute-start | bytes 1572872 | tf_op jit(solution)/shard_map/summed_chip_stage/ppermute | solution.py:18
  270.2 7.6 %collective-permute-start.26 = (f32[64,1024]{1,0:T(8,128)S(1)}, f32[64,1024]{1,0:T(8,128)S(1)}, u32[]{:S(2)}, u32[]{:S(2)}) collective-permute-start(f32[64,1024]{1,0:T(8,128)S(1)} %dynamic-slice_bitcast_fusion.5), channel_id=1, source_target_pairs={{0,2},{1,3},{2,0},{3,1},{4,6},{5,7},{6,4},{7,5},{8,10},{9,11},{10,... | collective-permute-start | bytes 786440 | tf_op jit(solution)/shard_map/summed_chip_stage/ppermute | solution.py:18
  272.2 7.3 %collective-permute-start.24 = (f32[64,1024]{1,0:T(8,128)S(1)}, f32[64,1024]{1,0:T(8,128)S(1)}, u32[]{:S(2)}, u32[]{:S(2)}) collective-permute-start(f32[64,1024]{1,0:T(8,128)S(1)} %dynamic-slice_bitcast_fusion.6), channel_id=1, source_target_pairs={{0,4},{1,5},{2,6},{3,7},{4,0},{5,1},{6,2},{7,3},{8,12},{9,13},{10,... | collective-permute-start | bytes 786440 | tf_op jit(solution)/shard_map/summed_chip_stage/ppermute | solution.py:18
  279.7 3.6 %collective-permute-start.27 = (f32[64]{0:T(128)S(1)}, f32[64]{0:T(128)S(1)}, u32[]{:S(2)}, u32[]{:S(2)}) collective-permute-start(f32[64]{0:T(128)S(1)} %multiply_reduce_fusion), channel_id=1, source_target_pairs={{0,8},{8,0},{16,24},{24,16},{1,9},{9,1},{17,25},{25,17},{2,10},{10... | collective-permute-start | bytes 776 | tf_op jit(solution)/shard_map/ppermute | solution.py:98
  283.3 4.5 %collective-permute-start.28 = (f32[64]{0:T(128)S(1)}, f32[64]{0:T(128)S(1)}, u32[]{:S(2)}, u32[]{:S(2)}) collective-permute-start(f32[64]{0:T(128)S(1)} %add.373), channel_id=1, source_target_pairs={{0,16},{8,24},{16,0},{24,8},{1,17},{9,25},{17,1},{25,9},{2,18},{10... | collective-permute-start | bytes 776 | tf_op jit(solution)/shard_map/ppermute | solution.py:98
Sparse Core Ops, SparseCore 0:
  185.7 44.3 all-gather.3

commit v8 on v4

--- a/solution.py
+++ b/solution.py
@@ -41,7 +41,9 @@
 
 def permute_all_to_all(x, axis_name, n, split_axis, concat_axis):
     me = lax.axis_index(axis_name)
-    pieces = jnp.stack(jnp.split(x, n, axis=split_axis))
+    shape = list(x.shape)
+    shape[split_axis : split_axis + 1] = [n, x.shape[split_axis] // n]
+    pieces = jnp.moveaxis(x.reshape(shape), split_axis, 0)
     got = [lax.dynamic_index_in_dim(pieces, me, axis=0, keepdims=False)]
     for shift in range(1, n):
         send = lax.dynamic_index_in_dim(pieces, (me + shift) % n, axis=0, keepdims=False)
@@ -80,18 +82,27 @@
     return joined.reshape(n * rows, cols)
 
 
+def butterfly_sum(x, axis_name, n):
+    levels = n.bit_length() - 1
+    for bit in range(levels):
+        perm = [(s, s ^ (1 << bit)) for s in range(n)]
+        x = x + lax.ppermute(x, axis_name, perm=perm)
+    return x
+
+
 def per_device(hidden, out_weight, token_blocks, counts):
     vocab_here, columns_here = out_weight.shape
+    n_vocab = lax.psum(1, "vocab")
+    n_dp = lax.psum(1, "dp")
     n_tb = vocab_here // TB
     block_lists = token_blocks[0]
     block_counts = counts[0]
     n_blk = block_lists.shape[0]
     own_blocks = hidden.shape[0] // BB
-    first_block = lax.axis_index("dp") * own_blocks
-    own_counts = lax.dynamic_slice_in_dim(block_counts, first_block, own_blocks, 0)
+    assert own_blocks == 1 and n_blk == n_dp
+    me_dp = lax.axis_index("dp")
+    own_counts = lax.dynamic_slice_in_dim(block_counts, me_dp, 1, 0)
 
-    n_vocab = lax.psum(1, "vocab")
-    n_dp = lax.psum(1, "dp")
     with jax.named_scope("hidden_spread"):
         row_slices = permute_all_to_all(hidden, "vocab", n_vocab, split_axis=0, concat_axis=1)
         plane_rows = permute_all_to_all(row_slices, "dp", n_dp, split_axis=1, concat_axis=0)
@@ -142,7 +153,7 @@
             preferred_element_type=jnp.float32,
         )
     summed = halving_reduce_scatter(embedding_part, n_vocab)
-    squares = lax.psum(jnp.sum(summed * summed, axis=1), "dp")
+    squares = butterfly_sum(jnp.sum(summed * summed, axis=1), "dp", n_dp)
     width = hidden.shape[1] * n_vocab
     expected = summed * lax.rsqrt(squares / width + 1e-06)[:, None]
     return (allowed_logprob[None], expected)

time: 271 us -> 265 us (0.978)
  blocking collectives: 18.6 us -> 9.09 us
  waiting for transfers between devices: 161 us -> 167 us
  local copies, waits for them, and re-layouts: 22.8 us -> 18.9 us
    psum x1 -> x0, blocking collectives: 9.51 us -> none  [per_device(): squares = lax.psum(jnp.sum(summed * summed, axis=1), 'dp')]
    ppermute x0 -> x2, waiting for transfers between devices: none -> 6.63 us  [butterfly_sum(): x = x + lax.ppermute(x, axis_name, perm=perm)]
    unnamed x27 -> x33, local copies, waits for them, and re-layouts: 8.34 us -> 3.51 us
  transfers between devices with their start and end apart: 23 -> 25, of which waited for: 16 -> 18; matrix products, arithmetic and copies ran while one was open for 1% -> 1% of each run, Pallas kernels for 0% -> 0%
where the time goes in v8:
time: 265 us
  waiting for transfers between devices  167 us (63%)
  starting transfers between devices  25 us (9%)
  matrix products  19.6 us (7%)
  local copies, waits for them, and re-layouts  18.9 us (7%)
  between operations  14.8 us (6%)
  other arithmetic  9.99 us (4%)
  blocking collectives  9.09 us (3%)
    reduce_scatter x1, waiting for transfers between devices, per_device(): logits = lax.psum_scatter(picked, 'dp', scatter_dimension=0, tiled=True)  74.3 us
    all_gather x1, waiting for transfers between devices, per_device(): prob_part = lax.all_gather(probabilities, 'dp', axis=0, tiled=True)  45.4 us
    ppermute x5, waiting for transfers between devices, exchange_stage(): got = lax.ppermute(send, 'vocab', perm=perm)  21.2 us
    ppermute x10, starting transfers between devices, permute_all_to_all(): got.append(lax.ppermute(send, axis_name, perm=perm))  14.6 us
    ppermute x6, waiting for transfers between devices, gather_stage(): got = lax.ppermute(x, 'vocab', perm=perm)  12.1 us
    all_gather x1, blocking collectives, per_device(): stats = lax.all_gather(jnp.stack([local_max, local_total]), 'vocab', axis=0)  9.09 us
    dot_general x1, matrix products, per_device(): jnp.einsum('bv,vd->bd', spread.reshape(n_blk * BB, n_tb * TB), out_weight...  8.98 us
    ppermute x10, waiting for transfers between devices, permute_all_to_all(): got.append(lax.ppermute(send, axis_name, perm=perm))  7.6 us
  transfers between devices with their start and end apart: 25, of which 18 were waited for; matrix products, arithmetic and copies ran while one was open for 1% of the time, Pallas kernels for 0%

profile of v8, /device:TPU:0, one launch (start us, length us, event | category | flops | bytes accessed | tf_op | source)
XLA Modules:
  0.0 264.6 jit_solution(13382919378605344371)
XLA Ops:
  7.3 0.9 dynamic-slice_bitcast_fusion.5
  8.2 0.5 collective-permute-start
  8.8 2.5 collective-permute-start.1
  11.3 2.4 collective-permute-start.2
  13.7 0.5 collective-permute-start.3
  14.5 1.5 collective-permute-start.5
  16.0 2.3 collective-permute-start.6
  18.4 0.2 collective-permute-done.5
  18.6 1.3 collective-permute-done.6
  19.9 0.6 gather_fusion
  20.7 0.2 reshape.613
  20.9 0.6 constant_dynamic-slice_fusion.3
  21.5 3.7 %collective-permute-start.9 = (bf16[16,2048]{1,0:T(8,128)(2,1)S(1)}, bf16[16,2048]{1,0:T(8,128)(2,1)S(1)}, u32[]{:S(2)}, u32[]{:S(2)}) collective-permute-start(bf16[16,2048]{1,0:T(8,128)(2,1)S(1)} %bitcast.203), channel_id=1, source_target_pairs={{0,24},{8,0},{16,8},{24,16},{1,25},{9,1},{17,9},{25,17},{2,26},{10... | collective-permute-start | bytes 196616 | tf_op jit(solution)/shard_map/hidden_spread/ppermute | solution.py:51
  25.3 1.0 collective-permute-start.7
  26.4 1.2 collective-permute-done.9
  27.7 4.8 %collective-permute-done.8 = bf16[16,2048]{1,0:T(8,128)(2,1)S(1)} collective-permute-done((bf16[16,2048]{1,0:T(8,128)(2,1)S(1)}, bf16[16,2048]{1,0:T(8,128)(2,1)S(1)}, u32[]{:S(2)}, u32[]{:S(2)}) %collective-permute-start.8) | collective-permute-done | bytes 65568 | tf_op jit(solution)/shard_map/hidden_spread/ppermute | solution.py:51
  32.5 0.6 gather_fusion.1
  33.3 0.6 collective-permute-start.13
  34.0 0.7 collective-permute-start.10
  34.7 4.2 %collective-permute-done.13 = bf16[64,1024]{1,0:T(8,128)(2,1)S(1)} collective-permute-done((bf16[64,1024]{1,0:T(8,128)(2,1)S(1)}, bf16[64,1024]{1,0:T(8,128)(2,1)S(1)}, u32[]{:S(2)}, u32[]{:S(2)}) %collective-permute-start.13) | collective-permute-done | bytes 131104 | tf_op jit(solution)/shard_map/hidden_spread/hidden_gather_stage/ppermute | solution.py:62
  38.9 1.3 collective-permute-start.14
  40.3 0.5 collective-permute-start.11
  40.9 5.5 %collective-permute-done.14 = bf16[2,64,1024]{2,1,0:T(8,128)(2,1)S(1)} collective-permute-done((bf16[2,64,1024]{2,1,0:T(8,128)(2,1)S(1)}, bf16[2,64,1024]{2,1,0:T(8,128)(2,1)S(1)}, u32[]{:S(2)}, u32[]{:S(2)}) %collective-permute-start.14) | collective-permute-done | bytes 262176 | tf_op jit(solution)/shard_map/hidden_spread/hidden_gather_stage/ppermute | solution.py:62
  46.5 1.0 collective-permute-done.11
  47.9 0.5 collective-permute-done.15
  48.4 0.2 maximum_select_fusion.1
  48.7 0.9 collective-permute-done.12
  49.6 0.2 maximum_select_fusion
  49.8 0.2 maximum_bitcast_fusion
  50.0 0.2 copy.39
  50.3 0.9 slice-done.1
  51.2 0.4 slice-done.2
  51.6 7.4 %fusion.27 = f32[4,128,19,128]{3,1,2,0:T(8,128)} fusion(bf16[4,128,2048,1]{2,1,3,0:T(8,128)(2,1)S(1)} %bitcast.188, bf16[19,128,2048,1]{2,1,0,3:T(8,128)(2,1)S(1)} %bitcast.218), kind=kOutput, calls=%fused_computation.131 | convolution fusion | flops 5100273664 | bytes 17039360 | tf_op jit(solution)/shard_map/dense_logits/bd,vd->bv/dot_general | solution.py:118
  59.0 5.3 %gather_fusion.2 = f32[64,128,128]{2,1,0:T(8,128)} fusion(f32[4,128,19,128]{3,1,2,0:T(8,128)} %fusion.27, s32[64]{0:T(128)S(1)} %reshape.630), kind=kCustom, calls=%fused_computation.2 | custom fusion | bytes 8389120 | tf_op jit(solution)/shard_map/dense_logits/gather | solution.py:123
  64.3 0.6 constant_dynamic-slice_fusion.4
  64.9 0.6 iota_compare_fusion.1
  65.5 74.3 %reduce-scatter.2.cloned.1.call-done = f32[1,16,128,128]{3,2,1,0:T(8,128)} async-done(((f32[4,16,128,128]{3,2,1,0:T(8,128)}), f32[1,16,128,128]{3,2,1,0:T(8,128)}) %reduce-scatter.2.cloned.1.call-update) | async-done | bytes 1048592 | tf_op jit(solution)/shard_map/reduce_scatter | solution.py:125
  139.9 1.5 select_reduce_fusion
  141.4 1.6 exponential_reduce_fusion
  143.0 9.1 %all-gather = f32[16,1,128]{2,1,0:T(1,128)S(1)} all-gather(f32[2,1,128]{2,1,0:T(1,128)S(1)} %pad_maximum_fusion.5), channel_id=2, replica_groups=mesh['dp'=4,'vocab'=8] {'vocab'}, dimensions={0}, use_global_device_ids=true | all-gather | bytes 9216 | tf_op jit(solution)/shard_map/softmax_stats/all_gather | solution.py:133
  152.1 1.6 select_convert_fusion
  153.7 45.4 %all-gather.3.cloned.1.call-done = bf16[4,16,128,128]{3,2,1,0:T(8,128)(2,1)} async-done(((bf16[1,16,128,128]{3,2,1,0:T(8,128)(2,1)}), bf16[4,16,128,128]{3,2,1,0:T(8,128)(2,1)}) %all-gather.3.cloned.1.call-update) | async-done | bytes 2097168 | tf_op jit(solution)/shard_map/all_gather | solution.py:140
  199.1 3.3 %convert_bitcast_fusion = bf16[4,128,19,128]{3,2,1,0:T(8,128)(2,1)S(1)} fusion(bf16[4,16,128,128]{3,2,1,0:T(8,128)(2,1)} %all-gather.3.cloned.1.call-done, s32[4,16]{1,0:T(4,128)S(1)} %bitcast.213), kind=kOutput, calls=%fused_computation.5 | convolution fusion | flops 41092288 | bytes 4587776 | tf_op jit(solution)/shard_map/dense_expected/bsk,bsrt->brkt/dot_general | solution.py:146
  202.4 2.8 %dot_general.19 = bf16[2,2,2,64,2432]{4,3,2,1,0:T(8,128)(2,1)} reshape(bf16[4,128,19,128]{3,2,1,0:T(8,128)(2,1)S(1)} %convert_bitcast_fusion) | data formatting | bytes 4980736 | tf_op jit(solution)/shard_map/dense_expected/bv,vd->bd/dot_general | solution.py:149
  205.2 9.0 %fusion = f32[2,2,2,64,2048]{4,3,2,1,0:T(8,128)S(1)} fusion(bf16[2,2,2,64,2432]{4,3,2,1,0:T(8,128)(2,1)} %dot_general.19, bf16[2432,2048]{1,0:T(8,128)(2,1)} %param.5), kind=kOutput, calls=%fused_computation.3 | convolution fusion | flops 5100273664 | bytes 16646144 | tf_op jit(solution)/shard_map/dense_expected/bv,vd->bd/dot_general | solution.py:149
  214.2 1.9 copy-done.3
  216.1 1.5 dynamic-slice_bitcast_fusion
  217.6 4.4 %collective-permute-done.16 = f32[2,2,64,2048]{3,2,1,0:T(8,128)S(1)} collective-permute-done((f32[2,2,64,2048]{3,2,1,0:T(8,128)}, f32[2,2,64,2048]{3,2,1,0:T(8,128)S(1)}, u32[]{:S(2)}, u32[]{:S(2)}) %collective-permute-start.16) | collective-permute-done | bytes 2097184 | tf_op jit(solution)/shard_map/summed_core_stage/ppermute | solution.py:18
  222.0 2.0 bitcast_add_fusion
  224.1 0.8 dynamic-slice_bitcast_fusion.1
  225.0 1.5 collective-permute-start.19
  226.4 0.9 dynamic-slice_bitcast_fusion.2
  227.3 1.5 collective-permute-start.17
  228.8 10.4 %collective-permute-done.19 = f32[2,64,1024]{2,1,0:T(8,128)S(1)} collective-permute-done((f32[2,64,1024]{2,1,0:T(8,128)}, f32[2,64,1024]{2,1,0:T(8,128)S(1)}, u32[]{:S(2)}, u32[]{:S(2)}) %collective-permute-start.19) | collective-permute-done | bytes 524320 | tf_op jit(solution)/shard_map/summed_chip_stage/ppermute | solution.py:18
  239.3 1.5 collective-permute-start.20
  240.8 0.4 collective-permute-done.17
  241.3 1.1 collective-permute-start.18
  242.4 4.4 %collective-permute-done.20 = f32[64,1024]{1,0:T(8,128)S(1)} collective-permute-done((f32[64,1024]{1,0:T(8,128)S(1)}, f32[64,1024]{1,0:T(8,128)S(1)}, u32[]{:S(2)}, u32[]{:S(2)}) %collective-permute-start.20) | collective-permute-done | bytes 262176 | tf_op jit(solution)/shard_map/summed_chip_stage/ppermute | solution.py:18
  246.8 1.7 collective-permute-done.18
  248.7 0.2 collective-permute-start.21
  249.0 3.4 %collective-permute-done.21 = f32[64]{0:T(128)S(1)} collective-permute-done((f32[64]{0:T(128)S(1)}, f32[64]{0:T(128)S(1)}, u32[]{:S(2)}, u32[]{:S(2)}) %collective-permute-start.21) | collective-permute-done | bytes 288 | tf_op jit(solution)/shard_map/ppermute | solution.py:89
  252.4 1.2 collective-permute-start.22
  253.6 3.2 %collective-permute-done.22 = f32[64]{0:T(128)S(1)} collective-permute-done((f32[64]{0:T(128)S(1)}, f32[64]{0:T(128)S(1)}, u32[]{:S(2)}, u32[]{:S(2)}) %collective-permute-start.22) | collective-permute-done | bytes 288 | tf_op jit(solution)/shard_map/ppermute | solution.py:89
  256.8 0.9 fusion.3
  (91 shorter events, 2.5 us)
Async XLA Ops:
  7.2 57.1 %copy-start = (s32[1,4]{1,0:T(1,128)S(1)}, s32[1,4]{1,0:T(1,128)}, u32[]{:S(2)}) copy-start(s32[1,4]{1,0:T(1,128)} %param.7) | copy-start | bytes 52
  7.2 132.7 %reduce-scatter.2.cloned.1.call-start = ((), (), s32[]{:S(2)}) async-start(), calls=%async_computation.1 | async-start | bytes 5242880 | tf_op jit(solution)/shard_map/reduce_scatter | solution.py:125
  8.2 6.3 %collective-permute-start = (bf16[16,1024]{1,0:T(8,128)(2,1)S(1)}, bf16[16,1024]{1,0:T(8,128)(2,1)S(1)}, u32[]{:S(2)}, u32[]{:S(2)}) collective-permute-start(bf16[16,1024]{1,0:T(8,128)(2,1)S(1)} %get-tuple-element.34), channel_id=1, source_target_pairs={{0,1},{1,2},{2,3},{3,4},{4,5},{5,6},{6,7},{7,0},{8,9},{9,10},{10,1... | collective-permute-start | bytes 98312 | tf_op jit(solution)/shard_map/hidden_spread/ppermute | solution.py:51
  8.8 7.2 %collective-permute-start.1 = (bf16[16,1024]{1,0:T(8,128)(2,1)S(1)}, bf16[16,1024]{1,0:T(8,128)(2,1)S(1)}, u32[]{:S(2)}, u32[]{:S(2)}) collective-permute-start(bf16[16,1024]{1,0:T(8,128)(2,1)S(1)} %get-tuple-element.33), channel_id=1, source_target_pairs={{0,2},{1,3},{2,4},{3,5},{4,6},{5,7},{6,0},{7,1},{8,10},{9,11},{10,... | collective-permute-start | bytes 98312 | tf_op jit(solution)/shard_map/hidden_spread/ppermute | solution.py:51
  11.3 7.0 %collective-permute-start.2 = (bf16[16,1024]{1,0:T(8,128)(2,1)S(1)}, bf16[16,1024]{1,0:T(8,128)(2,1)S(1)}, u32[]{:S(2)}, u32[]{:S(2)}) collective-permute-start(bf16[16,1024]{1,0:T(8,128)(2,1)S(1)} %get-tuple-element.32), channel_id=1, source_target_pairs={{0,3},{1,4},{2,5},{3,6},{4,7},{5,0},{6,1},{7,2},{8,11},{9,12},{10,... | collective-permute-start | bytes 98312 | tf_op jit(solution)/shard_map/hidden_spread/ppermute | solution.py:51
  13.7 4.6 %collective-permute-start.3 = (bf16[16,1024]{1,0:T(8,128)(2,1)S(1)}, bf16[16,1024]{1,0:T(8,128)(2,1)S(1)}, u32[]{:S(2)}, u32[]{:S(2)}) collective-permute-start(bf16[16,1024]{1,0:T(8,128)(2,1)S(1)} %get-tuple-element.31), channel_id=1, source_target_pairs={{0,4},{1,5},{2,6},{3,7},{4,0},{5,1},{6,2},{7,3},{8,12},{9,13},{10,... | collective-permute-start | bytes 98312 | tf_op jit(solution)/shard_map/hidden_spread/ppermute | solution.py:51
  14.2 4.2 %collective-permute-start.4 = (bf16[16,1024]{1,0:T(8,128)(2,1)S(1)}, bf16[16,1024]{1,0:T(8,128)(2,1)S(1)}, u32[]{:S(2)}, u32[]{:S(2)}) collective-permute-start(bf16[16,1024]{1,0:T(8,128)(2,1)S(1)} %get-tuple-element.30), channel_id=1, source_target_pairs={{0,5},{1,6},{2,7},{3,0},{4,1},{5,2},{6,3},{7,4},{8,13},{9,14},{10,... | collective-permute-start | bytes 98312 | tf_op jit(solution)/shard_map/hidden_spread/ppermute | solution.py:51
  14.5 4.1 %collective-permute-start.5 = (bf16[16,1024]{1,0:T(8,128)(2,1)S(1)}, bf16[16,1024]{1,0:T(8,128)(2,1)S(1)}, u32[]{:S(2)}, u32[]{:S(2)}) collective-permute-start(bf16[16,1024]{1,0:T(8,128)(2,1)S(1)} %get-tuple-element.29), channel_id=1, source_target_pairs={{0,6},{1,7},{2,0},{3,1},{4,2},{5,3},{6,4},{7,5},{8,14},{9,15},{10,... | collective-permute-start | bytes 98312 | tf_op jit(solution)/shard_map/hidden_spread/ppermute | solution.py:51
  16.0 3.9 %collective-permute-start.6 = (bf16[16,1024]{1,0:T(8,128)(2,1)S(1)}, bf16[16,1024]{1,0:T(8,128)(2,1)S(1)}, u32[]{:S(2)}, u32[]{:S(2)}) collective-permute-start(bf16[16,1024]{1,0:T(8,128)(2,1)S(1)} %get-tuple-element.28), channel_id=1, source_target_pairs={{0,7},{1,0},{2,1},{3,2},{4,3},{5,4},{6,5},{7,6},{8,15},{9,8},{10,9... | collective-permute-start | bytes 98312 | tf_op jit(solution)/shard_map/hidden_spread/ppermute | solution.py:51
  21.4 12.5 %copy-start.4 = (s32[1,4,16]{2,1,0:T(4,128)S(1)}, s32[1,4,16]{2,1,0:T(4,128)}, u32[]{:S(2)}) copy-start(s32[1,4,16]{2,1,0:T(4,128)} %param.6) | copy-start | bytes 772
  21.5 6.2 %collective-permute-start.9 = (bf16[16,2048]{1,0:T(8,128)(2,1)S(1)}, bf16[16,2048]{1,0:T(8,128)(2,1)S(1)}, u32[]{:S(2)}, u32[]{:S(2)}) collective-permute-start(bf16[16,2048]{1,0:T(8,128)(2,1)S(1)} %bitcast.203), channel_id=1, source_target_pairs={{0,24},{8,0},{16,8},{24,16},{1,25},{9,1},{17,9},{25,17},{2,26},{10... | collective-permute-start | bytes 196616 | tf_op jit(solution)/shard_map/hidden_spread/ppermute | solution.py:51
  25.2 7.3 %collective-permute-start.8 = (bf16[16,2048]{1,0:T(8,128)(2,1)S(1)}, bf16[16,2048]{1,0:T(8,128)(2,1)S(1)}, u32[]{:S(2)}, u32[]{:S(2)}) collective-permute-start(bf16[16,2048]{1,0:T(8,128)(2,1)S(1)} %bitcast.204), channel_id=1, source_target_pairs={{0,16},{8,24},{16,0},{24,8},{1,17},{9,25},{17,1},{25,9},{2,18},{10... | collective-permute-start | bytes 196616 | tf_op jit(solution)/shard_map/hidden_spread/ppermute | solution.py:51
  25.3 7.2 %collective-permute-start.7 = (bf16[16,2048]{1,0:T(8,128)(2,1)S(1)}, bf16[16,2048]{1,0:T(8,128)(2,1)S(1)}, u32[]{:S(2)}, u32[]{:S(2)}) collective-permute-start(bf16[16,2048]{1,0:T(8,128)(2,1)S(1)} %bitcast.205), channel_id=1, source_target_pairs={{0,8},{8,16},{16,24},{24,0},{1,9},{9,17},{17,25},{25,1},{2,10},{10... | collective-permute-start | bytes 196616 | tf_op jit(solution)/shard_map/hidden_spread/ppermute | solution.py:51
  33.3 5.5 %collective-permute-start.13 = (bf16[64,1024]{1,0:T(8,128)(2,1)S(1)}, bf16[64,1024]{1,0:T(8,128)(2,1)S(1)}, u32[]{:S(2)}, u32[]{:S(2)}) collective-permute-start(bf16[64,1024]{1,0:T(8,128)(2,1)S(1)} %get-tuple-element.18), channel_id=1, source_target_pairs={{0,4},{1,5},{2,6},{3,7},{4,0},{5,1},{6,2},{7,3},{8,12},{9,13},{10,... | collective-permute-start | bytes 393224 | tf_op jit(solution)/shard_map/hidden_spread/hidden_gather_stage/ppermute | solution.py:62
  34.0 6.2 %collective-permute-start.10 = (bf16[64,1024]{1,0:T(8,128)(2,1)S(1)}, bf16[64,1024]{1,0:T(8,128)(2,1)S(1)}, u32[]{:S(2)}, u32[]{:S(2)}) collective-permute-start(bf16[64,1024]{1,0:T(8,128)(2,1)S(1)} %get-tuple-element.19), channel_id=1, source_target_pairs={{0,2},{1,3},{2,0},{3,1},{4,6},{5,7},{6,4},{7,5},{8,10},{9,11},{10,... | collective-permute-start | bytes 393224 | tf_op jit(solution)/shard_map/hidden_spread/hidden_gather_stage/ppermute | solution.py:62
  38.9 7.5 %collective-permute-start.14 = (bf16[2,64,1024]{2,1,0:T(8,128)(2,1)S(1)}, bf16[2,64,1024]{2,1,0:T(8,128)(2,1)S(1)}, u32[]{:S(2)}, u32[]{:S(2)}) collective-permute-start(bf16[2,64,1024]{2,1,0:T(8,128)(2,1)S(1)} %maximum_select_fusion.7), channel_id=1, source_target_pairs={{0,2},{1,3},{2,0},{3,1},{4,6},{5,7},{6,4},{7,5},{8,10},{9,11},{10,... | collective-permute-start | bytes 786440 | tf_op jit(solution)/shard_map/hidden_spread/hidden_gather_stage/ppermute | solution.py:62
  40.3 7.3 %collective-permute-start.11 = (bf16[2,64,1024]{2,1,0:T(8,128)(2,1)S(1)}, bf16[2,64,1024]{2,1,0:T(8,128)(2,1)S(1)}, u32[]{:S(2)}, u32[]{:S(2)}) collective-permute-start(bf16[2,64,1024]{2,1,0:T(8,128)(2,1)S(1)} %maximum_select_fusion.5), channel_id=1, source_target_pairs={{0,4},{1,5},{2,6},{3,7},{4,0},{5,1},{6,2},{7,3},{8,12},{9,13},{10,... | collective-permute-start | bytes 786440 | tf_op jit(solution)/shard_map/hidden_spread/hidden_gather_stage/ppermute | solution.py:62
  46.5 2.0 collective-permute-start.15
  47.5 2.7 %slice-start = ((s8[9961472]{0:T(1024)(128)(4,1)}), s8[4194304]{0:T(1024)(128)(4,1)S(1)}, s32[]{:S(2)}) async-start(s8[9961472]{0:T(1024)(128)(4,1)} %bitcast.216), calls=%async_computation.3 | async-start | bytes 8388608
  47.6 2.0 collective-permute-start.12
  48.4 2.8 %slice-start.1 = ((s8[9961472]{0:T(1024)(128)(4,1)}), s8[4194304]{0:T(1024)(128)(4,1)S(1)}, s32[]{:S(2)}) async-start(s8[9961472]{0:T(1024)(128)(4,1)} %bitcast.216), calls=%async_computation.4 | async-start | bytes 8388608
  49.8 1.8 slice-start.2
  64.2 134.9 %all-gather.3.cloned.1.call-start = ((), (), s32[]{:S(2)}) async-start(), calls=%async_computation.2 | async-start | bytes 2621440 | tf_op jit(solution)/shard_map/all_gather | solution.py:140
  139.9 12.3 %copy-start.2 = (f32[1,16,128,128]{3,2,1,0:T(8,128)S(1)}, f32[1,16,128,128]{3,2,1,0:T(8,128)}, u32[]{:S(2)}) copy-start(f32[1,16,128,128]{3,2,1,0:T(8,128)} %reduce-scatter.2.cloned.1.call-done) | copy-start | bytes 3145732
  214.1 2.0 copy-start.3
  217.6 4.4 %collective-permute-start.16 = (f32[2,2,64,2048]{3,2,1,0:T(8,128)}, f32[2,2,64,2048]{3,2,1,0:T(8,128)S(1)}, u32[]{:S(2)}, u32[]{:S(2)}) collective-permute-start(f32[2,2,64,2048]{3,2,1,0:T(8,128)} %dynamic-slice_bitcast_fusion), channel_id=1, source_target_pairs={{0,1},{1,0},{2,3},{3,2},{4,5},{5,4},{6,7},{7,6},{8,9},{9,8},{10,11... | collective-permute-start | bytes 6291464 | tf_op jit(solution)/shard_map/summed_core_stage/ppermute | solution.py:18
  225.0 14.2 %collective-permute-start.19 = (f32[2,64,1024]{2,1,0:T(8,128)}, f32[2,64,1024]{2,1,0:T(8,128)S(1)}, u32[]{:S(2)}, u32[]{:S(2)}) collective-permute-start(f32[2,64,1024]{2,1,0:T(8,128)} %dynamic-slice_bitcast_fusion.1), channel_id=1, source_target_pairs={{0,4},{1,5},{2,6},{3,7},{4,0},{5,1},{6,2},{7,3},{8,12},{9,13},{10,... | collective-permute-start | bytes 1572872 | tf_op jit(solution)/shard_map/summed_chip_stage/ppermute | solution.py:18
  227.3 13.9 %collective-permute-start.17 = (f32[2,64,1024]{2,1,0:T(8,128)}, f32[2,64,1024]{2,1,0:T(8,128)S(1)}, u32[]{:S(2)}, u32[]{:S(2)}) collective-permute-start(f32[2,64,1024]{2,1,0:T(8,128)} %dynamic-slice_bitcast_fusion.2), channel_id=1, source_target_pairs={{0,2},{1,3},{2,0},{3,1},{4,6},{5,7},{6,4},{7,5},{8,10},{9,11},{10,... | collective-permute-start | bytes 1572872 | tf_op jit(solution)/shard_map/summed_chip_stage/ppermute | solution.py:18
  239.2 18.5 %copy-start.1 = (s32[1,4]{1,0:T(1,128)S(1)}, s32[1,4]{1,0:T(1,128)}, u32[]{:S(2)}) copy-start(s32[1,4]{1,0:T(1,128)} %param.7) | copy-start | bytes 52
  239.3 7.6 %collective-permute-start.20 = (f32[64,1024]{1,0:T(8,128)S(1)}, f32[64,1024]{1,0:T(8,128)S(1)}, u32[]{:S(2)}, u32[]{:S(2)}) collective-permute-start(f32[64,1024]{1,0:T(8,128)S(1)} %dynamic-slice_bitcast_fusion.3), channel_id=1, source_target_pairs={{0,2},{1,3},{2,0},{3,1},{4,6},{5,7},{6,4},{7,5},{8,10},{9,11},{10,... | collective-permute-start | bytes 786440 | tf_op jit(solution)/shard_map/summed_chip_stage/ppermute | solution.py:18
  241.3 7.3 %collective-permute-start.18 = (f32[64,1024]{1,0:T(8,128)S(1)}, f32[64,1024]{1,0:T(8,128)S(1)}, u32[]{:S(2)}, u32[]{:S(2)}) collective-permute-start(f32[64,1024]{1,0:T(8,128)S(1)} %dynamic-slice_bitcast_fusion.4), channel_id=1, source_target_pairs={{0,4},{1,5},{2,6},{3,7},{4,0},{5,1},{6,2},{7,3},{8,12},{9,13},{10,... | collective-permute-start | bytes 786440 | tf_op jit(solution)/shard_map/summed_chip_stage/ppermute | solution.py:18
  248.7 3.6 %collective-permute-start.21 = (f32[64]{0:T(128)S(1)}, f32[64]{0:T(128)S(1)}, u32[]{:S(2)}, u32[]{:S(2)}) collective-permute-start(f32[64]{0:T(128)S(1)} %multiply_reduce_fusion), channel_id=1, source_target_pairs={{0,8},{8,0},{16,24},{24,16},{1,9},{9,1},{17,25},{25,17},{2,10},{10... | collective-permute-start | bytes 776 | tf_op jit(solution)/shard_map/ppermute | solution.py:89
  252.4 4.5 %collective-permute-start.22 = (f32[64]{0:T(128)S(1)}, f32[64]{0:T(128)S(1)}, u32[]{:S(2)}, u32[]{:S(2)}) collective-permute-start(f32[64]{0:T(128)S(1)} %add.312), channel_id=1, source_target_pairs={{0,16},{8,24},{16,0},{24,8},{1,17},{9,25},{17,1},{25,9},{2,18},{10... | collective-permute-start | bytes 776 | tf_op jit(solution)/shard_map/ppermute | solution.py:89
Sparse Core Ops, SparseCore 0:
  64.4 75.4 reduce-scatter.1
  153.9 45.2 all-gather.2

commit v9 on v8

--- a/solution.py
+++ b/solution.py
@@ -39,22 +39,6 @@
     return jnp.concatenate([first, second], axis=-1)
 
 
-def permute_all_to_all(x, axis_name, n, split_axis, concat_axis):
-    me = lax.axis_index(axis_name)
-    shape = list(x.shape)
-    shape[split_axis : split_axis + 1] = [n, x.shape[split_axis] // n]
-    pieces = jnp.moveaxis(x.reshape(shape), split_axis, 0)
-    got = [lax.dynamic_index_in_dim(pieces, me, axis=0, keepdims=False)]
-    for shift in range(1, n):
-        send = lax.dynamic_index_in_dim(pieces, (me + shift) % n, axis=0, keepdims=False)
-        perm = [(s, (s + shift) % n) for s in range(n)]
-        got.append(lax.ppermute(send, axis_name, perm=perm))
-    received = jnp.stack(got)
-    order = (me - jnp.arange(n, dtype=jnp.int32)) % n
-    by_source = jnp.take(received, order, axis=0)
-    return jnp.concatenate([by_source[k] for k in range(n)], axis=concat_axis)
-
-
 def gather_stage(x, have, bit, n):
     me = lax.axis_index("vocab")
     mine = (me // (1 << bit)) % 2
@@ -90,6 +74,28 @@
     return x
 
 
+def bruck_all_to_all(x, axis_name, n, split_axis, concat_axis):
+    me = lax.axis_index(axis_name)
+    levels = n.bit_length() - 1
+    shape = list(x.shape)
+    shape[split_axis : split_axis + 1] = [n, x.shape[split_axis] // n]
+    pieces = jnp.moveaxis(x.reshape(shape), split_axis, 0)
+    rest = pieces.shape[1:]
+    held = pieces.reshape([2] * levels + list(rest))
+    for bit in range(levels):
+        pos = levels - 1 - bit
+        mine = (me // (1 << bit)) % 2
+        keep = lax.dynamic_index_in_dim(held, mine, axis=pos, keepdims=False)
+        send = lax.dynamic_index_in_dim(held, 1 - mine, axis=pos, keepdims=False)
+        perm = [(s, s ^ (1 << bit)) for s in range(n)]
+        got = lax.ppermute(send, axis_name, perm=perm)
+        low = jnp.stack([keep, got], axis=pos)
+        high = jnp.stack([got, keep], axis=pos)
+        held = jnp.where(mine == 0, low, high)
+    by_source = held.reshape((n,) + tuple(rest))
+    return jnp.concatenate([by_source[k] for k in range(n)], axis=concat_axis)
+
+
 def per_device(hidden, out_weight, token_blocks, counts):
     vocab_here, columns_here = out_weight.shape
     n_vocab = lax.psum(1, "vocab")
@@ -104,8 +110,8 @@
     own_counts = lax.dynamic_slice_in_dim(block_counts, me_dp, 1, 0)
 
     with jax.named_scope("hidden_spread"):
-        row_slices = permute_all_to_all(hidden, "vocab", n_vocab, split_axis=0, concat_axis=1)
-        plane_rows = permute_all_to_all(row_slices, "dp", n_dp, split_axis=1, concat_axis=0)
+        row_slices = bruck_all_to_all(hidden, "vocab", n_vocab, split_axis=0, concat_axis=1)
+        plane_rows = bruck_all_to_all(row_slices, "dp", n_dp, split_axis=1, concat_axis=0)
         gathered = doubling_all_gather(plane_rows, n_vocab)
         group = hidden.shape[0] // n_vocab
         beam_columns = (

time: 265 us -> 264 us (level)
  waiting for transfers between devices: 167 us -> 176 us
  local copies, waits for them, and re-layouts: 18.9 us -> 12.6 us
    ppermute x10 -> x5, waiting for transfers between devices: 7.6 us -> 15.5 us  [bruck_all_to_all(): got = lax.ppermute(send, axis_name, perm=perm)]
    ppermute x10 -> x5, starting transfers between devices: 14.6 us -> 10.5 us  [bruck_all_to_all(): got = lax.ppermute(send, axis_name, perm=perm)]
    squeeze x5, local copies, waits for them, and re-layouts: 3.25 us -> 0.35 us  [exchange_stage(): send = lax.dynamic_index_in_dim(x, 1 - mine, axis=axis, keepdims=False)]
  transfers between devices with their start and end apart: 25 -> 20, of which waited for: 18 -> 19; matrix products, arithmetic and copies ran while one was open for 1% -> 1% of each run, Pallas kernels for 0% -> 0%
where the time goes in v9:
time: 264 us
  waiting for transfers between devices  176 us (67%)
  starting transfers between devices  23.7 us (9%)
  matrix products  19.6 us (7%)
  between operations  14.5 us (5%)
  local copies, waits for them, and re-layouts  12.6 us (5%)
  blocking collectives  9.06 us (3%)
  other arithmetic  8.17 us (3%)
    reduce_scatter x1, waiting for transfers between devices, per_device(): logits = lax.psum_scatter(picked, 'dp', scatter_dimension=0, tiled=True)  76.7 us
    all_gather x1, waiting for transfers between devices, per_device(): prob_part = lax.all_gather(probabilities, 'dp', axis=0, tiled=True)  45.4 us
    ppermute x5, waiting for transfers between devices, exchange_stage(): got = lax.ppermute(send, 'vocab', perm=perm)  20.8 us
    ppermute x5, waiting for transfers between devices, bruck_all_to_all(): got = lax.ppermute(send, axis_name, perm=perm)  15.5 us
    ppermute x6, waiting for transfers between devices, gather_stage(): got = lax.ppermute(x, 'vocab', perm=perm)  10.9 us
    ppermute x5, starting transfers between devices, bruck_all_to_all(): got = lax.ppermute(send, axis_name, perm=perm)  10.5 us
    all_gather x1, blocking collectives, per_device(): stats = lax.all_gather(jnp.stack([local_max, local_total]), 'vocab', axis=0)  9.06 us
    dot_general x1, matrix products, per_device(): jnp.einsum('bv,vd->bd', spread.reshape(n_blk * BB, n_tb * TB), out_weight...  8.98 us
  transfers between devices with their start and end apart: 20, of which 19 were waited for; matrix products, arithmetic and copies ran while one was open for 1% of the time, Pallas kernels for 0%

profile of v9, /device:TPU:0, one launch (start us, length us, event | category | flops | bytes accessed | tf_op | source)
XLA Modules:
  0.0 263.5 jit_solution(10834545559782596634)
XLA Ops:
  7.3 1.0 constant_dynamic-slice_fusion.4
  8.3 0.6 collective-permute-start
  8.8 1.0 collective-permute-done
  9.9 2.9 %collective-permute-start.1 = (bf16[2,2,16,1024]{3,2,1,0:T(8,128)(2,1)S(1)}, bf16[2,2,16,1024]{3,2,1,0:T(8,128)(2,1)S(1)}, u32[]{:S(2)}, u32[]{:S(2)}) collective-permute-start(bf16[2,2,16,1024]{3,2,1,0:T(8,128)(2,1)S(1)} %get-tuple-element.33), channel_id=1, source_target_pairs={{0,2},{1,3},{2,0},{3,1},{4,6},{5,7},{6,4},{7,5},{8,10},{9,11},{10,... | collective-permute-start | bytes 393224 | tf_op jit(solution)/shard_map/hidden_spread/ppermute | solution.py:91
  12.8 3.8 %collective-permute-done.1 = bf16[2,2,16,1024]{3,2,1,0:T(8,128)(2,1)S(1)} collective-permute-done((bf16[2,2,16,1024]{3,2,1,0:T(8,128)(2,1)S(1)}, bf16[2,2,16,1024]{3,2,1,0:T(8,128)(2,1)S(1)}, u32[]{:S(2)}, u32[]{:S(2)}) %collective-permute-start.1) | collective-permute-done | bytes 131104 | tf_op jit(solution)/shard_map/hidden_spread/ppermute | solution.py:91
  16.6 1.8 collective-permute-start.2
  18.5 3.2 %collective-permute-done.2 = bf16[2,2,16,1024]{3,2,1,0:T(8,128)(2,1)S(1)} collective-permute-done((bf16[2,2,16,1024]{3,2,1,0:T(8,128)(2,1)S(1)}, bf16[2,2,16,1024]{3,2,1,0:T(8,128)(2,1)S(1)}, u32[]{:S(2)}, u32[]{:S(2)}) %collective-permute-start.2) | collective-permute-done | bytes 131104 | tf_op jit(solution)/shard_map/hidden_spread/ppermute | solution.py:91
  21.8 0.2 reshape.511
  22.0 0.2 copy.51
  22.2 1.9 collective-permute-start.3
  24.1 3.1 %collective-permute-done.3 = bf16[2,16,2048]{2,1,0:T(8,128)(2,1)S(1)} collective-permute-done((bf16[2,16,2048]{2,1,0:T(8,128)(2,1)S(1)}, bf16[2,16,2048]{2,1,0:T(8,128)(2,1)S(1)}, u32[]{:S(2)}, u32[]{:S(2)}) %collective-permute-start.3) | collective-permute-done | bytes 131104 | tf_op jit(solution)/shard_map/hidden_spread/ppermute | solution.py:91
  27.3 3.3 %collective-permute-start.4 = (bf16[2,16,2048]{2,1,0:T(8,128)(2,1)S(1)}, bf16[2,16,2048]{2,1,0:T(8,128)(2,1)S(1)}, u32[]{:S(2)}, u32[]{:S(2)}) collective-permute-start(bf16[2,16,2048]{2,1,0:T(8,128)(2,1)S(1)} %get-tuple-element.27), channel_id=1, source_target_pairs={{0,16},{8,24},{16,0},{24,8},{1,17},{9,25},{17,1},{25,9},{2,18},{10... | collective-permute-start | bytes 393224 | tf_op jit(solution)/shard_map/hidden_spread/ppermute | solution.py:91
  30.6 4.4 %collective-permute-done.4 = bf16[2,16,2048]{2,1,0:T(8,128)(2,1)S(1)} collective-permute-done((bf16[2,16,2048]{2,1,0:T(8,128)(2,1)S(1)}, bf16[2,16,2048]{2,1,0:T(8,128)(2,1)S(1)}, u32[]{:S(2)}, u32[]{:S(2)}) %collective-permute-start.4) | collective-permute-done | bytes 131104 | tf_op jit(solution)/shard_map/hidden_spread/ppermute | solution.py:91
  35.0 0.1 slice_bitcast_fusion.15
  35.1 1.6 collective-permute-start.5
  36.7 0.1 reshape.513
  36.8 1.5 collective-permute-start.8
  38.3 3.3 %collective-permute-done.5 = bf16[64,1024]{1,0:T(8,128)(2,1)S(1)} collective-permute-done((bf16[64,1024]{1,0:T(8,128)(2,1)S(1)}, bf16[64,1024]{1,0:T(8,128)(2,1)S(1)}, u32[]{:S(2)}, u32[]{:S(2)}) %collective-permute-start.5) | collective-permute-done | bytes 131104 | tf_op jit(solution)/shard_map/hidden_spread/hidden_gather_stage/ppermute | solution.py:46
  41.6 1.5 collective-permute-done.8
  43.2 0.6 collective-permute-start.9
  43.8 1.6 collective-permute-start.6
  45.5 4.2 %collective-permute-done.9 = bf16[2,64,1024]{2,1,0:T(8,128)(2,1)S(1)} collective-permute-done((bf16[2,64,1024]{2,1,0:T(8,128)(2,1)S(1)}, bf16[2,64,1024]{2,1,0:T(8,128)(2,1)S(1)}, u32[]{:S(2)}, u32[]{:S(2)}) %collective-permute-start.9) | collective-permute-done | bytes 262176 | tf_op jit(solution)/shard_map/hidden_spread/hidden_gather_stage/ppermute | solution.py:46
  49.8 0.5 collective-permute-done.6
  50.3 0.1 collective-permute-start.7
  50.4 0.1 pad_maximum_fusion
  50.5 0.1 maximum_select_fusion.3
  50.6 1.0 collective-permute-done.10
  51.7 0.2 maximum_select_fusion.1
  51.9 0.5 collective-permute-done.7
  52.4 0.2 maximum_select_fusion
  52.7 0.2 maximum_bitcast_fusion
  52.9 0.2 copy.60
  53.1 0.9 slice-done.1
  54.1 0.4 slice-done.2
  54.5 7.3 %fusion.21 = f32[4,128,19,128]{3,1,2,0:T(8,128)} fusion(bf16[4,128,2048,1]{2,1,3,0:T(8,128)(2,1)S(1)} %bitcast.163, bf16[19,128,2048,1]{2,1,0,3:T(8,128)(2,1)S(1)} %bitcast.202), kind=kOutput, calls=%fused_computation.92 | convolution fusion | flops 5100273664 | bytes 17039360 | tf_op jit(solution)/shard_map/dense_logits/bd,vd->bv/dot_general | solution.py:124
  61.8 5.3 %gather_fusion = f32[64,128,128]{2,1,0:T(8,128)} fusion(f32[4,128,19,128]{3,1,2,0:T(8,128)} %fusion.21, s32[64]{0:T(128)S(1)} %reshape.513), kind=kCustom, calls=%fused_computation | custom fusion | bytes 8389120 | tf_op jit(solution)/shard_map/dense_logits/gather | solution.py:129
  67.1 0.6 constant_dynamic-slice_fusion.5
  67.7 0.6 iota_compare_fusion.1
  68.4 76.7 %reduce-scatter.2.cloned.1.call-done = f32[1,16,128,128]{3,2,1,0:T(8,128)} async-done(((f32[4,16,128,128]{3,2,1,0:T(8,128)}), f32[1,16,128,128]{3,2,1,0:T(8,128)}) %reduce-scatter.2.cloned.1.call-update) | async-done | bytes 1048592 | tf_op jit(solution)/shard_map/reduce_scatter | solution.py:131
  145.1 1.5 select_reduce_fusion
  146.6 1.6 exponential_reduce_fusion
  148.2 9.1 %all-gather = f32[16,1,128]{2,1,0:T(1,128)S(1)} all-gather(f32[2,1,128]{2,1,0:T(1,128)S(1)} %pad_maximum_fusion.4), channel_id=2, replica_groups=mesh['dp'=4,'vocab'=8] {'vocab'}, dimensions={0}, use_global_device_ids=true | all-gather | bytes 9216 | tf_op jit(solution)/shard_map/softmax_stats/all_gather | solution.py:139
  157.3 1.6 select_convert_fusion
  158.9 45.4 %all-gather.3.cloned.1.call-done = bf16[4,16,128,128]{3,2,1,0:T(8,128)(2,1)} async-done(((bf16[1,16,128,128]{3,2,1,0:T(8,128)(2,1)}), bf16[4,16,128,128]{3,2,1,0:T(8,128)(2,1)}) %all-gather.3.cloned.1.call-update) | async-done | bytes 2097168 | tf_op jit(solution)/shard_map/all_gather | solution.py:146
  204.3 3.3 %convert_bitcast_fusion = bf16[4,128,19,128]{3,2,1,0:T(8,128)(2,1)S(1)} fusion(bf16[4,16,128,128]{3,2,1,0:T(8,128)(2,1)} %all-gather.3.cloned.1.call-done, s32[4,16]{1,0:T(4,128)S(1)} %bitcast.197), kind=kOutput, calls=%fused_computation.3 | convolution fusion | flops 41092288 | bytes 4587776 | tf_op jit(solution)/shard_map/dense_expected/bsk,bsrt->brkt/dot_general | solution.py:152
  207.6 2.8 %dot_general.19 = bf16[2,2,2,64,2432]{4,3,2,1,0:T(8,128)(2,1)} reshape(bf16[4,128,19,128]{3,2,1,0:T(8,128)(2,1)S(1)} %convert_bitcast_fusion) | data formatting | bytes 4980736 | tf_op jit(solution)/shard_map/dense_expected/bv,vd->bd/dot_general | solution.py:155
  210.3 9.0 %fusion = f32[2,2,2,64,2048]{4,3,2,1,0:T(8,128)S(1)} fusion(bf16[2,2,2,64,2432]{4,3,2,1,0:T(8,128)(2,1)} %dot_general.19, bf16[2432,2048]{1,0:T(8,128)(2,1)} %param.5), kind=kOutput, calls=%fused_computation.1 | convolution fusion | flops 5100273664 | bytes 16646144 | tf_op jit(solution)/shard_map/dense_expected/bv,vd->bd/dot_general | solution.py:155
  219.3 0.2 dynamic-slice_bitcast_fusion
  219.6 4.1 %collective-permute-done.11 = f32[2,2,64,2048]{3,2,1,0:T(8,128)S(1)} collective-permute-done((f32[2,2,64,2048]{3,2,1,0:T(8,128)S(1)}, f32[2,2,64,2048]{3,2,1,0:T(8,128)S(1)}, u32[]{:S(2)}, u32[]{:S(2)}) %collective-permute-start.11) | collective-permute-done | bytes 2097184 | tf_op jit(solution)/shard_map/summed_core_stage/ppermute | solution.py:18
  223.8 0.3 bitcast_add_fusion
  224.1 0.2 fusion.19
  224.4 1.5 collective-permute-start.14
  226.0 1.5 collective-permute-start.12
  227.5 10.9 %collective-permute-done.14 = f32[2,64,1024]{2,1,0:T(8,128)S(1)} collective-permute-done((f32[2,64,1024]{2,1,0:T(8,128)S(1)}, f32[2,64,1024]{2,1,0:T(8,128)S(1)}, u32[]{:S(2)}, u32[]{:S(2)}) %collective-permute-start.14) | collective-permute-done | bytes 524320 | tf_op jit(solution)/shard_map/summed_chip_stage/ppermute | solution.py:18
  238.6 1.5 collective-permute-start.15
  240.2 1.5 collective-permute-start.13
  241.8 4.4 %collective-permute-done.15 = f32[64,1024]{1,0:T(8,128)S(1)} collective-permute-done((f32[64,1024]{1,0:T(8,128)S(1)}, f32[64,1024]{1,0:T(8,128)S(1)}, u32[]{:S(2)}, u32[]{:S(2)}) %collective-permute-start.15) | collective-permute-done | bytes 262176 | tf_op jit(solution)/shard_map/summed_chip_stage/ppermute | solution.py:18
  246.2 1.3 collective-permute-done.13
  247.5 0.1 multiply_reduce_fusion
  247.7 0.2 collective-permute-start.16
  247.9 3.4 %collective-permute-done.16 = f32[64]{0:T(128)S(1)} collective-permute-done((f32[64]{0:T(128)S(1)}, f32[64]{0:T(128)S(1)}, u32[]{:S(2)}, u32[]{:S(2)}) %collective-permute-start.16) | collective-permute-done | bytes 288 | tf_op jit(solution)/shard_map/ppermute | solution.py:73
  251.3 1.2 collective-permute-start.17
  252.5 3.2 %collective-permute-done.17 = f32[64]{0:T(128)S(1)} collective-permute-done((f32[64]{0:T(128)S(1)}, f32[64]{0:T(128)S(1)}, u32[]{:S(2)}, u32[]{:S(2)}) %collective-permute-start.17) | collective-permute-done | bytes 288 | tf_op jit(solution)/shard_map/ppermute | solution.py:73
  255.8 0.9 fusion.3
  (66 shorter events, 1.5 us)
Async XLA Ops:
  7.2 60.0 %copy-start = (s32[1,4]{1,0:T(1,128)S(1)}, s32[1,4]{1,0:T(1,128)}, u32[]{:S(2)}) copy-start(s32[1,4]{1,0:T(1,128)} %param.7) | copy-start | bytes 52
  7.2 137.9 %reduce-scatter.2.cloned.1.call-start = ((), (), s32[]{:S(2)}) async-start(), calls=%async_computation.1 | async-start | bytes 5242880 | tf_op jit(solution)/shard_map/reduce_scatter | solution.py:131
  8.3 1.5 collective-permute-start
  9.9 6.7 %collective-permute-start.1 = (bf16[2,2,16,1024]{3,2,1,0:T(8,128)(2,1)S(1)}, bf16[2,2,16,1024]{3,2,1,0:T(8,128)(2,1)S(1)}, u32[]{:S(2)}, u32[]{:S(2)}) collective-permute-start(bf16[2,2,16,1024]{3,2,1,0:T(8,128)(2,1)S(1)} %get-tuple-element.33), channel_id=1, source_target_pairs={{0,2},{1,3},{2,0},{3,1},{4,6},{5,7},{6,4},{7,5},{8,10},{9,11},{10,... | collective-permute-start | bytes 393224 | tf_op jit(solution)/shard_map/hidden_spread/ppermute | solution.py:91
  16.6 5.0 %collective-permute-start.2 = (bf16[2,2,16,1024]{3,2,1,0:T(8,128)(2,1)S(1)}, bf16[2,2,16,1024]{3,2,1,0:T(8,128)(2,1)S(1)}, u32[]{:S(2)}, u32[]{:S(2)}) collective-permute-start(bf16[2,2,16,1024]{3,2,1,0:T(8,128)(2,1)S(1)} %get-tuple-element.31), channel_id=1, source_target_pairs={{0,4},{1,5},{2,6},{3,7},{4,0},{5,1},{6,2},{7,3},{8,12},{9,13},{10,... | collective-permute-start | bytes 393224 | tf_op jit(solution)/shard_map/hidden_spread/ppermute | solution.py:91
  22.0 14.7 %copy-start.3 = (s32[1,4,16]{2,1,0:T(4,128)S(1)}, s32[1,4,16]{2,1,0:T(4,128)}, u32[]{:S(2)}) copy-start(s32[1,4,16]{2,1,0:T(4,128)} %param.6) | copy-start | bytes 772
  22.2 5.0 %collective-permute-start.3 = (bf16[2,16,2048]{2,1,0:T(8,128)(2,1)S(1)}, bf16[2,16,2048]{2,1,0:T(8,128)(2,1)S(1)}, u32[]{:S(2)}, u32[]{:S(2)}) collective-permute-start(bf16[2,16,2048]{2,1,0:T(8,128)(2,1)S(1)} %get-tuple-element.29), channel_id=1, source_target_pairs={{0,8},{8,0},{16,24},{24,16},{1,9},{9,1},{17,25},{25,17},{2,10},{10... | collective-permute-start | bytes 393224 | tf_op jit(solution)/shard_map/hidden_spread/ppermute | solution.py:91
  27.3 7.6 %collective-permute-start.4 = (bf16[2,16,2048]{2,1,0:T(8,128)(2,1)S(1)}, bf16[2,16,2048]{2,1,0:T(8,128)(2,1)S(1)}, u32[]{:S(2)}, u32[]{:S(2)}) collective-permute-start(bf16[2,16,2048]{2,1,0:T(8,128)(2,1)S(1)} %get-tuple-element.27), channel_id=1, source_target_pairs={{0,16},{8,24},{16,0},{24,8},{1,17},{9,25},{17,1},{25,9},{2,18},{10... | collective-permute-start | bytes 393224 | tf_op jit(solution)/shard_map/hidden_spread/ppermute | solution.py:91
  35.1 6.4 %collective-permute-start.5 = (bf16[64,1024]{1,0:T(8,128)(2,1)S(1)}, bf16[64,1024]{1,0:T(8,128)(2,1)S(1)}, u32[]{:S(2)}, u32[]{:S(2)}) collective-permute-start(bf16[64,1024]{1,0:T(8,128)(2,1)S(1)} %get-tuple-element.21), channel_id=1, source_target_pairs={{0,2},{1,3},{2,0},{3,1},{4,6},{5,7},{6,4},{7,5},{8,10},{9,11},{10,... | collective-permute-start | bytes 393224 | tf_op jit(solution)/shard_map/hidden_spread/hidden_gather_stage/ppermute | solution.py:46
  36.8 6.4 %collective-permute-start.8 = (bf16[64,1024]{1,0:T(8,128)(2,1)S(1)}, bf16[64,1024]{1,0:T(8,128)(2,1)S(1)}, u32[]{:S(2)}, u32[]{:S(2)}) collective-permute-start(bf16[64,1024]{1,0:T(8,128)(2,1)S(1)} %get-tuple-element.20), channel_id=1, source_target_pairs={{0,4},{1,5},{2,6},{3,7},{4,0},{5,1},{6,2},{7,3},{8,12},{9,13},{10,... | collective-permute-start | bytes 393224 | tf_op jit(solution)/shard_map/hidden_spread/hidden_gather_stage/ppermute | solution.py:46
  43.2 6.4 %collective-permute-start.9 = (bf16[2,64,1024]{2,1,0:T(8,128)(2,1)S(1)}, bf16[2,64,1024]{2,1,0:T(8,128)(2,1)S(1)}, u32[]{:S(2)}, u32[]{:S(2)}) collective-permute-start(bf16[2,64,1024]{2,1,0:T(8,128)(2,1)S(1)} %maximum_select_fusion.12), channel_id=1, source_target_pairs={{0,2},{1,3},{2,0},{3,1},{4,6},{5,7},{6,4},{7,5},{8,10},{9,11},{10,... | collective-permute-start | bytes 786440 | tf_op jit(solution)/shard_map/hidden_spread/hidden_gather_stage/ppermute | solution.py:46
  43.8 6.4 %collective-permute-start.6 = (bf16[2,64,1024]{2,1,0:T(8,128)(2,1)S(1)}, bf16[2,64,1024]{2,1,0:T(8,128)(2,1)S(1)}, u32[]{:S(2)}, u32[]{:S(2)}) collective-permute-start(bf16[2,64,1024]{2,1,0:T(8,128)(2,1)S(1)} %maximum_select_fusion.10), channel_id=1, source_target_pairs={{0,4},{1,5},{2,6},{3,7},{4,0},{5,1},{6,2},{7,3},{8,12},{9,13},{10,... | collective-permute-start | bytes 786440 | tf_op jit(solution)/shard_map/hidden_spread/hidden_gather_stage/ppermute | solution.py:46
  49.7 2.0 collective-permute-start.10
  50.2 2.9 %slice-start = ((s8[9961472]{0:T(1024)(128)(4,1)}), s8[4194304]{0:T(1024)(128)(4,1)S(1)}, s32[]{:S(2)}) async-start(s8[9961472]{0:T(1024)(128)(4,1)} %bitcast.200), calls=%async_computation.3 | async-start | bytes 8388608
  50.3 2.1 collective-permute-start.7
  51.7 2.4 slice-start.1
  52.7 1.8 slice-start.2
  67.1 137.3 %all-gather.3.cloned.1.call-start = ((), (), s32[]{:S(2)}) async-start(), calls=%async_computation.2 | async-start | bytes 2621440 | tf_op jit(solution)/shard_map/all_gather | solution.py:146
  145.1 12.2 %copy-start.2 = (f32[1,16,128,128]{3,2,1,0:T(8,128)S(1)}, f32[1,16,128,128]{3,2,1,0:T(8,128)}, u32[]{:S(2)}) copy-start(f32[1,16,128,128]{3,2,1,0:T(8,128)} %reduce-scatter.2.cloned.1.call-done) | copy-start | bytes 3145732
  219.6 4.2 %collective-permute-start.11 = (f32[2,2,64,2048]{3,2,1,0:T(8,128)S(1)}, f32[2,2,64,2048]{3,2,1,0:T(8,128)S(1)}, u32[]{:S(2)}, u32[]{:S(2)}) collective-permute-start(f32[2,2,64,2048]{3,2,1,0:T(8,128)S(1)} %dynamic-slice_bitcast_fusion), channel_id=1, source_target_pairs={{0,1},{1,0},{2,3},{3,2},{4,5},{5,4},{6,7},{7,6},{8,9},{9,8},{10,11... | collective-permute-start | bytes 6291464 | tf_op jit(solution)/shard_map/summed_core_stage/ppermute | solution.py:18
  224.4 14.0 %collective-permute-start.14 = (f32[2,64,1024]{2,1,0:T(8,128)S(1)}, f32[2,64,1024]{2,1,0:T(8,128)S(1)}, u32[]{:S(2)}, u32[]{:S(2)}) collective-permute-start(f32[2,64,1024]{2,1,0:T(8,128)S(1)} %dynamic-slice_bitcast_fusion.1), channel_id=1, source_target_pairs={{0,4},{1,5},{2,6},{3,7},{4,0},{5,1},{6,2},{7,3},{8,12},{9,13},{10,... | collective-permute-start | bytes 1572872 | tf_op jit(solution)/shard_map/summed_chip_stage/ppermute | solution.py:18
  226.0 14.1 %collective-permute-start.12 = (f32[2,64,1024]{2,1,0:T(8,128)S(1)}, f32[2,64,1024]{2,1,0:T(8,128)S(1)}, u32[]{:S(2)}, u32[]{:S(2)}) collective-permute-start(f32[2,64,1024]{2,1,0:T(8,128)S(1)} %dynamic-slice_bitcast_fusion.2), channel_id=1, source_target_pairs={{0,2},{1,3},{2,0},{3,1},{4,6},{5,7},{6,4},{7,5},{8,10},{9,11},{10,... | collective-permute-start | bytes 1572872 | tf_op jit(solution)/shard_map/summed_chip_stage/ppermute | solution.py:18
  238.5 18.2 %copy-start.1 = (s32[1,4]{1,0:T(1,128)S(1)}, s32[1,4]{1,0:T(1,128)}, u32[]{:S(2)}) copy-start(s32[1,4]{1,0:T(1,128)} %param.7) | copy-start | bytes 52
  238.6 7.6 %collective-permute-start.15 = (f32[64,1024]{1,0:T(8,128)S(1)}, f32[64,1024]{1,0:T(8,128)S(1)}, u32[]{:S(2)}, u32[]{:S(2)}) collective-permute-start(f32[64,1024]{1,0:T(8,128)S(1)} %dynamic-slice_bitcast_fusion.3), channel_id=1, source_target_pairs={{0,2},{1,3},{2,0},{3,1},{4,6},{5,7},{6,4},{7,5},{8,10},{9,11},{10,... | collective-permute-start | bytes 786440 | tf_op jit(solution)/shard_map/summed_chip_stage/ppermute | solution.py:18
  240.2 7.3 %collective-permute-start.13 = (f32[64,1024]{1,0:T(8,128)S(1)}, f32[64,1024]{1,0:T(8,128)S(1)}, u32[]{:S(2)}, u32[]{:S(2)}) collective-permute-start(f32[64,1024]{1,0:T(8,128)S(1)} %dynamic-slice_bitcast_fusion.4), channel_id=1, source_target_pairs={{0,4},{1,5},{2,6},{3,7},{4,0},{5,1},{6,2},{7,3},{8,12},{9,13},{10,... | collective-permute-start | bytes 786440 | tf_op jit(solution)/shard_map/summed_chip_stage/ppermute | solution.py:18
  247.7 3.6 %collective-permute-start.16 = (f32[64]{0:T(128)S(1)}, f32[64]{0:T(128)S(1)}, u32[]{:S(2)}, u32[]{:S(2)}) collective-permute-start(f32[64]{0:T(128)S(1)} %multiply_reduce_fusion), channel_id=1, source_target_pairs={{0,8},{8,0},{16,24},{24,16},{1,9},{9,1},{17,25},{25,17},{2,10},{10... | collective-permute-start | bytes 776 | tf_op jit(solution)/shard_map/ppermute | solution.py:73
  251.3 4.5 %collective-permute-start.17 = (f32[64]{0:T(128)S(1)}, f32[64]{0:T(128)S(1)}, u32[]{:S(2)}, u32[]{:S(2)}) collective-permute-start(f32[64]{0:T(128)S(1)} %add.155), channel_id=1, source_target_pairs={{0,16},{8,24},{16,0},{24,8},{1,17},{9,25},{17,1},{25,9},{2,18},{10... | collective-permute-start | bytes 776 | tf_op jit(solution)/shard_map/ppermute | solution.py:73
Sparse Core Ops, SparseCore 0:
  67.2 77.8 reduce-scatter.1
  159.0 45.2 all-gather.2

commit v10 on v9

--- a/solution.py
+++ b/solution.py
@@ -66,14 +66,6 @@
     return joined.reshape(n * rows, cols)
 
 
-def butterfly_sum(x, axis_name, n):
-    levels = n.bit_length() - 1
-    for bit in range(levels):
-        perm = [(s, s ^ (1 << bit)) for s in range(n)]
-        x = x + lax.ppermute(x, axis_name, perm=perm)
-    return x
-
-
 def bruck_all_to_all(x, axis_name, n, split_axis, concat_axis):
     me = lax.axis_index(axis_name)
     levels = n.bit_length() - 1
@@ -94,6 +86,16 @@
         held = jnp.where(mine == 0, low, high)
     by_source = held.reshape((n,) + tuple(rest))
     return jnp.concatenate([by_source[k] for k in range(n)], axis=concat_axis)
+
+
+def small_gather(x, axis_name, n):
+    me = lax.axis_index(axis_name)
+    got = [x]
+    for shift in range(1, n):
+        perm = [(s, (s + shift) % n) for s in range(n)]
+        got.append(lax.ppermute(x, axis_name, perm=perm))
+    order = (me - jnp.arange(n, dtype=jnp.int32)) % n
+    return jnp.take(jnp.stack(got), order, axis=0)
 
 
 def per_device(hidden, out_weight, token_blocks, counts):
@@ -136,7 +138,7 @@
         masked = jnp.where(live_mask, logits, -jnp.inf)
         local_max = jnp.max(masked, axis=(1, 3))
         local_total = jnp.sum(jnp.exp(masked - local_max[:, None, :, None]), axis=(1, 3))
-        stats = lax.all_gather(jnp.stack([local_max, local_total]), "vocab", axis=0)
+        stats = small_gather(jnp.stack([local_max, local_total]), "vocab", n_vocab)
         beam_max = jnp.max(stats[:, 0], axis=0)
         beam_total = jnp.sum(stats[:, 1] * jnp.exp(stats[:, 0] - beam_max[None]), axis=0)
         shifted = logits - beam_max[:, None, :, None] - jnp.log(beam_total)[:, None, :, None]
@@ -159,7 +161,7 @@
             preferred_element_type=jnp.float32,
         )
     summed = halving_reduce_scatter(embedding_part, n_vocab)
-    squares = butterfly_sum(jnp.sum(summed * summed, axis=1), "dp", n_dp)
+    squares = jnp.sum(small_gather(jnp.sum(summed * summed, axis=1), "dp", n_dp), axis=0)
     width = hidden.shape[1] * n_vocab
     expected = summed * lax.rsqrt(squares / width + 1e-06)[:, None]
     return (allowed_logprob[None], expected)

time: 264 us -> 264 us (level)
  starting transfers between devices: 23.7 us -> 34.6 us
  blocking collectives: 9.06 us -> 0 us
  waiting for transfers between devices: 176 us -> 173 us
    ppermute x2 -> x10, starting transfers between devices: 1.46 us -> 11.6 us  [small_gather(): got.append(lax.ppermute(x, axis_name, perm=perm))]
    all_gather x1 -> x0, blocking collectives: 9.06 us -> none  [per_device(): stats = lax.all_gather(jnp.stack([local_max, local_total]), 'vocab', axis=0)]
    ppermute x2 -> x10, waiting for transfers between devices: 6.63 us -> 4.97 us  [small_gather(): got.append(lax.ppermute(x, axis_name, perm=perm))]
  transfers between devices with their start and end apart: 20 -> 28, of which waited for: 19 -> 19; matrix products, arithmetic and copies ran while one was open for 1% -> 1% of each run, Pallas kernels for 0% -> 0%
where the time goes in v10:
time: 264 us
  waiting for transfers between devices  173 us (66%)
  starting transfers between devices  34.6 us (13%)
  matrix products  19.6 us (7%)
  between operations  14.6 us (6%)
  local copies, waits for them, and re-layouts  13.8 us (5%)
  other arithmetic  8.42 us (3%)
    reduce_scatter x1, waiting for transfers between devices, per_device(): logits = lax.psum_scatter(picked, 'dp', scatter_dimension=0, tiled=True)  75.9 us
    all_gather x1, waiting for transfers between devices, per_device(): prob_part = lax.all_gather(probabilities, 'dp', axis=0, tiled=True)  46.6 us
    ppermute x5, waiting for transfers between devices, exchange_stage(): got = lax.ppermute(send, 'vocab', perm=perm)  20.7 us
    ppermute x5, waiting for transfers between devices, bruck_all_to_all(): got = lax.ppermute(send, axis_name, perm=perm)  15.5 us
    ppermute x10, starting transfers between devices, small_gather(): got.append(lax.ppermute(x, axis_name, perm=perm))  11.6 us
    ppermute x5, starting transfers between devices, bruck_all_to_all(): got = lax.ppermute(send, axis_name, perm=perm)  10.5 us
    ppermute x6, waiting for transfers between devices, gather_stage(): got = lax.ppermute(x, 'vocab', perm=perm)  9.32 us
    dot_general x1, matrix products, per_device(): jnp.einsum('bv,vd->bd', spread.reshape(n_blk * BB, n_tb * TB), out_weight...  8.98 us
  transfers between devices with their start and end apart: 28, of which 19 were waited for; matrix products, arithmetic and copies ran while one was open for 1% of the time, Pallas kernels for 0%

profile of v10, /device:TPU:0, one launch (start us, length us, event | category | flops | bytes accessed | tf_op | source)
XLA Modules:
  0.0 264.2 jit_solution(9611009688587119056)
XLA Ops:
  7.3 1.0 constant_dynamic-slice_fusion.4
  8.3 0.6 collective-permute-start
  8.8 1.0 collective-permute-done
  9.9 2.9 %collective-permute-start.1 = (bf16[2,2,16,1024]{3,2,1,0:T(8,128)(2,1)S(1)}, bf16[2,2,16,1024]{3,2,1,0:T(8,128)(2,1)S(1)}, u32[]{:S(2)}, u32[]{:S(2)}) collective-permute-start(bf16[2,2,16,1024]{3,2,1,0:T(8,128)(2,1)S(1)} %get-tuple-element.33), channel_id=1, source_target_pairs={{0,2},{1,3},{2,0},{3,1},{4,6},{5,7},{6,4},{7,5},{8,10},{9,11},{10,... | collective-permute-start | bytes 393224 | tf_op jit(solution)/shard_map/hidden_spread/ppermute | solution.py:83
  12.8 3.8 %collective-permute-done.1 = bf16[2,2,16,1024]{3,2,1,0:T(8,128)(2,1)S(1)} collective-permute-done((bf16[2,2,16,1024]{3,2,1,0:T(8,128)(2,1)S(1)}, bf16[2,2,16,1024]{3,2,1,0:T(8,128)(2,1)S(1)}, u32[]{:S(2)}, u32[]{:S(2)}) %collective-permute-start.1) | collective-permute-done | bytes 131104 | tf_op jit(solution)/shard_map/hidden_spread/ppermute | solution.py:83
  16.6 1.8 collective-permute-start.2
  18.5 3.2 %collective-permute-done.2 = bf16[2,2,16,1024]{3,2,1,0:T(8,128)(2,1)S(1)} collective-permute-done((bf16[2,2,16,1024]{3,2,1,0:T(8,128)(2,1)S(1)}, bf16[2,2,16,1024]{3,2,1,0:T(8,128)(2,1)S(1)}, u32[]{:S(2)}, u32[]{:S(2)}) %collective-permute-start.2) | collective-permute-done | bytes 131104 | tf_op jit(solution)/shard_map/hidden_spread/ppermute | solution.py:83
  21.8 0.2 reshape.631
  22.2 1.9 collective-permute-start.3
  24.1 3.1 %collective-permute-done.3 = bf16[2,16,2048]{2,1,0:T(8,128)(2,1)S(1)} collective-permute-done((bf16[2,16,2048]{2,1,0:T(8,128)(2,1)S(1)}, bf16[2,16,2048]{2,1,0:T(8,128)(2,1)S(1)}, u32[]{:S(2)}, u32[]{:S(2)}) %collective-permute-start.3) | collective-permute-done | bytes 131104 | tf_op jit(solution)/shard_map/hidden_spread/ppermute | solution.py:83
  27.3 3.3 %collective-permute-start.4 = (bf16[2,16,2048]{2,1,0:T(8,128)(2,1)S(1)}, bf16[2,16,2048]{2,1,0:T(8,128)(2,1)S(1)}, u32[]{:S(2)}, u32[]{:S(2)}) collective-permute-start(bf16[2,16,2048]{2,1,0:T(8,128)(2,1)S(1)} %get-tuple-element.27), channel_id=1, source_target_pairs={{0,16},{8,24},{16,0},{24,8},{1,17},{9,25},{17,1},{25,9},{2,18},{10... | collective-permute-start | bytes 393224 | tf_op jit(solution)/shard_map/hidden_spread/ppermute | solution.py:83
  30.6 4.4 %collective-permute-done.4 = bf16[2,16,2048]{2,1,0:T(8,128)(2,1)S(1)} collective-permute-done((bf16[2,16,2048]{2,1,0:T(8,128)(2,1)S(1)}, bf16[2,16,2048]{2,1,0:T(8,128)(2,1)S(1)}, u32[]{:S(2)}, u32[]{:S(2)}) %collective-permute-start.4) | collective-permute-done | bytes 131104 | tf_op jit(solution)/shard_map/hidden_spread/ppermute | solution.py:83
  35.1 1.6 collective-permute-start.8
  36.8 1.5 collective-permute-start.5
  38.3 3.3 %collective-permute-done.8 = bf16[64,1024]{1,0:T(8,128)(2,1)S(1)} collective-permute-done((bf16[64,1024]{1,0:T(8,128)(2,1)S(1)}, bf16[64,1024]{1,0:T(8,128)(2,1)S(1)}, u32[]{:S(2)}, u32[]{:S(2)}) %collective-permute-start.8) | collective-permute-done | bytes 131104 | tf_op jit(solution)/shard_map/hidden_spread/hidden_gather_stage/ppermute | solution.py:46
  41.6 1.6 collective-permute-start.9
  43.3 1.5 collective-permute-start.6
  44.9 3.2 %collective-permute-done.9 = bf16[2,64,1024]{2,1,0:T(8,128)(2,1)S(1)} collective-permute-done((bf16[2,64,1024]{2,1,0:T(8,128)(2,1)S(1)}, bf16[2,64,1024]{2,1,0:T(8,128)(2,1)S(1)}, u32[]{:S(2)}, u32[]{:S(2)}) %collective-permute-start.9) | collective-permute-done | bytes 262176 | tf_op jit(solution)/shard_map/hidden_spread/hidden_gather_stage/ppermute | solution.py:46
  48.2 1.5 collective-permute-done.6
  50.1 0.2 maximum_select_fusion.1
  50.4 1.4 collective-permute-done.7
  51.7 0.2 maximum_select_fusion
  52.0 0.2 maximum_bitcast_fusion
  52.2 0.2 copy.84
  52.4 0.8 slice-done.1
  53.3 0.5 slice-done.2
  53.8 7.4 %fusion.27 = f32[4,128,19,128]{3,1,2,0:T(8,128)} fusion(bf16[4,128,2048,1]{2,1,3,0:T(8,128)(2,1)S(1)} %bitcast.193, bf16[19,128,2048,1]{2,1,0,3:T(8,128)(2,1)S(1)} %bitcast.244), kind=kOutput, calls=%fused_computation.131 | convolution fusion | flops 5100273664 | bytes 17039360 | tf_op jit(solution)/shard_map/dense_logits/bd,vd->bv/dot_general | solution.py:126
  61.2 5.2 %gather_fusion = f32[64,128,128]{2,1,0:T(8,128)} fusion(f32[4,128,19,128]{3,1,2,0:T(8,128)} %fusion.27, s32[64]{0:T(128)S(1)} %reshape.633), kind=kCustom, calls=%fused_computation | custom fusion | bytes 8389120 | tf_op jit(solution)/shard_map/dense_logits/gather | solution.py:131
  66.5 0.6 constant_dynamic-slice_fusion.5
  67.1 0.7 iota_compare_fusion.1
  67.8 75.9 %reduce-scatter.2.cloned.1.call-done = f32[1,16,128,128]{3,2,1,0:T(8,128)} async-done(((f32[4,16,128,128]{3,2,1,0:T(8,128)}), f32[1,16,128,128]{3,2,1,0:T(8,128)}) %reduce-scatter.2.cloned.1.call-update) | async-done | bytes 1048592 | tf_op jit(solution)/shard_map/reduce_scatter | solution.py:133
  143.7 1.5 select_reduce_fusion
  145.2 1.6 exponential_reduce_fusion
  146.9 1.5 collective-permute-start.12
  148.4 2.3 collective-permute-start.13
  150.7 0.6 collective-permute-start.14
  151.3 1.5 collective-permute-start.16
  152.8 2.3 collective-permute-start.17
  155.2 1.2 collective-permute-done.17
  156.4 0.6 gather_fusion.1
  157.1 1.6 select_convert_fusion
  158.8 46.6 %all-gather.2.cloned.1.call-done = bf16[4,16,128,128]{3,2,1,0:T(8,128)(2,1)} async-done(((bf16[1,16,128,128]{3,2,1,0:T(8,128)(2,1)}), bf16[4,16,128,128]{3,2,1,0:T(8,128)(2,1)}) %all-gather.2.cloned.1.call-update) | async-done | bytes 2097168 | tf_op jit(solution)/shard_map/all_gather | solution.py:148
  205.3 3.3 %convert_bitcast_fusion = bf16[4,128,19,128]{3,2,1,0:T(8,128)(2,1)S(1)} fusion(bf16[4,16,128,128]{3,2,1,0:T(8,128)(2,1)} %all-gather.2.cloned.1.call-done, s32[4,16]{1,0:T(4,128)S(1)} %bitcast.227), kind=kOutput, calls=%fused_computation.5 | convolution fusion | flops 41092288 | bytes 4587776 | tf_op jit(solution)/shard_map/dense_expected/bsk,bsrt->brkt/dot_general | solution.py:154
  208.6 2.8 %dot_general.19 = bf16[2,2,2,64,2432]{4,3,2,1,0:T(8,128)(2,1)} reshape(bf16[4,128,19,128]{3,2,1,0:T(8,128)(2,1)S(1)} %convert_bitcast_fusion) | data formatting | bytes 4980736 | tf_op jit(solution)/shard_map/dense_expected/bv,vd->bd/dot_general | solution.py:157
  211.4 9.0 %fusion = f32[2,2,2,64,2048]{4,3,2,1,0:T(8,128)S(1)} fusion(bf16[2,2,2,64,2432]{4,3,2,1,0:T(8,128)(2,1)} %dot_general.19, bf16[2432,2048]{1,0:T(8,128)(2,1)} %param.5), kind=kOutput, calls=%fused_computation.3 | convolution fusion | flops 5100273664 | bytes 16646144 | tf_op jit(solution)/shard_map/dense_expected/bv,vd->bd/dot_general | solution.py:157
  220.3 0.2 dynamic-slice_bitcast_fusion
  220.6 4.1 %collective-permute-done.18 = f32[2,2,64,2048]{3,2,1,0:T(8,128)S(1)} collective-permute-done((f32[2,2,64,2048]{3,2,1,0:T(8,128)S(1)}, f32[2,2,64,2048]{3,2,1,0:T(8,128)S(1)}, u32[]{:S(2)}, u32[]{:S(2)}) %collective-permute-start.18) | collective-permute-done | bytes 2097184 | tf_op jit(solution)/shard_map/summed_core_stage/ppermute | solution.py:18
  224.8 0.3 bitcast_add_fusion
  225.1 0.2 fusion.25
  225.4 1.5 collective-permute-start.21
  227.0 1.5 collective-permute-start.19
  228.6 10.9 %collective-permute-done.21 = f32[2,64,1024]{2,1,0:T(8,128)S(1)} collective-permute-done((f32[2,64,1024]{2,1,0:T(8,128)S(1)}, f32[2,64,1024]{2,1,0:T(8,128)S(1)}, u32[]{:S(2)}, u32[]{:S(2)}) %collective-permute-start.21) | collective-permute-done | bytes 524320 | tf_op jit(solution)/shard_map/summed_chip_stage/ppermute | solution.py:18
  239.6 1.5 collective-permute-start.22
  241.2 1.5 collective-permute-start.20
  242.8 4.4 %collective-permute-done.22 = f32[64,1024]{1,0:T(8,128)S(1)} collective-permute-done((f32[64,1024]{1,0:T(8,128)S(1)}, f32[64,1024]{1,0:T(8,128)S(1)}, u32[]{:S(2)}, u32[]{:S(2)}) %collective-permute-start.22) | collective-permute-done | bytes 262176 | tf_op jit(solution)/shard_map/summed_chip_stage/ppermute | solution.py:18
  247.2 1.3 collective-permute-done.20
  248.7 1.2 collective-permute-start.25
  249.9 0.5 collective-permute-start.24
  250.4 1.6 collective-permute-start.23
  252.0 0.3 collective-permute-done.25
  252.3 2.1 collective-permute-done.24
  254.4 1.4 collective-permute-done.23
  255.8 0.6 gather_fusion.2
  256.4 0.9 fusion.3
  (99 shorter events, 2.7 us)
Async XLA Ops:
  7.2 59.3 %copy-start = (s32[1,4]{1,0:T(1,128)S(1)}, s32[1,4]{1,0:T(1,128)}, u32[]{:S(2)}) copy-start(s32[1,4]{1,0:T(1,128)} %param.7) | copy-start | bytes 52
  7.2 136.5 %reduce-scatter.2.cloned.1.call-start = ((), (), s32[]{:S(2)}) async-start(), calls=%async_computation.1 | async-start | bytes 5242880 | tf_op jit(solution)/shard_map/reduce_scatter | solution.py:133
  8.3 1.5 collective-permute-start
  9.9 6.7 %collective-permute-start.1 = (bf16[2,2,16,1024]{3,2,1,0:T(8,128)(2,1)S(1)}, bf16[2,2,16,1024]{3,2,1,0:T(8,128)(2,1)S(1)}, u32[]{:S(2)}, u32[]{:S(2)}) collective-permute-start(bf16[2,2,16,1024]{3,2,1,0:T(8,128)(2,1)S(1)} %get-tuple-element.33), channel_id=1, source_target_pairs={{0,2},{1,3},{2,0},{3,1},{4,6},{5,7},{6,4},{7,5},{8,10},{9,11},{10,... | collective-permute-start | bytes 393224 | tf_op jit(solution)/shard_map/hidden_spread/ppermute | solution.py:83
  16.6 5.0 %collective-permute-start.2 = (bf16[2,2,16,1024]{3,2,1,0:T(8,128)(2,1)S(1)}, bf16[2,2,16,1024]{3,2,1,0:T(8,128)(2,1)S(1)}, u32[]{:S(2)}, u32[]{:S(2)}) collective-permute-start(bf16[2,2,16,1024]{3,2,1,0:T(8,128)(2,1)S(1)} %get-tuple-element.31), channel_id=1, source_target_pairs={{0,4},{1,5},{2,6},{3,7},{4,0},{5,1},{6,2},{7,3},{8,12},{9,13},{10,... | collective-permute-start | bytes 393224 | tf_op jit(solution)/shard_map/hidden_spread/ppermute | solution.py:83
  22.0 14.7 %copy-start.3 = (s32[1,4,16]{2,1,0:T(4,128)S(1)}, s32[1,4,16]{2,1,0:T(4,128)}, u32[]{:S(2)}) copy-start(s32[1,4,16]{2,1,0:T(4,128)} %param.6) | copy-start | bytes 772
  22.2 5.0 %collective-permute-start.3 = (bf16[2,16,2048]{2,1,0:T(8,128)(2,1)S(1)}, bf16[2,16,2048]{2,1,0:T(8,128)(2,1)S(1)}, u32[]{:S(2)}, u32[]{:S(2)}) collective-permute-start(bf16[2,16,2048]{2,1,0:T(8,128)(2,1)S(1)} %get-tuple-element.29), channel_id=1, source_target_pairs={{0,8},{8,0},{16,24},{24,16},{1,9},{9,1},{17,25},{25,17},{2,10},{10... | collective-permute-start | bytes 393224 | tf_op jit(solution)/shard_map/hidden_spread/ppermute | solution.py:83
  27.3 7.6 %collective-permute-start.4 = (bf16[2,16,2048]{2,1,0:T(8,128)(2,1)S(1)}, bf16[2,16,2048]{2,1,0:T(8,128)(2,1)S(1)}, u32[]{:S(2)}, u32[]{:S(2)}) collective-permute-start(bf16[2,16,2048]{2,1,0:T(8,128)(2,1)S(1)} %get-tuple-element.27), channel_id=1, source_target_pairs={{0,16},{8,24},{16,0},{24,8},{1,17},{9,25},{17,1},{25,9},{2,18},{10... | collective-permute-start | bytes 393224 | tf_op jit(solution)/shard_map/hidden_spread/ppermute | solution.py:83
  35.1 6.4 %collective-permute-start.8 = (bf16[64,1024]{1,0:T(8,128)(2,1)S(1)}, bf16[64,1024]{1,0:T(8,128)(2,1)S(1)}, u32[]{:S(2)}, u32[]{:S(2)}) collective-permute-start(bf16[64,1024]{1,0:T(8,128)(2,1)S(1)} %get-tuple-element.20), channel_id=1, source_target_pairs={{0,4},{1,5},{2,6},{3,7},{4,0},{5,1},{6,2},{7,3},{8,12},{9,13},{10,... | collective-permute-start | bytes 393224 | tf_op jit(solution)/shard_map/hidden_spread/hidden_gather_stage/ppermute | solution.py:46
  36.8 6.4 %collective-permute-start.5 = (bf16[64,1024]{1,0:T(8,128)(2,1)S(1)}, bf16[64,1024]{1,0:T(8,128)(2,1)S(1)}, u32[]{:S(2)}, u32[]{:S(2)}) collective-permute-start(bf16[64,1024]{1,0:T(8,128)(2,1)S(1)} %get-tuple-element.21), channel_id=1, source_target_pairs={{0,2},{1,3},{2,0},{3,1},{4,6},{5,7},{6,4},{7,5},{8,10},{9,11},{10,... | collective-permute-start | bytes 393224 | tf_op jit(solution)/shard_map/hidden_spread/hidden_gather_stage/ppermute | solution.py:46
  41.6 6.4 %collective-permute-start.9 = (bf16[2,64,1024]{2,1,0:T(8,128)(2,1)S(1)}, bf16[2,64,1024]{2,1,0:T(8,128)(2,1)S(1)}, u32[]{:S(2)}, u32[]{:S(2)}) collective-permute-start(bf16[2,64,1024]{2,1,0:T(8,128)(2,1)S(1)} %maximum_select_fusion.12), channel_id=1, source_target_pairs={{0,2},{1,3},{2,0},{3,1},{4,6},{5,7},{6,4},{7,5},{8,10},{9,11},{10,... | collective-permute-start | bytes 786440 | tf_op jit(solution)/shard_map/hidden_spread/hidden_gather_stage/ppermute | solution.py:46
  43.3 6.4 %collective-permute-start.6 = (bf16[2,64,1024]{2,1,0:T(8,128)(2,1)S(1)}, bf16[2,64,1024]{2,1,0:T(8,128)(2,1)S(1)}, u32[]{:S(2)}, u32[]{:S(2)}) collective-permute-start(bf16[2,64,1024]{2,1,0:T(8,128)(2,1)S(1)} %maximum_select_fusion.10), channel_id=1, source_target_pairs={{0,4},{1,5},{2,6},{3,7},{4,0},{5,1},{6,2},{7,3},{8,12},{9,13},{10,... | collective-permute-start | bytes 786440 | tf_op jit(solution)/shard_map/hidden_spread/hidden_gather_stage/ppermute | solution.py:46
  48.1 2.0 collective-permute-start.10
  49.7 2.7 %slice-start = ((s8[9961472]{0:T(1024)(128)(4,1)}), s8[4194304]{0:T(1024)(128)(4,1)S(1)}, s32[]{:S(2)}) async-start(s8[9961472]{0:T(1024)(128)(4,1)} %bitcast.242), calls=%async_computation.3 | async-start | bytes 8388608
  49.8 2.0 collective-permute-start.7
  50.1 3.2 %slice-start.1 = ((s8[9961472]{0:T(1024)(128)(4,1)}), s8[4194304]{0:T(1024)(128)(4,1)S(1)}, s32[]{:S(2)}) async-start(s8[9961472]{0:T(1024)(128)(4,1)} %bitcast.242), calls=%async_computation.4 | async-start | bytes 8388608
  52.0 1.8 slice-start.2
  66.4 138.9 %all-gather.2.cloned.1.call-start = ((), (), s32[]{:S(2)}) async-start(), calls=%async_computation.2 | async-start | bytes 2621440 | tf_op jit(solution)/shard_map/all_gather | solution.py:148
  143.7 13.4 %copy-start.2 = (f32[1,16,128,128]{3,2,1,0:T(8,128)S(1)}, f32[1,16,128,128]{3,2,1,0:T(8,128)}, u32[]{:S(2)}) copy-start(f32[1,16,128,128]{3,2,1,0:T(8,128)} %reduce-scatter.2.cloned.1.call-done) | copy-start | bytes 3145732
  146.8 4.5 %collective-permute-start.11 = (f32[2,1,128]{2,0,1:T(2,128)S(1)}, f32[2,1,128]{2,0,1:T(2,128)S(1)}, u32[]{:S(2)}, u32[]{:S(2)}) collective-permute-start(f32[2,1,128]{2,0,1:T(2,128)S(1)} %bitcast.229), channel_id=1, source_target_pairs={{0,1},{1,2},{2,3},{3,4},{4,5},{5,6},{6,7},{7,0},{8,9},{9,10},{10,1... | collective-permute-start | bytes 3080 | tf_op jit(solution)/shard_map/softmax_stats/ppermute | solution.py:96
  146.9 5.9 %collective-permute-start.12 = (f32[2,1,128]{2,0,1:T(2,128)S(1)}, f32[2,1,128]{2,0,1:T(2,128)S(1)}, u32[]{:S(2)}, u32[]{:S(2)}) collective-permute-start(f32[2,1,128]{2,0,1:T(2,128)S(1)} %bitcast.230), channel_id=1, source_target_pairs={{0,2},{1,3},{2,4},{3,5},{4,6},{5,7},{6,0},{7,1},{8,10},{9,11},{10,... | collective-permute-start | bytes 3080 | tf_op jit(solution)/shard_map/softmax_stats/ppermute | solution.py:96
  148.4 6.7 %collective-permute-start.13 = (f32[2,1,128]{2,0,1:T(2,128)S(1)}, f32[2,1,128]{2,0,1:T(2,128)S(1)}, u32[]{:S(2)}, u32[]{:S(2)}) collective-permute-start(f32[2,1,128]{2,0,1:T(2,128)S(1)} %bitcast.231), channel_id=1, source_target_pairs={{0,3},{1,4},{2,5},{3,6},{4,7},{5,0},{6,1},{7,2},{8,11},{9,12},{10,... | collective-permute-start | bytes 3080 | tf_op jit(solution)/shard_map/softmax_stats/ppermute | solution.py:96
  150.7 4.4 %collective-permute-start.14 = (f32[2,1,128]{2,0,1:T(2,128)S(1)}, f32[2,1,128]{2,0,1:T(2,128)S(1)}, u32[]{:S(2)}, u32[]{:S(2)}) collective-permute-start(f32[2,1,128]{2,0,1:T(2,128)S(1)} %bitcast.232), channel_id=1, source_target_pairs={{0,4},{1,5},{2,6},{3,7},{4,0},{5,1},{6,2},{7,3},{8,12},{9,13},{10,... | collective-permute-start | bytes 3080 | tf_op jit(solution)/shard_map/softmax_stats/ppermute | solution.py:96
  151.2 3.9 %collective-permute-start.15 = (f32[2,1,128]{2,0,1:T(2,128)S(1)}, f32[2,1,128]{2,0,1:T(2,128)S(1)}, u32[]{:S(2)}, u32[]{:S(2)}) collective-permute-start(f32[2,1,128]{2,0,1:T(2,128)S(1)} %bitcast.233), channel_id=1, source_target_pairs={{0,5},{1,6},{2,7},{3,0},{4,1},{5,2},{6,3},{7,4},{8,13},{9,14},{10,... | collective-permute-start | bytes 3080 | tf_op jit(solution)/shard_map/softmax_stats/ppermute | solution.py:96
  151.3 3.8 %collective-permute-start.16 = (f32[2,1,128]{2,0,1:T(2,128)S(1)}, f32[2,1,128]{2,0,1:T(2,128)S(1)}, u32[]{:S(2)}, u32[]{:S(2)}) collective-permute-start(f32[2,1,128]{2,0,1:T(2,128)S(1)} %bitcast.235), channel_id=1, source_target_pairs={{0,6},{1,7},{2,0},{3,1},{4,2},{5,3},{6,4},{7,5},{8,14},{9,15},{10,... | collective-permute-start | bytes 3080 | tf_op jit(solution)/shard_map/softmax_stats/ppermute | solution.py:96
  152.8 3.6 %collective-permute-start.17 = (f32[2,1,128]{2,1,0:T(1,128)S(1)}, f32[2,1,128]{2,1,0:T(1,128)S(1)}, u32[]{:S(2)}, u32[]{:S(2)}) collective-permute-start(f32[2,1,128]{2,1,0:T(1,128)S(1)} %pad_maximum_fusion.5), channel_id=1, source_target_pairs={{0,7},{1,0},{2,1},{3,2},{4,3},{5,4},{6,5},{7,6},{8,15},{9,8},{10,9... | collective-permute-start | bytes 3080 | tf_op jit(solution)/shard_map/softmax_stats/ppermute | solution.py:96
  220.6 4.2 %collective-permute-start.18 = (f32[2,2,64,2048]{3,2,1,0:T(8,128)S(1)}, f32[2,2,64,2048]{3,2,1,0:T(8,128)S(1)}, u32[]{:S(2)}, u32[]{:S(2)}) collective-permute-start(f32[2,2,64,2048]{3,2,1,0:T(8,128)S(1)} %dynamic-slice_bitcast_fusion), channel_id=1, source_target_pairs={{0,1},{1,0},{2,3},{3,2},{4,5},{5,4},{6,7},{7,6},{8,9},{9,8},{10,11... | collective-permute-start | bytes 6291464 | tf_op jit(solution)/shard_map/summed_core_stage/ppermute | solution.py:18
  225.4 14.0 %collective-permute-start.21 = (f32[2,64,1024]{2,1,0:T(8,128)S(1)}, f32[2,64,1024]{2,1,0:T(8,128)S(1)}, u32[]{:S(2)}, u32[]{:S(2)}) collective-permute-start(f32[2,64,1024]{2,1,0:T(8,128)S(1)} %dynamic-slice_bitcast_fusion.1), channel_id=1, source_target_pairs={{0,4},{1,5},{2,6},{3,7},{4,0},{5,1},{6,2},{7,3},{8,12},{9,13},{10,... | collective-permute-start | bytes 1572872 | tf_op jit(solution)/shard_map/summed_chip_stage/ppermute | solution.py:18
  227.0 14.1 %collective-permute-start.19 = (f32[2,64,1024]{2,1,0:T(8,128)S(1)}, f32[2,64,1024]{2,1,0:T(8,128)S(1)}, u32[]{:S(2)}, u32[]{:S(2)}) collective-permute-start(f32[2,64,1024]{2,1,0:T(8,128)S(1)} %dynamic-slice_bitcast_fusion.2), channel_id=1, source_target_pairs={{0,2},{1,3},{2,0},{3,1},{4,6},{5,7},{6,4},{7,5},{8,10},{9,11},{10,... | collective-permute-start | bytes 1572872 | tf_op jit(solution)/shard_map/summed_chip_stage/ppermute | solution.py:18
  239.5 17.8 %copy-start.1 = (s32[1,4]{1,0:T(1,128)S(1)}, s32[1,4]{1,0:T(1,128)}, u32[]{:S(2)}) copy-start(s32[1,4]{1,0:T(1,128)} %param.7) | copy-start | bytes 52
  239.6 7.6 %collective-permute-start.22 = (f32[64,1024]{1,0:T(8,128)S(1)}, f32[64,1024]{1,0:T(8,128)S(1)}, u32[]{:S(2)}, u32[]{:S(2)}) collective-permute-start(f32[64,1024]{1,0:T(8,128)S(1)} %dynamic-slice_bitcast_fusion.3), channel_id=1, source_target_pairs={{0,2},{1,3},{2,0},{3,1},{4,6},{5,7},{6,4},{7,5},{8,10},{9,11},{10,... | collective-permute-start | bytes 786440 | tf_op jit(solution)/shard_map/summed_chip_stage/ppermute | solution.py:18
  241.2 7.3 %collective-permute-start.20 = (f32[64,1024]{1,0:T(8,128)S(1)}, f32[64,1024]{1,0:T(8,128)S(1)}, u32[]{:S(2)}, u32[]{:S(2)}) collective-permute-start(f32[64,1024]{1,0:T(8,128)S(1)} %dynamic-slice_bitcast_fusion.4), channel_id=1, source_target_pairs={{0,4},{1,5},{2,6},{3,7},{4,0},{5,1},{6,2},{7,3},{8,12},{9,13},{10,... | collective-permute-start | bytes 786440 | tf_op jit(solution)/shard_map/summed_chip_stage/ppermute | solution.py:18
  248.7 3.6 %collective-permute-start.25 = (f32[64]{0:T(128)S(1)}, f32[64]{0:T(128)S(1)}, u32[]{:S(2)}, u32[]{:S(2)}) collective-permute-start(f32[64]{0:T(128)S(1)} %multiply_reduce_fusion), channel_id=1, source_target_pairs={{0,24},{8,0},{16,8},{24,16},{1,25},{9,1},{17,9},{25,17},{2,26},{10... | collective-permute-start | bytes 776 | tf_op jit(solution)/shard_map/ppermute | solution.py:96
  249.9 4.5 %collective-permute-start.24 = (f32[64]{0:T(128)S(1)}, f32[64]{0:T(128)S(1)}, u32[]{:S(2)}, u32[]{:S(2)}) collective-permute-start(f32[64]{0:T(128)S(1)} %multiply_reduce_fusion), channel_id=1, source_target_pairs={{0,16},{8,24},{16,0},{24,8},{1,17},{9,25},{17,1},{25,9},{2,18},{10... | collective-permute-start | bytes 776 | tf_op jit(solution)/shard_map/ppermute | solution.py:96
  250.4 5.4 %collective-permute-start.23 = (f32[64]{0:T(128)S(1)}, f32[64]{0:T(128)S(1)}, u32[]{:S(2)}, u32[]{:S(2)}) collective-permute-start(f32[64]{0:T(128)S(1)} %multiply_reduce_fusion), channel_id=1, source_target_pairs={{0,8},{8,16},{16,24},{24,0},{1,9},{9,17},{17,25},{25,1},{2,10},{10... | collective-permute-start | bytes 776 | tf_op jit(solution)/shard_map/ppermute | solution.py:96
Sparse Core Ops, SparseCore 0:
  66.6 77.0 reduce-scatter.1
  158.9 46.4 all-gather.1

commit v11 on v9

--- a/solution.py
+++ b/solution.py
@@ -19,14 +19,14 @@
     return keep + got, [b for b in remaining if b != bit]
 
 
-def halving_reduce_scatter(part, n):
+def halving_reduce_scatter(keep, send, n):
     levels = n.bit_length() - 1
-    rows, cols = part.shape
-    group = rows // n
-    remaining = list(range(levels - 1, -1, -1))
-    x = part.reshape([2] * levels + [group, cols])
+    _, group, cols = keep.shape
+    perm = [(s, s ^ 1) for s in range(n)]
     with jax.named_scope("summed_core_stage"):
-        x, remaining = exchange_stage(x, remaining, 0, n)
+        x = keep + lax.ppermute(send, "vocab", perm=perm)
+    x = x.reshape([2] * (levels - 1) + [group, cols])
+    remaining = list(range(levels - 1, 0, -1))
     half = cols // 2
     first, second = x[..., :half], x[..., half:]
     rest_a, rest_b = list(remaining), list(remaining)
@@ -145,20 +145,32 @@
 
     prob_part = lax.all_gather(probabilities, "dp", axis=0, tiled=True)
 
-    with jax.named_scope("dense_expected"):
-        onehot = (
-            block_lists[:, :, None] == jnp.arange(n_tb, dtype=jnp.int32)[None, None, :]
-        ).astype(jnp.bfloat16)
-        spread = jnp.einsum(
-            "bsk,bsrt->brkt", onehot, prob_part, preferred_element_type=jnp.float32
-        ).astype(jnp.bfloat16)
-        embedding_part = jnp.einsum(
-            "bv,vd->bd",
-            spread.reshape(n_blk * BB, n_tb * TB),
-            out_weight,
-            preferred_element_type=jnp.float32,
-        )
-    summed = halving_reduce_scatter(embedding_part, n_vocab)
+    rows_per_dev = n_blk * BB // n_vocab
+    pairs = BB // rows_per_dev // 2
+    onehot = (
+        block_lists[:, :, None] == jnp.arange(n_tb, dtype=jnp.int32)[None, None, :]
+    ).astype(jnp.bfloat16)
+    halves = prob_part.reshape(n_blk, MOST, pairs, 2, rows_per_dev, TB)
+    low_bit = lax.axis_index("vocab") % 2
+
+    def expected_half(which):
+        with jax.named_scope("dense_expected"):
+            chosen = lax.dynamic_index_in_dim(halves, which, axis=3, keepdims=False)
+            chosen = chosen.reshape(n_blk, MOST, pairs * rows_per_dev, TB)
+            spread = jnp.einsum(
+                "bsk,bsrt->brkt", onehot, chosen, preferred_element_type=jnp.float32
+            ).astype(jnp.bfloat16)
+            term = jnp.einsum(
+                "brkt,ktd->brd",
+                spread,
+                out_weight.reshape(n_tb, TB, columns_here),
+                preferred_element_type=jnp.float32,
+            )
+            return term.reshape(n_blk * pairs, rows_per_dev, columns_here)
+
+    send_half = expected_half(1 - low_bit)
+    keep_half = expected_half(low_bit)
+    summed = halving_reduce_scatter(keep_half, send_half, n_vocab)
     squares = butterfly_sum(jnp.sum(summed * summed, axis=1), "dp", n_dp)
     width = hidden.shape[1] * n_vocab
     expected = summed * lax.rsqrt(squares / width + 1e-06)[:, None]

time: 264 us -> 260 us (0.985)
    ppermute x5 -> x4, waiting for transfers between devices: 20.8 us -> 16.6 us  [exchange_stage(): got = lax.ppermute(send, 'vocab', perm=perm)]
    ppermute x0 -> x1, waiting for transfers between devices: none -> 3.21 us  [halving_reduce_scatter(): x = keep + lax.ppermute(send, 'vocab', perm=perm)]
    dot_general x1 -> x0, local copies, waits for them, and re-layouts: 2.75 us -> none  [per_device(): jnp.einsum('bv,vd->bd', spread.reshape(n_blk * BB, n_tb * TB), out_weight...]
    dot_general x2 -> x4, matrix products: 12.2 us -> 10.6 us  [the longest x2 8.79 us: expected_half(): jnp.einsum('brkt,ktd->brd', spread, out_weight.reshape(n_tb, TB, columns_...]
    ppermute x5 -> x4, starting transfers between devices: 6.22 us -> 6.15 us  [exchange_stage(): got = lax.ppermute(send, 'vocab', perm=perm)]
where the time goes in v11:
time: 260 us; the launch traced here: 259 us
  waiting for transfers between devices  175 us (67%)
  starting transfers between devices  23.7 us (9%)
  matrix products  18 us (7%)
  between operations  14.5 us (6%)
  local copies, waits for them, and re-layouts  11.3 us (4%)
  blocking collectives  9.06 us (3%)
  other arithmetic  7.84 us (3%)
    reduce_scatter x1, waiting for transfers between devices, per_device(): logits = lax.psum_scatter(picked, 'dp', scatter_dimension=0, tiled=True)  76.7 us
    all_gather x1, waiting for transfers between devices, per_device(): prob_part = lax.all_gather(probabilities, 'dp', axis=0, tiled=True)  45.4 us
    ppermute x4, waiting for transfers between devices, exchange_stage(): got = lax.ppermute(send, 'vocab', perm=perm)  16.6 us
    ppermute x5, waiting for transfers between devices, bruck_all_to_all(): got = lax.ppermute(send, axis_name, perm=perm)  15.5 us
    ppermute x6, waiting for transfers between devices, gather_stage(): got = lax.ppermute(x, 'vocab', perm=perm)  10.9 us
    ppermute x5, starting transfers between devices, bruck_all_to_all(): got = lax.ppermute(send, axis_name, perm=perm)  10.5 us
    all_gather x1, blocking collectives, per_device(): stats = lax.all_gather(jnp.stack([local_max, local_total]), 'vocab', axis=0)  9.06 us
    dot_general x2, matrix products, expected_half(): jnp.einsum('brkt,ktd->brd', spread, out_weight.reshape(n_tb, TB, columns_...  8.79 us
  transfers between devices with their start and end apart: 20, of which 19 were waited for; matrix products, arithmetic and copies ran while one was open for 1% of the time, Pallas kernels for 0%

profile of v11, /device:TPU:0, one launch (start us, length us, event | category | flops | bytes accessed | tf_op | source)
XLA Modules:
  0.0 259.4 jit_solution(10023143507022618255)
XLA Ops:
  7.3 1.0 constant_dynamic-slice_fusion.6
  8.3 0.6 collective-permute-start
  8.8 1.0 collective-permute-done
  9.9 2.9 %collective-permute-start.1 = (bf16[2,2,16,1024]{3,2,1,0:T(8,128)(2,1)S(1)}, bf16[2,2,16,1024]{3,2,1,0:T(8,128)(2,1)S(1)}, u32[]{:S(2)}, u32[]{:S(2)}) collective-permute-start(bf16[2,2,16,1024]{3,2,1,0:T(8,128)(2,1)S(1)} %get-tuple-element.27), channel_id=1, source_target_pairs={{0,2},{1,3},{2,0},{3,1},{4,6},{5,7},{6,4},{7,5},{8,10},{9,11},{10,... | collective-permute-start | bytes 393224 | tf_op jit(solution)/shard_map/hidden_spread/ppermute | solution.py:91
  12.8 3.8 %collective-permute-done.1 = bf16[2,2,16,1024]{3,2,1,0:T(8,128)(2,1)S(1)} collective-permute-done((bf16[2,2,16,1024]{3,2,1,0:T(8,128)(2,1)S(1)}, bf16[2,2,16,1024]{3,2,1,0:T(8,128)(2,1)S(1)}, u32[]{:S(2)}, u32[]{:S(2)}) %collective-permute-start.1) | collective-permute-done | bytes 131104 | tf_op jit(solution)/shard_map/hidden_spread/ppermute | solution.py:91
  16.6 1.8 collective-permute-start.2
  18.5 3.2 %collective-permute-done.2 = bf16[2,2,16,1024]{3,2,1,0:T(8,128)(2,1)S(1)} collective-permute-done((bf16[2,2,16,1024]{3,2,1,0:T(8,128)(2,1)S(1)}, bf16[2,2,16,1024]{3,2,1,0:T(8,128)(2,1)S(1)}, u32[]{:S(2)}, u32[]{:S(2)}) %collective-permute-start.2) | collective-permute-done | bytes 131104 | tf_op jit(solution)/shard_map/hidden_spread/ppermute | solution.py:91
  21.8 0.2 reshape.523
  22.0 0.2 copy.51
  22.2 1.9 collective-permute-start.3
  24.1 3.1 %collective-permute-done.3 = bf16[2,16,2048]{2,1,0:T(8,128)(2,1)S(1)} collective-permute-done((bf16[2,16,2048]{2,1,0:T(8,128)(2,1)S(1)}, bf16[2,16,2048]{2,1,0:T(8,128)(2,1)S(1)}, u32[]{:S(2)}, u32[]{:S(2)}) %collective-permute-start.3) | collective-permute-done | bytes 131104 | tf_op jit(solution)/shard_map/hidden_spread/ppermute | solution.py:91
  27.3 3.3 %collective-permute-start.4 = (bf16[2,16,2048]{2,1,0:T(8,128)(2,1)S(1)}, bf16[2,16,2048]{2,1,0:T(8,128)(2,1)S(1)}, u32[]{:S(2)}, u32[]{:S(2)}) collective-permute-start(bf16[2,16,2048]{2,1,0:T(8,128)(2,1)S(1)} %get-tuple-element.21), channel_id=1, source_target_pairs={{0,16},{8,24},{16,0},{24,8},{1,17},{9,25},{17,1},{25,9},{2,18},{10... | collective-permute-start | bytes 393224 | tf_op jit(solution)/shard_map/hidden_spread/ppermute | solution.py:91
  30.6 4.4 %collective-permute-done.4 = bf16[2,16,2048]{2,1,0:T(8,128)(2,1)S(1)} collective-permute-done((bf16[2,16,2048]{2,1,0:T(8,128)(2,1)S(1)}, bf16[2,16,2048]{2,1,0:T(8,128)(2,1)S(1)}, u32[]{:S(2)}, u32[]{:S(2)}) %collective-permute-start.4) | collective-permute-done | bytes 131104 | tf_op jit(solution)/shard_map/hidden_spread/ppermute | solution.py:91
  35.0 0.1 slice_bitcast_fusion.15
  35.1 1.6 collective-permute-start.5
  36.7 0.1 reshape.529
  36.8 1.5 collective-permute-start.8
  38.3 3.3 %collective-permute-done.5 = bf16[64,1024]{1,0:T(8,128)(2,1)S(1)} collective-permute-done((bf16[64,1024]{1,0:T(8,128)(2,1)S(1)}, bf16[64,1024]{1,0:T(8,128)(2,1)S(1)}, u32[]{:S(2)}, u32[]{:S(2)}) %collective-permute-start.5) | collective-permute-done | bytes 131104 | tf_op jit(solution)/shard_map/hidden_spread/hidden_gather_stage/ppermute | solution.py:46
  41.6 1.5 collective-permute-done.8
  43.2 0.6 collective-permute-start.9
  43.8 1.6 collective-permute-start.6
  45.5 4.2 %collective-permute-done.9 = bf16[2,64,1024]{2,1,0:T(8,128)(2,1)S(1)} collective-permute-done((bf16[2,64,1024]{2,1,0:T(8,128)(2,1)S(1)}, bf16[2,64,1024]{2,1,0:T(8,128)(2,1)S(1)}, u32[]{:S(2)}, u32[]{:S(2)}) %collective-permute-start.9) | collective-permute-done | bytes 262176 | tf_op jit(solution)/shard_map/hidden_spread/hidden_gather_stage/ppermute | solution.py:46
  49.8 0.5 collective-permute-done.6
  50.3 0.1 collective-permute-start.7
  50.4 0.1 pad_maximum_fusion
  50.5 0.1 maximum_select_fusion.3
  50.6 1.0 collective-permute-done.10
  51.7 0.2 maximum_select_fusion.1
  51.9 0.5 collective-permute-done.7
  52.4 0.2 maximum_select_fusion
  52.7 0.2 maximum_bitcast_fusion
  52.9 0.2 copy.60
  53.1 0.9 slice-done.1
  54.1 0.4 slice-done.2
  54.5 7.4 %fusion.25 = f32[4,128,19,128]{3,1,2,0:T(8,128)} fusion(bf16[4,128,2048,1]{2,1,3,0:T(8,128)(2,1)S(1)} %bitcast.176, bf16[19,128,2048,1]{2,1,0,3:T(8,128)(2,1)S(1)} %bitcast.217), kind=kOutput, calls=%fused_computation.100 | convolution fusion | flops 5100273664 | bytes 17039360 | tf_op jit(solution)/shard_map/dense_logits/bd,vd->bv/dot_general | solution.py:124
  61.8 5.2 %gather_fusion = f32[64,128,128]{2,1,0:T(8,128)} fusion(f32[4,128,19,128]{3,1,2,0:T(8,128)} %fusion.25, s32[64]{0:T(128)S(1)} %reshape.529), kind=kCustom, calls=%fused_computation | custom fusion | bytes 8389120 | tf_op jit(solution)/shard_map/dense_logits/gather | solution.py:129
  67.2 0.6 constant_dynamic-slice_fusion.7
  67.8 0.6 iota_compare_fusion.1
  68.4 76.7 %reduce-scatter.2.cloned.1.call-done = f32[1,16,128,128]{3,2,1,0:T(8,128)} async-done(((f32[4,16,128,128]{3,2,1,0:T(8,128)}), f32[1,16,128,128]{3,2,1,0:T(8,128)}) %reduce-scatter.2.cloned.1.call-update) | async-done | bytes 1048592 | tf_op jit(solution)/shard_map/reduce_scatter | solution.py:131
  145.1 1.5 select_reduce_fusion
  146.6 1.6 exponential_reduce_fusion
  148.2 9.1 %all-gather = f32[16,1,128]{2,1,0:T(1,128)S(1)} all-gather(f32[2,1,128]{2,1,0:T(1,128)S(1)} %pad_maximum_fusion.4), channel_id=2, replica_groups=mesh['dp'=4,'vocab'=8] {'vocab'}, dimensions={0}, use_global_device_ids=true | all-gather | bytes 9216 | tf_op jit(solution)/shard_map/softmax_stats/all_gather | solution.py:139
  157.3 1.6 select_convert_fusion
  158.9 45.4 %all-gather.3.cloned.1.call-done = bf16[4,16,128,128]{3,2,1,0:T(8,128)(2,1)} async-done(((bf16[1,16,128,128]{3,2,1,0:T(8,128)(2,1)}), bf16[4,16,128,128]{3,2,1,0:T(8,128)(2,1)}) %all-gather.3.cloned.1.call-update) | async-done | bytes 2097168 | tf_op jit(solution)/shard_map/all_gather | solution.py:146
  204.4 1.7 constant_dynamic-slice_fusion.1
  206.1 0.9 fusion.2
  207.1 5.8 %convolution_bitcast_fusion = f32[4,64,2048]{2,1,0:T(8,128)S(1)} fusion(bf16[19,128,2048,1]{2,1,0,3:T(8,128)(2,1)} %bitcast.214, bf16[4,64,19,128]{3,2,1,0:T(8,128)(2,1)S(1)} %fusion.2), kind=kOutput, calls=%fused_computation.1 | convolution fusion | flops 2550136832 | bytes 13303808 | tf_op jit(solution)/shard_map/dense_expected/brkt,ktd->brd/dot_general | solution.py:163
  213.0 0.9 fusion.1
  213.9 3.2 %collective-permute-done.11 = f32[4,64,2048]{2,1,0:T(8,128)S(1)} collective-permute-done((f32[4,64,2048]{2,1,0:T(8,128)S(1)}, f32[4,64,2048]{2,1,0:T(8,128)S(1)}, u32[]{:S(2)}, u32[]{:S(2)}) %collective-permute-start.11) | collective-permute-done | bytes 2097184 | tf_op jit(solution)/shard_map/summed_core_stage/ppermute | solution.py:27
  217.1 3.0 %fusion = f32[4,64,2048]{2,1,0:T(8,128)S(1)} fusion(f32[4,64,2048]{2,1,0:T(8,128)S(1)} %collective-permute-done.11, bf16[19,128,2048,1]{2,1,0,3:T(8,128)(2,1)S(1)} %bitcast.220, bf16[4,64,19,128]{3,2,1,0:T(8,128)(2,1)S(1)} %fusion.1), kind=kOutput, calls=%fused_computation.3 | convolution fusion | flops 2550661120 | bytes 15400960 | tf_op jit(solution)/shard_map/dense_expected/brkt,ktd->brd/dot_general | solution.py:163
  220.1 0.1 fusion.23
  220.3 1.5 collective-permute-start.14
  221.9 1.5 collective-permute-start.12
  223.4 10.9 %collective-permute-done.14 = f32[2,64,1024]{2,1,0:T(8,128)S(1)} collective-permute-done((f32[2,64,1024]{2,1,0:T(8,128)S(1)}, f32[2,64,1024]{2,1,0:T(8,128)S(1)}, u32[]{:S(2)}, u32[]{:S(2)}) %collective-permute-start.14) | collective-permute-done | bytes 524320 | tf_op jit(solution)/shard_map/summed_chip_stage/ppermute | solution.py:18
  234.4 1.5 collective-permute-start.15
  236.1 1.5 collective-permute-start.13
  237.6 4.4 %collective-permute-done.15 = f32[64,1024]{1,0:T(8,128)S(1)} collective-permute-done((f32[64,1024]{1,0:T(8,128)S(1)}, f32[64,1024]{1,0:T(8,128)S(1)}, u32[]{:S(2)}, u32[]{:S(2)}) %collective-permute-start.15) | collective-permute-done | bytes 262176 | tf_op jit(solution)/shard_map/summed_chip_stage/ppermute | solution.py:18
  242.0 1.3 collective-permute-done.13
  243.4 0.1 multiply_reduce_fusion
  243.5 0.2 collective-permute-start.16
  243.8 3.4 %collective-permute-done.16 = f32[64]{0:T(128)S(1)} collective-permute-done((f32[64]{0:T(128)S(1)}, f32[64]{0:T(128)S(1)}, u32[]{:S(2)}, u32[]{:S(2)}) %collective-permute-start.16) | collective-permute-done | bytes 288 | tf_op jit(solution)/shard_map/ppermute | solution.py:73
  247.2 1.2 collective-permute-start.17
  248.4 3.2 %collective-permute-done.17 = f32[64]{0:T(128)S(1)} collective-permute-done((f32[64]{0:T(128)S(1)}, f32[64]{0:T(128)S(1)}, u32[]{:S(2)}, u32[]{:S(2)}) %collective-permute-start.17) | collective-permute-done | bytes 288 | tf_op jit(solution)/shard_map/ppermute | solution.py:73
  251.6 0.9 fusion.5
  (71 shorter events, 1.5 us)
Async XLA Ops:
  7.2 60.0 %copy-start = (s32[1,4]{1,0:T(1,128)S(1)}, s32[1,4]{1,0:T(1,128)}, u32[]{:S(2)}) copy-start(s32[1,4]{1,0:T(1,128)} %param.7) | copy-start | bytes 52
  7.2 137.9 %reduce-scatter.2.cloned.1.call-start = ((), (), s32[]{:S(2)}) async-start(), calls=%async_computation.1 | async-start | bytes 5242880 | tf_op jit(solution)/shard_map/reduce_scatter | solution.py:131
  8.3 1.5 collective-permute-start
  9.9 6.7 %collective-permute-start.1 = (bf16[2,2,16,1024]{3,2,1,0:T(8,128)(2,1)S(1)}, bf16[2,2,16,1024]{3,2,1,0:T(8,128)(2,1)S(1)}, u32[]{:S(2)}, u32[]{:S(2)}) collective-permute-start(bf16[2,2,16,1024]{3,2,1,0:T(8,128)(2,1)S(1)} %get-tuple-element.27), channel_id=1, source_target_pairs={{0,2},{1,3},{2,0},{3,1},{4,6},{5,7},{6,4},{7,5},{8,10},{9,11},{10,... | collective-permute-start | bytes 393224 | tf_op jit(solution)/shard_map/hidden_spread/ppermute | solution.py:91
  16.6 5.0 %collective-permute-start.2 = (bf16[2,2,16,1024]{3,2,1,0:T(8,128)(2,1)S(1)}, bf16[2,2,16,1024]{3,2,1,0:T(8,128)(2,1)S(1)}, u32[]{:S(2)}, u32[]{:S(2)}) collective-permute-start(bf16[2,2,16,1024]{3,2,1,0:T(8,128)(2,1)S(1)} %get-tuple-element.25), channel_id=1, source_target_pairs={{0,4},{1,5},{2,6},{3,7},{4,0},{5,1},{6,2},{7,3},{8,12},{9,13},{10,... | collective-permute-start | bytes 393224 | tf_op jit(solution)/shard_map/hidden_spread/ppermute | solution.py:91
  22.2 14.5 %copy-start.2 = (s32[1,4,16]{2,1,0:T(4,128)S(1)}, s32[1,4,16]{2,1,0:T(4,128)}, u32[]{:S(2)}) copy-start(s32[1,4,16]{2,1,0:T(4,128)} %param.6) | copy-start | bytes 772
  22.2 5.0 %collective-permute-start.3 = (bf16[2,16,2048]{2,1,0:T(8,128)(2,1)S(1)}, bf16[2,16,2048]{2,1,0:T(8,128)(2,1)S(1)}, u32[]{:S(2)}, u32[]{:S(2)}) collective-permute-start(bf16[2,16,2048]{2,1,0:T(8,128)(2,1)S(1)} %get-tuple-element.23), channel_id=1, source_target_pairs={{0,8},{8,0},{16,24},{24,16},{1,9},{9,1},{17,25},{25,17},{2,10},{10... | collective-permute-start | bytes 393224 | tf_op jit(solution)/shard_map/hidden_spread/ppermute | solution.py:91
  27.3 7.6 %collective-permute-start.4 = (bf16[2,16,2048]{2,1,0:T(8,128)(2,1)S(1)}, bf16[2,16,2048]{2,1,0:T(8,128)(2,1)S(1)}, u32[]{:S(2)}, u32[]{:S(2)}) collective-permute-start(bf16[2,16,2048]{2,1,0:T(8,128)(2,1)S(1)} %get-tuple-element.21), channel_id=1, source_target_pairs={{0,16},{8,24},{16,0},{24,8},{1,17},{9,25},{17,1},{25,9},{2,18},{10... | collective-permute-start | bytes 393224 | tf_op jit(solution)/shard_map/hidden_spread/ppermute | solution.py:91
  35.1 6.4 %collective-permute-start.5 = (bf16[64,1024]{1,0:T(8,128)(2,1)S(1)}, bf16[64,1024]{1,0:T(8,128)(2,1)S(1)}, u32[]{:S(2)}, u32[]{:S(2)}) collective-permute-start(bf16[64,1024]{1,0:T(8,128)(2,1)S(1)} %get-tuple-element.15), channel_id=1, source_target_pairs={{0,2},{1,3},{2,0},{3,1},{4,6},{5,7},{6,4},{7,5},{8,10},{9,11},{10,... | collective-permute-start | bytes 393224 | tf_op jit(solution)/shard_map/hidden_spread/hidden_gather_stage/ppermute | solution.py:46
  36.8 6.4 %collective-permute-start.8 = (bf16[64,1024]{1,0:T(8,128)(2,1)S(1)}, bf16[64,1024]{1,0:T(8,128)(2,1)S(1)}, u32[]{:S(2)}, u32[]{:S(2)}) collective-permute-start(bf16[64,1024]{1,0:T(8,128)(2,1)S(1)} %get-tuple-element.14), channel_id=1, source_target_pairs={{0,4},{1,5},{2,6},{3,7},{4,0},{5,1},{6,2},{7,3},{8,12},{9,13},{10,... | collective-permute-start | bytes 393224 | tf_op jit(solution)/shard_map/hidden_spread/hidden_gather_stage/ppermute | solution.py:46
  43.2 6.4 %collective-permute-start.9 = (bf16[2,64,1024]{2,1,0:T(8,128)(2,1)S(1)}, bf16[2,64,1024]{2,1,0:T(8,128)(2,1)S(1)}, u32[]{:S(2)}, u32[]{:S(2)}) collective-permute-start(bf16[2,64,1024]{2,1,0:T(8,128)(2,1)S(1)} %maximum_select_fusion.12), channel_id=1, source_target_pairs={{0,2},{1,3},{2,0},{3,1},{4,6},{5,7},{6,4},{7,5},{8,10},{9,11},{10,... | collective-permute-start | bytes 786440 | tf_op jit(solution)/shard_map/hidden_spread/hidden_gather_stage/ppermute | solution.py:46
  43.8 6.4 %collective-permute-start.6 = (bf16[2,64,1024]{2,1,0:T(8,128)(2,1)S(1)}, bf16[2,64,1024]{2,1,0:T(8,128)(2,1)S(1)}, u32[]{:S(2)}, u32[]{:S(2)}) collective-permute-start(bf16[2,64,1024]{2,1,0:T(8,128)(2,1)S(1)} %maximum_select_fusion.10), channel_id=1, source_target_pairs={{0,4},{1,5},{2,6},{3,7},{4,0},{5,1},{6,2},{7,3},{8,12},{9,13},{10,... | collective-permute-start | bytes 786440 | tf_op jit(solution)/shard_map/hidden_spread/hidden_gather_stage/ppermute | solution.py:46
  49.7 2.0 collective-permute-start.10
  50.2 2.9 %slice-start = ((s8[9961472]{0:T(1024)(128)(4,1)}), s8[4194304]{0:T(1024)(128)(4,1)S(1)}, s32[]{:S(2)}) async-start(s8[9961472]{0:T(1024)(128)(4,1)} %bitcast.215), calls=%async_computation.3 | async-start | bytes 8388608
  50.3 2.1 collective-permute-start.7
  51.7 2.4 slice-start.1
  52.7 1.8 slice-start.2
  67.1 137.3 %all-gather.3.cloned.1.call-start = ((), (), s32[]{:S(2)}) async-start(), calls=%async_computation.2 | async-start | bytes 2621440 | tf_op jit(solution)/shard_map/all_gather | solution.py:146
  145.1 12.2 %copy-start.1 = (f32[1,16,128,128]{3,2,1,0:T(8,128)S(1)}, f32[1,16,128,128]{3,2,1,0:T(8,128)}, u32[]{:S(2)}) copy-start(f32[1,16,128,128]{3,2,1,0:T(8,128)} %reduce-scatter.2.cloned.1.call-done) | copy-start | bytes 3145732
  206.1 11.0 %slice-start.3 = ((s8[9961472]{0:T(1024)(128)(4,1)}), s8[4194304]{0:T(1024)(128)(4,1)S(1)}, s32[]{:S(2)}) async-start(s8[9961472]{0:T(1024)(128)(4,1)} %bitcast.218), calls=%async_computation.6 | async-start | bytes 8388608
  207.0 10.1 %slice-start.4 = ((s8[9961472]{0:T(1024)(128)(4,1)}), s8[4194304]{0:T(1024)(128)(4,1)S(1)}, s32[]{:S(2)}) async-start(s8[9961472]{0:T(1024)(128)(4,1)} %bitcast.218), calls=%async_computation.7 | async-start | bytes 8388608
  207.1 10.1 %slice-start.5 = ((s8[9961472]{0:T(1024)(128)(4,1)}), s8[1572864]{0:T(1024)(128)(4,1)S(1)}, s32[]{:S(2)}) async-start(s8[9961472]{0:T(1024)(128)(4,1)} %bitcast.218), calls=%async_computation.8 | async-start | bytes 3145728
  212.9 4.2 %collective-permute-start.11 = (f32[4,64,2048]{2,1,0:T(8,128)S(1)}, f32[4,64,2048]{2,1,0:T(8,128)S(1)}, u32[]{:S(2)}, u32[]{:S(2)}) collective-permute-start(f32[4,64,2048]{2,1,0:T(8,128)S(1)} %convolution_bitcast_fusion), channel_id=1, source_target_pairs={{0,1},{1,0},{2,3},{3,2},{4,5},{5,4},{6,7},{7,6},{8,9},{9,8},{10,11... | collective-permute-start | bytes 6291464 | tf_op jit(solution)/shard_map/summed_core_stage/ppermute | solution.py:27
  220.3 14.0 %collective-permute-start.14 = (f32[2,64,1024]{2,1,0:T(8,128)S(1)}, f32[2,64,1024]{2,1,0:T(8,128)S(1)}, u32[]{:S(2)}, u32[]{:S(2)}) collective-permute-start(f32[2,64,1024]{2,1,0:T(8,128)S(1)} %dynamic-slice_bitcast_fusion), channel_id=1, source_target_pairs={{0,4},{1,5},{2,6},{3,7},{4,0},{5,1},{6,2},{7,3},{8,12},{9,13},{10,... | collective-permute-start | bytes 1572872 | tf_op jit(solution)/shard_map/summed_chip_stage/ppermute | solution.py:18
  221.9 14.1 %collective-permute-start.12 = (f32[2,64,1024]{2,1,0:T(8,128)S(1)}, f32[2,64,1024]{2,1,0:T(8,128)S(1)}, u32[]{:S(2)}, u32[]{:S(2)}) collective-permute-start(f32[2,64,1024]{2,1,0:T(8,128)S(1)} %dynamic-slice_bitcast_fusion.1), channel_id=1, source_target_pairs={{0,2},{1,3},{2,0},{3,1},{4,6},{5,7},{6,4},{7,5},{8,10},{9,11},{10,... | collective-permute-start | bytes 1572872 | tf_op jit(solution)/shard_map/summed_chip_stage/ppermute | solution.py:18
  234.4 7.5 %collective-permute-start.15 = (f32[64,1024]{1,0:T(8,128)S(1)}, f32[64,1024]{1,0:T(8,128)S(1)}, u32[]{:S(2)}, u32[]{:S(2)}) collective-permute-start(f32[64,1024]{1,0:T(8,128)S(1)} %dynamic-slice_bitcast_fusion.2), channel_id=1, source_target_pairs={{0,2},{1,3},{2,0},{3,1},{4,6},{5,7},{6,4},{7,5},{8,10},{9,11},{10,... | collective-permute-start | bytes 786440 | tf_op jit(solution)/shard_map/summed_chip_stage/ppermute | solution.py:18
  236.1 7.3 %collective-permute-start.13 = (f32[64,1024]{1,0:T(8,128)S(1)}, f32[64,1024]{1,0:T(8,128)S(1)}, u32[]{:S(2)}, u32[]{:S(2)}) collective-permute-start(f32[64,1024]{1,0:T(8,128)S(1)} %dynamic-slice_bitcast_fusion.3), channel_id=1, source_target_pairs={{0,4},{1,5},{2,6},{3,7},{4,0},{5,1},{6,2},{7,3},{8,12},{9,13},{10,... | collective-permute-start | bytes 786440 | tf_op jit(solution)/shard_map/summed_chip_stage/ppermute | solution.py:18
  243.5 3.6 %collective-permute-start.16 = (f32[64]{0:T(128)S(1)}, f32[64]{0:T(128)S(1)}, u32[]{:S(2)}, u32[]{:S(2)}) collective-permute-start(f32[64]{0:T(128)S(1)} %multiply_reduce_fusion), channel_id=1, source_target_pairs={{0,8},{8,0},{16,24},{24,16},{1,9},{9,1},{17,25},{25,17},{2,10},{10... | collective-permute-start | bytes 776 | tf_op jit(solution)/shard_map/ppermute | solution.py:73
  247.2 4.5 %collective-permute-start.17 = (f32[64]{0:T(128)S(1)}, f32[64]{0:T(128)S(1)}, u32[]{:S(2)}, u32[]{:S(2)}) collective-permute-start(f32[64]{0:T(128)S(1)} %add.156), channel_id=1, source_target_pairs={{0,16},{8,24},{16,0},{24,8},{1,17},{9,25},{17,1},{25,9},{2,18},{10... | collective-permute-start | bytes 776 | tf_op jit(solution)/shard_map/ppermute | solution.py:73
Sparse Core Ops, SparseCore 0:
  67.2 77.8 reduce-scatter.1
  159.1 45.2 all-gather.2

commit v12 on v11

--- a/solution.py
+++ b/solution.py
@@ -96,6 +96,31 @@
     return jnp.concatenate([by_source[k] for k in range(n)], axis=concat_axis)
 
 
+def direct_spread(hidden, n_vocab, n_dp):
+    rows, chunk = hidden.shape
+    per_slice = n_vocab // n_dp
+    group = rows // n_vocab
+    me_v = lax.axis_index("vocab")
+    me_d = lax.axis_index("dp")
+    pieces = hidden.reshape(n_vocab, group, chunk)
+    got = []
+    for shift in range(n_vocab):
+        target = (me_v % per_slice + per_slice * me_d + shift) % n_vocab
+        send = lax.dynamic_index_in_dim(pieces, target, axis=0, keepdims=False)
+        perm = []
+        for d in range(n_dp):
+            for v in range(n_vocab):
+                k = (v % per_slice + per_slice * d + shift) % n_vocab
+                perm.append((d * n_vocab + v, (v // per_slice) * n_vocab + k))
+        got.append(lax.ppermute(send, ("dp", "vocab"), perm=perm))
+    received = jnp.stack(got)
+    slot = jnp.arange(n_vocab, dtype=jnp.int32)
+    order = (me_v - slot) % n_vocab
+    placed = jnp.take(received, order, axis=0)
+    placed = placed.reshape(n_dp, per_slice, group, chunk).transpose(0, 2, 1, 3)
+    return placed.reshape(n_dp * group, per_slice * chunk)
+
+
 def per_device(hidden, out_weight, token_blocks, counts):
     vocab_here, columns_here = out_weight.shape
     n_vocab = lax.psum(1, "vocab")
@@ -110,8 +135,7 @@
     own_counts = lax.dynamic_slice_in_dim(block_counts, me_dp, 1, 0)
 
     with jax.named_scope("hidden_spread"):
-        row_slices = bruck_all_to_all(hidden, "vocab", n_vocab, split_axis=0, concat_axis=1)
-        plane_rows = bruck_all_to_all(row_slices, "dp", n_dp, split_axis=1, concat_axis=0)
+        plane_rows = direct_spread(hidden, n_vocab, n_dp)
         gathered = doubling_all_gather(plane_rows, n_vocab)
         group = hidden.shape[0] // n_vocab
         beam_columns = (

time: 260 us -> 260 us (level)
  waiting for transfers between devices: 175 us -> 166 us
  starting transfers between devices: 23.7 us -> 28.4 us
  matrix products: 18 us -> 20.7 us
    ppermute x5 -> x8, waiting for transfers between devices: 15.5 us -> 6.39 us  [direct_spread(): got.append(lax.ppermute(send, ('dp', 'vocab'), perm=perm))]
    ppermute x5 -> x8, starting transfers between devices: 10.5 us -> 17.7 us  [direct_spread(): got.append(lax.ppermute(send, ('dp', 'vocab'), perm=perm))]
    dot_general x2, matrix products: 8.79 us -> 11.5 us  [expected_half(): jnp.einsum('brkt,ktd->brd', spread, out_weight.reshape(n_tb, TB, columns_...]
  transfers between devices with their start and end apart: 20 -> 23, of which waited for: 19 -> 17; matrix products, arithmetic and copies ran while one was open for 1% -> 2% of each run, Pallas kernels for 0% -> 0%
where the time goes in v12:
time: 260 us
  waiting for transfers between devices  166 us (64%)
  starting transfers between devices  28.4 us (11%)
  matrix products  20.7 us (8%)
  between operations  14.6 us (6%)
  local copies, waits for them, and re-layouts  13.2 us (5%)
  blocking collectives  9.08 us (3%)
  other arithmetic  7.82 us (3%)
    reduce_scatter x1, waiting for transfers between devices, per_device(): logits = lax.psum_scatter(picked, 'dp', scatter_dimension=0, tiled=True)  75.5 us
    all_gather x1, waiting for transfers between devices, per_device(): prob_part = lax.all_gather(probabilities, 'dp', axis=0, tiled=True)  45.4 us
    ppermute x8, starting transfers between devices, direct_spread(): got.append(lax.ppermute(send, ('dp', 'vocab'), perm=perm))  17.7 us
    ppermute x4, waiting for transfers between devices, exchange_stage(): got = lax.ppermute(send, 'vocab', perm=perm)  16.8 us
    ppermute x6, waiting for transfers between devices, gather_stage(): got = lax.ppermute(x, 'vocab', perm=perm)  12.2 us
    dot_general x2, matrix products, expected_half(): jnp.einsum('brkt,ktd->brd', spread, out_weight.reshape(n_tb, TB, columns_...  11.5 us
    all_gather x1, blocking collectives, per_device(): stats = lax.all_gather(jnp.stack([local_max, local_total]), 'vocab', axis=0)  9.08 us
    dot_general x1, matrix products, per_device(): jnp.einsum('bd,vd->bv', beam_columns, out_weight, preferred_element_type=...  7.35 us
  transfers between devices with their start and end apart: 23, of which 17 were waited for; matrix products, arithmetic and copies ran while one was open for 2% of the time, Pallas kernels for 0%

profile of v12, /device:TPU:0, one launch (start us, length us, event | category | flops | bytes accessed | tf_op | source)
XLA Modules:
  0.0 260.1 jit_solution(13994286810952327155)
XLA Ops:
  7.4 0.9 dynamic-slice_bitcast_fusion.4
  8.3 0.7 collective-permute-start
  8.9 0.5 collective-permute-start.1
  9.5 5.8 %collective-permute-start.2 = (bf16[16,1024]{1,0:T(8,128)(2,1)S(1)}, bf16[16,1024]{1,0:T(8,128)(2,1)S(1)}, u32[]{:S(2)}, u32[]{:S(2)}) collective-permute-start(bf16[16,1024]{1,0:T(8,128)(2,1)S(1)} %get-tuple-element.21), channel_id=1, source_target_pairs={{0,2},{1,3},{2,10},{3,11},{4,18},{5,19},{6,26},{7,27},{8,4},{9,5},... | collective-permute-start | bytes 98312 | tf_op jit(solution)/shard_map/hidden_spread/ppermute | solution.py:115
  15.3 2.9 %collective-permute-start.3 = (bf16[16,1024]{1,0:T(8,128)(2,1)S(1)}, bf16[16,1024]{1,0:T(8,128)(2,1)S(1)}, u32[]{:S(2)}, u32[]{:S(2)}) collective-permute-start(bf16[16,1024]{1,0:T(8,128)(2,1)S(1)} %get-tuple-element.20), channel_id=1, source_target_pairs={{0,3},{1,4},{2,11},{3,12},{4,19},{5,20},{6,27},{7,28},{8,5},{9,6},... | collective-permute-start | bytes 98312 | tf_op jit(solution)/shard_map/hidden_spread/ppermute | solution.py:115
  18.2 3.3 %collective-permute-start.4 = (bf16[16,1024]{1,0:T(8,128)(2,1)S(1)}, bf16[16,1024]{1,0:T(8,128)(2,1)S(1)}, u32[]{:S(2)}, u32[]{:S(2)}) collective-permute-start(bf16[16,1024]{1,0:T(8,128)(2,1)S(1)} %get-tuple-element.19), channel_id=1, source_target_pairs={{0,4},{1,5},{2,12},{3,13},{4,20},{5,21},{6,28},{7,29},{8,6},{9,7},... | collective-permute-start | bytes 98312 | tf_op jit(solution)/shard_map/hidden_spread/ppermute | solution.py:115
  21.6 1.3 collective-permute-start.5
  23.0 1.9 collective-permute-start.6
  24.9 1.2 collective-permute-start.7
  26.1 5.7 %collective-permute-done.5 = bf16[16,1024]{1,0:T(8,128)(2,1)S(1)} collective-permute-done((bf16[16,1024]{1,0:T(8,128)(2,1)S(1)}, bf16[16,1024]{1,0:T(8,128)(2,1)S(1)}, u32[]{:S(2)}, u32[]{:S(2)}) %collective-permute-start.5) | collective-permute-done | bytes 32800 | tf_op jit(solution)/shard_map/hidden_spread/ppermute | solution.py:115
  31.8 0.7 collective-permute-done.6
  32.5 0.6 gather_fusion
  33.1 0.1 select_bitcast_fusion.1
  33.2 0.3 copy.31
  33.5 0.1 slice_bitcast_fusion.3
  33.6 2.2 collective-permute-start.8
  35.9 0.1 reshape.581
  36.0 3.6 %collective-permute-done.8 = bf16[64,1024]{1,0:T(8,128)(2,1)S(1)} collective-permute-done((bf16[64,1024]{1,0:T(8,128)(2,1)S(1)}, bf16[64,1024]{1,0:T(8,128)(2,1)S(1)}, u32[]{:S(2)}, u32[]{:S(2)}) %collective-permute-start.8) | collective-permute-done | bytes 131104 | tf_op jit(solution)/shard_map/hidden_spread/hidden_gather_stage/ppermute | solution.py:46
  39.8 1.1 collective-permute-done.11
  41.0 0.6 collective-permute-start.12
  41.6 5.8 %collective-permute-done.9 = bf16[2,64,1024]{2,1,0:T(8,128)(2,1)S(1)} collective-permute-done((bf16[2,64,1024]{2,1,0:T(8,128)(2,1)S(1)}, bf16[2,64,1024]{2,1,0:T(8,128)(2,1)S(1)}, u32[]{:S(2)}, u32[]{:S(2)}) %collective-permute-start.9) | collective-permute-done | bytes 262176 | tf_op jit(solution)/shard_map/hidden_spread/hidden_gather_stage/ppermute | solution.py:46
  47.7 0.5 collective-permute-start.13
  48.2 0.1 pad_maximum_fusion
  48.5 1.0 collective-permute-done.10
  49.5 0.2 maximum_select_fusion
  49.7 0.5 collective-permute-done.13
  50.2 0.2 maximum_select_fusion.1
  50.5 0.2 maximum_bitcast_fusion
  50.7 0.2 copy.38
  50.9 0.8 slice-done.1
  51.7 0.5 slice-done.2
  52.3 7.4 %fusion.20 = f32[4,128,19,128]{3,1,2,0:T(8,128)} fusion(bf16[4,128,2048,1]{2,1,3,0:T(8,128)(2,1)S(1)} %bitcast.154, bf16[19,128,2048,1]{2,1,0,3:T(8,128)(2,1)S(1)} %bitcast.183), kind=kOutput, calls=%fused_computation.95 | convolution fusion | flops 5100273664 | bytes 17039360 | tf_op jit(solution)/shard_map/dense_logits/bd,vd->bv/dot_general | solution.py:148
  59.6 5.2 %gather_fusion.1 = f32[64,128,128]{2,1,0:T(8,128)} fusion(f32[4,128,19,128]{3,1,2,0:T(8,128)} %fusion.20, s32[64]{0:T(128)S(1)} %reshape.581), kind=kCustom, calls=%fused_computation.1 | custom fusion | bytes 8389120 | tf_op jit(solution)/shard_map/dense_logits/gather | solution.py:153
  65.0 0.6 constant_dynamic-slice_fusion.2
  65.6 0.6 iota_compare_fusion.1
  66.2 75.5 %reduce-scatter.2.cloned.1.call-done = f32[1,16,128,128]{3,2,1,0:T(8,128)} async-done(((f32[4,16,128,128]{3,2,1,0:T(8,128)}), f32[1,16,128,128]{3,2,1,0:T(8,128)}) %reduce-scatter.2.cloned.1.call-update) | async-done | bytes 1048592 | tf_op jit(solution)/shard_map/reduce_scatter | solution.py:155
  141.7 1.5 select_reduce_fusion
  143.2 1.6 exponential_reduce_fusion
  144.8 9.1 %all-gather = f32[16,1,128]{2,1,0:T(1,128)S(1)} all-gather(f32[2,1,128]{2,1,0:T(1,128)S(1)} %pad_maximum_fusion.3), channel_id=2, replica_groups=mesh['dp'=4,'vocab'=8] {'vocab'}, dimensions={0}, use_global_device_ids=true | all-gather | bytes 9216 | tf_op jit(solution)/shard_map/softmax_stats/all_gather | solution.py:163
  153.9 1.6 select_convert_fusion
  155.6 45.4 %all-gather.3.cloned.1.call-done = bf16[4,16,128,128]{3,2,1,0:T(8,128)(2,1)} async-done(((bf16[1,16,128,128]{3,2,1,0:T(8,128)(2,1)}), bf16[4,16,128,128]{3,2,1,0:T(8,128)(2,1)}) %all-gather.3.cloned.1.call-update) | async-done | bytes 2097168 | tf_op jit(solution)/shard_map/all_gather | solution.py:170
  201.0 1.7 constant_dynamic-slice_fusion.1
  202.7 0.9 fusion.2
  203.6 5.5 %convolution_bitcast_fusion = f32[4,64,2048]{2,1,0:T(8,128)S(1)} fusion(bf16[19,128,2048,1]{2,1,0,3:T(8,128)(2,1)} %bitcast.179, bf16[4,64,19,128]{3,2,1,0:T(8,128)(2,1)S(1)} %fusion.2), kind=kOutput, calls=%fused_computation.2 | convolution fusion | flops 2550136832 | bytes 13303808 | tf_op jit(solution)/shard_map/dense_expected/brkt,ktd->brd/dot_general | solution.py:187
  209.2 0.9 fusion.1
  210.2 3.3 %collective-permute-done.14 = f32[4,64,2048]{2,1,0:T(8,128)} collective-permute-done((f32[4,64,2048]{2,1,0:T(8,128)S(1)}, f32[4,64,2048]{2,1,0:T(8,128)}, u32[]{:S(2)}, u32[]{:S(2)}) %collective-permute-start.14) | collective-permute-done | bytes 2097184 | tf_op jit(solution)/shard_map/summed_core_stage/ppermute | solution.py:27
  213.5 6.0 %fusion = f32[4,64,2048]{2,1,0:T(8,128)S(1)} fusion(f32[4,64,2048]{2,1,0:T(8,128)} %collective-permute-done.14, bf16[19,128,2048,1]{2,1,0,3:T(8,128)(2,1)} %bitcast.180, bf16[4,64,19,128]{3,2,1,0:T(8,128)(2,1)S(1)} %fusion.1), kind=kOutput, calls=%fused_computation.4 | convolution fusion | flops 2550661120 | bytes 15400960 | tf_op jit(solution)/shard_map/dense_expected/brkt,ktd->brd/dot_general | solution.py:187
  219.5 0.1 fusion.18
  219.6 0.8 dynamic-slice_bitcast_fusion.1
  220.5 1.5 collective-permute-start.15
  222.0 0.8 dynamic-slice_bitcast_fusion
  222.8 1.5 collective-permute-start.17
  224.3 10.4 %collective-permute-done.15 = f32[2,64,1024]{2,1,0:T(8,128)S(1)} collective-permute-done((f32[2,64,1024]{2,1,0:T(8,128)}, f32[2,64,1024]{2,1,0:T(8,128)S(1)}, u32[]{:S(2)}, u32[]{:S(2)}) %collective-permute-start.15) | collective-permute-done | bytes 524320 | tf_op jit(solution)/shard_map/summed_chip_stage/ppermute | solution.py:18
  234.8 1.5 collective-permute-start.16
  236.3 0.4 collective-permute-done.17
  236.8 1.2 collective-permute-start.18
  238.0 4.4 %collective-permute-done.16 = f32[64,1024]{1,0:T(8,128)S(1)} collective-permute-done((f32[64,1024]{1,0:T(8,128)S(1)}, f32[64,1024]{1,0:T(8,128)S(1)}, u32[]{:S(2)}, u32[]{:S(2)}) %collective-permute-start.16) | collective-permute-done | bytes 262176 | tf_op jit(solution)/shard_map/summed_chip_stage/ppermute | solution.py:18
  242.4 1.7 collective-permute-done.18
  244.1 0.1 multiply_reduce_fusion
  244.2 0.2 collective-permute-start.19
  244.5 3.4 %collective-permute-done.19 = f32[64]{0:T(128)S(1)} collective-permute-done((f32[64]{0:T(128)S(1)}, f32[64]{0:T(128)S(1)}, u32[]{:S(2)}, u32[]{:S(2)}) %collective-permute-start.19) | collective-permute-done | bytes 288 | tf_op jit(solution)/shard_map/ppermute | solution.py:73
  247.9 1.2 collective-permute-start.20
  249.1 3.2 %collective-permute-done.20 = f32[64]{0:T(128)S(1)} collective-permute-done((f32[64]{0:T(128)S(1)}, f32[64]{0:T(128)S(1)}, u32[]{:S(2)}, u32[]{:S(2)}) %collective-permute-start.20) | collective-permute-done | bytes 288 | tf_op jit(solution)/shard_map/ppermute | solution.py:73
  252.3 0.9 fusion.5
  (64 shorter events, 1.5 us)
Async XLA Ops:
  7.2 57.8 %copy-start = (s32[1,4]{1,0:T(1,128)S(1)}, s32[1,4]{1,0:T(1,128)}, u32[]{:S(2)}) copy-start(s32[1,4]{1,0:T(1,128)} %param.7) | copy-start | bytes 52
  7.2 134.5 %reduce-scatter.2.cloned.1.call-start = ((), (), s32[]{:S(2)}) async-start(), calls=%async_computation.1 | async-start | bytes 5242880 | tf_op jit(solution)/shard_map/reduce_scatter | solution.py:155
  7.3 28.5 %copy-start.2 = (s32[1,4,16]{2,1,0:T(4,128)S(1)}, s32[1,4,16]{2,1,0:T(4,128)}, u32[]{:S(2)}) copy-start(s32[1,4,16]{2,1,0:T(4,128)} %param.6) | copy-start | bytes 772
  8.3 13.3 %collective-permute-start = (bf16[16,1024]{1,0:T(8,128)(2,1)S(1)}, bf16[16,1024]{1,0:T(8,128)(2,1)S(1)}, u32[]{:S(2)}, u32[]{:S(2)}) collective-permute-start(bf16[16,1024]{1,0:T(8,128)(2,1)S(1)} %get-tuple-element.23), channel_id=1, source_target_pairs={{0,0},{1,1},{2,8},{3,9},{4,16},{5,17},{6,24},{7,25},{8,2},{9,3},{1... | collective-permute-start | bytes 98312 | tf_op jit(solution)/shard_map/hidden_spread/ppermute | solution.py:115
  8.9 14.0 %collective-permute-start.1 = (bf16[16,1024]{1,0:T(8,128)(2,1)S(1)}, bf16[16,1024]{1,0:T(8,128)(2,1)S(1)}, u32[]{:S(2)}, u32[]{:S(2)}) collective-permute-start(bf16[16,1024]{1,0:T(8,128)(2,1)S(1)} %get-tuple-element.22), channel_id=1, source_target_pairs={{0,1},{1,2},{2,9},{3,10},{4,17},{5,18},{6,25},{7,26},{8,3},{9,4},{... | collective-permute-start | bytes 98312 | tf_op jit(solution)/shard_map/hidden_spread/ppermute | solution.py:115
  9.5 15.4 %collective-permute-start.2 = (bf16[16,1024]{1,0:T(8,128)(2,1)S(1)}, bf16[16,1024]{1,0:T(8,128)(2,1)S(1)}, u32[]{:S(2)}, u32[]{:S(2)}) collective-permute-start(bf16[16,1024]{1,0:T(8,128)(2,1)S(1)} %get-tuple-element.21), channel_id=1, source_target_pairs={{0,2},{1,3},{2,10},{3,11},{4,18},{5,19},{6,26},{7,27},{8,4},{9,5},... | collective-permute-start | bytes 98312 | tf_op jit(solution)/shard_map/hidden_spread/ppermute | solution.py:115
  15.3 10.8 %collective-permute-start.3 = (bf16[16,1024]{1,0:T(8,128)(2,1)S(1)}, bf16[16,1024]{1,0:T(8,128)(2,1)S(1)}, u32[]{:S(2)}, u32[]{:S(2)}) collective-permute-start(bf16[16,1024]{1,0:T(8,128)(2,1)S(1)} %get-tuple-element.20), channel_id=1, source_target_pairs={{0,3},{1,4},{2,11},{3,12},{4,19},{5,20},{6,27},{7,28},{8,5},{9,6},... | collective-permute-start | bytes 98312 | tf_op jit(solution)/shard_map/hidden_spread/ppermute | solution.py:115
  18.2 8.0 %collective-permute-start.4 = (bf16[16,1024]{1,0:T(8,128)(2,1)S(1)}, bf16[16,1024]{1,0:T(8,128)(2,1)S(1)}, u32[]{:S(2)}, u32[]{:S(2)}) collective-permute-start(bf16[16,1024]{1,0:T(8,128)(2,1)S(1)} %get-tuple-element.19), channel_id=1, source_target_pairs={{0,4},{1,5},{2,12},{3,13},{4,20},{5,21},{6,28},{7,29},{8,6},{9,7},... | collective-permute-start | bytes 98312 | tf_op jit(solution)/shard_map/hidden_spread/ppermute | solution.py:115
  21.6 10.2 %collective-permute-start.5 = (bf16[16,1024]{1,0:T(8,128)(2,1)S(1)}, bf16[16,1024]{1,0:T(8,128)(2,1)S(1)}, u32[]{:S(2)}, u32[]{:S(2)}) collective-permute-start(bf16[16,1024]{1,0:T(8,128)(2,1)S(1)} %get-tuple-element.18), channel_id=1, source_target_pairs={{0,5},{1,6},{2,13},{3,14},{4,21},{5,22},{6,29},{7,30},{8,7},{9,0},... | collective-permute-start | bytes 98312 | tf_op jit(solution)/shard_map/hidden_spread/ppermute | solution.py:115
  23.0 9.6 %collective-permute-start.6 = (bf16[16,1024]{1,0:T(8,128)(2,1)S(1)}, bf16[16,1024]{1,0:T(8,128)(2,1)S(1)}, u32[]{:S(2)}, u32[]{:S(2)}) collective-permute-start(bf16[16,1024]{1,0:T(8,128)(2,1)S(1)} %get-tuple-element.17), channel_id=1, source_target_pairs={{0,6},{1,7},{2,14},{3,15},{4,22},{5,23},{6,30},{7,31},{8,0},{9,1},... | collective-permute-start | bytes 98312 | tf_op jit(solution)/shard_map/hidden_spread/ppermute | solution.py:115
  24.9 7.6 %collective-permute-start.7 = (bf16[16,1024]{1,0:T(8,128)(2,1)S(1)}, bf16[16,1024]{1,0:T(8,128)(2,1)S(1)}, u32[]{:S(2)}, u32[]{:S(2)}) collective-permute-start(bf16[16,1024]{1,0:T(8,128)(2,1)S(1)} %get-tuple-element.16), channel_id=1, source_target_pairs={{0,7},{1,0},{2,15},{3,8},{4,23},{5,16},{6,31},{7,24},{8,1},{9,2},{... | collective-permute-start | bytes 98312 | tf_op jit(solution)/shard_map/hidden_spread/ppermute | solution.py:115
  33.6 6.0 %collective-permute-start.8 = (bf16[64,1024]{1,0:T(8,128)(2,1)S(1)}, bf16[64,1024]{1,0:T(8,128)(2,1)S(1)}, u32[]{:S(2)}, u32[]{:S(2)}) collective-permute-start(bf16[64,1024]{1,0:T(8,128)(2,1)S(1)} %get-tuple-element.15), channel_id=1, source_target_pairs={{0,2},{1,3},{2,0},{3,1},{4,6},{5,7},{6,4},{7,5},{8,10},{9,11},{10,... | collective-permute-start | bytes 393224 | tf_op jit(solution)/shard_map/hidden_spread/hidden_gather_stage/ppermute | solution.py:46
  36.0 5.0 %collective-permute-start.11 = (bf16[64,1024]{1,0:T(8,128)(2,1)S(1)}, bf16[64,1024]{1,0:T(8,128)(2,1)S(1)}, u32[]{:S(2)}, u32[]{:S(2)}) collective-permute-start(bf16[64,1024]{1,0:T(8,128)(2,1)S(1)} %get-tuple-element.14), channel_id=1, source_target_pairs={{0,4},{1,5},{2,6},{3,7},{4,0},{5,1},{6,2},{7,3},{8,12},{9,13},{10,... | collective-permute-start | bytes 393224 | tf_op jit(solution)/shard_map/hidden_spread/hidden_gather_stage/ppermute | solution.py:46
  39.6 7.8 %collective-permute-start.9 = (bf16[2,64,1024]{2,1,0:T(8,128)(2,1)S(1)}, bf16[2,64,1024]{2,1,0:T(8,128)(2,1)S(1)}, u32[]{:S(2)}, u32[]{:S(2)}) collective-permute-start(bf16[2,64,1024]{2,1,0:T(8,128)(2,1)S(1)} %maximum_select_fusion.5), channel_id=1, source_target_pairs={{0,4},{1,5},{2,6},{3,7},{4,0},{5,1},{6,2},{7,3},{8,12},{9,13},{10,... | collective-permute-start | bytes 786440 | tf_op jit(solution)/shard_map/hidden_spread/hidden_gather_stage/ppermute | solution.py:46
  41.0 6.7 %collective-permute-start.12 = (bf16[2,64,1024]{2,1,0:T(8,128)(2,1)S(1)}, bf16[2,64,1024]{2,1,0:T(8,128)(2,1)S(1)}, u32[]{:S(2)}, u32[]{:S(2)}) collective-permute-start(bf16[2,64,1024]{2,1,0:T(8,128)(2,1)S(1)} %maximum_select_fusion.7), channel_id=1, source_target_pairs={{0,2},{1,3},{2,0},{3,1},{4,6},{5,7},{6,4},{7,5},{8,10},{9,11},{10,... | collective-permute-start | bytes 786440 | tf_op jit(solution)/shard_map/hidden_spread/hidden_gather_stage/ppermute | solution.py:46
  47.5 2.0 collective-permute-start.10
  47.6 3.3 %slice-start = ((s8[9961472]{0:T(1024)(128)(4,1)}), s8[4194304]{0:T(1024)(128)(4,1)S(1)}, s32[]{:S(2)}) async-start(s8[9961472]{0:T(1024)(128)(4,1)} %bitcast.181), calls=%async_computation.3 | async-start | bytes 8388608
  47.7 2.5 collective-permute-start.13
  49.5 2.3 slice-start.1
  50.5 1.8 slice-start.2
  64.9 136.1 %all-gather.3.cloned.1.call-start = ((), (), s32[]{:S(2)}) async-start(), calls=%async_computation.2 | async-start | bytes 2621440 | tf_op jit(solution)/shard_map/all_gather | solution.py:170
  141.7 12.2 %copy-start.1 = (f32[1,16,128,128]{3,2,1,0:T(8,128)S(1)}, f32[1,16,128,128]{3,2,1,0:T(8,128)}, u32[]{:S(2)}) copy-start(f32[1,16,128,128]{3,2,1,0:T(8,128)} %reduce-scatter.2.cloned.1.call-done) | copy-start | bytes 3145732
  209.1 4.4 %collective-permute-start.14 = (f32[4,64,2048]{2,1,0:T(8,128)S(1)}, f32[4,64,2048]{2,1,0:T(8,128)}, u32[]{:S(2)}, u32[]{:S(2)}) collective-permute-start(f32[4,64,2048]{2,1,0:T(8,128)S(1)} %convolution_bitcast_fusion), channel_id=1, source_target_pairs={{0,1},{1,0},{2,3},{3,2},{4,5},{5,4},{6,7},{7,6},{8,9},{9,8},{10,11... | collective-permute-start | bytes 6291464 | tf_op jit(solution)/shard_map/summed_core_stage/ppermute | solution.py:27
  220.5 14.2 %collective-permute-start.15 = (f32[2,64,1024]{2,1,0:T(8,128)}, f32[2,64,1024]{2,1,0:T(8,128)S(1)}, u32[]{:S(2)}, u32[]{:S(2)}) collective-permute-start(f32[2,64,1024]{2,1,0:T(8,128)} %dynamic-slice_bitcast_fusion.1), channel_id=1, source_target_pairs={{0,2},{1,3},{2,0},{3,1},{4,6},{5,7},{6,4},{7,5},{8,10},{9,11},{10,... | collective-permute-start | bytes 1572872 | tf_op jit(solution)/shard_map/summed_chip_stage/ppermute | solution.py:18
  222.8 13.9 %collective-permute-start.17 = (f32[2,64,1024]{2,1,0:T(8,128)}, f32[2,64,1024]{2,1,0:T(8,128)S(1)}, u32[]{:S(2)}, u32[]{:S(2)}) collective-permute-start(f32[2,64,1024]{2,1,0:T(8,128)} %dynamic-slice_bitcast_fusion), channel_id=1, source_target_pairs={{0,4},{1,5},{2,6},{3,7},{4,0},{5,1},{6,2},{7,3},{8,12},{9,13},{10,... | collective-permute-start | bytes 1572872 | tf_op jit(solution)/shard_map/summed_chip_stage/ppermute | solution.py:18
  234.8 7.6 %collective-permute-start.16 = (f32[64,1024]{1,0:T(8,128)S(1)}, f32[64,1024]{1,0:T(8,128)S(1)}, u32[]{:S(2)}, u32[]{:S(2)}) collective-permute-start(f32[64,1024]{1,0:T(8,128)S(1)} %dynamic-slice_bitcast_fusion.3), channel_id=1, source_target_pairs={{0,4},{1,5},{2,6},{3,7},{4,0},{5,1},{6,2},{7,3},{8,12},{9,13},{10,... | collective-permute-start | bytes 786440 | tf_op jit(solution)/shard_map/summed_chip_stage/ppermute | solution.py:18
  236.8 7.3 %collective-permute-start.18 = (f32[64,1024]{1,0:T(8,128)S(1)}, f32[64,1024]{1,0:T(8,128)S(1)}, u32[]{:S(2)}, u32[]{:S(2)}) collective-permute-start(f32[64,1024]{1,0:T(8,128)S(1)} %dynamic-slice_bitcast_fusion.2), channel_id=1, source_target_pairs={{0,2},{1,3},{2,0},{3,1},{4,6},{5,7},{6,4},{7,5},{8,10},{9,11},{10,... | collective-permute-start | bytes 786440 | tf_op jit(solution)/shard_map/summed_chip_stage/ppermute | solution.py:18
  244.2 3.6 %collective-permute-start.19 = (f32[64]{0:T(128)S(1)}, f32[64]{0:T(128)S(1)}, u32[]{:S(2)}, u32[]{:S(2)}) collective-permute-start(f32[64]{0:T(128)S(1)} %multiply_reduce_fusion), channel_id=1, source_target_pairs={{0,8},{8,0},{16,24},{24,16},{1,9},{9,1},{17,25},{25,17},{2,10},{10... | collective-permute-start | bytes 776 | tf_op jit(solution)/shard_map/ppermute | solution.py:73
  247.9 4.5 %collective-permute-start.20 = (f32[64]{0:T(128)S(1)}, f32[64]{0:T(128)S(1)}, u32[]{:S(2)}, u32[]{:S(2)}) collective-permute-start(f32[64]{0:T(128)S(1)} %add.264), channel_id=1, source_target_pairs={{0,16},{8,24},{16,0},{24,8},{1,17},{9,25},{17,1},{25,9},{2,18},{10... | collective-permute-start | bytes 776 | tf_op jit(solution)/shard_map/ppermute | solution.py:73
Sparse Core Ops, SparseCore 0:
  65.0 76.6 reduce-scatter.1
  155.7 45.2 all-gather.2

commit v13 on v12

--- a/solution.py
+++ b/solution.py
@@ -121,6 +121,48 @@
     return placed.reshape(n_dp * group, per_slice * chunk)
 
 
+def line_reduce_scatter(partials, n):
+    me = lax.axis_index("dp")
+    own = lambda block: lax.dynamic_index_in_dim(
+        partials, jnp.clip(block, 0, n - 1), axis=0, keepdims=False
+    )
+    from_left = None
+    from_right = None
+    for step in range(1, n):
+        send_up = own(me + n - step)
+        send_down = own(me - n + step)
+        if from_left is not None:
+            send_up = send_up + from_left
+            send_down = send_down + from_right
+        send_up, send_down = lax.optimization_barrier((send_up, send_down))
+        upward = [(s, s + 1) for s in range(0, step)]
+        downward = [(s, s - 1) for s in range(n - step, n)]
+        from_left = lax.ppermute(send_up, "dp", perm=upward)
+        from_right = lax.ppermute(send_down, "dp", perm=downward)
+    return (own(me) + from_left + from_right)[None]
+
+
+def line_all_gather(own_part, n):
+    me = lax.axis_index("dp")
+    got = [own_part]
+    from_left, from_right = own_part, own_part
+    for step in range(1, n):
+        upward = [(s, s + 1) for s in range(step - 1, n - 1)]
+        downward = [(s, s - 1) for s in range(1, n - step + 1)]
+        from_left, from_right = lax.optimization_barrier((from_left, from_right))
+        from_left = lax.ppermute(from_left, "dp", perm=upward)
+        from_right = lax.ppermute(from_right, "dp", perm=downward)
+        got += [from_left, from_right]
+    blocks = []
+    for block in range(n):
+        pick = jnp.where(me == block, got[0], jnp.zeros_like(got[0]))
+        for step in range(1, n):
+            pick = jnp.where(me - step == block, got[2 * step - 1], pick)
+            pick = jnp.where(me + step == block, got[2 * step], pick)
+        blocks.append(pick)
+    return jnp.stack(blocks)
+
+
 def per_device(hidden, out_weight, token_blocks, counts):
     vocab_here, columns_here = out_weight.shape
     n_vocab = lax.psum(1, "vocab")
@@ -152,7 +194,8 @@
         rows = jnp.arange(n_blk, dtype=jnp.int32)[:, None]
         picked = full4[rows, :, block_lists, :]
 
-    logits = lax.psum_scatter(picked, "dp", scatter_dimension=0, tiled=True)
+    with jax.named_scope("logits_line_reduce"):
+        logits = line_reduce_scatter(picked, n_dp)
 
     with jax.named_scope("softmax_stats"):
         live = jnp.arange(MOST, dtype=jnp.int32)[None, :] < own_counts[:, None]

time: 260 us -> 272 us (1.046)
  starting transfers between devices: 28.4 us -> 46.3 us
  waiting for transfers between devices: 166 us -> 153 us
  other arithmetic: 7.82 us -> 12.7 us
    reduce_scatter x1 -> x0, waiting for transfers between devices: 75.5 us -> none  [per_device(): logits = lax.psum_scatter(picked, 'dp', scatter_dimension=0, tiled=True)]
    ppermute x0 -> x6, waiting for transfers between devices: none -> 64.9 us  [the longest x3 61 us: line_reduce_scatter(): from_left = lax.ppermute(send_up, 'dp', perm=upward)]
    ppermute x0 -> x6, starting transfers between devices: none -> 17.9 us  [the longest x3 14.3 us: line_reduce_scatter(): from_left = lax.ppermute(send_up, 'dp', perm=upward)]
    add x0 -> x2, other arithmetic: none -> 5.97 us  [line_reduce_scatter(): send_down = send_down + from_right]
  transfers between devices with their start and end apart: 23 -> 28, of which waited for: 17 -> 20; matrix products, arithmetic and copies ran while one was open for 2% -> 2% of each run, Pallas kernels for 0% -> 0%
where the time goes in v13:
time: 272 us
  waiting for transfers between devices  153 us (56%)
  starting transfers between devices  46.3 us (17%)
  matrix products  20.7 us (8%)
  local copies, waits for them, and re-layouts  14.9 us (5%)
  between operations  14.7 us (5%)
  other arithmetic  12.7 us (5%)
  blocking collectives  9.32 us (3%)
    ppermute x3, waiting for transfers between devices, line_reduce_scatter(): from_left = lax.ppermute(send_up, 'dp', perm=upward)  61 us
    all_gather x1, waiting for transfers between devices, per_device(): prob_part = lax.all_gather(probabilities, 'dp', axis=0, tiled=True)  43 us
    ppermute x8, starting transfers between devices, direct_spread(): got.append(lax.ppermute(send, ('dp', 'vocab'), perm=perm))  17.7 us
    ppermute x4, waiting for transfers between devices, exchange_stage(): got = lax.ppermute(send, 'vocab', perm=perm)  16.8 us
    ppermute x3, starting transfers between devices, line_reduce_scatter(): from_left = lax.ppermute(send_up, 'dp', perm=upward)  14.3 us
    ppermute x6, waiting for transfers between devices, gather_stage(): got = lax.ppermute(x, 'vocab', perm=perm)  12.2 us
    dot_general x2, matrix products, expected_half(): jnp.einsum('brkt,ktd->brd', spread, out_weight.reshape(n_tb, TB, columns_...  11.5 us
    all_gather x1, blocking collectives, per_device(): stats = lax.all_gather(jnp.stack([local_max, local_total]), 'vocab', axis=0)  9.32 us
  transfers between devices with their start and end apart: 28, of which 20 were waited for; matrix products, arithmetic and copies ran while one was open for 2% of the time, Pallas kernels for 0%

profile of v13, /device:TPU:0, one launch (start us, length us, event | category | flops | bytes accessed | tf_op | source)
XLA Modules:
  0.0 271.8 jit_solution(8528666415881251157)
XLA Ops:
  7.4 0.9 dynamic-slice_bitcast_fusion.6
  8.3 0.7 collective-permute-start
  8.9 0.5 collective-permute-start.1
  9.5 5.8 %collective-permute-start.2 = (bf16[16,1024]{1,0:T(8,128)(2,1)S(1)}, bf16[16,1024]{1,0:T(8,128)(2,1)S(1)}, u32[]{:S(2)}, u32[]{:S(2)}) collective-permute-start(bf16[16,1024]{1,0:T(8,128)(2,1)S(1)} %get-tuple-element.41), channel_id=1, source_target_pairs={{0,2},{1,3},{2,10},{3,11},{4,18},{5,19},{6,26},{7,27},{8,4},{9,5},... | collective-permute-start | bytes 98312 | tf_op jit(solution)/shard_map/hidden_spread/ppermute | solution.py:115
  15.3 2.9 %collective-permute-start.3 = (bf16[16,1024]{1,0:T(8,128)(2,1)S(1)}, bf16[16,1024]{1,0:T(8,128)(2,1)S(1)}, u32[]{:S(2)}, u32[]{:S(2)}) collective-permute-start(bf16[16,1024]{1,0:T(8,128)(2,1)S(1)} %get-tuple-element.40), channel_id=1, source_target_pairs={{0,3},{1,4},{2,11},{3,12},{4,19},{5,20},{6,27},{7,28},{8,5},{9,6},... | collective-permute-start | bytes 98312 | tf_op jit(solution)/shard_map/hidden_spread/ppermute | solution.py:115
  18.2 3.3 %collective-permute-start.4 = (bf16[16,1024]{1,0:T(8,128)(2,1)S(1)}, bf16[16,1024]{1,0:T(8,128)(2,1)S(1)}, u32[]{:S(2)}, u32[]{:S(2)}) collective-permute-start(bf16[16,1024]{1,0:T(8,128)(2,1)S(1)} %get-tuple-element.39), channel_id=1, source_target_pairs={{0,4},{1,5},{2,12},{3,13},{4,20},{5,21},{6,28},{7,29},{8,6},{9,7},... | collective-permute-start | bytes 98312 | tf_op jit(solution)/shard_map/hidden_spread/ppermute | solution.py:115
  21.6 1.3 collective-permute-start.5
  23.0 1.9 collective-permute-start.6
  24.9 1.2 collective-permute-start.7
  26.1 5.7 %collective-permute-done.5 = bf16[16,1024]{1,0:T(8,128)(2,1)S(1)} collective-permute-done((bf16[16,1024]{1,0:T(8,128)(2,1)S(1)}, bf16[16,1024]{1,0:T(8,128)(2,1)S(1)}, u32[]{:S(2)}, u32[]{:S(2)}) %collective-permute-start.5) | collective-permute-done | bytes 32800 | tf_op jit(solution)/shard_map/hidden_spread/ppermute | solution.py:115
  31.8 0.7 collective-permute-done.6
  32.5 0.6 gather_fusion
  33.6 2.2 collective-permute-start.8
  36.0 3.6 %collective-permute-done.8 = bf16[64,1024]{1,0:T(8,128)(2,1)S(1)} collective-permute-done((bf16[64,1024]{1,0:T(8,128)(2,1)S(1)}, bf16[64,1024]{1,0:T(8,128)(2,1)S(1)}, u32[]{:S(2)}, u32[]{:S(2)}) %collective-permute-start.8) | collective-permute-done | bytes 131104 | tf_op jit(solution)/shard_map/hidden_spread/hidden_gather_stage/ppermute | solution.py:46
  39.8 1.1 collective-permute-done.11
  41.0 0.6 collective-permute-start.12
  41.6 5.8 %collective-permute-done.9 = bf16[2,64,1024]{2,1,0:T(8,128)(2,1)S(1)} collective-permute-done((bf16[2,64,1024]{2,1,0:T(8,128)(2,1)S(1)}, bf16[2,64,1024]{2,1,0:T(8,128)(2,1)S(1)}, u32[]{:S(2)}, u32[]{:S(2)}) %collective-permute-start.9) | collective-permute-done | bytes 262176 | tf_op jit(solution)/shard_map/hidden_spread/hidden_gather_stage/ppermute | solution.py:46
  47.7 0.5 collective-permute-start.13
  48.5 1.0 collective-permute-done.10
  49.7 0.5 collective-permute-done.13
  50.9 0.8 slice-done.1
  51.7 0.5 slice-done.2
  52.3 7.4 %fusion.22 = f32[4,128,19,128]{3,1,2,0:T(8,128)} fusion(bf16[4,128,2048,1]{2,1,3,0:T(8,128)(2,1)S(1)} %bitcast.174, bf16[19,128,2048,1]{2,1,0,3:T(8,128)(2,1)S(1)} %bitcast.203), kind=kOutput, calls=%fused_computation.103 | convolution fusion | flops 5100273664 | bytes 17039360 | tf_op jit(solution)/shard_map/dense_logits/bd,vd->bv/dot_general | solution.py:190
  59.7 5.2 %gather_fusion.1 = f32[64,128,128]{2,1,0:T(8,128)} fusion(f32[4,128,19,128]{3,1,2,0:T(8,128)} %fusion.22, s32[64]{0:T(128)S(1)} %reshape.591), kind=kCustom, calls=%fused_computation.1 | custom fusion | bytes 8389120 | tf_op jit(solution)/shard_map/dense_logits/gather | solution.py:195
  64.9 1.7 dynamic-slice_bitcast_fusion
  66.6 1.6 collective-permute-start.14
  68.2 1.7 collective-permute-start.15
  69.8 21.0 %collective-permute-done.14 = f32[16,128,128]{2,1,0:T(8,128)S(1)} collective-permute-done((f32[16,128,128]{2,1,0:T(8,128)S(1)}, f32[16,128,128]{2,1,0:T(8,128)S(1)}, u32[]{:S(2)}, u32[]{:S(2)}) %collective-permute-start.14) | collective-permute-done | bytes 1048608 | tf_op jit(solution)/shard_map/logits_line_reduce/ppermute | solution.py:140
  90.8 3.2 %bitcast_add_fusion.1 = (f32[16,128,128]{2,1,0:T(8,128)S(1)}, f32[16,128,128]{2,1,0:T(8,128)}) fusion(f32[16,128,128]{2,1,0:T(8,128)} %collective-permute-done.15, f32[4,16,128,128]{3,2,1,0:T(8,128)} %bitcast.167, s32[]{:T(128)S(6)} %min.27, f32[16,128,128]{2,1,0:T(8,128)S(1)} %collective-permute-done.14, s32[]{:T(128)S(6)} %min.24), kind=kLoop, calls=%fused_computation.17 | loop fusion | flops 524288 | bytes 6291464 | tf_op jit(solution)/shard_map/logits_line_reduce/add | solution.py:136
  94.0 4.4 %collective-permute-start.16 = (f32[16,128,128]{2,1,0:T(8,128)}, f32[16,128,128]{2,1,0:T(8,128)S(1)}, u32[]{:S(2)}, u32[]{:S(2)}) collective-permute-start(f32[16,128,128]{2,1,0:T(8,128)} %get-tuple-element.10), channel_id=1, source_target_pairs={{0,8},{8,16},{1,9},{9,17},{2,10},{10,18},{3,11},{11,19},{4,12},{12... | collective-permute-start | bytes 3145736 | tf_op jit(solution)/shard_map/logits_line_reduce/ppermute | solution.py:140
  98.5 0.7 collective-permute-start.17
  99.2 21.4 %collective-permute-done.16 = f32[16,128,128]{2,1,0:T(8,128)S(1)} collective-permute-done((f32[16,128,128]{2,1,0:T(8,128)}, f32[16,128,128]{2,1,0:T(8,128)S(1)}, u32[]{:S(2)}, u32[]{:S(2)}) %collective-permute-start.16) | collective-permute-done | bytes 1048608 | tf_op jit(solution)/shard_map/logits_line_reduce/ppermute | solution.py:140
  120.6 2.8 %bitcast_add_fusion = (f32[16,128,128]{2,1,0:T(8,128)S(1)}, f32[16,128,128]{2,1,0:T(8,128)}) fusion(f32[16,128,128]{2,1,0:T(8,128)S(1)} %collective-permute-done.17, f32[4,16,128,128]{3,2,1,0:T(8,128)} %bitcast.168, s32[]{:T(128)S(6)} %min.28, f32[16,128,128]{2,1,0:T(8,128)S(1)} %collective-permute-done.16, s32[]{:T(128)S(6)} %min.23), kind=kLoop, calls=%fused_computation.16 | loop fusion | flops 524288 | bytes 6291464 | tf_op jit(solution)/shard_map/logits_line_reduce/add | solution.py:136
  123.4 8.3 %collective-permute-start.18 = (f32[16,128,128]{2,1,0:T(8,128)}, f32[16,128,128]{2,1,0:T(8,128)S(1)}, u32[]{:S(2)}, u32[]{:S(2)}) collective-permute-start(f32[16,128,128]{2,1,0:T(8,128)} %get-tuple-element.12), channel_id=1, source_target_pairs={{0,8},{8,16},{16,24},{1,9},{9,17},{17,25},{2,10},{10,18},{18,26},{... | collective-permute-start | bytes 3145736 | tf_op jit(solution)/shard_map/logits_line_reduce/ppermute | solution.py:140
  131.7 1.3 collective-permute-start.19
  133.0 0.6 constant_dynamic-slice_fusion.2
  133.6 0.6 iota_compare_fusion.1
  134.2 18.6 %collective-permute-done.18 = f32[16,128,128]{2,1,0:T(8,128)S(1)} collective-permute-done((f32[16,128,128]{2,1,0:T(8,128)}, f32[16,128,128]{2,1,0:T(8,128)S(1)}, u32[]{:S(2)}, u32[]{:S(2)}) %collective-permute-start.18) | collective-permute-done | bytes 1048608 | tf_op jit(solution)/shard_map/logits_line_reduce/ppermute | solution.py:140
  152.8 3.9 %collective-permute-done.19 = f32[16,128,128]{2,1,0:T(8,128)S(1)} collective-permute-done((f32[16,128,128]{2,1,0:T(8,128)S(1)}, f32[16,128,128]{2,1,0:T(8,128)S(1)}, u32[]{:S(2)}, u32[]{:S(2)}) %collective-permute-start.19) | collective-permute-done | bytes 1048608 | tf_op jit(solution)/shard_map/logits_line_reduce/ppermute | solution.py:141
  156.7 1.6 select_reduce_fusion
  158.3 0.3 exponential_reduce_fusion
  158.6 9.3 %all-gather = f32[16,1,128]{2,1,0:T(1,128)S(1)} all-gather(f32[2,1,128]{2,1,0:T(1,128)S(1)} %pad_maximum_fusion.3), channel_id=2, replica_groups=mesh['dp'=4,'vocab'=8] {'vocab'}, dimensions={0}, use_global_device_ids=true | all-gather | bytes 9216 | tf_op jit(solution)/shard_map/softmax_stats/all_gather | solution.py:206
  168.0 1.6 select_convert_fusion
  169.7 43.0 %all-gather.4.cloned.1.call-done = bf16[64,128,128]{2,1,0:T(8,128)(2,1)} async-done(((bf16[16,128,128]{2,1,0:T(8,128)(2,1)}), bf16[64,128,128]{2,1,0:T(8,128)(2,1)}) %all-gather.4.cloned.1.call-update) | async-done | bytes 2097168 | tf_op jit(solution)/shard_map/all_gather | solution.py:213
  212.7 1.7 constant_dynamic-slice_fusion.1
  214.4 0.9 fusion.2
  215.4 5.5 %convolution_bitcast_fusion = f32[4,64,2048]{2,1,0:T(8,128)S(1)} fusion(bf16[19,128,2048,1]{2,1,0,3:T(8,128)(2,1)} %bitcast.199, bf16[4,64,19,128]{3,2,1,0:T(8,128)(2,1)S(1)} %fusion.2), kind=kOutput, calls=%fused_computation.2 | convolution fusion | flops 2550136832 | bytes 13303808 | tf_op jit(solution)/shard_map/dense_expected/brkt,ktd->brd/dot_general | solution.py:230
  220.9 0.9 fusion.1
  221.9 3.3 %collective-permute-done.20 = f32[4,64,2048]{2,1,0:T(8,128)} collective-permute-done((f32[4,64,2048]{2,1,0:T(8,128)S(1)}, f32[4,64,2048]{2,1,0:T(8,128)}, u32[]{:S(2)}, u32[]{:S(2)}) %collective-permute-start.20) | collective-permute-done | bytes 2097184 | tf_op jit(solution)/shard_map/summed_core_stage/ppermute | solution.py:27
  225.2 6.0 %fusion = f32[4,64,2048]{2,1,0:T(8,128)S(1)} fusion(f32[4,64,2048]{2,1,0:T(8,128)} %collective-permute-done.20, bf16[19,128,2048,1]{2,1,0,3:T(8,128)(2,1)} %bitcast.200, bf16[4,64,19,128]{3,2,1,0:T(8,128)(2,1)S(1)} %fusion.1), kind=kOutput, calls=%fused_computation.4 | convolution fusion | flops 2550661120 | bytes 15400960 | tf_op jit(solution)/shard_map/dense_expected/brkt,ktd->brd/dot_general | solution.py:230
  231.3 0.8 dynamic-slice_bitcast_fusion.3
  232.2 1.5 collective-permute-start.21
  233.6 0.8 dynamic-slice_bitcast_fusion.2
  234.5 1.5 collective-permute-start.23
  236.0 10.4 %collective-permute-done.21 = f32[2,64,1024]{2,1,0:T(8,128)S(1)} collective-permute-done((f32[2,64,1024]{2,1,0:T(8,128)}, f32[2,64,1024]{2,1,0:T(8,128)S(1)}, u32[]{:S(2)}, u32[]{:S(2)}) %collective-permute-start.21) | collective-permute-done | bytes 524320 | tf_op jit(solution)/shard_map/summed_chip_stage/ppermute | solution.py:18
  246.5 1.5 collective-permute-start.22
  248.0 0.4 collective-permute-done.23
  248.5 1.2 collective-permute-start.24
  249.7 4.4 %collective-permute-done.22 = f32[64,1024]{1,0:T(8,128)S(1)} collective-permute-done((f32[64,1024]{1,0:T(8,128)S(1)}, f32[64,1024]{1,0:T(8,128)S(1)}, u32[]{:S(2)}, u32[]{:S(2)}) %collective-permute-start.22) | collective-permute-done | bytes 262176 | tf_op jit(solution)/shard_map/summed_chip_stage/ppermute | solution.py:18
  254.1 1.7 collective-permute-done.24
  256.2 3.4 %collective-permute-done.25 = f32[64]{0:T(128)S(1)} collective-permute-done((f32[64]{0:T(128)S(1)}, f32[64]{0:T(128)S(1)}, u32[]{:S(2)}, u32[]{:S(2)}) %collective-permute-start.25) | collective-permute-done | bytes 288 | tf_op jit(solution)/shard_map/ppermute | solution.py:73
  259.6 1.2 collective-permute-start.26
  260.8 3.2 %collective-permute-done.26 = f32[64]{0:T(128)S(1)} collective-permute-done((f32[64]{0:T(128)S(1)}, f32[64]{0:T(128)S(1)}, u32[]{:S(2)}, u32[]{:S(2)}) %collective-permute-start.26) | collective-permute-done | bytes 288 | tf_op jit(solution)/shard_map/ppermute | solution.py:73
  264.0 0.9 fusion.6
  (74 shorter events, 3.3 us)
Async XLA Ops:
  7.2 125.8 %copy-start = (s32[1,4]{1,0:T(1,128)S(1)}, s32[1,4]{1,0:T(1,128)}, u32[]{:S(2)}) copy-start(s32[1,4]{1,0:T(1,128)} %param.7) | copy-start | bytes 52
  7.2 205.5 %all-gather.4.cloned.1.call-start = ((), (), s32[]{:S(2)}) async-start(), calls=%async_computation | async-start | bytes 2621440 | tf_op jit(solution)/shard_map/all_gather | solution.py:213
  7.3 28.5 %copy-start.1 = (s32[1,4,16]{2,1,0:T(4,128)S(1)}, s32[1,4,16]{2,1,0:T(4,128)}, u32[]{:S(2)}) copy-start(s32[1,4,16]{2,1,0:T(4,128)} %param.6) | copy-start | bytes 772
  8.3 13.3 %collective-permute-start = (bf16[16,1024]{1,0:T(8,128)(2,1)S(1)}, bf16[16,1024]{1,0:T(8,128)(2,1)S(1)}, u32[]{:S(2)}, u32[]{:S(2)}) collective-permute-start(bf16[16,1024]{1,0:T(8,128)(2,1)S(1)} %get-tuple-element.43), channel_id=1, source_target_pairs={{0,0},{1,1},{2,8},{3,9},{4,16},{5,17},{6,24},{7,25},{8,2},{9,3},{1... | collective-permute-start | bytes 98312 | tf_op jit(solution)/shard_map/hidden_spread/ppermute | solution.py:115
  8.9 14.0 %collective-permute-start.1 = (bf16[16,1024]{1,0:T(8,128)(2,1)S(1)}, bf16[16,1024]{1,0:T(8,128)(2,1)S(1)}, u32[]{:S(2)}, u32[]{:S(2)}) collective-permute-start(bf16[16,1024]{1,0:T(8,128)(2,1)S(1)} %get-tuple-element.42), channel_id=1, source_target_pairs={{0,1},{1,2},{2,9},{3,10},{4,17},{5,18},{6,25},{7,26},{8,3},{9,4},{... | collective-permute-start | bytes 98312 | tf_op jit(solution)/shard_map/hidden_spread/ppermute | solution.py:115
  9.5 15.4 %collective-permute-start.2 = (bf16[16,1024]{1,0:T(8,128)(2,1)S(1)}, bf16[16,1024]{1,0:T(8,128)(2,1)S(1)}, u32[]{:S(2)}, u32[]{:S(2)}) collective-permute-start(bf16[16,1024]{1,0:T(8,128)(2,1)S(1)} %get-tuple-element.41), channel_id=1, source_target_pairs={{0,2},{1,3},{2,10},{3,11},{4,18},{5,19},{6,26},{7,27},{8,4},{9,5},... | collective-permute-start | bytes 98312 | tf_op jit(solution)/shard_map/hidden_spread/ppermute | solution.py:115
  15.3 10.8 %collective-permute-start.3 = (bf16[16,1024]{1,0:T(8,128)(2,1)S(1)}, bf16[16,1024]{1,0:T(8,128)(2,1)S(1)}, u32[]{:S(2)}, u32[]{:S(2)}) collective-permute-start(bf16[16,1024]{1,0:T(8,128)(2,1)S(1)} %get-tuple-element.40), channel_id=1, source_target_pairs={{0,3},{1,4},{2,11},{3,12},{4,19},{5,20},{6,27},{7,28},{8,5},{9,6},... | collective-permute-start | bytes 98312 | tf_op jit(solution)/shard_map/hidden_spread/ppermute | solution.py:115
  18.2 8.0 %collective-permute-start.4 = (bf16[16,1024]{1,0:T(8,128)(2,1)S(1)}, bf16[16,1024]{1,0:T(8,128)(2,1)S(1)}, u32[]{:S(2)}, u32[]{:S(2)}) collective-permute-start(bf16[16,1024]{1,0:T(8,128)(2,1)S(1)} %get-tuple-element.39), channel_id=1, source_target_pairs={{0,4},{1,5},{2,12},{3,13},{4,20},{5,21},{6,28},{7,29},{8,6},{9,7},... | collective-permute-start | bytes 98312 | tf_op jit(solution)/shard_map/hidden_spread/ppermute | solution.py:115
  21.6 10.2 %collective-permute-start.5 = (bf16[16,1024]{1,0:T(8,128)(2,1)S(1)}, bf16[16,1024]{1,0:T(8,128)(2,1)S(1)}, u32[]{:S(2)}, u32[]{:S(2)}) collective-permute-start(bf16[16,1024]{1,0:T(8,128)(2,1)S(1)} %get-tuple-element.38), channel_id=1, source_target_pairs={{0,5},{1,6},{2,13},{3,14},{4,21},{5,22},{6,29},{7,30},{8,7},{9,0},... | collective-permute-start | bytes 98312 | tf_op jit(solution)/shard_map/hidden_spread/ppermute | solution.py:115
  23.0 9.6 %collective-permute-start.6 = (bf16[16,1024]{1,0:T(8,128)(2,1)S(1)}, bf16[16,1024]{1,0:T(8,128)(2,1)S(1)}, u32[]{:S(2)}, u32[]{:S(2)}) collective-permute-start(bf16[16,1024]{1,0:T(8,128)(2,1)S(1)} %get-tuple-element.37), channel_id=1, source_target_pairs={{0,6},{1,7},{2,14},{3,15},{4,22},{5,23},{6,30},{7,31},{8,0},{9,1},... | collective-permute-start | bytes 98312 | tf_op jit(solution)/shard_map/hidden_spread/ppermute | solution.py:115
  24.9 7.6 %collective-permute-start.7 = (bf16[16,1024]{1,0:T(8,128)(2,1)S(1)}, bf16[16,1024]{1,0:T(8,128)(2,1)S(1)}, u32[]{:S(2)}, u32[]{:S(2)}) collective-permute-start(bf16[16,1024]{1,0:T(8,128)(2,1)S(1)} %get-tuple-element.36), channel_id=1, source_target_pairs={{0,7},{1,0},{2,15},{3,8},{4,23},{5,16},{6,31},{7,24},{8,1},{9,2},{... | collective-permute-start | bytes 98312 | tf_op jit(solution)/shard_map/hidden_spread/ppermute | solution.py:115
  33.6 6.0 %collective-permute-start.8 = (bf16[64,1024]{1,0:T(8,128)(2,1)S(1)}, bf16[64,1024]{1,0:T(8,128)(2,1)S(1)}, u32[]{:S(2)}, u32[]{:S(2)}) collective-permute-start(bf16[64,1024]{1,0:T(8,128)(2,1)S(1)} %get-tuple-element.35), channel_id=1, source_target_pairs={{0,2},{1,3},{2,0},{3,1},{4,6},{5,7},{6,4},{7,5},{8,10},{9,11},{10,... | collective-permute-start | bytes 393224 | tf_op jit(solution)/shard_map/hidden_spread/hidden_gather_stage/ppermute | solution.py:46
  36.0 5.0 %collective-permute-start.11 = (bf16[64,1024]{1,0:T(8,128)(2,1)S(1)}, bf16[64,1024]{1,0:T(8,128)(2,1)S(1)}, u32[]{:S(2)}, u32[]{:S(2)}) collective-permute-start(bf16[64,1024]{1,0:T(8,128)(2,1)S(1)} %get-tuple-element.34), channel_id=1, source_target_pairs={{0,4},{1,5},{2,6},{3,7},{4,0},{5,1},{6,2},{7,3},{8,12},{9,13},{10,... | collective-permute-start | bytes 393224 | tf_op jit(solution)/shard_map/hidden_spread/hidden_gather_stage/ppermute | solution.py:46
  39.6 7.8 %collective-permute-start.9 = (bf16[2,64,1024]{2,1,0:T(8,128)(2,1)S(1)}, bf16[2,64,1024]{2,1,0:T(8,128)(2,1)S(1)}, u32[]{:S(2)}, u32[]{:S(2)}) collective-permute-start(bf16[2,64,1024]{2,1,0:T(8,128)(2,1)S(1)} %maximum_select_fusion.5), channel_id=1, source_target_pairs={{0,4},{1,5},{2,6},{3,7},{4,0},{5,1},{6,2},{7,3},{8,12},{9,13},{10,... | collective-permute-start | bytes 786440 | tf_op jit(solution)/shard_map/hidden_spread/hidden_gather_stage/ppermute | solution.py:46
  41.0 6.7 %collective-permute-start.12 = (bf16[2,64,1024]{2,1,0:T(8,128)(2,1)S(1)}, bf16[2,64,1024]{2,1,0:T(8,128)(2,1)S(1)}, u32[]{:S(2)}, u32[]{:S(2)}) collective-permute-start(bf16[2,64,1024]{2,1,0:T(8,128)(2,1)S(1)} %maximum_select_fusion.7), channel_id=1, source_target_pairs={{0,2},{1,3},{2,0},{3,1},{4,6},{5,7},{6,4},{7,5},{8,10},{9,11},{10,... | collective-permute-start | bytes 786440 | tf_op jit(solution)/shard_map/hidden_spread/hidden_gather_stage/ppermute | solution.py:46
  47.5 2.0 collective-permute-start.10
  47.6 3.3 %slice-start = ((s8[9961472]{0:T(1024)(128)(4,1)}), s8[4194304]{0:T(1024)(128)(4,1)S(1)}, s32[]{:S(2)}) async-start(s8[9961472]{0:T(1024)(128)(4,1)} %bitcast.201), calls=%async_computation.1 | async-start | bytes 8388608
  47.7 2.5 collective-permute-start.13
  49.5 2.3 slice-start.1
  50.5 1.8 slice-start.2
  66.6 24.3 %collective-permute-start.14 = (f32[16,128,128]{2,1,0:T(8,128)S(1)}, f32[16,128,128]{2,1,0:T(8,128)S(1)}, u32[]{:S(2)}, u32[]{:S(2)}) collective-permute-start(f32[16,128,128]{2,1,0:T(8,128)S(1)} %get-tuple-element.8), channel_id=1, source_target_pairs={{0,8},{1,9},{2,10},{3,11},{4,12},{5,13},{6,14},{7,15}} | collective-permute-start | bytes 3145736 | tf_op jit(solution)/shard_map/logits_line_reduce/ppermute | solution.py:140
  68.2 22.7 %collective-permute-start.15 = (f32[16,128,128]{2,1,0:T(8,128)S(1)}, f32[16,128,128]{2,1,0:T(8,128)}, u32[]{:S(2)}, u32[]{:S(2)}) collective-permute-start(f32[16,128,128]{2,1,0:T(8,128)S(1)} %get-tuple-element.9), channel_id=1, source_target_pairs={{24,16},{25,17},{26,18},{27,19},{28,20},{29,21},{30,22},{31,23}} | collective-permute-start | bytes 3145736 | tf_op jit(solution)/shard_map/logits_line_reduce/ppermute | solution.py:141
  94.0 26.6 %collective-permute-start.16 = (f32[16,128,128]{2,1,0:T(8,128)}, f32[16,128,128]{2,1,0:T(8,128)S(1)}, u32[]{:S(2)}, u32[]{:S(2)}) collective-permute-start(f32[16,128,128]{2,1,0:T(8,128)} %get-tuple-element.10), channel_id=1, source_target_pairs={{0,8},{8,16},{1,9},{9,17},{2,10},{10,18},{3,11},{11,19},{4,12},{12... | collective-permute-start | bytes 3145736 | tf_op jit(solution)/shard_map/logits_line_reduce/ppermute | solution.py:140
  98.5 22.1 %collective-permute-start.17 = (f32[16,128,128]{2,1,0:T(8,128)S(1)}, f32[16,128,128]{2,1,0:T(8,128)S(1)}, u32[]{:S(2)}, u32[]{:S(2)}) collective-permute-start(f32[16,128,128]{2,1,0:T(8,128)S(1)} %get-tuple-element.11), channel_id=1, source_target_pairs={{16,8},{24,16},{17,9},{25,17},{18,10},{26,18},{19,11},{27,19},{20,... | collective-permute-start | bytes 3145736 | tf_op jit(solution)/shard_map/logits_line_reduce/ppermute | solution.py:141
  123.4 29.4 %collective-permute-start.18 = (f32[16,128,128]{2,1,0:T(8,128)}, f32[16,128,128]{2,1,0:T(8,128)S(1)}, u32[]{:S(2)}, u32[]{:S(2)}) collective-permute-start(f32[16,128,128]{2,1,0:T(8,128)} %get-tuple-element.12), channel_id=1, source_target_pairs={{0,8},{8,16},{16,24},{1,9},{9,17},{17,25},{2,10},{10,18},{18,26},{... | collective-permute-start | bytes 3145736 | tf_op jit(solution)/shard_map/logits_line_reduce/ppermute | solution.py:140
  131.7 25.0 %collective-permute-start.19 = (f32[16,128,128]{2,1,0:T(8,128)S(1)}, f32[16,128,128]{2,1,0:T(8,128)S(1)}, u32[]{:S(2)}, u32[]{:S(2)}) collective-permute-start(f32[16,128,128]{2,1,0:T(8,128)S(1)} %get-tuple-element.13), channel_id=1, source_target_pairs={{8,0},{16,8},{24,16},{9,1},{17,9},{25,17},{10,2},{18,10},{26,18},{... | collective-permute-start | bytes 3145736 | tf_op jit(solution)/shard_map/logits_line_reduce/ppermute | solution.py:141
  220.9 4.4 %collective-permute-start.20 = (f32[4,64,2048]{2,1,0:T(8,128)S(1)}, f32[4,64,2048]{2,1,0:T(8,128)}, u32[]{:S(2)}, u32[]{:S(2)}) collective-permute-start(f32[4,64,2048]{2,1,0:T(8,128)S(1)} %convolution_bitcast_fusion), channel_id=1, source_target_pairs={{0,1},{1,0},{2,3},{3,2},{4,5},{5,4},{6,7},{7,6},{8,9},{9,8},{10,11... | collective-permute-start | bytes 6291464 | tf_op jit(solution)/shard_map/summed_core_stage/ppermute | solution.py:27
  232.2 14.2 %collective-permute-start.21 = (f32[2,64,1024]{2,1,0:T(8,128)}, f32[2,64,1024]{2,1,0:T(8,128)S(1)}, u32[]{:S(2)}, u32[]{:S(2)}) collective-permute-start(f32[2,64,1024]{2,1,0:T(8,128)} %dynamic-slice_bitcast_fusion.3), channel_id=1, source_target_pairs={{0,2},{1,3},{2,0},{3,1},{4,6},{5,7},{6,4},{7,5},{8,10},{9,11},{10,... | collective-permute-start | bytes 1572872 | tf_op jit(solution)/shard_map/summed_chip_stage/ppermute | solution.py:18
  234.5 13.9 %collective-permute-start.23 = (f32[2,64,1024]{2,1,0:T(8,128)}, f32[2,64,1024]{2,1,0:T(8,128)S(1)}, u32[]{:S(2)}, u32[]{:S(2)}) collective-permute-start(f32[2,64,1024]{2,1,0:T(8,128)} %dynamic-slice_bitcast_fusion.2), channel_id=1, source_target_pairs={{0,4},{1,5},{2,6},{3,7},{4,0},{5,1},{6,2},{7,3},{8,12},{9,13},{10,... | collective-permute-start | bytes 1572872 | tf_op jit(solution)/shard_map/summed_chip_stage/ppermute | solution.py:18
  246.5 7.6 %collective-permute-start.22 = (f32[64,1024]{1,0:T(8,128)S(1)}, f32[64,1024]{1,0:T(8,128)S(1)}, u32[]{:S(2)}, u32[]{:S(2)}) collective-permute-start(f32[64,1024]{1,0:T(8,128)S(1)} %dynamic-slice_bitcast_fusion.5), channel_id=1, source_target_pairs={{0,4},{1,5},{2,6},{3,7},{4,0},{5,1},{6,2},{7,3},{8,12},{9,13},{10,... | collective-permute-start | bytes 786440 | tf_op jit(solution)/shard_map/summed_chip_stage/ppermute | solution.py:18
  248.5 7.3 %collective-permute-start.24 = (f32[64,1024]{1,0:T(8,128)S(1)}, f32[64,1024]{1,0:T(8,128)S(1)}, u32[]{:S(2)}, u32[]{:S(2)}) collective-permute-start(f32[64,1024]{1,0:T(8,128)S(1)} %dynamic-slice_bitcast_fusion.4), channel_id=1, source_target_pairs={{0,2},{1,3},{2,0},{3,1},{4,6},{5,7},{6,4},{7,5},{8,10},{9,11},{10,... | collective-permute-start | bytes 786440 | tf_op jit(solution)/shard_map/summed_chip_stage/ppermute | solution.py:18
  255.9 3.6 %collective-permute-start.25 = (f32[64]{0:T(128)S(1)}, f32[64]{0:T(128)S(1)}, u32[]{:S(2)}, u32[]{:S(2)}) collective-permute-start(f32[64]{0:T(128)S(1)} %multiply_reduce_fusion), channel_id=1, source_target_pairs={{0,8},{8,0},{16,24},{24,16},{1,9},{9,1},{17,25},{25,17},{2,10},{10... | collective-permute-start | bytes 776 | tf_op jit(solution)/shard_map/ppermute | solution.py:73
  259.6 4.5 %collective-permute-start.26 = (f32[64]{0:T(128)S(1)}, f32[64]{0:T(128)S(1)}, u32[]{:S(2)}, u32[]{:S(2)}) collective-permute-start(f32[64]{0:T(128)S(1)} %add.325), channel_id=1, source_target_pairs={{0,16},{8,24},{16,0},{24,8},{1,17},{9,25},{17,1},{25,9},{2,18},{10... | collective-permute-start | bytes 776 | tf_op jit(solution)/shard_map/ppermute | solution.py:73
Sparse Core Ops, SparseCore 0:
  169.8 42.8 all-gather.3

commit v14 on v12

--- a/solution.py
+++ b/solution.py
@@ -193,7 +193,8 @@
             return term.reshape(n_blk * pairs, rows_per_dev, columns_here)
 
     send_half = expected_half(1 - low_bit)
-    keep_half = expected_half(low_bit)
+    send_half, halves = lax.optimization_barrier((send_half, halves))
+    keep_half = lax.optimization_barrier(expected_half(low_bit))
     summed = halving_reduce_scatter(keep_half, send_half, n_vocab)
     squares = butterfly_sum(jnp.sum(summed * summed, axis=1), "dp", n_dp)
     width = hidden.shape[1] * n_vocab

time: 260 us -> 261 us (level)
    ppermute x1, waiting for transfers between devices: 3.33 us -> 0.01 us  [halving_reduce_scatter(): x = keep + lax.ppermute(send, 'vocab', perm=perm)]
  transfers between devices with their start and end apart: 23 -> 23, of which waited for: 17 -> 16; matrix products, arithmetic and copies ran while one was open for 2% -> 4% of each run, Pallas kernels for 0% -> 0%
where the time goes in v14:
time: 261 us
  waiting for transfers between devices  164 us (63%)
  starting transfers between devices  28.4 us (11%)
  matrix products  21 us (8%)
  between operations  14.6 us (6%)
  local copies, waits for them, and re-layouts  14.2 us (5%)
  other arithmetic  9.83 us (4%)
  blocking collectives  9.08 us (3%)
    reduce_scatter x1, waiting for transfers between devices, per_device(): logits = lax.psum_scatter(picked, 'dp', scatter_dimension=0, tiled=True)  75.5 us
    all_gather x1, waiting for transfers between devices, per_device(): prob_part = lax.all_gather(probabilities, 'dp', axis=0, tiled=True)  45.4 us
    ppermute x8, starting transfers between devices, direct_spread(): got.append(lax.ppermute(send, ('dp', 'vocab'), perm=perm))  17.7 us
    ppermute x4, waiting for transfers between devices, exchange_stage(): got = lax.ppermute(send, 'vocab', perm=perm)  17.6 us
    ppermute x6, waiting for transfers between devices, gather_stage(): got = lax.ppermute(x, 'vocab', perm=perm)  12.2 us
    dot_general x2, matrix products, expected_half(): jnp.einsum('brkt,ktd->brd', spread, out_weight.reshape(n_tb, TB, columns_...  12.1 us
    all_gather x1, blocking collectives, per_device(): stats = lax.all_gather(jnp.stack([local_max, local_total]), 'vocab', axis=0)  9.08 us
    dot_general x1, matrix products, per_device(): jnp.einsum('bd,vd->bv', beam_columns, out_weight, preferred_element_type=...  7.35 us
  transfers between devices with their start and end apart: 23, of which 16 were waited for; matrix products, arithmetic and copies ran while one was open for 4% of the time, Pallas kernels for 0%

profile of v14, /device:TPU:0, one launch (start us, length us, event | category | flops | bytes accessed | tf_op | source)
XLA Modules:
  0.0 260.8 jit_solution(17005932491923605354)
XLA Ops:
  7.4 0.9 dynamic-slice_bitcast_fusion.4
  8.3 0.7 collective-permute-start
  8.9 0.5 collective-permute-start.1
  9.5 5.8 %collective-permute-start.2 = (bf16[16,1024]{1,0:T(8,128)(2,1)S(1)}, bf16[16,1024]{1,0:T(8,128)(2,1)S(1)}, u32[]{:S(2)}, u32[]{:S(2)}) collective-permute-start(bf16[16,1024]{1,0:T(8,128)(2,1)S(1)} %get-tuple-element.23), channel_id=1, source_target_pairs={{0,2},{1,3},{2,10},{3,11},{4,18},{5,19},{6,26},{7,27},{8,4},{9,5},... | collective-permute-start | bytes 98312 | tf_op jit(solution)/shard_map/hidden_spread/ppermute | solution.py:115
  15.3 2.9 %collective-permute-start.3 = (bf16[16,1024]{1,0:T(8,128)(2,1)S(1)}, bf16[16,1024]{1,0:T(8,128)(2,1)S(1)}, u32[]{:S(2)}, u32[]{:S(2)}) collective-permute-start(bf16[16,1024]{1,0:T(8,128)(2,1)S(1)} %get-tuple-element.22), channel_id=1, source_target_pairs={{0,3},{1,4},{2,11},{3,12},{4,19},{5,20},{6,27},{7,28},{8,5},{9,6},... | collective-permute-start | bytes 98312 | tf_op jit(solution)/shard_map/hidden_spread/ppermute | solution.py:115
  18.2 3.3 %collective-permute-start.4 = (bf16[16,1024]{1,0:T(8,128)(2,1)S(1)}, bf16[16,1024]{1,0:T(8,128)(2,1)S(1)}, u32[]{:S(2)}, u32[]{:S(2)}) collective-permute-start(bf16[16,1024]{1,0:T(8,128)(2,1)S(1)} %get-tuple-element.21), channel_id=1, source_target_pairs={{0,4},{1,5},{2,12},{3,13},{4,20},{5,21},{6,28},{7,29},{8,6},{9,7},... | collective-permute-start | bytes 98312 | tf_op jit(solution)/shard_map/hidden_spread/ppermute | solution.py:115
  21.6 1.3 collective-permute-start.5
  23.0 1.9 collective-permute-start.6
  24.9 1.2 collective-permute-start.7
  26.1 5.7 %collective-permute-done.5 = bf16[16,1024]{1,0:T(8,128)(2,1)S(1)} collective-permute-done((bf16[16,1024]{1,0:T(8,128)(2,1)S(1)}, bf16[16,1024]{1,0:T(8,128)(2,1)S(1)}, u32[]{:S(2)}, u32[]{:S(2)}) %collective-permute-start.5) | collective-permute-done | bytes 32800 | tf_op jit(solution)/shard_map/hidden_spread/ppermute | solution.py:115
  31.8 0.7 collective-permute-done.6
  32.5 0.6 gather_fusion
  33.1 0.1 select_bitcast_fusion.1
  33.2 0.3 copy.31
  33.5 0.1 slice_bitcast_fusion.3
  33.6 2.2 collective-permute-start.8
  35.9 0.1 reshape.581
  36.0 3.6 %collective-permute-done.8 = bf16[64,1024]{1,0:T(8,128)(2,1)S(1)} collective-permute-done((bf16[64,1024]{1,0:T(8,128)(2,1)S(1)}, bf16[64,1024]{1,0:T(8,128)(2,1)S(1)}, u32[]{:S(2)}, u32[]{:S(2)}) %collective-permute-start.8) | collective-permute-done | bytes 131104 | tf_op jit(solution)/shard_map/hidden_spread/hidden_gather_stage/ppermute | solution.py:46
  39.8 1.1 collective-permute-done.11
  41.0 0.6 collective-permute-start.12
  41.6 5.8 %collective-permute-done.9 = bf16[2,64,1024]{2,1,0:T(8,128)(2,1)S(1)} collective-permute-done((bf16[2,64,1024]{2,1,0:T(8,128)(2,1)S(1)}, bf16[2,64,1024]{2,1,0:T(8,128)(2,1)S(1)}, u32[]{:S(2)}, u32[]{:S(2)}) %collective-permute-start.9) | collective-permute-done | bytes 262176 | tf_op jit(solution)/shard_map/hidden_spread/hidden_gather_stage/ppermute | solution.py:46
  47.7 0.5 collective-permute-start.13
  48.5 1.0 collective-permute-done.10
  49.5 0.2 maximum_select_fusion
  49.7 0.5 collective-permute-done.13
  50.2 0.2 maximum_select_fusion.1
  50.5 0.2 maximum_bitcast_fusion
  50.7 0.2 copy.38
  50.9 0.8 slice-done.1
  51.7 0.5 slice-done.2
  52.3 7.4 %fusion.22 = f32[4,128,19,128]{3,1,2,0:T(8,128)} fusion(bf16[4,128,2048,1]{2,1,3,0:T(8,128)(2,1)S(1)} %bitcast.153, bf16[19,128,2048,1]{2,1,0,3:T(8,128)(2,1)S(1)} %bitcast.182), kind=kOutput, calls=%fused_computation.95 | convolution fusion | flops 5100273664 | bytes 17039360 | tf_op jit(solution)/shard_map/dense_logits/bd,vd->bv/dot_general | solution.py:148
  59.6 5.2 %gather_fusion.1 = f32[64,128,128]{2,1,0:T(8,128)} fusion(f32[4,128,19,128]{3,1,2,0:T(8,128)} %fusion.22, s32[64]{0:T(128)S(1)} %reshape.581), kind=kCustom, calls=%fused_computation.1 | custom fusion | bytes 8389120 | tf_op jit(solution)/shard_map/dense_logits/gather | solution.py:153
  65.0 0.6 constant_dynamic-slice_fusion.1
  65.6 0.6 iota_compare_fusion.1
  66.2 75.5 %reduce-scatter.2.cloned.1.call-done = f32[1,16,128,128]{3,2,1,0:T(8,128)} async-done(((f32[4,16,128,128]{3,2,1,0:T(8,128)}), f32[1,16,128,128]{3,2,1,0:T(8,128)}) %reduce-scatter.2.cloned.1.call-update) | async-done | bytes 1048592 | tf_op jit(solution)/shard_map/reduce_scatter | solution.py:155
  141.7 1.5 select_reduce_fusion
  143.2 1.6 exponential_reduce_fusion
  144.8 9.1 %all-gather = f32[16,1,128]{2,1,0:T(1,128)S(1)} all-gather(f32[2,1,128]{2,1,0:T(1,128)S(1)} %pad_maximum_fusion.3), channel_id=2, replica_groups=mesh['dp'=4,'vocab'=8] {'vocab'}, dimensions={0}, use_global_device_ids=true | all-gather | bytes 9216 | tf_op jit(solution)/shard_map/softmax_stats/all_gather | solution.py:163
  153.9 1.6 select_convert_fusion
  155.6 45.4 %all-gather.3.cloned.1.call-done = bf16[4,16,128,128]{3,2,1,0:T(8,128)(2,1)} async-done(((bf16[1,16,128,128]{3,2,1,0:T(8,128)(2,1)}), bf16[4,16,128,128]{3,2,1,0:T(8,128)(2,1)}) %all-gather.3.cloned.1.call-update) | async-done | bytes 2097168 | tf_op jit(solution)/shard_map/all_gather | solution.py:170
  201.0 1.3 constant_dynamic-slice_fusion
  202.3 0.9 fusion
  203.3 6.6 %convolution_bitcast_fusion.1 = f32[4,64,2048]{2,1,0:T(8,128)} fusion(bf16[19,128,2048,1]{2,1,0,3:T(8,128)(2,1)} %bitcast.178, bf16[4,64,19,128]{3,2,1,0:T(8,128)(2,1)S(1)} %fusion), kind=kOutput, calls=%fused_computation.3 | convolution fusion | flops 2550136832 | bytes 13303808 | tf_op jit(solution)/shard_map/dense_expected/brkt,ktd->brd/dot_general | solution.py:187
  209.9 1.4 copy.42
  211.2 0.7 fusion.1
  211.9 5.5 %convolution_bitcast_fusion = f32[4,64,2048]{2,1,0:T(8,128)S(1)} fusion(bf16[19,128,2048,1]{2,1,0,3:T(8,128)(2,1)} %bitcast.179, bf16[4,64,19,128]{3,2,1,0:T(8,128)(2,1)S(1)} %fusion.1), kind=kOutput, calls=%fused_computation.2 | convolution fusion | flops 2550136832 | bytes 13303808 | tf_op jit(solution)/shard_map/dense_expected/brkt,ktd->brd/dot_general | solution.py:187
  217.4 2.0 add.255
  219.4 0.1 fusion.20
  219.6 0.8 dynamic-slice_bitcast_fusion.1
  220.4 1.5 collective-permute-start.15
  221.9 0.8 dynamic-slice_bitcast_fusion
  222.7 1.5 collective-permute-start.17
  224.2 10.8 %collective-permute-done.15 = f32[2,64,1024]{2,1,0:T(8,128)S(1)} collective-permute-done((f32[2,64,1024]{2,1,0:T(8,128)}, f32[2,64,1024]{2,1,0:T(8,128)S(1)}, u32[]{:S(2)}, u32[]{:S(2)}) %collective-permute-start.15) | collective-permute-done | bytes 524320 | tf_op jit(solution)/shard_map/summed_chip_stage/ppermute | solution.py:18
  235.1 1.5 collective-permute-start.16
  236.6 0.4 collective-permute-done.17
  237.1 1.2 collective-permute-start.18
  238.3 4.7 %collective-permute-done.16 = f32[64,1024]{1,0:T(8,128)S(1)} collective-permute-done((f32[64,1024]{1,0:T(8,128)S(1)}, f32[64,1024]{1,0:T(8,128)S(1)}, u32[]{:S(2)}, u32[]{:S(2)}) %collective-permute-start.16) | collective-permute-done | bytes 262176 | tf_op jit(solution)/shard_map/summed_chip_stage/ppermute | solution.py:18
  243.0 1.7 collective-permute-done.18
  244.8 0.1 multiply_reduce_fusion
  244.9 0.2 collective-permute-start.19
  245.1 3.4 %collective-permute-done.19 = f32[64]{0:T(128)S(1)} collective-permute-done((f32[64]{0:T(128)S(1)}, f32[64]{0:T(128)S(1)}, u32[]{:S(2)}, u32[]{:S(2)}) %collective-permute-start.19) | collective-permute-done | bytes 288 | tf_op jit(solution)/shard_map/ppermute | solution.py:73
  248.5 1.2 collective-permute-start.20
  249.8 3.2 %collective-permute-done.20 = f32[64]{0:T(128)S(1)} collective-permute-done((f32[64]{0:T(128)S(1)}, f32[64]{0:T(128)S(1)}, u32[]{:S(2)}, u32[]{:S(2)}) %collective-permute-start.20) | collective-permute-done | bytes 288 | tf_op jit(solution)/shard_map/ppermute | solution.py:73
  253.0 0.9 fusion.6
  (68 shorter events, 1.5 us)
Async XLA Ops:
  7.2 57.8 %copy-start = (s32[1,4]{1,0:T(1,128)S(1)}, s32[1,4]{1,0:T(1,128)}, u32[]{:S(2)}) copy-start(s32[1,4]{1,0:T(1,128)} %param.7) | copy-start | bytes 52
  7.2 134.5 %reduce-scatter.2.cloned.1.call-start = ((), (), s32[]{:S(2)}) async-start(), calls=%async_computation.1 | async-start | bytes 5242880 | tf_op jit(solution)/shard_map/reduce_scatter | solution.py:155
  7.3 28.5 %copy-start.3 = (s32[1,4,16]{2,1,0:T(4,128)S(1)}, s32[1,4,16]{2,1,0:T(4,128)}, u32[]{:S(2)}) copy-start(s32[1,4,16]{2,1,0:T(4,128)} %param.6) | copy-start | bytes 772
  8.3 13.3 %collective-permute-start = (bf16[16,1024]{1,0:T(8,128)(2,1)S(1)}, bf16[16,1024]{1,0:T(8,128)(2,1)S(1)}, u32[]{:S(2)}, u32[]{:S(2)}) collective-permute-start(bf16[16,1024]{1,0:T(8,128)(2,1)S(1)} %get-tuple-element.25), channel_id=1, source_target_pairs={{0,0},{1,1},{2,8},{3,9},{4,16},{5,17},{6,24},{7,25},{8,2},{9,3},{1... | collective-permute-start | bytes 98312 | tf_op jit(solution)/shard_map/hidden_spread/ppermute | solution.py:115
  8.9 14.0 %collective-permute-start.1 = (bf16[16,1024]{1,0:T(8,128)(2,1)S(1)}, bf16[16,1024]{1,0:T(8,128)(2,1)S(1)}, u32[]{:S(2)}, u32[]{:S(2)}) collective-permute-start(bf16[16,1024]{1,0:T(8,128)(2,1)S(1)} %get-tuple-element.24), channel_id=1, source_target_pairs={{0,1},{1,2},{2,9},{3,10},{4,17},{5,18},{6,25},{7,26},{8,3},{9,4},{... | collective-permute-start | bytes 98312 | tf_op jit(solution)/shard_map/hidden_spread/ppermute | solution.py:115
  9.5 15.4 %collective-permute-start.2 = (bf16[16,1024]{1,0:T(8,128)(2,1)S(1)}, bf16[16,1024]{1,0:T(8,128)(2,1)S(1)}, u32[]{:S(2)}, u32[]{:S(2)}) collective-permute-start(bf16[16,1024]{1,0:T(8,128)(2,1)S(1)} %get-tuple-element.23), channel_id=1, source_target_pairs={{0,2},{1,3},{2,10},{3,11},{4,18},{5,19},{6,26},{7,27},{8,4},{9,5},... | collective-permute-start | bytes 98312 | tf_op jit(solution)/shard_map/hidden_spread/ppermute | solution.py:115
  15.3 10.8 %collective-permute-start.3 = (bf16[16,1024]{1,0:T(8,128)(2,1)S(1)}, bf16[16,1024]{1,0:T(8,128)(2,1)S(1)}, u32[]{:S(2)}, u32[]{:S(2)}) collective-permute-start(bf16[16,1024]{1,0:T(8,128)(2,1)S(1)} %get-tuple-element.22), channel_id=1, source_target_pairs={{0,3},{1,4},{2,11},{3,12},{4,19},{5,20},{6,27},{7,28},{8,5},{9,6},... | collective-permute-start | bytes 98312 | tf_op jit(solution)/shard_map/hidden_spread/ppermute | solution.py:115
  18.2 8.0 %collective-permute-start.4 = (bf16[16,1024]{1,0:T(8,128)(2,1)S(1)}, bf16[16,1024]{1,0:T(8,128)(2,1)S(1)}, u32[]{:S(2)}, u32[]{:S(2)}) collective-permute-start(bf16[16,1024]{1,0:T(8,128)(2,1)S(1)} %get-tuple-element.21), channel_id=1, source_target_pairs={{0,4},{1,5},{2,12},{3,13},{4,20},{5,21},{6,28},{7,29},{8,6},{9,7},... | collective-permute-start | bytes 98312 | tf_op jit(solution)/shard_map/hidden_spread/ppermute | solution.py:115
  21.6 10.2 %collective-permute-start.5 = (bf16[16,1024]{1,0:T(8,128)(2,1)S(1)}, bf16[16,1024]{1,0:T(8,128)(2,1)S(1)}, u32[]{:S(2)}, u32[]{:S(2)}) collective-permute-start(bf16[16,1024]{1,0:T(8,128)(2,1)S(1)} %get-tuple-element.20), channel_id=1, source_target_pairs={{0,5},{1,6},{2,13},{3,14},{4,21},{5,22},{6,29},{7,30},{8,7},{9,0},... | collective-permute-start | bytes 98312 | tf_op jit(solution)/shard_map/hidden_spread/ppermute | solution.py:115
  23.0 9.6 %collective-permute-start.6 = (bf16[16,1024]{1,0:T(8,128)(2,1)S(1)}, bf16[16,1024]{1,0:T(8,128)(2,1)S(1)}, u32[]{:S(2)}, u32[]{:S(2)}) collective-permute-start(bf16[16,1024]{1,0:T(8,128)(2,1)S(1)} %get-tuple-element.19), channel_id=1, source_target_pairs={{0,6},{1,7},{2,14},{3,15},{4,22},{5,23},{6,30},{7,31},{8,0},{9,1},... | collective-permute-start | bytes 98312 | tf_op jit(solution)/shard_map/hidden_spread/ppermute | solution.py:115
  24.9 7.6 %collective-permute-start.7 = (bf16[16,1024]{1,0:T(8,128)(2,1)S(1)}, bf16[16,1024]{1,0:T(8,128)(2,1)S(1)}, u32[]{:S(2)}, u32[]{:S(2)}) collective-permute-start(bf16[16,1024]{1,0:T(8,128)(2,1)S(1)} %get-tuple-element.18), channel_id=1, source_target_pairs={{0,7},{1,0},{2,15},{3,8},{4,23},{5,16},{6,31},{7,24},{8,1},{9,2},{... | collective-permute-start | bytes 98312 | tf_op jit(solution)/shard_map/hidden_spread/ppermute | solution.py:115
  33.6 6.0 %collective-permute-start.8 = (bf16[64,1024]{1,0:T(8,128)(2,1)S(1)}, bf16[64,1024]{1,0:T(8,128)(2,1)S(1)}, u32[]{:S(2)}, u32[]{:S(2)}) collective-permute-start(bf16[64,1024]{1,0:T(8,128)(2,1)S(1)} %get-tuple-element.17), channel_id=1, source_target_pairs={{0,2},{1,3},{2,0},{3,1},{4,6},{5,7},{6,4},{7,5},{8,10},{9,11},{10,... | collective-permute-start | bytes 393224 | tf_op jit(solution)/shard_map/hidden_spread/hidden_gather_stage/ppermute | solution.py:46
  36.0 5.0 %collective-permute-start.11 = (bf16[64,1024]{1,0:T(8,128)(2,1)S(1)}, bf16[64,1024]{1,0:T(8,128)(2,1)S(1)}, u32[]{:S(2)}, u32[]{:S(2)}) collective-permute-start(bf16[64,1024]{1,0:T(8,128)(2,1)S(1)} %get-tuple-element.16), channel_id=1, source_target_pairs={{0,4},{1,5},{2,6},{3,7},{4,0},{5,1},{6,2},{7,3},{8,12},{9,13},{10,... | collective-permute-start | bytes 393224 | tf_op jit(solution)/shard_map/hidden_spread/hidden_gather_stage/ppermute | solution.py:46
  39.6 7.8 %collective-permute-start.9 = (bf16[2,64,1024]{2,1,0:T(8,128)(2,1)S(1)}, bf16[2,64,1024]{2,1,0:T(8,128)(2,1)S(1)}, u32[]{:S(2)}, u32[]{:S(2)}) collective-permute-start(bf16[2,64,1024]{2,1,0:T(8,128)(2,1)S(1)} %maximum_select_fusion.5), channel_id=1, source_target_pairs={{0,4},{1,5},{2,6},{3,7},{4,0},{5,1},{6,2},{7,3},{8,12},{9,13},{10,... | collective-permute-start | bytes 786440 | tf_op jit(solution)/shard_map/hidden_spread/hidden_gather_stage/ppermute | solution.py:46
  41.0 6.7 %collective-permute-start.12 = (bf16[2,64,1024]{2,1,0:T(8,128)(2,1)S(1)}, bf16[2,64,1024]{2,1,0:T(8,128)(2,1)S(1)}, u32[]{:S(2)}, u32[]{:S(2)}) collective-permute-start(bf16[2,64,1024]{2,1,0:T(8,128)(2,1)S(1)} %maximum_select_fusion.7), channel_id=1, source_target_pairs={{0,2},{1,3},{2,0},{3,1},{4,6},{5,7},{6,4},{7,5},{8,10},{9,11},{10,... | collective-permute-start | bytes 786440 | tf_op jit(solution)/shard_map/hidden_spread/hidden_gather_stage/ppermute | solution.py:46
  47.5 2.0 collective-permute-start.10
  47.6 3.3 %slice-start = ((s8[9961472]{0:T(1024)(128)(4,1)}), s8[4194304]{0:T(1024)(128)(4,1)S(1)}, s32[]{:S(2)}) async-start(s8[9961472]{0:T(1024)(128)(4,1)} %bitcast.180), calls=%async_computation.3 | async-start | bytes 8388608
  47.7 2.5 collective-permute-start.13
  49.5 2.3 slice-start.1
  50.5 1.8 slice-start.2
  64.9 136.1 %all-gather.3.cloned.1.call-start = ((), (), s32[]{:S(2)}) async-start(), calls=%async_computation.2 | async-start | bytes 2621440 | tf_op jit(solution)/shard_map/all_gather | solution.py:170
  141.7 12.2 %copy-start.1 = (f32[1,16,128,128]{3,2,1,0:T(8,128)S(1)}, f32[1,16,128,128]{3,2,1,0:T(8,128)}, u32[]{:S(2)}) copy-start(f32[1,16,128,128]{3,2,1,0:T(8,128)} %reduce-scatter.2.cloned.1.call-done) | copy-start | bytes 3145732
  203.3 6.6 %copy-start.2 = (bf16[4,16,128,128]{3,2,1,0:T(8,128)(2,1)S(1)}, bf16[4,16,128,128]{3,2,1,0:T(8,128)(2,1)}, u32[]{:S(2)}) copy-start(bf16[4,16,128,128]{3,2,1,0:T(8,128)(2,1)} %all-gather.3.cloned.1.call-done) | copy-start | bytes 6291460
  209.9 7.6 %collective-permute-start.14 = (f32[4,64,2048]{2,1,0:T(8,128)}, f32[4,64,2048]{2,1,0:T(8,128)}, u32[]{:S(2)}, u32[]{:S(2)}) collective-permute-start(f32[4,64,2048]{2,1,0:T(8,128)} %convolution_bitcast_fusion.1), channel_id=1, source_target_pairs={{0,1},{1,0},{2,3},{3,2},{4,5},{5,4},{6,7},{7,6},{8,9},{9,8},{10,11... | collective-permute-start | bytes 6291464 | tf_op jit(solution)/shard_map/summed_core_stage/ppermute | solution.py:27
  220.4 14.5 %collective-permute-start.15 = (f32[2,64,1024]{2,1,0:T(8,128)}, f32[2,64,1024]{2,1,0:T(8,128)S(1)}, u32[]{:S(2)}, u32[]{:S(2)}) collective-permute-start(f32[2,64,1024]{2,1,0:T(8,128)} %dynamic-slice_bitcast_fusion.1), channel_id=1, source_target_pairs={{0,2},{1,3},{2,0},{3,1},{4,6},{5,7},{6,4},{7,5},{8,10},{9,11},{10,... | collective-permute-start | bytes 1572872 | tf_op jit(solution)/shard_map/summed_chip_stage/ppermute | solution.py:18
  222.7 14.3 %collective-permute-start.17 = (f32[2,64,1024]{2,1,0:T(8,128)}, f32[2,64,1024]{2,1,0:T(8,128)S(1)}, u32[]{:S(2)}, u32[]{:S(2)}) collective-permute-start(f32[2,64,1024]{2,1,0:T(8,128)} %dynamic-slice_bitcast_fusion), channel_id=1, source_target_pairs={{0,4},{1,5},{2,6},{3,7},{4,0},{5,1},{6,2},{7,3},{8,12},{9,13},{10,... | collective-permute-start | bytes 1572872 | tf_op jit(solution)/shard_map/summed_chip_stage/ppermute | solution.py:18
  235.1 7.9 %collective-permute-start.16 = (f32[64,1024]{1,0:T(8,128)S(1)}, f32[64,1024]{1,0:T(8,128)S(1)}, u32[]{:S(2)}, u32[]{:S(2)}) collective-permute-start(f32[64,1024]{1,0:T(8,128)S(1)} %dynamic-slice_bitcast_fusion.3), channel_id=1, source_target_pairs={{0,4},{1,5},{2,6},{3,7},{4,0},{5,1},{6,2},{7,3},{8,12},{9,13},{10,... | collective-permute-start | bytes 786440 | tf_op jit(solution)/shard_map/summed_chip_stage/ppermute | solution.py:18
  237.1 7.6 %collective-permute-start.18 = (f32[64,1024]{1,0:T(8,128)S(1)}, f32[64,1024]{1,0:T(8,128)S(1)}, u32[]{:S(2)}, u32[]{:S(2)}) collective-permute-start(f32[64,1024]{1,0:T(8,128)S(1)} %dynamic-slice_bitcast_fusion.2), channel_id=1, source_target_pairs={{0,2},{1,3},{2,0},{3,1},{4,6},{5,7},{6,4},{7,5},{8,10},{9,11},{10,... | collective-permute-start | bytes 786440 | tf_op jit(solution)/shard_map/summed_chip_stage/ppermute | solution.py:18
  244.9 3.6 %collective-permute-start.19 = (f32[64]{0:T(128)S(1)}, f32[64]{0:T(128)S(1)}, u32[]{:S(2)}, u32[]{:S(2)}) collective-permute-start(f32[64]{0:T(128)S(1)} %multiply_reduce_fusion), channel_id=1, source_target_pairs={{0,8},{8,0},{16,24},{24,16},{1,9},{9,1},{17,25},{25,17},{2,10},{10... | collective-permute-start | bytes 776 | tf_op jit(solution)/shard_map/ppermute | solution.py:73
  248.5 4.5 %collective-permute-start.20 = (f32[64]{0:T(128)S(1)}, f32[64]{0:T(128)S(1)}, u32[]{:S(2)}, u32[]{:S(2)}) collective-permute-start(f32[64]{0:T(128)S(1)} %add.264), channel_id=1, source_target_pairs={{0,16},{8,24},{16,0},{24,8},{1,17},{9,25},{17,1},{25,9},{2,18},{10... | collective-permute-start | bytes 776 | tf_op jit(solution)/shard_map/ppermute | solution.py:73
Sparse Core Ops, SparseCore 0:
  65.0 76.6 reduce-scatter.1
  155.7 45.2 all-gather.2

commit v15 on v12

--- a/solution.py
+++ b/solution.py
@@ -149,8 +149,13 @@
             "bd,vd->bv", beam_columns, out_weight, preferred_element_type=jnp.float32
         )
         full4 = full.reshape(n_blk, BB, n_tb, TB)
-        rows = jnp.arange(n_blk, dtype=jnp.int32)[:, None]
-        picked = full4[rows, :, block_lists, :]
+        pick = (
+            block_lists[:, :, None] == jnp.arange(n_tb, dtype=jnp.int32)[None, None, :]
+        ).astype(jnp.float32)
+        picked = jnp.einsum(
+            "bsk,brkt->bsrt", pick, full4, precision=lax.Precision.HIGHEST,
+            preferred_element_type=jnp.float32,
+        )
 
     logits = lax.psum_scatter(picked, "dp", scatter_dimension=0, tiled=True)
 

time: 260 us -> 265 us (1.019)
  matrix products: 20.7 us -> 26.2 us
  other arithmetic: 7.82 us -> 11.2 us
  local copies, waits for them, and re-layouts: 13.2 us -> 10.1 us
    dot_general x0 -> x1, matrix products: none -> 6.32 us  [per_device(): jnp.einsum('bsk,brkt->bsrt', pick, full4, precision=lax.Precision.HIGHEST...]
    gather x1 -> x0, local copies, waits for them, and re-layouts: 5.24 us -> none  [per_device(): picked = full4[rows, :, block_lists, :]]
  transfers between devices with their start and end apart: 23 -> 23, of which waited for: 17 -> 17; matrix products, arithmetic and copies ran while one was open for 2% -> 3% of each run, Pallas kernels for 0% -> 0%
where the time goes in v15:
time: 265 us; the launch traced here: 264 us
  waiting for transfers between devices  165 us (62%)
  starting transfers between devices  29 us (11%)
  matrix products  26.2 us (10%)
  between operations  14.5 us (5%)
  other arithmetic  11.2 us (4%)
  local copies, waits for them, and re-layouts  10.1 us (4%)
  blocking collectives  8.89 us (3%)
    reduce_scatter x1, waiting for transfers between devices, per_device(): logits = lax.psum_scatter(picked, 'dp', scatter_dimension=0, tiled=True)  75.3 us
    all_gather x1, waiting for transfers between devices, per_device(): prob_part = lax.all_gather(probabilities, 'dp', axis=0, tiled=True)  45.4 us
    ppermute x8, starting transfers between devices, direct_spread(): got.append(lax.ppermute(send, ('dp', 'vocab'), perm=perm))  17.7 us
    ppermute x4, waiting for transfers between devices, exchange_stage(): got = lax.ppermute(send, 'vocab', perm=perm)  16.2 us
    dot_general x2, matrix products, expected_half(): jnp.einsum('brkt,ktd->brd', spread, out_weight.reshape(n_tb, TB, columns_...  12.5 us
    ppermute x6, waiting for transfers between devices, gather_stage(): got = lax.ppermute(x, 'vocab', perm=perm)  12.3 us
    all_gather x1, blocking collectives, per_device(): stats = lax.all_gather(jnp.stack([local_max, local_total]), 'vocab', axis=0)  8.89 us
    ppermute x8, waiting for transfers between devices, direct_spread(): got.append(lax.ppermute(send, ('dp', 'vocab'), perm=perm))  6.41 us
  transfers between devices with their start and end apart: 23, of which 17 were waited for; matrix products, arithmetic and copies ran while one was open for 3% of the time, Pallas kernels for 0%

profile of v15, /device:TPU:0, one launch (start us, length us, event | category | flops | bytes accessed | tf_op | source)
XLA Modules:
  0.0 264.4 jit_solution(14652246664501934427)
XLA Ops:
  7.3 0.9 dynamic-slice_bitcast_fusion.4
  8.3 0.7 collective-permute-start
  8.9 0.5 collective-permute-start.1
  9.5 5.8 %collective-permute-start.2 = (bf16[16,1024]{1,0:T(8,128)(2,1)S(1)}, bf16[16,1024]{1,0:T(8,128)(2,1)S(1)}, u32[]{:S(2)}, u32[]{:S(2)}) collective-permute-start(bf16[16,1024]{1,0:T(8,128)(2,1)S(1)} %get-tuple-element.29), channel_id=1, source_target_pairs={{0,2},{1,3},{2,10},{3,11},{4,18},{5,19},{6,26},{7,27},{8,4},{9,5},... | collective-permute-start | bytes 98312 | tf_op jit(solution)/shard_map/hidden_spread/ppermute | solution.py:115
  15.3 2.9 %collective-permute-start.3 = (bf16[16,1024]{1,0:T(8,128)(2,1)S(1)}, bf16[16,1024]{1,0:T(8,128)(2,1)S(1)}, u32[]{:S(2)}, u32[]{:S(2)}) collective-permute-start(bf16[16,1024]{1,0:T(8,128)(2,1)S(1)} %get-tuple-element.28), channel_id=1, source_target_pairs={{0,3},{1,4},{2,11},{3,12},{4,19},{5,20},{6,27},{7,28},{8,5},{9,6},... | collective-permute-start | bytes 98312 | tf_op jit(solution)/shard_map/hidden_spread/ppermute | solution.py:115
  18.2 3.3 %collective-permute-start.4 = (bf16[16,1024]{1,0:T(8,128)(2,1)S(1)}, bf16[16,1024]{1,0:T(8,128)(2,1)S(1)}, u32[]{:S(2)}, u32[]{:S(2)}) collective-permute-start(bf16[16,1024]{1,0:T(8,128)(2,1)S(1)} %get-tuple-element.27), channel_id=1, source_target_pairs={{0,4},{1,5},{2,12},{3,13},{4,20},{5,21},{6,28},{7,29},{8,6},{9,7},... | collective-permute-start | bytes 98312 | tf_op jit(solution)/shard_map/hidden_spread/ppermute | solution.py:115
  21.5 1.3 collective-permute-start.5
  22.9 1.9 collective-permute-start.6
  24.8 1.3 collective-permute-start.7
  26.1 0.3 collective-permute-done.4
  26.4 5.4 %collective-permute-done.5 = bf16[16,1024]{1,0:T(8,128)(2,1)S(1)} collective-permute-done((bf16[16,1024]{1,0:T(8,128)(2,1)S(1)}, bf16[16,1024]{1,0:T(8,128)(2,1)S(1)}, u32[]{:S(2)}, u32[]{:S(2)}) %collective-permute-start.5) | collective-permute-done | bytes 32800 | tf_op jit(solution)/shard_map/hidden_spread/ppermute | solution.py:115
  31.8 0.7 collective-permute-done.6
  32.5 0.6 gather_fusion
  33.2 0.3 copy.32
  33.6 2.2 collective-permute-start.8
  35.8 3.8 %collective-permute-done.8 = bf16[64,1024]{1,0:T(8,128)(2,1)S(1)} collective-permute-done((bf16[64,1024]{1,0:T(8,128)(2,1)S(1)}, bf16[64,1024]{1,0:T(8,128)(2,1)S(1)}, u32[]{:S(2)}, u32[]{:S(2)}) %collective-permute-start.8) | collective-permute-done | bytes 131104 | tf_op jit(solution)/shard_map/hidden_spread/hidden_gather_stage/ppermute | solution.py:46
  39.8 1.0 collective-permute-done.11
  40.8 0.6 collective-permute-start.12
  41.5 5.9 %collective-permute-done.9 = bf16[2,64,1024]{2,1,0:T(8,128)(2,1)S(1)} collective-permute-done((bf16[2,64,1024]{2,1,0:T(8,128)(2,1)S(1)}, bf16[2,64,1024]{2,1,0:T(8,128)(2,1)S(1)}, u32[]{:S(2)}, u32[]{:S(2)}) %collective-permute-start.9) | collective-permute-done | bytes 262176 | tf_op jit(solution)/shard_map/hidden_spread/hidden_gather_stage/ppermute | solution.py:46
  47.7 0.5 collective-permute-start.13
  48.4 1.0 collective-permute-done.10
  49.5 0.2 maximum_select_fusion
  49.7 0.5 collective-permute-done.13
  50.2 0.2 maximum_select_fusion.1
  50.5 0.2 maximum_bitcast_fusion
  50.7 0.2 copy.39
  50.9 0.8 slice-done.1
  51.7 0.5 slice-done.2
  52.3 5.6 %fusion.21 = f32[4,128,19,128]{3,1,2,0:T(8,128)S(1)} fusion(bf16[4,128,2048,1]{2,1,3,0:T(8,128)(2,1)S(1)} %bitcast.149, bf16[19,128,2048,1]{2,1,0,3:T(8,128)(2,1)S(1)} %bitcast.179), kind=kOutput, calls=%fused_computation.93 | convolution fusion | flops 5100273664 | bytes 17039360 | tf_op jit(solution)/shard_map/dense_logits/bd,vd->bv/dot_general | solution.py:148
  57.9 6.3 %fusion = f32[4,16,128,128]{3,1,2,0:T(8,128)} fusion(f32[4,128,19,128]{3,1,2,0:T(8,128)S(1)} %fusion.21, s32[4,16]{1,0:T(4,128)S(1)} %bitcast.169), kind=kOutput, calls=%fused_computation.1 | convolution fusion | flops 239076544 | bytes 9175296 | tf_op jit(solution)/shard_map/dense_logits/bsk,brkt->bsrt/dot_general | solution.py:155
  64.2 0.2 all-gather.3.cloned.1.call-start
  64.5 0.6 constant_dynamic-slice_fusion.2
  65.1 0.6 iota_compare_fusion.1
  65.7 75.3 %reduce-scatter.2.cloned.1.call-done = f32[1,16,128,128]{3,1,2,0:T(8,128)} async-done(((f32[4,16,128,128]{3,1,2,0:T(8,128)}), f32[1,16,128,128]{3,1,2,0:T(8,128)}) %reduce-scatter.2.cloned.1.call-update) | async-done | bytes 1048592 | tf_op jit(solution)/shard_map/reduce_scatter | solution.py:160
  141.0 2.4 select_reduce_fusion
  143.4 3.1 %exponential_reduce_fusion = f32[128]{0:T(128)S(1)} fusion(f32[1,16,128,128]{3,1,2,0:T(8,128)} %reduce-scatter.2.cloned.1.call-done, f32[128]{0:T(128)S(1)} %select_reduce_fusion, pred[16]{0:T(512)(128)(4,1)S(1)} %iota_compare_fusion.1), kind=kLoop, calls=%fused_computation.20 | loop fusion | flops 786304 | bytes 1049616 | tf_op jit(solution)/shard_map/softmax_stats/reduce_sum | solution.py:167
  146.6 8.9 %all-gather = f32[16,1,128]{2,1,0:T(1,128)S(1)} all-gather(f32[2,1,128]{2,1,0:T(1,128)S(1)} %pad_maximum_fusion.3), channel_id=2, replica_groups=mesh['dp'=4,'vocab'=8] {'vocab'}, dimensions={0}, use_global_device_ids=true | all-gather | bytes 9216 | tf_op jit(solution)/shard_map/softmax_stats/all_gather | solution.py:168
  155.5 0.4 select_convert_fusion
  156.0 0.9 copy.42
  156.9 45.4 %all-gather.3.cloned.1.call-done = bf16[4,16,128,128]{3,2,1,0:T(8,128)(2,1)} async-done(((bf16[1,16,128,128]{3,2,1,0:T(8,128)(2,1)}), bf16[4,16,128,128]{3,2,1,0:T(8,128)(2,1)}) %all-gather.3.cloned.1.call-update) | async-done | bytes 2097168 | tf_op jit(solution)/shard_map/all_gather | solution.py:175
  202.3 1.7 constant_dynamic-slice_fusion.1
  204.1 0.9 fusion.4
  205.0 6.4 %convolution_bitcast_fusion = f32[4,64,2048]{2,1,0:T(8,128)} fusion(bf16[19,128,2048,1]{2,1,0,3:T(8,128)(2,1)} %bitcast.175, bf16[4,64,19,128]{3,2,1,0:T(8,128)(2,1)S(1)} %fusion.4), kind=kOutput, calls=%fused_computation.3 | convolution fusion | flops 2550136832 | bytes 13303808 | tf_op jit(solution)/shard_map/dense_expected/brkt,ktd->brd/dot_general | solution.py:192
  211.4 0.9 fusion.3
  212.4 3.6 %collective-permute-done.14 = f32[4,64,2048]{2,1,0:T(8,128)} collective-permute-done((f32[4,64,2048]{2,1,0:T(8,128)}, f32[4,64,2048]{2,1,0:T(8,128)}, u32[]{:S(2)}, u32[]{:S(2)}) %collective-permute-start.14) | collective-permute-done | bytes 2097184 | tf_op jit(solution)/shard_map/summed_core_stage/ppermute | solution.py:27
  215.9 6.0 %fusion.2 = f32[4,64,2048]{2,1,0:T(8,128)S(1)} fusion(f32[4,64,2048]{2,1,0:T(8,128)} %collective-permute-done.14, bf16[19,128,2048,1]{2,1,0,3:T(8,128)(2,1)} %bitcast.176, bf16[4,64,19,128]{3,2,1,0:T(8,128)(2,1)S(1)} %fusion.3), kind=kOutput, calls=%fused_computation.5 | convolution fusion | flops 2550661120 | bytes 15400960 | tf_op jit(solution)/shard_map/dense_expected/brkt,ktd->brd/dot_general | solution.py:192
  222.1 0.8 dynamic-slice_bitcast_fusion.1
  222.9 1.5 collective-permute-start.15
  224.4 0.8 dynamic-slice_bitcast_fusion
  225.2 1.5 collective-permute-start.17
  226.7 10.5 %collective-permute-done.15 = f32[2,64,1024]{2,1,0:T(8,128)} collective-permute-done((f32[2,64,1024]{2,1,0:T(8,128)}, f32[2,64,1024]{2,1,0:T(8,128)}, u32[]{:S(2)}, u32[]{:S(2)}) %collective-permute-start.15) | collective-permute-done | bytes 524320 | tf_op jit(solution)/shard_map/summed_chip_stage/ppermute | solution.py:18
  237.2 1.1 bitcast_add_fusion.1
  238.4 1.5 collective-permute-start.16
  239.9 1.1 bitcast_add_fusion
  241.1 1.5 collective-permute-start.18
  242.6 3.3 %collective-permute-done.16 = f32[64,1024]{1,0:T(8,128)S(1)} collective-permute-done((f32[64,1024]{1,0:T(8,128)S(1)}, f32[64,1024]{1,0:T(8,128)S(1)}, u32[]{:S(2)}, u32[]{:S(2)}) %collective-permute-start.16) | collective-permute-done | bytes 262176 | tf_op jit(solution)/shard_map/summed_chip_stage/ppermute | solution.py:18
  246.0 2.4 collective-permute-done.18
  248.4 0.1 multiply_reduce_fusion
  248.6 0.2 collective-permute-start.19
  248.8 3.4 %collective-permute-done.19 = f32[64]{0:T(128)S(1)} collective-permute-done((f32[64]{0:T(128)S(1)}, f32[64]{0:T(128)S(1)}, u32[]{:S(2)}, u32[]{:S(2)}) %collective-permute-start.19) | collective-permute-done | bytes 288 | tf_op jit(solution)/shard_map/ppermute | solution.py:73
  252.2 1.2 collective-permute-start.20
  253.4 1.3 copy.47
  254.7 1.9 collective-permute-done.20
  256.7 0.9 fusion.7
  (64 shorter events, 1.6 us)
Async XLA Ops:
  7.2 57.3 %copy-start = (s32[1,4]{1,0:T(1,128)S(1)}, s32[1,4]{1,0:T(1,128)}, u32[]{:S(2)}) copy-start(s32[1,4]{1,0:T(1,128)} %param.7) | copy-start | bytes 52
  7.2 133.9 %reduce-scatter.2.cloned.1.call-start = ((), (), s32[]{:S(2)}) async-start(), calls=%async_computation.1 | async-start | bytes 5242880 | tf_op jit(solution)/shard_map/reduce_scatter | solution.py:160
  8.3 13.3 %collective-permute-start = (bf16[16,1024]{1,0:T(8,128)(2,1)S(1)}, bf16[16,1024]{1,0:T(8,128)(2,1)S(1)}, u32[]{:S(2)}, u32[]{:S(2)}) collective-permute-start(bf16[16,1024]{1,0:T(8,128)(2,1)S(1)} %get-tuple-element.31), channel_id=1, source_target_pairs={{0,0},{1,1},{2,8},{3,9},{4,16},{5,17},{6,24},{7,25},{8,2},{9,3},{1... | collective-permute-start | bytes 98312 | tf_op jit(solution)/shard_map/hidden_spread/ppermute | solution.py:115
  8.9 13.9 %collective-permute-start.1 = (bf16[16,1024]{1,0:T(8,128)(2,1)S(1)}, bf16[16,1024]{1,0:T(8,128)(2,1)S(1)}, u32[]{:S(2)}, u32[]{:S(2)}) collective-permute-start(bf16[16,1024]{1,0:T(8,128)(2,1)S(1)} %get-tuple-element.30), channel_id=1, source_target_pairs={{0,1},{1,2},{2,9},{3,10},{4,17},{5,18},{6,25},{7,26},{8,3},{9,4},{... | collective-permute-start | bytes 98312 | tf_op jit(solution)/shard_map/hidden_spread/ppermute | solution.py:115
  9.5 15.3 %collective-permute-start.2 = (bf16[16,1024]{1,0:T(8,128)(2,1)S(1)}, bf16[16,1024]{1,0:T(8,128)(2,1)S(1)}, u32[]{:S(2)}, u32[]{:S(2)}) collective-permute-start(bf16[16,1024]{1,0:T(8,128)(2,1)S(1)} %get-tuple-element.29), channel_id=1, source_target_pairs={{0,2},{1,3},{2,10},{3,11},{4,18},{5,19},{6,26},{7,27},{8,4},{9,5},... | collective-permute-start | bytes 98312 | tf_op jit(solution)/shard_map/hidden_spread/ppermute | solution.py:115
  15.3 10.8 %collective-permute-start.3 = (bf16[16,1024]{1,0:T(8,128)(2,1)S(1)}, bf16[16,1024]{1,0:T(8,128)(2,1)S(1)}, u32[]{:S(2)}, u32[]{:S(2)}) collective-permute-start(bf16[16,1024]{1,0:T(8,128)(2,1)S(1)} %get-tuple-element.28), channel_id=1, source_target_pairs={{0,3},{1,4},{2,11},{3,12},{4,19},{5,20},{6,27},{7,28},{8,5},{9,6},... | collective-permute-start | bytes 98312 | tf_op jit(solution)/shard_map/hidden_spread/ppermute | solution.py:115
  18.2 8.2 %collective-permute-start.4 = (bf16[16,1024]{1,0:T(8,128)(2,1)S(1)}, bf16[16,1024]{1,0:T(8,128)(2,1)S(1)}, u32[]{:S(2)}, u32[]{:S(2)}) collective-permute-start(bf16[16,1024]{1,0:T(8,128)(2,1)S(1)} %get-tuple-element.27), channel_id=1, source_target_pairs={{0,4},{1,5},{2,12},{3,13},{4,20},{5,21},{6,28},{7,29},{8,6},{9,7},... | collective-permute-start | bytes 98312 | tf_op jit(solution)/shard_map/hidden_spread/ppermute | solution.py:115
  21.5 10.3 %collective-permute-start.5 = (bf16[16,1024]{1,0:T(8,128)(2,1)S(1)}, bf16[16,1024]{1,0:T(8,128)(2,1)S(1)}, u32[]{:S(2)}, u32[]{:S(2)}) collective-permute-start(bf16[16,1024]{1,0:T(8,128)(2,1)S(1)} %get-tuple-element.26), channel_id=1, source_target_pairs={{0,5},{1,6},{2,13},{3,14},{4,21},{5,22},{6,29},{7,30},{8,7},{9,0},... | collective-permute-start | bytes 98312 | tf_op jit(solution)/shard_map/hidden_spread/ppermute | solution.py:115
  22.9 9.6 %collective-permute-start.6 = (bf16[16,1024]{1,0:T(8,128)(2,1)S(1)}, bf16[16,1024]{1,0:T(8,128)(2,1)S(1)}, u32[]{:S(2)}, u32[]{:S(2)}) collective-permute-start(bf16[16,1024]{1,0:T(8,128)(2,1)S(1)} %get-tuple-element.25), channel_id=1, source_target_pairs={{0,6},{1,7},{2,14},{3,15},{4,22},{5,23},{6,30},{7,31},{8,0},{9,1},... | collective-permute-start | bytes 98312 | tf_op jit(solution)/shard_map/hidden_spread/ppermute | solution.py:115
  24.8 7.7 %collective-permute-start.7 = (bf16[16,1024]{1,0:T(8,128)(2,1)S(1)}, bf16[16,1024]{1,0:T(8,128)(2,1)S(1)}, u32[]{:S(2)}, u32[]{:S(2)}) collective-permute-start(bf16[16,1024]{1,0:T(8,128)(2,1)S(1)} %get-tuple-element.24), channel_id=1, source_target_pairs={{0,7},{1,0},{2,15},{3,8},{4,23},{5,16},{6,31},{7,24},{8,1},{9,2},{... | collective-permute-start | bytes 98312 | tf_op jit(solution)/shard_map/hidden_spread/ppermute | solution.py:115
  33.6 6.0 %collective-permute-start.8 = (bf16[64,1024]{1,0:T(8,128)(2,1)S(1)}, bf16[64,1024]{1,0:T(8,128)(2,1)S(1)}, u32[]{:S(2)}, u32[]{:S(2)}) collective-permute-start(bf16[64,1024]{1,0:T(8,128)(2,1)S(1)} %get-tuple-element.23), channel_id=1, source_target_pairs={{0,2},{1,3},{2,0},{3,1},{4,6},{5,7},{6,4},{7,5},{8,10},{9,11},{10,... | collective-permute-start | bytes 393224 | tf_op jit(solution)/shard_map/hidden_spread/hidden_gather_stage/ppermute | solution.py:46
  35.8 5.0 %collective-permute-start.11 = (bf16[64,1024]{1,0:T(8,128)(2,1)S(1)}, bf16[64,1024]{1,0:T(8,128)(2,1)S(1)}, u32[]{:S(2)}, u32[]{:S(2)}) collective-permute-start(bf16[64,1024]{1,0:T(8,128)(2,1)S(1)} %get-tuple-element.22), channel_id=1, source_target_pairs={{0,4},{1,5},{2,6},{3,7},{4,0},{5,1},{6,2},{7,3},{8,12},{9,13},{10,... | collective-permute-start | bytes 393224 | tf_op jit(solution)/shard_map/hidden_spread/hidden_gather_stage/ppermute | solution.py:46
  39.6 7.8 %collective-permute-start.9 = (bf16[2,64,1024]{2,1,0:T(8,128)(2,1)S(1)}, bf16[2,64,1024]{2,1,0:T(8,128)(2,1)S(1)}, u32[]{:S(2)}, u32[]{:S(2)}) collective-permute-start(bf16[2,64,1024]{2,1,0:T(8,128)(2,1)S(1)} %maximum_select_fusion.5), channel_id=1, source_target_pairs={{0,4},{1,5},{2,6},{3,7},{4,0},{5,1},{6,2},{7,3},{8,12},{9,13},{10,... | collective-permute-start | bytes 786440 | tf_op jit(solution)/shard_map/hidden_spread/hidden_gather_stage/ppermute | solution.py:46
  40.8 6.8 %collective-permute-start.12 = (bf16[2,64,1024]{2,1,0:T(8,128)(2,1)S(1)}, bf16[2,64,1024]{2,1,0:T(8,128)(2,1)S(1)}, u32[]{:S(2)}, u32[]{:S(2)}) collective-permute-start(bf16[2,64,1024]{2,1,0:T(8,128)(2,1)S(1)} %maximum_select_fusion.7), channel_id=1, source_target_pairs={{0,2},{1,3},{2,0},{3,1},{4,6},{5,7},{6,4},{7,5},{8,10},{9,11},{10,... | collective-permute-start | bytes 786440 | tf_op jit(solution)/shard_map/hidden_spread/hidden_gather_stage/ppermute | solution.py:46
  47.5 2.0 collective-permute-start.10
  47.6 3.3 %slice-start = ((s8[9961472]{0:T(1024)(128)(4,1)}), s8[4194304]{0:T(1024)(128)(4,1)S(1)}, s32[]{:S(2)}) async-start(s8[9961472]{0:T(1024)(128)(4,1)} %bitcast.177), calls=%async_computation.3 | async-start | bytes 8388608
  47.7 2.5 collective-permute-start.13
  49.5 2.3 slice-start.1
  50.5 1.8 slice-start.2
  52.3 5.6 %copy-start.2 = (s32[1,4,16]{2,1,0:T(4,128)S(1)}, s32[1,4,16]{2,1,0:T(4,128)}, u32[]{:S(2)}) copy-start(s32[1,4,16]{2,1,0:T(4,128)} %param.6) | copy-start | bytes 772
  64.2 138.1 %all-gather.3.cloned.1.call-start = ((), (), s32[]{:S(2)}) async-start(), calls=%async_computation.2 | async-start | bytes 2621440 | tf_op jit(solution)/shard_map/all_gather | solution.py:175
  141.0 14.5 %copy-start.1 = (f32[1,16,128,128]{3,1,2,0:T(8,128)S(1)}, f32[1,16,128,128]{3,1,2,0:T(8,128)}, u32[]{:S(2)}) copy-start(f32[1,16,128,128]{3,1,2,0:T(8,128)} %reduce-scatter.2.cloned.1.call-done) | copy-start | bytes 3145732
  211.4 4.5 %collective-permute-start.14 = (f32[4,64,2048]{2,1,0:T(8,128)}, f32[4,64,2048]{2,1,0:T(8,128)}, u32[]{:S(2)}, u32[]{:S(2)}) collective-permute-start(f32[4,64,2048]{2,1,0:T(8,128)} %convolution_bitcast_fusion), channel_id=1, source_target_pairs={{0,1},{1,0},{2,3},{3,2},{4,5},{5,4},{6,7},{7,6},{8,9},{9,8},{10,11... | collective-permute-start | bytes 6291464 | tf_op jit(solution)/shard_map/summed_core_stage/ppermute | solution.py:27
  222.9 14.3 %collective-permute-start.15 = (f32[2,64,1024]{2,1,0:T(8,128)}, f32[2,64,1024]{2,1,0:T(8,128)}, u32[]{:S(2)}, u32[]{:S(2)}) collective-permute-start(f32[2,64,1024]{2,1,0:T(8,128)} %dynamic-slice_bitcast_fusion.1), channel_id=1, source_target_pairs={{0,2},{1,3},{2,0},{3,1},{4,6},{5,7},{6,4},{7,5},{8,10},{9,11},{10,... | collective-permute-start | bytes 1572872 | tf_op jit(solution)/shard_map/summed_chip_stage/ppermute | solution.py:18
  225.2 14.7 %collective-permute-start.17 = (f32[2,64,1024]{2,1,0:T(8,128)}, f32[2,64,1024]{2,1,0:T(8,128)}, u32[]{:S(2)}, u32[]{:S(2)}) collective-permute-start(f32[2,64,1024]{2,1,0:T(8,128)} %dynamic-slice_bitcast_fusion), channel_id=1, source_target_pairs={{0,4},{1,5},{2,6},{3,7},{4,0},{5,1},{6,2},{7,3},{8,12},{9,13},{10,... | collective-permute-start | bytes 1572872 | tf_op jit(solution)/shard_map/summed_chip_stage/ppermute | solution.py:18
  238.4 7.6 %collective-permute-start.16 = (f32[64,1024]{1,0:T(8,128)S(1)}, f32[64,1024]{1,0:T(8,128)S(1)}, u32[]{:S(2)}, u32[]{:S(2)}) collective-permute-start(f32[64,1024]{1,0:T(8,128)S(1)} %dynamic-slice_bitcast_fusion.3), channel_id=1, source_target_pairs={{0,4},{1,5},{2,6},{3,7},{4,0},{5,1},{6,2},{7,3},{8,12},{9,13},{10,... | collective-permute-start | bytes 786440 | tf_op jit(solution)/shard_map/summed_chip_stage/ppermute | solution.py:18
  241.1 7.3 %collective-permute-start.18 = (f32[64,1024]{1,0:T(8,128)S(1)}, f32[64,1024]{1,0:T(8,128)S(1)}, u32[]{:S(2)}, u32[]{:S(2)}) collective-permute-start(f32[64,1024]{1,0:T(8,128)S(1)} %dynamic-slice_bitcast_fusion.2), channel_id=1, source_target_pairs={{0,2},{1,3},{2,0},{3,1},{4,6},{5,7},{6,4},{7,5},{8,10},{9,11},{10,... | collective-permute-start | bytes 786440 | tf_op jit(solution)/shard_map/summed_chip_stage/ppermute | solution.py:18
  248.6 3.6 %collective-permute-start.19 = (f32[64]{0:T(128)S(1)}, f32[64]{0:T(128)S(1)}, u32[]{:S(2)}, u32[]{:S(2)}) collective-permute-start(f32[64]{0:T(128)S(1)} %multiply_reduce_fusion), channel_id=1, source_target_pairs={{0,8},{8,0},{16,24},{24,16},{1,9},{9,1},{17,25},{25,17},{2,10},{10... | collective-permute-start | bytes 776 | tf_op jit(solution)/shard_map/ppermute | solution.py:73
  252.2 4.5 %collective-permute-start.20 = (f32[64]{0:T(128)S(1)}, f32[64]{0:T(128)S(1)}, u32[]{:S(2)}, u32[]{:S(2)}) collective-permute-start(f32[64]{0:T(128)S(1)} %add.248), channel_id=1, source_target_pairs={{0,16},{8,24},{16,0},{24,8},{1,17},{9,25},{17,1},{25,9},{2,18},{10... | collective-permute-start | bytes 776 | tf_op jit(solution)/shard_map/ppermute | solution.py:73
Sparse Core Ops, SparseCore 0:
  64.4 76.6 reduce-scatter.1
  157.0 45.2 all-gather.2

commit v16 on v11

--- a/solution.py
+++ b/solution.py
@@ -96,6 +96,27 @@
     return jnp.concatenate([by_source[k] for k in range(n)], axis=concat_axis)
 
 
+def line_all_gather(own_part, n):
+    me = lax.axis_index("dp")
+    got = [own_part]
+    from_left, from_right = own_part, own_part
+    for step in range(1, n):
+        upward = [(s, s + 1) for s in range(step - 1, n - 1)]
+        downward = [(s, s - 1) for s in range(1, n - step + 1)]
+        from_left, from_right = lax.optimization_barrier((from_left, from_right))
+        from_left = lax.ppermute(from_left, "dp", perm=upward)
+        from_right = lax.ppermute(from_right, "dp", perm=downward)
+        got += [from_left, from_right]
+    blocks = []
+    for block in range(n):
+        pick = jnp.where(me == block, got[0], jnp.zeros_like(got[0]))
+        for step in range(1, n):
+            pick = jnp.where(me - step == block, got[2 * step - 1], pick)
+            pick = jnp.where(me + step == block, got[2 * step], pick)
+        blocks.append(pick)
+    return jnp.stack(blocks)
+
+
 def per_device(hidden, out_weight, token_blocks, counts):
     vocab_here, columns_here = out_weight.shape
     n_vocab = lax.psum(1, "vocab")
@@ -143,7 +164,12 @@
         allowed_logprob = jnp.where(live_mask, shifted, 0.0)
         probabilities = jnp.where(live_mask, jnp.exp(shifted), 0.0).astype(jnp.bfloat16)
 
-    prob_part = lax.all_gather(probabilities, "dp", axis=0, tiled=True)
+    with jax.named_scope("probs_two_routes"):
+        first_rows = probabilities[:, :, : BB // 2]
+        second_rows = probabilities[0, :, BB // 2 :]
+        by_queue = lax.all_gather(first_rows, "dp", axis=0, tiled=True)
+        by_permute = line_all_gather(second_rows, n_dp)
+        prob_part = jnp.concatenate([by_queue, by_permute], axis=2)
 
     rows_per_dev = n_blk * BB // n_vocab
     pairs = BB // rows_per_dev // 2

time: 260 us -> 264 us (1.015)
  starting transfers between devices: 23.7 us -> 33.6 us
  waiting for transfers between devices: 175 us -> 168 us
    all_gather x1, waiting for transfers between devices: 45.4 us -> 1.87 us  [per_device(): by_queue = lax.all_gather(first_rows, 'dp', axis=0, tiled=True)]
    ppermute x0 -> x6, waiting for transfers between devices: none -> 39.7 us  [the longest x3 35 us: line_all_gather(): from_right = lax.ppermute(from_right, 'dp', perm=downward)]
    ppermute x0 -> x6, starting transfers between devices: none -> 8.77 us  [the longest x3 4.91 us: line_all_gather(): from_left = lax.ppermute(from_left, 'dp', perm=upward)]
  transfers between devices with their start and end apart: 20 -> 26, of which waited for: 19 -> 21; matrix products, arithmetic and copies ran while one was open for 1% -> 1% of each run, Pallas kernels for 0% -> 0%
where the time goes in v16:
time: 264 us
  waiting for transfers between devices  168 us (64%)
  starting transfers between devices  33.6 us (13%)
  matrix products  18 us (7%)
  between operations  14.7 us (6%)
  local copies, waits for them, and re-layouts  10.5 us (4%)
  other arithmetic  9.41 us (4%)
  blocking collectives  8.91 us (3%)
    reduce_scatter x1, waiting for transfers between devices, per_device(): logits = lax.psum_scatter(picked, 'dp', scatter_dimension=0, tiled=True)  75.9 us
    ppermute x3, waiting for transfers between devices, line_all_gather(): from_right = lax.ppermute(from_right, 'dp', perm=downward)  35 us
    ppermute x4, waiting for transfers between devices, exchange_stage(): got = lax.ppermute(send, 'vocab', perm=perm)  18.4 us
    ppermute x5, waiting for transfers between devices, bruck_all_to_all(): got = lax.ppermute(send, axis_name, perm=perm)  15.5 us
    ppermute x5, starting transfers between devices, bruck_all_to_all(): got = lax.ppermute(send, axis_name, perm=perm)  10.5 us
    ppermute x6, waiting for transfers between devices, gather_stage(): got = lax.ppermute(x, 'vocab', perm=perm)  9.37 us
    all_gather x1, blocking collectives, per_device(): stats = lax.all_gather(jnp.stack([local_max, local_total]), 'vocab', axis=0)  8.91 us
    dot_general x2, matrix products, expected_half(): jnp.einsum('brkt,ktd->brd', spread, out_weight.reshape(n_tb, TB, columns_...  8.79 us
  transfers between devices with their start and end apart: 26, of which 21 were waited for; matrix products, arithmetic and copies ran while one was open for 1% of the time, Pallas kernels for 0%

profile of v16, /device:TPU:0, one launch (start us, length us, event | category | flops | bytes accessed | tf_op | source)
XLA Modules:
  0.0 263.7 jit_solution(13127574126202773598)
XLA Ops:
  7.3 1.0 constant_dynamic-slice_fusion.6
  8.3 0.6 collective-permute-start
  8.8 1.0 collective-permute-done
  9.9 2.9 %collective-permute-start.1 = (bf16[2,2,16,1024]{3,2,1,0:T(8,128)(2,1)S(1)}, bf16[2,2,16,1024]{3,2,1,0:T(8,128)(2,1)S(1)}, u32[]{:S(2)}, u32[]{:S(2)}) collective-permute-start(bf16[2,2,16,1024]{3,2,1,0:T(8,128)(2,1)S(1)} %get-tuple-element.41), channel_id=1, source_target_pairs={{0,2},{1,3},{2,0},{3,1},{4,6},{5,7},{6,4},{7,5},{8,10},{9,11},{10,... | collective-permute-start | bytes 393224 | tf_op jit(solution)/shard_map/hidden_spread/ppermute | solution.py:91
  12.8 3.8 %collective-permute-done.1 = bf16[2,2,16,1024]{3,2,1,0:T(8,128)(2,1)S(1)} collective-permute-done((bf16[2,2,16,1024]{3,2,1,0:T(8,128)(2,1)S(1)}, bf16[2,2,16,1024]{3,2,1,0:T(8,128)(2,1)S(1)}, u32[]{:S(2)}, u32[]{:S(2)}) %collective-permute-start.1) | collective-permute-done | bytes 131104 | tf_op jit(solution)/shard_map/hidden_spread/ppermute | solution.py:91
  16.6 1.8 collective-permute-start.2
  18.5 3.2 %collective-permute-done.2 = bf16[2,2,16,1024]{3,2,1,0:T(8,128)(2,1)S(1)} collective-permute-done((bf16[2,2,16,1024]{3,2,1,0:T(8,128)(2,1)S(1)}, bf16[2,2,16,1024]{3,2,1,0:T(8,128)(2,1)S(1)}, u32[]{:S(2)}, u32[]{:S(2)}) %collective-permute-start.2) | collective-permute-done | bytes 131104 | tf_op jit(solution)/shard_map/hidden_spread/ppermute | solution.py:91
  21.8 0.2 reshape.523
  22.2 1.9 collective-permute-start.3
  24.1 3.1 %collective-permute-done.3 = bf16[2,16,2048]{2,1,0:T(8,128)(2,1)S(1)} collective-permute-done((bf16[2,16,2048]{2,1,0:T(8,128)(2,1)S(1)}, bf16[2,16,2048]{2,1,0:T(8,128)(2,1)S(1)}, u32[]{:S(2)}, u32[]{:S(2)}) %collective-permute-start.3) | collective-permute-done | bytes 131104 | tf_op jit(solution)/shard_map/hidden_spread/ppermute | solution.py:91
  27.3 3.3 %collective-permute-start.4 = (bf16[2,16,2048]{2,1,0:T(8,128)(2,1)S(1)}, bf16[2,16,2048]{2,1,0:T(8,128)(2,1)S(1)}, u32[]{:S(2)}, u32[]{:S(2)}) collective-permute-start(bf16[2,16,2048]{2,1,0:T(8,128)(2,1)S(1)} %get-tuple-element.35), channel_id=1, source_target_pairs={{0,16},{8,24},{16,0},{24,8},{1,17},{9,25},{17,1},{25,9},{2,18},{10... | collective-permute-start | bytes 393224 | tf_op jit(solution)/shard_map/hidden_spread/ppermute | solution.py:91
  30.6 4.4 %collective-permute-done.4 = bf16[2,16,2048]{2,1,0:T(8,128)(2,1)S(1)} collective-permute-done((bf16[2,16,2048]{2,1,0:T(8,128)(2,1)S(1)}, bf16[2,16,2048]{2,1,0:T(8,128)(2,1)S(1)}, u32[]{:S(2)}, u32[]{:S(2)}) %collective-permute-start.4) | collective-permute-done | bytes 131104 | tf_op jit(solution)/shard_map/hidden_spread/ppermute | solution.py:91
  35.1 1.6 collective-permute-start.5
  36.8 1.5 collective-permute-start.8
  38.3 3.3 %collective-permute-done.5 = bf16[64,1024]{1,0:T(8,128)(2,1)S(1)} collective-permute-done((bf16[64,1024]{1,0:T(8,128)(2,1)S(1)}, bf16[64,1024]{1,0:T(8,128)(2,1)S(1)}, u32[]{:S(2)}, u32[]{:S(2)}) %collective-permute-start.5) | collective-permute-done | bytes 131104 | tf_op jit(solution)/shard_map/hidden_spread/hidden_gather_stage/ppermute | solution.py:46
  41.6 1.6 collective-permute-start.6
  43.3 1.5 collective-permute-start.9
  44.9 3.2 %collective-permute-done.6 = bf16[2,64,1024]{2,1,0:T(8,128)(2,1)S(1)} collective-permute-done((bf16[2,64,1024]{2,1,0:T(8,128)(2,1)S(1)}, bf16[2,64,1024]{2,1,0:T(8,128)(2,1)S(1)}, u32[]{:S(2)}, u32[]{:S(2)}) %collective-permute-start.6) | collective-permute-done | bytes 262176 | tf_op jit(solution)/shard_map/hidden_spread/hidden_gather_stage/ppermute | solution.py:46
  48.2 1.6 collective-permute-done.9
  50.4 1.4 collective-permute-done.10
  52.1 0.2 maximum_bitcast_fusion
  52.2 0.2 copy.60
  52.5 0.8 slice-done.1
  53.3 0.5 slice-done.2
  53.8 7.4 %fusion.26 = f32[4,128,19,128]{3,1,2,0:T(8,128)} fusion(bf16[4,128,2048,1]{2,1,3,0:T(8,128)(2,1)S(1)} %bitcast.194, bf16[19,128,2048,1]{2,1,0,3:T(8,128)(2,1)S(1)} %bitcast.235), kind=kOutput, calls=%fused_computation.107 | convolution fusion | flops 5100273664 | bytes 17039360 | tf_op jit(solution)/shard_map/dense_logits/bd,vd->bv/dot_general | solution.py:145
  61.2 5.3 %gather_fusion = f32[64,128,128]{2,1,0:T(8,128)} fusion(f32[4,128,19,128]{3,1,2,0:T(8,128)} %fusion.26, s32[64]{0:T(128)S(1)} %reshape.529), kind=kCustom, calls=%fused_computation | custom fusion | bytes 8389120 | tf_op jit(solution)/shard_map/dense_logits/gather | solution.py:150
  66.5 0.6 constant_dynamic-slice_fusion.7
  67.1 0.6 iota_compare_fusion.1
  67.8 75.9 %reduce-scatter.2.cloned.1.call-done = f32[1,16,128,128]{3,2,1,0:T(8,128)} async-done(((f32[4,16,128,128]{3,2,1,0:T(8,128)}), f32[1,16,128,128]{3,2,1,0:T(8,128)}) %reduce-scatter.2.cloned.1.call-update) | async-done | bytes 1048592 | tf_op jit(solution)/shard_map/reduce_scatter | solution.py:152
  143.6 1.5 select_reduce_fusion
  145.2 1.6 exponential_reduce_fusion
  146.7 8.9 %all-gather = f32[16,1,128]{2,1,0:T(1,128)S(1)} all-gather(f32[2,1,128]{2,1,0:T(1,128)S(1)} %pad_maximum_fusion.4), channel_id=2, replica_groups=mesh['dp'=4,'vocab'=8] {'vocab'}, dimensions={0}, use_global_device_ids=true | all-gather | bytes 9216 | tf_op jit(solution)/shard_map/softmax_stats/all_gather | solution.py:160
  155.7 1.4 select_convert_fusion
  157.1 0.7 fusion.24
  157.9 3.4 %collective-permute-start.11 = (bf16[16,64,128]{2,1,0:T(8,128)(2,1)S(1)}, bf16[16,64,128]{2,1,0:T(8,128)(2,1)S(1)}, u32[]{:S(2)}, u32[]{:S(2)}) collective-permute-start(bf16[16,64,128]{2,1,0:T(8,128)(2,1)S(1)} %get-tuple-element.9), channel_id=1, source_target_pairs={{0,8},{8,16},{16,24},{1,9},{9,17},{17,25},{2,10},{10,18},{18,26},{... | collective-permute-start | bytes 786440 | tf_op jit(solution)/shard_map/probs_two_routes/ppermute | solution.py:107
  161.3 1.3 collective-permute-start.12
  162.6 4.7 %collective-permute-done.11 = bf16[16,64,128]{2,1,0:T(8,128)(2,1)S(1)} collective-permute-done((bf16[16,64,128]{2,1,0:T(8,128)(2,1)S(1)}, bf16[16,64,128]{2,1,0:T(8,128)(2,1)S(1)}, u32[]{:S(2)}, u32[]{:S(2)}) %collective-permute-start.11) | collective-permute-done | bytes 262176 | tf_op jit(solution)/shard_map/probs_two_routes/ppermute | solution.py:107
  167.3 4.4 %collective-permute-done.12 = bf16[16,64,128]{2,1,0:T(8,128)(2,1)S(1)} collective-permute-done((bf16[16,64,128]{2,1,0:T(8,128)(2,1)S(1)}, bf16[16,64,128]{2,1,0:T(8,128)(2,1)S(1)}, u32[]{:S(2)}, u32[]{:S(2)}) %collective-permute-start.12) | collective-permute-done | bytes 262176 | tf_op jit(solution)/shard_map/probs_two_routes/ppermute | solution.py:108
  171.7 0.7 collective-permute-start.13
  172.4 1.3 collective-permute-start.14
  173.7 9.4 %collective-permute-done.14 = bf16[16,64,128]{2,1,0:T(8,128)(2,1)S(1)} collective-permute-done((bf16[16,64,128]{2,1,0:T(8,128)(2,1)S(1)}, bf16[16,64,128]{2,1,0:T(8,128)(2,1)S(1)}, u32[]{:S(2)}, u32[]{:S(2)}) %collective-permute-start.14) | collective-permute-done | bytes 262176 | tf_op jit(solution)/shard_map/probs_two_routes/ppermute | solution.py:108
  183.1 1.3 collective-permute-start.15
  184.4 0.9 collective-permute-start.16
  185.3 21.2 %collective-permute-done.15 = bf16[16,64,128]{2,1,0:T(8,128)(2,1)S(1)} collective-permute-done((bf16[16,64,128]{2,1,0:T(8,128)(2,1)S(1)}, bf16[16,64,128]{2,1,0:T(8,128)(2,1)S(1)}, u32[]{:S(2)}, u32[]{:S(2)}) %collective-permute-start.15) | collective-permute-done | bytes 262176 | tf_op jit(solution)/shard_map/probs_two_routes/ppermute | solution.py:108
  206.9 1.9 all-gather.3.cloned.1.call-done
  208.8 1.4 maximum_maximum_fusion
  210.2 0.2 constant_dynamic-slice_fusion.1
  210.4 0.9 fusion.2
  211.4 5.8 %convolution_bitcast_fusion = f32[4,64,2048]{2,1,0:T(8,128)S(1)} fusion(bf16[19,128,2048,1]{2,1,0,3:T(8,128)(2,1)} %bitcast.232, bf16[4,64,19,128]{3,2,1,0:T(8,128)(2,1)S(1)} %fusion.2), kind=kOutput, calls=%fused_computation.1 | convolution fusion | flops 2550136832 | bytes 13303808 | tf_op jit(solution)/shard_map/dense_expected/brkt,ktd->brd/dot_general | solution.py:189
  217.3 0.9 fusion.1
  218.2 3.2 %collective-permute-done.17 = f32[4,64,2048]{2,1,0:T(8,128)S(1)} collective-permute-done((f32[4,64,2048]{2,1,0:T(8,128)S(1)}, f32[4,64,2048]{2,1,0:T(8,128)S(1)}, u32[]{:S(2)}, u32[]{:S(2)}) %collective-permute-start.17) | collective-permute-done | bytes 2097184 | tf_op jit(solution)/shard_map/summed_core_stage/ppermute | solution.py:27
  221.4 3.0 %fusion = f32[4,64,2048]{2,1,0:T(8,128)S(1)} fusion(f32[4,64,2048]{2,1,0:T(8,128)S(1)} %collective-permute-done.17, bf16[19,128,2048,1]{2,1,0,3:T(8,128)(2,1)S(1)} %bitcast.238, bf16[4,64,19,128]{3,2,1,0:T(8,128)(2,1)S(1)} %fusion.1), kind=kOutput, calls=%fused_computation.3 | convolution fusion | flops 2550661120 | bytes 15400960 | tf_op jit(solution)/shard_map/dense_expected/brkt,ktd->brd/dot_general | solution.py:189
  224.6 1.5 collective-permute-start.18
  226.2 0.6 collective-permute-start.20
  226.8 11.8 %collective-permute-done.18 = f32[2,64,1024]{2,1,0:T(8,128)S(1)} collective-permute-done((f32[2,64,1024]{2,1,0:T(8,128)S(1)}, f32[2,64,1024]{2,1,0:T(8,128)S(1)}, u32[]{:S(2)}, u32[]{:S(2)}) %collective-permute-start.18) | collective-permute-done | bytes 524320 | tf_op jit(solution)/shard_map/summed_chip_stage/ppermute | solution.py:18
  238.7 1.5 collective-permute-start.19
  240.4 0.6 collective-permute-start.21
  241.0 5.3 %collective-permute-done.19 = f32[64,1024]{1,0:T(8,128)S(1)} collective-permute-done((f32[64,1024]{1,0:T(8,128)S(1)}, f32[64,1024]{1,0:T(8,128)S(1)}, u32[]{:S(2)}, u32[]{:S(2)}) %collective-permute-start.19) | collective-permute-done | bytes 262176 | tf_op jit(solution)/shard_map/summed_chip_stage/ppermute | solution.py:18
  246.3 1.3 collective-permute-done.21
  247.8 1.6 collective-permute-start.22
  249.4 2.1 collective-permute-done.22
  251.5 2.1 collective-permute-start.23
  253.5 2.4 collective-permute-done.23
  255.9 0.9 fusion.5
  (91 shorter events, 3.1 us)
Async XLA Ops:
  7.2 59.4 %copy-start = (s32[1,4]{1,0:T(1,128)S(1)}, s32[1,4]{1,0:T(1,128)}, u32[]{:S(2)}) copy-start(s32[1,4]{1,0:T(1,128)} %param.7) | copy-start | bytes 52
  7.2 136.5 %reduce-scatter.2.cloned.1.call-start = ((), (), s32[]{:S(2)}) async-start(), calls=%async_computation.1 | async-start | bytes 5242880 | tf_op jit(solution)/shard_map/reduce_scatter | solution.py:152
  8.3 1.5 collective-permute-start
  9.9 6.7 %collective-permute-start.1 = (bf16[2,2,16,1024]{3,2,1,0:T(8,128)(2,1)S(1)}, bf16[2,2,16,1024]{3,2,1,0:T(8,128)(2,1)S(1)}, u32[]{:S(2)}, u32[]{:S(2)}) collective-permute-start(bf16[2,2,16,1024]{3,2,1,0:T(8,128)(2,1)S(1)} %get-tuple-element.41), channel_id=1, source_target_pairs={{0,2},{1,3},{2,0},{3,1},{4,6},{5,7},{6,4},{7,5},{8,10},{9,11},{10,... | collective-permute-start | bytes 393224 | tf_op jit(solution)/shard_map/hidden_spread/ppermute | solution.py:91
  16.6 5.0 %collective-permute-start.2 = (bf16[2,2,16,1024]{3,2,1,0:T(8,128)(2,1)S(1)}, bf16[2,2,16,1024]{3,2,1,0:T(8,128)(2,1)S(1)}, u32[]{:S(2)}, u32[]{:S(2)}) collective-permute-start(bf16[2,2,16,1024]{3,2,1,0:T(8,128)(2,1)S(1)} %get-tuple-element.39), channel_id=1, source_target_pairs={{0,4},{1,5},{2,6},{3,7},{4,0},{5,1},{6,2},{7,3},{8,12},{9,13},{10,... | collective-permute-start | bytes 393224 | tf_op jit(solution)/shard_map/hidden_spread/ppermute | solution.py:91
  22.2 14.5 %copy-start.3 = (s32[1,4,16]{2,1,0:T(4,128)S(1)}, s32[1,4,16]{2,1,0:T(4,128)}, u32[]{:S(2)}) copy-start(s32[1,4,16]{2,1,0:T(4,128)} %param.6) | copy-start | bytes 772
  22.2 5.0 %collective-permute-start.3 = (bf16[2,16,2048]{2,1,0:T(8,128)(2,1)S(1)}, bf16[2,16,2048]{2,1,0:T(8,128)(2,1)S(1)}, u32[]{:S(2)}, u32[]{:S(2)}) collective-permute-start(bf16[2,16,2048]{2,1,0:T(8,128)(2,1)S(1)} %get-tuple-element.37), channel_id=1, source_target_pairs={{0,8},{8,0},{16,24},{24,16},{1,9},{9,1},{17,25},{25,17},{2,10},{10... | collective-permute-start | bytes 393224 | tf_op jit(solution)/shard_map/hidden_spread/ppermute | solution.py:91
  27.3 7.6 %collective-permute-start.4 = (bf16[2,16,2048]{2,1,0:T(8,128)(2,1)S(1)}, bf16[2,16,2048]{2,1,0:T(8,128)(2,1)S(1)}, u32[]{:S(2)}, u32[]{:S(2)}) collective-permute-start(bf16[2,16,2048]{2,1,0:T(8,128)(2,1)S(1)} %get-tuple-element.35), channel_id=1, source_target_pairs={{0,16},{8,24},{16,0},{24,8},{1,17},{9,25},{17,1},{25,9},{2,18},{10... | collective-permute-start | bytes 393224 | tf_op jit(solution)/shard_map/hidden_spread/ppermute | solution.py:91
  35.1 6.4 %collective-permute-start.5 = (bf16[64,1024]{1,0:T(8,128)(2,1)S(1)}, bf16[64,1024]{1,0:T(8,128)(2,1)S(1)}, u32[]{:S(2)}, u32[]{:S(2)}) collective-permute-start(bf16[64,1024]{1,0:T(8,128)(2,1)S(1)} %get-tuple-element.29), channel_id=1, source_target_pairs={{0,2},{1,3},{2,0},{3,1},{4,6},{5,7},{6,4},{7,5},{8,10},{9,11},{10,... | collective-permute-start | bytes 393224 | tf_op jit(solution)/shard_map/hidden_spread/hidden_gather_stage/ppermute | solution.py:46
  36.8 6.5 %collective-permute-start.8 = (bf16[64,1024]{1,0:T(8,128)(2,1)S(1)}, bf16[64,1024]{1,0:T(8,128)(2,1)S(1)}, u32[]{:S(2)}, u32[]{:S(2)}) collective-permute-start(bf16[64,1024]{1,0:T(8,128)(2,1)S(1)} %get-tuple-element.28), channel_id=1, source_target_pairs={{0,4},{1,5},{2,6},{3,7},{4,0},{5,1},{6,2},{7,3},{8,12},{9,13},{10,... | collective-permute-start | bytes 393224 | tf_op jit(solution)/shard_map/hidden_spread/hidden_gather_stage/ppermute | solution.py:46
  41.6 6.4 %collective-permute-start.6 = (bf16[2,64,1024]{2,1,0:T(8,128)(2,1)S(1)}, bf16[2,64,1024]{2,1,0:T(8,128)(2,1)S(1)}, u32[]{:S(2)}, u32[]{:S(2)}) collective-permute-start(bf16[2,64,1024]{2,1,0:T(8,128)(2,1)S(1)} %maximum_select_fusion.10), channel_id=1, source_target_pairs={{0,4},{1,5},{2,6},{3,7},{4,0},{5,1},{6,2},{7,3},{8,12},{9,13},{10,... | collective-permute-start | bytes 786440 | tf_op jit(solution)/shard_map/hidden_spread/hidden_gather_stage/ppermute | solution.py:46
  43.3 6.4 %collective-permute-start.9 = (bf16[2,64,1024]{2,1,0:T(8,128)(2,1)S(1)}, bf16[2,64,1024]{2,1,0:T(8,128)(2,1)S(1)}, u32[]{:S(2)}, u32[]{:S(2)}) collective-permute-start(bf16[2,64,1024]{2,1,0:T(8,128)(2,1)S(1)} %maximum_select_fusion.12), channel_id=1, source_target_pairs={{0,2},{1,3},{2,0},{3,1},{4,6},{5,7},{6,4},{7,5},{8,10},{9,11},{10,... | collective-permute-start | bytes 786440 | tf_op jit(solution)/shard_map/hidden_spread/hidden_gather_stage/ppermute | solution.py:46
  48.1 2.1 collective-permute-start.7
  49.7 2.8 %slice-start = ((s8[9961472]{0:T(1024)(128)(4,1)}), s8[4194304]{0:T(1024)(128)(4,1)S(1)}, s32[]{:S(2)}) async-start(s8[9961472]{0:T(1024)(128)(4,1)} %bitcast.233), calls=%async_computation.3 | async-start | bytes 8388608
  49.8 2.0 collective-permute-start.10
  50.1 3.2 %slice-start.1 = ((s8[9961472]{0:T(1024)(128)(4,1)}), s8[4194304]{0:T(1024)(128)(4,1)S(1)}, s32[]{:S(2)}) async-start(s8[9961472]{0:T(1024)(128)(4,1)} %bitcast.233), calls=%async_computation.4 | async-start | bytes 8388608
  52.0 1.8 slice-start.2
  66.5 142.3 %all-gather.3.cloned.1.call-start = ((), (), s32[]{:S(2)}) async-start(), calls=%async_computation.2 | async-start | bytes 1310720 | tf_op jit(solution)/shard_map/probs_two_routes/all_gather | solution.py:170
  143.6 12.1 %copy-start.2 = (f32[1,16,128,128]{3,2,1,0:T(8,128)S(1)}, f32[1,16,128,128]{3,2,1,0:T(8,128)}, u32[]{:S(2)}) copy-start(f32[1,16,128,128]{3,2,1,0:T(8,128)} %reduce-scatter.2.cloned.1.call-done) | copy-start | bytes 3145732
  157.9 9.4 %collective-permute-start.11 = (bf16[16,64,128]{2,1,0:T(8,128)(2,1)S(1)}, bf16[16,64,128]{2,1,0:T(8,128)(2,1)S(1)}, u32[]{:S(2)}, u32[]{:S(2)}) collective-permute-start(bf16[16,64,128]{2,1,0:T(8,128)(2,1)S(1)} %get-tuple-element.9), channel_id=1, source_target_pairs={{0,8},{8,16},{16,24},{1,9},{9,17},{17,25},{2,10},{10,18},{18,26},{... | collective-permute-start | bytes 786440 | tf_op jit(solution)/shard_map/probs_two_routes/ppermute | solution.py:107
  161.3 10.5 %collective-permute-start.12 = (bf16[16,64,128]{2,1,0:T(8,128)(2,1)S(1)}, bf16[16,64,128]{2,1,0:T(8,128)(2,1)S(1)}, u32[]{:S(2)}, u32[]{:S(2)}) collective-permute-start(bf16[16,64,128]{2,1,0:T(8,128)(2,1)S(1)} %get-tuple-element.9), channel_id=1, source_target_pairs={{8,0},{16,8},{24,16},{9,1},{17,9},{25,17},{10,2},{18,10},{26,18},{... | collective-permute-start | bytes 786440 | tf_op jit(solution)/shard_map/probs_two_routes/ppermute | solution.py:108
  171.7 2.0 collective-permute-start.13
  172.4 10.7 %collective-permute-start.14 = (bf16[16,64,128]{2,1,0:T(8,128)(2,1)S(1)}, bf16[16,64,128]{2,1,0:T(8,128)(2,1)S(1)}, u32[]{:S(2)}, u32[]{:S(2)}) collective-permute-start(bf16[16,64,128]{2,1,0:T(8,128)(2,1)S(1)} %collective-permute-done.12), channel_id=1, source_target_pairs={{8,0},{16,8},{9,1},{17,9},{10,2},{18,10},{11,3},{19,11},{12,4},{20... | collective-permute-start | bytes 786440 | tf_op jit(solution)/shard_map/probs_two_routes/ppermute | solution.py:108
  183.1 23.4 %collective-permute-start.15 = (bf16[16,64,128]{2,1,0:T(8,128)(2,1)S(1)}, bf16[16,64,128]{2,1,0:T(8,128)(2,1)S(1)}, u32[]{:S(2)}, u32[]{:S(2)}) collective-permute-start(bf16[16,64,128]{2,1,0:T(8,128)(2,1)S(1)} %collective-permute-done.14), channel_id=1, source_target_pairs={{8,0},{9,1},{10,2},{11,3},{12,4},{13,5},{14,6},{15,7}} | collective-permute-start | bytes 786440 | tf_op jit(solution)/shard_map/probs_two_routes/ppermute | solution.py:108
  184.4 22.1 %collective-permute-start.16 = (bf16[16,64,128]{2,1,0:T(8,128)(2,1)S(1)}, bf16[16,64,128]{2,1,0:T(8,128)(2,1)S(1)}, u32[]{:S(2)}, u32[]{:S(2)}) collective-permute-start(bf16[16,64,128]{2,1,0:T(8,128)(2,1)S(1)} %collective-permute-done.13), channel_id=1, source_target_pairs={{16,24},{17,25},{18,26},{19,27},{20,28},{21,29},{22,30},{23,31}} | collective-permute-start | bytes 786440 | tf_op jit(solution)/shard_map/probs_two_routes/ppermute | solution.py:107
  210.4 11.0 %slice-start.3 = ((s8[9961472]{0:T(1024)(128)(4,1)}), s8[4194304]{0:T(1024)(128)(4,1)S(1)}, s32[]{:S(2)}) async-start(s8[9961472]{0:T(1024)(128)(4,1)} %bitcast.236), calls=%async_computation.6 | async-start | bytes 8388608
  211.3 10.1 %slice-start.4 = ((s8[9961472]{0:T(1024)(128)(4,1)}), s8[4194304]{0:T(1024)(128)(4,1)S(1)}, s32[]{:S(2)}) async-start(s8[9961472]{0:T(1024)(128)(4,1)} %bitcast.236), calls=%async_computation.7 | async-start | bytes 8388608
  211.3 10.1 %slice-start.5 = ((s8[9961472]{0:T(1024)(128)(4,1)}), s8[1572864]{0:T(1024)(128)(4,1)S(1)}, s32[]{:S(2)}) async-start(s8[9961472]{0:T(1024)(128)(4,1)} %bitcast.236), calls=%async_computation.8 | async-start | bytes 3145728
  217.2 4.2 %collective-permute-start.17 = (f32[4,64,2048]{2,1,0:T(8,128)S(1)}, f32[4,64,2048]{2,1,0:T(8,128)S(1)}, u32[]{:S(2)}, u32[]{:S(2)}) collective-permute-start(f32[4,64,2048]{2,1,0:T(8,128)S(1)} %convolution_bitcast_fusion), channel_id=1, source_target_pairs={{0,1},{1,0},{2,3},{3,2},{4,5},{5,4},{6,7},{7,6},{8,9},{9,8},{10,11... | collective-permute-start | bytes 6291464 | tf_op jit(solution)/shard_map/summed_core_stage/ppermute | solution.py:27
  224.6 14.0 %collective-permute-start.18 = (f32[2,64,1024]{2,1,0:T(8,128)S(1)}, f32[2,64,1024]{2,1,0:T(8,128)S(1)}, u32[]{:S(2)}, u32[]{:S(2)}) collective-permute-start(f32[2,64,1024]{2,1,0:T(8,128)S(1)} %dynamic-slice_bitcast_fusion.1), channel_id=1, source_target_pairs={{0,2},{1,3},{2,0},{3,1},{4,6},{5,7},{6,4},{7,5},{8,10},{9,11},{10,... | collective-permute-start | bytes 1572872 | tf_op jit(solution)/shard_map/summed_chip_stage/ppermute | solution.py:18
  226.2 14.1 %collective-permute-start.20 = (f32[2,64,1024]{2,1,0:T(8,128)S(1)}, f32[2,64,1024]{2,1,0:T(8,128)S(1)}, u32[]{:S(2)}, u32[]{:S(2)}) collective-permute-start(f32[2,64,1024]{2,1,0:T(8,128)S(1)} %dynamic-slice_bitcast_fusion), channel_id=1, source_target_pairs={{0,4},{1,5},{2,6},{3,7},{4,0},{5,1},{6,2},{7,3},{8,12},{9,13},{10,... | collective-permute-start | bytes 1572872 | tf_op jit(solution)/shard_map/summed_chip_stage/ppermute | solution.py:18
  238.7 7.5 %collective-permute-start.19 = (f32[64,1024]{1,0:T(8,128)S(1)}, f32[64,1024]{1,0:T(8,128)S(1)}, u32[]{:S(2)}, u32[]{:S(2)}) collective-permute-start(f32[64,1024]{1,0:T(8,128)S(1)} %dynamic-slice_bitcast_fusion.3), channel_id=1, source_target_pairs={{0,4},{1,5},{2,6},{3,7},{4,0},{5,1},{6,2},{7,3},{8,12},{9,13},{10,... | collective-permute-start | bytes 786440 | tf_op jit(solution)/shard_map/summed_chip_stage/ppermute | solution.py:18
  240.3 16.6 %copy-start.1 = (s32[1,4]{1,0:T(1,128)S(1)}, s32[1,4]{1,0:T(1,128)}, u32[]{:S(2)}) copy-start(s32[1,4]{1,0:T(1,128)} %param.7) | copy-start | bytes 52
  240.4 7.3 %collective-permute-start.21 = (f32[64,1024]{1,0:T(8,128)S(1)}, f32[64,1024]{1,0:T(8,128)S(1)}, u32[]{:S(2)}, u32[]{:S(2)}) collective-permute-start(f32[64,1024]{1,0:T(8,128)S(1)} %dynamic-slice_bitcast_fusion.2), channel_id=1, source_target_pairs={{0,2},{1,3},{2,0},{3,1},{4,6},{5,7},{6,4},{7,5},{8,10},{9,11},{10,... | collective-permute-start | bytes 786440 | tf_op jit(solution)/shard_map/summed_chip_stage/ppermute | solution.py:18
  247.8 3.6 %collective-permute-start.22 = (f32[64]{0:T(128)S(1)}, f32[64]{0:T(128)S(1)}, u32[]{:S(2)}, u32[]{:S(2)}) collective-permute-start(f32[64]{0:T(128)S(1)} %multiply_reduce_fusion), channel_id=1, source_target_pairs={{0,8},{8,0},{16,24},{24,16},{1,9},{9,1},{17,25},{25,17},{2,10},{10... | collective-permute-start | bytes 776 | tf_op jit(solution)/shard_map/ppermute | solution.py:73
  251.5 4.5 %collective-permute-start.23 = (f32[64]{0:T(128)S(1)}, f32[64]{0:T(128)S(1)}, u32[]{:S(2)}, u32[]{:S(2)}) collective-permute-start(f32[64]{0:T(128)S(1)} %add.180), channel_id=1, source_target_pairs={{0,16},{8,24},{16,0},{24,8},{1,17},{9,25},{17,1},{25,9},{2,18},{10... | collective-permute-start | bytes 776 | tf_op jit(solution)/shard_map/ppermute | solution.py:73
Sparse Core Ops, SparseCore 0:
  66.6 77.0 reduce-scatter.1
  173.8 34.9 all-gather.2

commit v17 on v11

--- a/solution.py
+++ b/solution.py
@@ -54,7 +54,9 @@
     levels = n.bit_length() - 1
     rows, cols = x.shape
     half = cols // 2
-    first, second = x[:, :half], x[:, half:]
+    quarter = cols // 4
+    offloaded = lax.all_gather(x[:, :half], "vocab", axis=0, tiled=True)
+    first, second = x[:, half : half + quarter], x[:, half + quarter :]
     have_a, have_b = [], []
     order_a = list(range(1, levels)) + [0]
     order_b = list(range(levels - 1, 0, -1)) + [0]
@@ -62,8 +64,8 @@
         with jax.named_scope("hidden_gather_stage"):
             first, have_a = gather_stage(first, have_a, order_a[step], n)
             second, have_b = gather_stage(second, have_b, order_b[step], n)
-    joined = jnp.concatenate([first, second], axis=-1)
-    return joined.reshape(n * rows, cols)
+    joined = jnp.concatenate([first, second], axis=-1).reshape(n * rows, cols - half)
+    return jnp.concatenate([offloaded, joined], axis=-1)
 
 
 def butterfly_sum(x, axis_name, n):

time: 260 us -> 269 us (1.035)
  waiting for transfers between devices: 175 us -> 181 us
    all_gather x0 -> x1, waiting for transfers between devices: none -> 11.7 us  [doubling_all_gather(): offloaded = lax.all_gather(x[:, :half], 'vocab', axis=0, tiled=True)]
    ppermute x6, waiting for transfers between devices: 10.9 us -> 6.04 us  [gather_stage(): got = lax.ppermute(x, 'vocab', perm=perm)]
  transfers between devices with their start and end apart: 20 -> 21, of which waited for: 19 -> 18; matrix products, arithmetic and copies ran while one was open for 1% -> 1% of each run, Pallas kernels for 0% -> 0%
where the time goes in v17:
time: 269 us
  waiting for transfers between devices  181 us (67%)
  starting transfers between devices  25.1 us (9%)
  matrix products  20.4 us (8%)
  between operations  14.2 us (5%)
  local copies, waits for them, and re-layouts  10.5 us (4%)
  blocking collectives  9.08 us (3%)
  other arithmetic  8.66 us (3%)
    reduce_scatter x1, waiting for transfers between devices, per_device(): logits = lax.psum_scatter(picked, 'dp', scatter_dimension=0, tiled=True)  75.7 us
    all_gather x1, waiting for transfers between devices, per_device(): prob_part = lax.all_gather(probabilities, 'dp', axis=0, tiled=True)  45.4 us
    ppermute x4, waiting for transfers between devices, exchange_stage(): got = lax.ppermute(send, 'vocab', perm=perm)  16.6 us
    ppermute x5, waiting for transfers between devices, bruck_all_to_all(): got = lax.ppermute(send, axis_name, perm=perm)  15.5 us
    all_gather x1, waiting for transfers between devices, doubling_all_gather(): offloaded = lax.all_gather(x[:, :half], 'vocab', axis=0, tiled=True)  11.7 us
    ppermute x5, starting transfers between devices, bruck_all_to_all(): got = lax.ppermute(send, axis_name, perm=perm)  10.5 us
    dot_general x1, matrix products, per_device(): jnp.einsum('bd,vd->bv', beam_columns, out_weight, preferred_element_type=...  9.79 us
    all_gather x1, blocking collectives, per_device(): stats = lax.all_gather(jnp.stack([local_max, local_total]), 'vocab', axis=0)  9.08 us
  transfers between devices with their start and end apart: 21, of which 18 were waited for; matrix products, arithmetic and copies ran while one was open for 1% of the time, Pallas kernels for 0%

profile of v17, /device:TPU:0, one launch (start us, length us, event | category | flops | bytes accessed | tf_op | source)
XLA Modules:
  0.0 268.7 jit_solution(2758251007320273070)
XLA Ops:
  7.3 1.0 constant_dynamic-slice_fusion.6
  8.3 0.6 collective-permute-start
  8.8 1.0 collective-permute-done
  9.9 2.9 %collective-permute-start.1 = (bf16[2,2,16,1024]{3,2,1,0:T(8,128)(2,1)S(1)}, bf16[2,2,16,1024]{3,2,1,0:T(8,128)(2,1)S(1)}, u32[]{:S(2)}, u32[]{:S(2)}) collective-permute-start(bf16[2,2,16,1024]{3,2,1,0:T(8,128)(2,1)S(1)} %get-tuple-element.23), channel_id=1, source_target_pairs={{0,2},{1,3},{2,0},{3,1},{4,6},{5,7},{6,4},{7,5},{8,10},{9,11},{10,... | collective-permute-start | bytes 393224 | tf_op jit(solution)/shard_map/hidden_spread/ppermute | solution.py:93
  12.8 3.8 %collective-permute-done.1 = bf16[2,2,16,1024]{3,2,1,0:T(8,128)(2,1)S(1)} collective-permute-done((bf16[2,2,16,1024]{3,2,1,0:T(8,128)(2,1)S(1)}, bf16[2,2,16,1024]{3,2,1,0:T(8,128)(2,1)S(1)}, u32[]{:S(2)}, u32[]{:S(2)}) %collective-permute-start.1) | collective-permute-done | bytes 131104 | tf_op jit(solution)/shard_map/hidden_spread/ppermute | solution.py:93
  16.6 1.8 collective-permute-start.2
  18.5 3.2 %collective-permute-done.2 = bf16[2,2,16,1024]{3,2,1,0:T(8,128)(2,1)S(1)} collective-permute-done((bf16[2,2,16,1024]{3,2,1,0:T(8,128)(2,1)S(1)}, bf16[2,2,16,1024]{3,2,1,0:T(8,128)(2,1)S(1)}, u32[]{:S(2)}, u32[]{:S(2)}) %collective-permute-start.2) | collective-permute-done | bytes 131104 | tf_op jit(solution)/shard_map/hidden_spread/ppermute | solution.py:93
  21.8 0.2 reshape.526
  22.0 0.2 copy.51
  22.2 1.9 collective-permute-start.3
  24.1 3.1 %collective-permute-done.3 = bf16[2,16,2048]{2,1,0:T(8,128)(2,1)S(1)} collective-permute-done((bf16[2,16,2048]{2,1,0:T(8,128)(2,1)S(1)}, bf16[2,16,2048]{2,1,0:T(8,128)(2,1)S(1)}, u32[]{:S(2)}, u32[]{:S(2)}) %collective-permute-start.3) | collective-permute-done | bytes 131104 | tf_op jit(solution)/shard_map/hidden_spread/ppermute | solution.py:93
  27.3 3.3 %collective-permute-start.4 = (bf16[2,16,2048]{2,1,0:T(8,128)(2,1)S(1)}, bf16[2,16,2048]{2,1,0:T(8,128)(2,1)S(1)}, u32[]{:S(2)}, u32[]{:S(2)}) collective-permute-start(bf16[2,16,2048]{2,1,0:T(8,128)(2,1)S(1)} %get-tuple-element.17), channel_id=1, source_target_pairs={{0,16},{8,24},{16,0},{24,8},{1,17},{9,25},{17,1},{25,9},{2,18},{10... | collective-permute-start | bytes 393224 | tf_op jit(solution)/shard_map/hidden_spread/ppermute | solution.py:93
  30.6 4.4 %collective-permute-done.4 = bf16[2,16,2048]{2,1,0:T(8,128)(2,1)S(1)} collective-permute-done((bf16[2,16,2048]{2,1,0:T(8,128)(2,1)S(1)}, bf16[2,16,2048]{2,1,0:T(8,128)(2,1)S(1)}, u32[]{:S(2)}, u32[]{:S(2)}) %collective-permute-start.4) | collective-permute-done | bytes 131104 | tf_op jit(solution)/shard_map/hidden_spread/ppermute | solution.py:93
  35.0 0.7 slice.91
  35.7 0.0 reduce-scatter.2.cloned.1.call-start
  35.8 1.6 collective-permute-start.5
  37.4 0.1 reshape.533
  37.4 1.5 collective-permute-start.8
  39.0 1.2 collective-permute-done.5
  40.2 1.6 collective-permute-start.6
  41.8 1.5 collective-permute-start.9
  43.4 3.8 %collective-permute-done.9 = bf16[2,64,512]{2,1,0:T(8,128)(2,1)S(1)} collective-permute-done((bf16[2,64,512]{2,1,0:T(8,128)(2,1)S(1)}, bf16[2,64,512]{2,1,0:T(8,128)(2,1)S(1)}, u32[]{:S(2)}, u32[]{:S(2)}) %collective-permute-start.9) | collective-permute-done | bytes 131104 | tf_op jit(solution)/shard_map/hidden_spread/hidden_gather_stage/ppermute | solution.py:46
  47.2 0.1 collective-permute-start.10
  47.3 0.6 collective-permute-start.7
  48.0 0.8 collective-permute-done.10
  48.8 0.1 maximum_select_fusion.1
  49.0 0.2 collective-permute-done.7
  49.2 0.1 maximum_select_fusion
  49.3 11.7 %all-gather.4.cloned.1.call-done = bf16[512,1024]{1,0:T(8,128)(2,1)} async-done(((bf16[64,1024]{1,0:T(8,128)(2,1)}), bf16[512,1024]{1,0:T(8,128)(2,1)}) %all-gather.4.cloned.1.call-update) | async-done | bytes 1048592 | tf_op jit(solution)/shard_map/hidden_spread/all_gather | solution.py:58
  61.0 1.5 pad_maximum_fusion
  62.4 0.2 copy.60
  62.7 9.8 %fusion.25 = f32[4,128,19,128]{3,1,2,0:T(8,128)} fusion(bf16[4,128,2048,1]{2,1,3,0:T(8,128)(2,1)S(1)} %bitcast.172, bf16[19,128,2048,1]{2,1,0,3:T(8,128)(2,1)} %bitcast.218), kind=kOutput, calls=%fused_computation.98 | convolution fusion | flops 5100273664 | bytes 17039360 | tf_op jit(solution)/shard_map/dense_logits/bd,vd->bv/dot_general | solution.py:126
  72.5 5.3 %gather_fusion = f32[64,128,128]{2,1,0:T(8,128)} fusion(f32[4,128,19,128]{3,1,2,0:T(8,128)} %fusion.25, s32[64]{0:T(128)S(1)} %reshape.533), kind=kCustom, calls=%fused_computation | custom fusion | bytes 8389120 | tf_op jit(solution)/shard_map/dense_logits/gather | solution.py:131
  77.8 0.6 constant_dynamic-slice_fusion.7
  78.4 0.6 iota_compare_fusion.1
  79.1 75.7 %reduce-scatter.2.cloned.1.call-done = f32[1,16,128,128]{3,2,1,0:T(8,128)} async-done(((f32[4,16,128,128]{3,2,1,0:T(8,128)}), f32[1,16,128,128]{3,2,1,0:T(8,128)}) %reduce-scatter.2.cloned.1.call-update) | async-done | bytes 1048592 | tf_op jit(solution)/shard_map/reduce_scatter | solution.py:133
  154.7 1.5 select_reduce_fusion
  156.3 1.6 exponential_reduce_fusion
  157.8 9.1 %all-gather = f32[16,1,128]{2,1,0:T(1,128)S(1)} all-gather(f32[2,1,128]{2,1,0:T(1,128)S(1)} %pad_maximum_fusion.7), channel_id=2, replica_groups=mesh['dp'=4,'vocab'=8] {'vocab'}, dimensions={0}, use_global_device_ids=true | all-gather | bytes 9216 | tf_op jit(solution)/shard_map/softmax_stats/all_gather | solution.py:141
  167.0 1.6 select_convert_fusion
  168.6 45.4 %all-gather.6.cloned.1.call-done = bf16[4,16,128,128]{3,2,1,0:T(8,128)(2,1)} async-done(((bf16[1,16,128,128]{3,2,1,0:T(8,128)(2,1)}), bf16[4,16,128,128]{3,2,1,0:T(8,128)(2,1)}) %all-gather.6.cloned.1.call-update) | async-done | bytes 2097168 | tf_op jit(solution)/shard_map/all_gather | solution.py:148
  214.0 1.7 constant_dynamic-slice_fusion.1
  215.7 0.9 fusion.2
  216.7 5.8 %convolution_bitcast_fusion = f32[4,64,2048]{2,1,0:T(8,128)S(1)} fusion(bf16[19,128,2048,1]{2,1,0,3:T(8,128)(2,1)} %bitcast.219, bf16[4,64,19,128]{3,2,1,0:T(8,128)(2,1)S(1)} %fusion.2), kind=kOutput, calls=%fused_computation.1 | convolution fusion | flops 2550136832 | bytes 13303808 | tf_op jit(solution)/shard_map/dense_expected/brkt,ktd->brd/dot_general | solution.py:165
  222.5 0.1 collective-permute-start.11
  222.6 0.9 fusion.1
  223.5 3.2 %collective-permute-done.11 = f32[4,64,2048]{2,1,0:T(8,128)S(1)} collective-permute-done((f32[4,64,2048]{2,1,0:T(8,128)S(1)}, f32[4,64,2048]{2,1,0:T(8,128)S(1)}, u32[]{:S(2)}, u32[]{:S(2)}) %collective-permute-start.11) | collective-permute-done | bytes 2097184 | tf_op jit(solution)/shard_map/summed_core_stage/ppermute | solution.py:27
  226.8 3.0 %fusion = f32[4,64,2048]{2,1,0:T(8,128)S(1)} fusion(f32[4,64,2048]{2,1,0:T(8,128)S(1)} %collective-permute-done.11, bf16[19,128,2048,1]{2,1,0,3:T(8,128)(2,1)S(1)} %bitcast.222, bf16[4,64,19,128]{3,2,1,0:T(8,128)(2,1)S(1)} %fusion.1), kind=kOutput, calls=%fused_computation.3 | convolution fusion | flops 2550661120 | bytes 15400960 | tf_op jit(solution)/shard_map/dense_expected/brkt,ktd->brd/dot_general | solution.py:165
  229.7 0.1 fusion.23
  229.9 1.5 collective-permute-start.14
  231.5 1.5 collective-permute-start.12
  233.0 10.9 %collective-permute-done.14 = f32[2,64,1024]{2,1,0:T(8,128)S(1)} collective-permute-done((f32[2,64,1024]{2,1,0:T(8,128)S(1)}, f32[2,64,1024]{2,1,0:T(8,128)S(1)}, u32[]{:S(2)}, u32[]{:S(2)}) %collective-permute-start.14) | collective-permute-done | bytes 524320 | tf_op jit(solution)/shard_map/summed_chip_stage/ppermute | solution.py:18
  244.0 0.1 bitcast_add_fusion
  244.1 1.5 collective-permute-start.15
  245.6 0.1 bitcast_add_fusion.1
  245.7 1.5 collective-permute-start.13
  247.3 4.4 %collective-permute-done.15 = f32[64,1024]{1,0:T(8,128)S(1)} collective-permute-done((f32[64,1024]{1,0:T(8,128)S(1)}, f32[64,1024]{1,0:T(8,128)S(1)}, u32[]{:S(2)}, u32[]{:S(2)}) %collective-permute-start.15) | collective-permute-done | bytes 262176 | tf_op jit(solution)/shard_map/summed_chip_stage/ppermute | solution.py:18
  251.7 1.3 collective-permute-done.13
  253.0 0.1 multiply_reduce_fusion
  253.2 0.2 collective-permute-start.16
  253.4 3.4 %collective-permute-done.16 = f32[64]{0:T(128)S(1)} collective-permute-done((f32[64]{0:T(128)S(1)}, f32[64]{0:T(128)S(1)}, u32[]{:S(2)}, u32[]{:S(2)}) %collective-permute-start.16) | collective-permute-done | bytes 288 | tf_op jit(solution)/shard_map/ppermute | solution.py:75
  256.8 1.2 collective-permute-start.17
  258.0 3.2 %collective-permute-done.17 = f32[64]{0:T(128)S(1)} collective-permute-done((f32[64]{0:T(128)S(1)}, f32[64]{0:T(128)S(1)}, u32[]{:S(2)}, u32[]{:S(2)}) %collective-permute-start.17) | collective-permute-done | bytes 288 | tf_op jit(solution)/shard_map/ppermute | solution.py:75
  261.3 0.9 fusion.5
  (68 shorter events, 1.1 us)
Async XLA Ops:
  7.2 70.7 %copy-start = (s32[1,4]{1,0:T(1,128)S(1)}, s32[1,4]{1,0:T(1,128)}, u32[]{:S(2)}) copy-start(s32[1,4]{1,0:T(1,128)} %param.7) | copy-start | bytes 52
  7.2 53.8 %all-gather.4.cloned.1.call-start = ((), (), s32[]{:S(2)}) async-start(), calls=%async_computation.1 | async-start | bytes 1179648 | tf_op jit(solution)/shard_map/hidden_spread/all_gather | solution.py:58
  8.3 1.5 collective-permute-start
  9.9 6.7 %collective-permute-start.1 = (bf16[2,2,16,1024]{3,2,1,0:T(8,128)(2,1)S(1)}, bf16[2,2,16,1024]{3,2,1,0:T(8,128)(2,1)S(1)}, u32[]{:S(2)}, u32[]{:S(2)}) collective-permute-start(bf16[2,2,16,1024]{3,2,1,0:T(8,128)(2,1)S(1)} %get-tuple-element.23), channel_id=1, source_target_pairs={{0,2},{1,3},{2,0},{3,1},{4,6},{5,7},{6,4},{7,5},{8,10},{9,11},{10,... | collective-permute-start | bytes 393224 | tf_op jit(solution)/shard_map/hidden_spread/ppermute | solution.py:93
  16.6 5.0 %collective-permute-start.2 = (bf16[2,2,16,1024]{3,2,1,0:T(8,128)(2,1)S(1)}, bf16[2,2,16,1024]{3,2,1,0:T(8,128)(2,1)S(1)}, u32[]{:S(2)}, u32[]{:S(2)}) collective-permute-start(bf16[2,2,16,1024]{3,2,1,0:T(8,128)(2,1)S(1)} %get-tuple-element.21), channel_id=1, source_target_pairs={{0,4},{1,5},{2,6},{3,7},{4,0},{5,1},{6,2},{7,3},{8,12},{9,13},{10,... | collective-permute-start | bytes 393224 | tf_op jit(solution)/shard_map/hidden_spread/ppermute | solution.py:93
  22.2 15.2 %copy-start.2 = (s32[1,4,16]{2,1,0:T(4,128)S(1)}, s32[1,4,16]{2,1,0:T(4,128)}, u32[]{:S(2)}) copy-start(s32[1,4,16]{2,1,0:T(4,128)} %param.6) | copy-start | bytes 772
  22.2 5.0 %collective-permute-start.3 = (bf16[2,16,2048]{2,1,0:T(8,128)(2,1)S(1)}, bf16[2,16,2048]{2,1,0:T(8,128)(2,1)S(1)}, u32[]{:S(2)}, u32[]{:S(2)}) collective-permute-start(bf16[2,16,2048]{2,1,0:T(8,128)(2,1)S(1)} %get-tuple-element.19), channel_id=1, source_target_pairs={{0,8},{8,0},{16,24},{24,16},{1,9},{9,1},{17,25},{25,17},{2,10},{10... | collective-permute-start | bytes 393224 | tf_op jit(solution)/shard_map/hidden_spread/ppermute | solution.py:93
  27.3 7.6 %collective-permute-start.4 = (bf16[2,16,2048]{2,1,0:T(8,128)(2,1)S(1)}, bf16[2,16,2048]{2,1,0:T(8,128)(2,1)S(1)}, u32[]{:S(2)}, u32[]{:S(2)}) collective-permute-start(bf16[2,16,2048]{2,1,0:T(8,128)(2,1)S(1)} %get-tuple-element.17), channel_id=1, source_target_pairs={{0,16},{8,24},{16,0},{24,8},{1,17},{9,25},{17,1},{25,9},{2,18},{10... | collective-permute-start | bytes 393224 | tf_op jit(solution)/shard_map/hidden_spread/ppermute | solution.py:93
  35.7 119.0 %reduce-scatter.2.cloned.1.call-start = ((), (), s32[]{:S(2)}) async-start(), calls=%async_computation.2 | async-start | bytes 5242880 | tf_op jit(solution)/shard_map/reduce_scatter | solution.py:133
  35.8 4.4 %collective-permute-start.5 = (bf16[64,512]{1,0:T(8,128)(2,1)S(1)}, bf16[64,512]{1,0:T(8,128)(2,1)S(1)}, u32[]{:S(2)}, u32[]{:S(2)}) collective-permute-start(bf16[64,512]{1,0:T(8,128)(2,1)S(1)} %get-tuple-element.10), channel_id=1, source_target_pairs={{0,2},{1,3},{2,0},{3,1},{4,6},{5,7},{6,4},{7,5},{8,10},{9,11},{10,... | collective-permute-start | bytes 196616 | tf_op jit(solution)/shard_map/hidden_spread/hidden_gather_stage/ppermute | solution.py:46
  37.4 4.3 %collective-permute-start.8 = (bf16[64,512]{1,0:T(8,128)(2,1)S(1)}, bf16[64,512]{1,0:T(8,128)(2,1)S(1)}, u32[]{:S(2)}, u32[]{:S(2)}) collective-permute-start(bf16[64,512]{1,0:T(8,128)(2,1)S(1)} %get-tuple-element.11), channel_id=1, source_target_pairs={{0,4},{1,5},{2,6},{3,7},{4,0},{5,1},{6,2},{7,3},{8,12},{9,13},{10,... | collective-permute-start | bytes 196616 | tf_op jit(solution)/shard_map/hidden_spread/hidden_gather_stage/ppermute | solution.py:46
  40.2 7.1 %collective-permute-start.6 = (bf16[2,64,512]{2,1,0:T(8,128)(2,1)S(1)}, bf16[2,64,512]{2,1,0:T(8,128)(2,1)S(1)}, u32[]{:S(2)}, u32[]{:S(2)}) collective-permute-start(bf16[2,64,512]{2,1,0:T(8,128)(2,1)S(1)} %maximum_select_fusion.10), channel_id=1, source_target_pairs={{0,4},{1,5},{2,6},{3,7},{4,0},{5,1},{6,2},{7,3},{8,12},{9,13},{10,... | collective-permute-start | bytes 393224 | tf_op jit(solution)/shard_map/hidden_spread/hidden_gather_stage/ppermute | solution.py:46
  41.8 5.4 %collective-permute-start.9 = (bf16[2,64,512]{2,1,0:T(8,128)(2,1)S(1)}, bf16[2,64,512]{2,1,0:T(8,128)(2,1)S(1)}, u32[]{:S(2)}, u32[]{:S(2)}) collective-permute-start(bf16[2,64,512]{2,1,0:T(8,128)(2,1)S(1)} %maximum_select_fusion.12), channel_id=1, source_target_pairs={{0,2},{1,3},{2,0},{3,1},{4,6},{5,7},{6,4},{7,5},{8,10},{9,11},{10,... | collective-permute-start | bytes 393224 | tf_op jit(solution)/shard_map/hidden_spread/hidden_gather_stage/ppermute | solution.py:46
  47.2 1.6 collective-permute-start.10
  47.3 1.9 collective-permute-start.7
  77.8 136.2 %all-gather.6.cloned.1.call-start = ((), (), s32[]{:S(2)}) async-start(), calls=%async_computation.3 | async-start | bytes 2621440 | tf_op jit(solution)/shard_map/all_gather | solution.py:148
  154.7 12.2 %copy-start.1 = (f32[1,16,128,128]{3,2,1,0:T(8,128)S(1)}, f32[1,16,128,128]{3,2,1,0:T(8,128)}, u32[]{:S(2)}) copy-start(f32[1,16,128,128]{3,2,1,0:T(8,128)} %reduce-scatter.2.cloned.1.call-done) | copy-start | bytes 3145732
  215.7 11.0 %slice-start = ((s8[9961472]{0:T(1024)(128)(4,1)}), s8[4194304]{0:T(1024)(128)(4,1)S(1)}, s32[]{:S(2)}) async-start(s8[9961472]{0:T(1024)(128)(4,1)} %bitcast.220), calls=%async_computation.4 | async-start | bytes 8388608
  216.7 10.1 %slice-start.1 = ((s8[9961472]{0:T(1024)(128)(4,1)}), s8[4194304]{0:T(1024)(128)(4,1)S(1)}, s32[]{:S(2)}) async-start(s8[9961472]{0:T(1024)(128)(4,1)} %bitcast.220), calls=%async_computation.5 | async-start | bytes 8388608
  216.7 10.1 %slice-start.2 = ((s8[9961472]{0:T(1024)(128)(4,1)}), s8[1572864]{0:T(1024)(128)(4,1)S(1)}, s32[]{:S(2)}) async-start(s8[9961472]{0:T(1024)(128)(4,1)} %bitcast.220), calls=%async_computation.6 | async-start | bytes 3145728
  222.5 4.2 %collective-permute-start.11 = (f32[4,64,2048]{2,1,0:T(8,128)S(1)}, f32[4,64,2048]{2,1,0:T(8,128)S(1)}, u32[]{:S(2)}, u32[]{:S(2)}) collective-permute-start(f32[4,64,2048]{2,1,0:T(8,128)S(1)} %convolution_bitcast_fusion), channel_id=1, source_target_pairs={{0,1},{1,0},{2,3},{3,2},{4,5},{5,4},{6,7},{7,6},{8,9},{9,8},{10,11... | collective-permute-start | bytes 6291464 | tf_op jit(solution)/shard_map/summed_core_stage/ppermute | solution.py:27
  229.9 14.0 %collective-permute-start.14 = (f32[2,64,1024]{2,1,0:T(8,128)S(1)}, f32[2,64,1024]{2,1,0:T(8,128)S(1)}, u32[]{:S(2)}, u32[]{:S(2)}) collective-permute-start(f32[2,64,1024]{2,1,0:T(8,128)S(1)} %dynamic-slice_bitcast_fusion), channel_id=1, source_target_pairs={{0,4},{1,5},{2,6},{3,7},{4,0},{5,1},{6,2},{7,3},{8,12},{9,13},{10,... | collective-permute-start | bytes 1572872 | tf_op jit(solution)/shard_map/summed_chip_stage/ppermute | solution.py:18
  231.5 14.1 %collective-permute-start.12 = (f32[2,64,1024]{2,1,0:T(8,128)S(1)}, f32[2,64,1024]{2,1,0:T(8,128)S(1)}, u32[]{:S(2)}, u32[]{:S(2)}) collective-permute-start(f32[2,64,1024]{2,1,0:T(8,128)S(1)} %dynamic-slice_bitcast_fusion.1), channel_id=1, source_target_pairs={{0,2},{1,3},{2,0},{3,1},{4,6},{5,7},{6,4},{7,5},{8,10},{9,11},{10,... | collective-permute-start | bytes 1572872 | tf_op jit(solution)/shard_map/summed_chip_stage/ppermute | solution.py:18
  244.1 7.5 %collective-permute-start.15 = (f32[64,1024]{1,0:T(8,128)S(1)}, f32[64,1024]{1,0:T(8,128)S(1)}, u32[]{:S(2)}, u32[]{:S(2)}) collective-permute-start(f32[64,1024]{1,0:T(8,128)S(1)} %dynamic-slice_bitcast_fusion.2), channel_id=1, source_target_pairs={{0,2},{1,3},{2,0},{3,1},{4,6},{5,7},{6,4},{7,5},{8,10},{9,11},{10,... | collective-permute-start | bytes 786440 | tf_op jit(solution)/shard_map/summed_chip_stage/ppermute | solution.py:18
  245.7 7.3 %collective-permute-start.13 = (f32[64,1024]{1,0:T(8,128)S(1)}, f32[64,1024]{1,0:T(8,128)S(1)}, u32[]{:S(2)}, u32[]{:S(2)}) collective-permute-start(f32[64,1024]{1,0:T(8,128)S(1)} %dynamic-slice_bitcast_fusion.3), channel_id=1, source_target_pairs={{0,4},{1,5},{2,6},{3,7},{4,0},{5,1},{6,2},{7,3},{8,12},{9,13},{10,... | collective-permute-start | bytes 786440 | tf_op jit(solution)/shard_map/summed_chip_stage/ppermute | solution.py:18
  253.2 3.6 %collective-permute-start.16 = (f32[64]{0:T(128)S(1)}, f32[64]{0:T(128)S(1)}, u32[]{:S(2)}, u32[]{:S(2)}) collective-permute-start(f32[64]{0:T(128)S(1)} %multiply_reduce_fusion), channel_id=1, source_target_pairs={{0,8},{8,0},{16,24},{24,16},{1,9},{9,1},{17,25},{25,17},{2,10},{10... | collective-permute-start | bytes 776 | tf_op jit(solution)/shard_map/ppermute | solution.py:75
  256.8 4.5 %collective-permute-start.17 = (f32[64]{0:T(128)S(1)}, f32[64]{0:T(128)S(1)}, u32[]{:S(2)}, u32[]{:S(2)}) collective-permute-start(f32[64]{0:T(128)S(1)} %add.156), channel_id=1, source_target_pairs={{0,16},{8,24},{16,0},{24,8},{1,17},{9,25},{17,1},{25,9},{2,18},{10... | collective-permute-start | bytes 776 | tf_op jit(solution)/shard_map/ppermute | solution.py:75
Sparse Core Ops, SparseCore 0:
  35.9 25.0 all-gather.3
  77.9 76.7 reduce-scatter.1
  168.7 45.2 all-gather.5

commit v18 on v11

--- a/solution.py
+++ b/solution.py
@@ -114,19 +114,14 @@
         plane_rows = bruck_all_to_all(row_slices, "dp", n_dp, split_axis=1, concat_axis=0)
         gathered = doubling_all_gather(plane_rows, n_vocab)
         group = hidden.shape[0] // n_vocab
-        beam_columns = (
-            gathered.reshape(n_vocab, n_dp, group, columns_here)
-            .transpose(1, 0, 2, 3)
-            .reshape(n_dp * n_vocab * group, columns_here)
-        )
 
     with jax.named_scope("dense_logits"):
         full = jnp.einsum(
-            "bd,vd->bv", beam_columns, out_weight, preferred_element_type=jnp.float32
+            "bd,vd->bv", gathered, out_weight, preferred_element_type=jnp.float32
         )
-        full4 = full.reshape(n_blk, BB, n_tb, TB)
+        full6 = full.reshape(n_vocab, n_blk, group, n_tb, TB)
         rows = jnp.arange(n_blk, dtype=jnp.int32)[:, None]
-        picked = full4[rows, :, block_lists, :]
+        picked = full6[:, rows, :, block_lists, :].reshape(n_blk, MOST, BB, TB)
 
     logits = lax.psum_scatter(picked, "dp", scatter_dimension=0, tiled=True)
 

time: 260 us -> 260 us (level)
  transfers between devices with their start and end apart: 20 -> 20, of which waited for: 19 -> 18; matrix products, arithmetic and copies ran while one was open for 1% -> 1% of each run, Pallas kernels for 0% -> 0%
where the time goes in v18:
time: 260 us
  waiting for transfers between devices  175 us (67%)
  starting transfers between devices  23.6 us (9%)
  matrix products  20.3 us (8%)
  between operations  14.5 us (6%)
  local copies, waits for them, and re-layouts  9.32 us (4%)
  blocking collectives  9.1 us (4%)
  other arithmetic  7.59 us (3%)
    reduce_scatter x1, waiting for transfers between devices, per_device(): logits = lax.psum_scatter(picked, 'dp', scatter_dimension=0, tiled=True)  76.7 us
    all_gather x1, waiting for transfers between devices, per_device(): prob_part = lax.all_gather(probabilities, 'dp', axis=0, tiled=True)  45.4 us
    ppermute x4, waiting for transfers between devices, exchange_stage(): got = lax.ppermute(send, 'vocab', perm=perm)  16.6 us
    ppermute x5, waiting for transfers between devices, bruck_all_to_all(): got = lax.ppermute(send, axis_name, perm=perm)  15.5 us
    ppermute x6, waiting for transfers between devices, gather_stage(): got = lax.ppermute(x, 'vocab', perm=perm)  11.2 us
    ppermute x5, starting transfers between devices, bruck_all_to_all(): got = lax.ppermute(send, axis_name, perm=perm)  10.5 us
    dot_general x1, matrix products, per_device(): jnp.einsum('bd,vd->bv', gathered, out_weight, preferred_element_type=jnp....  9.84 us
    all_gather x1, blocking collectives, per_device(): stats = lax.all_gather(jnp.stack([local_max, local_total]), 'vocab', axis=0)  9.1 us
  transfers between devices with their start and end apart: 20, of which 18 were waited for; matrix products, arithmetic and copies ran while one was open for 1% of the time, Pallas kernels for 0%

profile of v18, /device:TPU:0, one launch (start us, length us, event | category | flops | bytes accessed | tf_op | source)
XLA Modules:
  0.0 259.7 jit_solution(7552805806521408125)
XLA Ops:
  7.3 1.0 constant_dynamic-slice_fusion.4
  8.3 0.6 collective-permute-start
  8.8 1.0 collective-permute-done
  9.9 2.9 %collective-permute-start.1 = (bf16[2,2,16,1024]{3,2,1,0:T(8,128)(2,1)S(1)}, bf16[2,2,16,1024]{3,2,1,0:T(8,128)(2,1)S(1)}, u32[]{:S(2)}, u32[]{:S(2)}) collective-permute-start(bf16[2,2,16,1024]{3,2,1,0:T(8,128)(2,1)S(1)} %get-tuple-element.27), channel_id=1, source_target_pairs={{0,2},{1,3},{2,0},{3,1},{4,6},{5,7},{6,4},{7,5},{8,10},{9,11},{10,... | collective-permute-start | bytes 393224 | tf_op jit(solution)/shard_map/hidden_spread/ppermute | solution.py:91
  12.8 3.8 %collective-permute-done.1 = bf16[2,2,16,1024]{3,2,1,0:T(8,128)(2,1)S(1)} collective-permute-done((bf16[2,2,16,1024]{3,2,1,0:T(8,128)(2,1)S(1)}, bf16[2,2,16,1024]{3,2,1,0:T(8,128)(2,1)S(1)}, u32[]{:S(2)}, u32[]{:S(2)}) %collective-permute-start.1) | collective-permute-done | bytes 131104 | tf_op jit(solution)/shard_map/hidden_spread/ppermute | solution.py:91
  16.6 1.8 collective-permute-start.2
  18.5 3.2 %collective-permute-done.2 = bf16[2,2,16,1024]{3,2,1,0:T(8,128)(2,1)S(1)} collective-permute-done((bf16[2,2,16,1024]{3,2,1,0:T(8,128)(2,1)S(1)}, bf16[2,2,16,1024]{3,2,1,0:T(8,128)(2,1)S(1)}, u32[]{:S(2)}, u32[]{:S(2)}) %collective-permute-start.2) | collective-permute-done | bytes 131104 | tf_op jit(solution)/shard_map/hidden_spread/ppermute | solution.py:91
  21.9 1.9 collective-permute-start.3
  23.8 3.1 %collective-permute-done.3 = bf16[2,16,2048]{2,1,0:T(8,128)(2,1)S(1)} collective-permute-done((bf16[2,16,2048]{2,1,0:T(8,128)(2,1)S(1)}, bf16[2,16,2048]{2,1,0:T(8,128)(2,1)S(1)}, u32[]{:S(2)}, u32[]{:S(2)}) %collective-permute-start.3) | collective-permute-done | bytes 131104 | tf_op jit(solution)/shard_map/hidden_spread/ppermute | solution.py:91
  27.0 3.3 %collective-permute-start.4 = (bf16[2,16,2048]{2,1,0:T(8,128)(2,1)S(1)}, bf16[2,16,2048]{2,1,0:T(8,128)(2,1)S(1)}, u32[]{:S(2)}, u32[]{:S(2)}) collective-permute-start(bf16[2,16,2048]{2,1,0:T(8,128)(2,1)S(1)} %get-tuple-element.21), channel_id=1, source_target_pairs={{0,16},{8,24},{16,0},{24,8},{1,17},{9,25},{17,1},{25,9},{2,18},{10... | collective-permute-start | bytes 393224 | tf_op jit(solution)/shard_map/hidden_spread/ppermute | solution.py:91
  30.3 4.4 %collective-permute-done.4 = bf16[2,16,2048]{2,1,0:T(8,128)(2,1)S(1)} collective-permute-done((bf16[2,16,2048]{2,1,0:T(8,128)(2,1)S(1)}, bf16[2,16,2048]{2,1,0:T(8,128)(2,1)S(1)}, u32[]{:S(2)}, u32[]{:S(2)}) %collective-permute-start.4) | collective-permute-done | bytes 131104 | tf_op jit(solution)/shard_map/hidden_spread/ppermute | solution.py:91
  34.7 0.1 slice_bitcast_fusion.15
  34.8 1.6 collective-permute-start.5
  36.4 0.1 reshape.537
  36.5 1.5 collective-permute-start.8
  38.0 3.3 %collective-permute-done.5 = bf16[64,1024]{1,0:T(8,128)(2,1)S(1)} collective-permute-done((bf16[64,1024]{1,0:T(8,128)(2,1)S(1)}, bf16[64,1024]{1,0:T(8,128)(2,1)S(1)}, u32[]{:S(2)}, u32[]{:S(2)}) %collective-permute-start.5) | collective-permute-done | bytes 131104 | tf_op jit(solution)/shard_map/hidden_spread/hidden_gather_stage/ppermute | solution.py:46
  41.3 1.5 collective-permute-done.8
  42.9 0.6 collective-permute-start.9
  43.5 1.6 collective-permute-start.6
  45.1 4.2 %collective-permute-done.9 = bf16[2,64,1024]{2,1,0:T(8,128)(2,1)S(1)} collective-permute-done((bf16[2,64,1024]{2,1,0:T(8,128)(2,1)S(1)}, bf16[2,64,1024]{2,1,0:T(8,128)(2,1)S(1)}, u32[]{:S(2)}, u32[]{:S(2)}) %collective-permute-start.9) | collective-permute-done | bytes 262176 | tf_op jit(solution)/shard_map/hidden_spread/hidden_gather_stage/ppermute | solution.py:46
  49.4 0.1 collective-permute-start.10
  49.4 0.5 collective-permute-done.6
  49.9 0.1 maximum_select_fusion.3
  50.0 0.1 collective-permute-start.7
  50.1 0.1 pad_maximum_fusion
  50.2 0.1 maximum_select_fusion.2
  50.3 0.1 copy_select_fusion
  50.3 1.7 collective-permute-done.7
  52.1 0.2 maximum_select_fusion
  52.3 0.1 copy.13
  52.3 0.1 maximum_select_fusion.1
  52.4 9.8 %fusion.1 = f32[8,4,16,19,128]{4,2,3,1,0:T(8,128)} fusion(bf16[19,128,2048,1,1]{2,1,0,4,3:T(8,128)(2,1)} %bitcast.204, bf16[8,4,16,1024]{3,2,1,0:T(8,128)(2,1)S(1)} %bitcast.179, bf16[8,4,16,1024]{3,2,1,0:T(8,128)(2,1)S(1)} %bitcast.181), kind=kOutput, calls=%fused_computation.7 | convolution fusion | flops 5104467968 | bytes 17039360 | tf_op jit(solution)/shard_map/dense_logits/bd,vd->bv/dot_general | solution.py:119
  62.3 5.3 %gather_fusion = f32[64,8,16,128]{3,2,1,0:T(8,128)} fusion(f32[8,4,16,19,128]{4,2,3,1,0:T(8,128)} %fusion.1, s32[64]{0:T(128)S(1)} %reshape.537), kind=kCustom, calls=%fused_computation | custom fusion | bytes 8389120 | tf_op jit(solution)/shard_map/dense_logits/gather | solution.py:124
  67.6 0.6 constant_dynamic-slice_fusion.5
  68.2 0.6 iota_compare_fusion.1
  68.9 76.7 %reduce-scatter.2.cloned.1.call-done = f32[1,16,128,128]{3,2,1,0:T(8,128)} async-done(((f32[4,16,128,128]{3,2,1,0:T(8,128)}), f32[1,16,128,128]{3,2,1,0:T(8,128)}) %reduce-scatter.2.cloned.1.call-update) | async-done | bytes 1048592 | tf_op jit(solution)/shard_map/reduce_scatter | solution.py:126
  145.6 1.5 select_reduce_fusion
  147.1 1.6 exponential_reduce_fusion
  148.7 9.1 %all-gather = f32[16,1,128]{2,1,0:T(1,128)S(1)} all-gather(f32[2,1,128]{2,1,0:T(1,128)S(1)} %pad_maximum_fusion.4), channel_id=2, replica_groups=mesh['dp'=4,'vocab'=8] {'vocab'}, dimensions={0}, use_global_device_ids=true | all-gather | bytes 9216 | tf_op jit(solution)/shard_map/softmax_stats/all_gather | solution.py:134
  157.9 1.6 select_convert_fusion
  159.5 45.4 %all-gather.3.cloned.1.call-done = bf16[4,16,128,128]{3,2,1,0:T(8,128)(2,1)} async-done(((bf16[1,16,128,128]{3,2,1,0:T(8,128)(2,1)}), bf16[4,16,128,128]{3,2,1,0:T(8,128)(2,1)}) %all-gather.3.cloned.1.call-update) | async-done | bytes 2097168 | tf_op jit(solution)/shard_map/all_gather | solution.py:141
  204.9 1.7 dynamic-slice_bitcast_fusion.1
  206.6 0.9 fusion.8
  207.6 5.6 %convolution_bitcast_fusion = f32[4,64,2048]{2,1,0:T(8,128)S(1)} fusion(bf16[19,128,2048,1]{2,1,0,3:T(8,128)(2,1)} %bitcast.205, bf16[4,64,128,19]{2,3,1,0:T(8,128)(2,1)S(1)} %fusion.8), kind=kOutput, calls=%fused_computation.1 | convolution fusion | flops 2550136832 | bytes 13303808 | tf_op jit(solution)/shard_map/dense_expected/brkt,ktd->brd/dot_general | solution.py:158
  213.2 0.1 collective-permute-start.11
  213.3 0.9 fusion.10
  214.3 3.2 %collective-permute-done.11 = f32[4,64,2048]{2,1,0:T(8,128)S(1)} collective-permute-done((f32[4,64,2048]{2,1,0:T(8,128)S(1)}, f32[4,64,2048]{2,1,0:T(8,128)S(1)}, u32[]{:S(2)}, u32[]{:S(2)}) %collective-permute-start.11) | collective-permute-done | bytes 2097184 | tf_op jit(solution)/shard_map/summed_core_stage/ppermute | solution.py:27
  217.5 3.0 %fusion = f32[4,64,2048]{2,1,0:T(8,128)S(1)} fusion(f32[4,64,2048]{2,1,0:T(8,128)S(1)} %collective-permute-done.11, bf16[19,128,2048,1]{2,1,0,3:T(8,128)(2,1)S(1)} %bitcast.208, bf16[4,64,128,19]{2,3,1,0:T(8,128)(2,1)S(1)} %fusion.10), kind=kOutput, calls=%fused_computation.3 | convolution fusion | flops 2550661120 | bytes 15400960 | tf_op jit(solution)/shard_map/dense_expected/brkt,ktd->brd/dot_general | solution.py:158
  220.5 0.1 fusion.30
  220.7 1.5 collective-permute-start.14
  222.2 1.5 collective-permute-start.12
  223.8 10.9 %collective-permute-done.14 = f32[2,64,1024]{2,1,0:T(8,128)S(1)} collective-permute-done((f32[2,64,1024]{2,1,0:T(8,128)S(1)}, f32[2,64,1024]{2,1,0:T(8,128)S(1)}, u32[]{:S(2)}, u32[]{:S(2)}) %collective-permute-start.14) | collective-permute-done | bytes 524320 | tf_op jit(solution)/shard_map/summed_chip_stage/ppermute | solution.py:18
  234.7 0.1 bitcast_add_fusion
  234.8 1.5 collective-permute-start.15
  236.3 0.1 bitcast_add_fusion.1
  236.5 1.5 collective-permute-start.13
  238.0 4.4 %collective-permute-done.15 = f32[64,1024]{1,0:T(8,128)S(1)} collective-permute-done((f32[64,1024]{1,0:T(8,128)S(1)}, f32[64,1024]{1,0:T(8,128)S(1)}, u32[]{:S(2)}, u32[]{:S(2)}) %collective-permute-start.15) | collective-permute-done | bytes 262176 | tf_op jit(solution)/shard_map/summed_chip_stage/ppermute | solution.py:18
  242.4 1.3 collective-permute-done.13
  243.8 0.1 multiply_reduce_fusion
  243.9 0.2 collective-permute-start.16
  244.1 3.4 %collective-permute-done.16 = f32[64]{0:T(128)S(1)} collective-permute-done((f32[64]{0:T(128)S(1)}, f32[64]{0:T(128)S(1)}, u32[]{:S(2)}, u32[]{:S(2)}) %collective-permute-start.16) | collective-permute-done | bytes 288 | tf_op jit(solution)/shard_map/ppermute | solution.py:73
  247.5 1.2 collective-permute-start.17
  248.8 3.2 %collective-permute-done.17 = f32[64]{0:T(128)S(1)} collective-permute-done((f32[64]{0:T(128)S(1)}, f32[64]{0:T(128)S(1)}, u32[]{:S(2)}, u32[]{:S(2)}) %collective-permute-start.17) | collective-permute-done | bytes 288 | tf_op jit(solution)/shard_map/ppermute | solution.py:73
  252.0 0.9 fusion.12
  (60 shorter events, 1.0 us)
Async XLA Ops:
  7.2 60.5 %copy-start = (s32[1,4]{1,0:T(1,128)S(1)}, s32[1,4]{1,0:T(1,128)}, u32[]{:S(2)}) copy-start(s32[1,4]{1,0:T(1,128)} %param.7) | copy-start | bytes 52
  7.2 138.4 %reduce-scatter.2.cloned.1.call-start = ((), (), s32[]{:S(2)}) async-start(), calls=%async_computation.1 | async-start | bytes 5242880 | tf_op jit(solution)/shard_map/reduce_scatter | solution.py:126
  8.3 1.5 collective-permute-start
  9.9 6.7 %collective-permute-start.1 = (bf16[2,2,16,1024]{3,2,1,0:T(8,128)(2,1)S(1)}, bf16[2,2,16,1024]{3,2,1,0:T(8,128)(2,1)S(1)}, u32[]{:S(2)}, u32[]{:S(2)}) collective-permute-start(bf16[2,2,16,1024]{3,2,1,0:T(8,128)(2,1)S(1)} %get-tuple-element.27), channel_id=1, source_target_pairs={{0,2},{1,3},{2,0},{3,1},{4,6},{5,7},{6,4},{7,5},{8,10},{9,11},{10,... | collective-permute-start | bytes 393224 | tf_op jit(solution)/shard_map/hidden_spread/ppermute | solution.py:91
  16.6 5.0 %collective-permute-start.2 = (bf16[2,2,16,1024]{3,2,1,0:T(8,128)(2,1)S(1)}, bf16[2,2,16,1024]{3,2,1,0:T(8,128)(2,1)S(1)}, u32[]{:S(2)}, u32[]{:S(2)}) collective-permute-start(bf16[2,2,16,1024]{3,2,1,0:T(8,128)(2,1)S(1)} %get-tuple-element.25), channel_id=1, source_target_pairs={{0,4},{1,5},{2,6},{3,7},{4,0},{5,1},{6,2},{7,3},{8,12},{9,13},{10,... | collective-permute-start | bytes 393224 | tf_op jit(solution)/shard_map/hidden_spread/ppermute | solution.py:91
  21.8 14.5 %copy-start.2 = (s32[1,4,16]{2,1,0:T(4,128)S(1)}, s32[1,4,16]{2,1,0:T(4,128)}, u32[]{:S(2)}) copy-start(s32[1,4,16]{2,1,0:T(4,128)} %param.6) | copy-start | bytes 772
  21.9 5.0 %collective-permute-start.3 = (bf16[2,16,2048]{2,1,0:T(8,128)(2,1)S(1)}, bf16[2,16,2048]{2,1,0:T(8,128)(2,1)S(1)}, u32[]{:S(2)}, u32[]{:S(2)}) collective-permute-start(bf16[2,16,2048]{2,1,0:T(8,128)(2,1)S(1)} %get-tuple-element.23), channel_id=1, source_target_pairs={{0,8},{8,0},{16,24},{24,16},{1,9},{9,1},{17,25},{25,17},{2,10},{10... | collective-permute-start | bytes 393224 | tf_op jit(solution)/shard_map/hidden_spread/ppermute | solution.py:91
  27.0 7.6 %collective-permute-start.4 = (bf16[2,16,2048]{2,1,0:T(8,128)(2,1)S(1)}, bf16[2,16,2048]{2,1,0:T(8,128)(2,1)S(1)}, u32[]{:S(2)}, u32[]{:S(2)}) collective-permute-start(bf16[2,16,2048]{2,1,0:T(8,128)(2,1)S(1)} %get-tuple-element.21), channel_id=1, source_target_pairs={{0,16},{8,24},{16,0},{24,8},{1,17},{9,25},{17,1},{25,9},{2,18},{10... | collective-permute-start | bytes 393224 | tf_op jit(solution)/shard_map/hidden_spread/ppermute | solution.py:91
  34.8 6.4 %collective-permute-start.5 = (bf16[64,1024]{1,0:T(8,128)(2,1)S(1)}, bf16[64,1024]{1,0:T(8,128)(2,1)S(1)}, u32[]{:S(2)}, u32[]{:S(2)}) collective-permute-start(bf16[64,1024]{1,0:T(8,128)(2,1)S(1)} %get-tuple-element.15), channel_id=1, source_target_pairs={{0,2},{1,3},{2,0},{3,1},{4,6},{5,7},{6,4},{7,5},{8,10},{9,11},{10,... | collective-permute-start | bytes 393224 | tf_op jit(solution)/shard_map/hidden_spread/hidden_gather_stage/ppermute | solution.py:46
  36.5 6.4 %collective-permute-start.8 = (bf16[64,1024]{1,0:T(8,128)(2,1)S(1)}, bf16[64,1024]{1,0:T(8,128)(2,1)S(1)}, u32[]{:S(2)}, u32[]{:S(2)}) collective-permute-start(bf16[64,1024]{1,0:T(8,128)(2,1)S(1)} %get-tuple-element.14), channel_id=1, source_target_pairs={{0,4},{1,5},{2,6},{3,7},{4,0},{5,1},{6,2},{7,3},{8,12},{9,13},{10,... | collective-permute-start | bytes 393224 | tf_op jit(solution)/shard_map/hidden_spread/hidden_gather_stage/ppermute | solution.py:46
  42.9 6.4 %collective-permute-start.9 = (bf16[2,64,1024]{2,1,0:T(8,128)(2,1)S(1)}, bf16[2,64,1024]{2,1,0:T(8,128)(2,1)S(1)}, u32[]{:S(2)}, u32[]{:S(2)}) collective-permute-start(bf16[2,64,1024]{2,1,0:T(8,128)(2,1)S(1)} %maximum_select_fusion.13), channel_id=1, source_target_pairs={{0,2},{1,3},{2,0},{3,1},{4,6},{5,7},{6,4},{7,5},{8,10},{9,11},{10,... | collective-permute-start | bytes 786440 | tf_op jit(solution)/shard_map/hidden_spread/hidden_gather_stage/ppermute | solution.py:46
  43.5 6.4 %collective-permute-start.6 = (bf16[2,64,1024]{2,1,0:T(8,128)(2,1)S(1)}, bf16[2,64,1024]{2,1,0:T(8,128)(2,1)S(1)}, u32[]{:S(2)}, u32[]{:S(2)}) collective-permute-start(bf16[2,64,1024]{2,1,0:T(8,128)(2,1)S(1)} %maximum_select_fusion.11), channel_id=1, source_target_pairs={{0,4},{1,5},{2,6},{3,7},{4,0},{5,1},{6,2},{7,3},{8,12},{9,13},{10,... | collective-permute-start | bytes 786440 | tf_op jit(solution)/shard_map/hidden_spread/hidden_gather_stage/ppermute | solution.py:46
  49.4 3.0 %collective-permute-start.10 = (bf16[2,2,64,1024]{3,2,1,0:T(8,128)(2,1)S(1)}, bf16[2,2,64,1024]{3,2,1,0:T(8,128)(2,1)S(1)}, u32[]{:S(2)}, u32[]{:S(2)}) collective-permute-start(bf16[2,2,64,1024]{3,2,1,0:T(8,128)(2,1)S(1)} %maximum_select_fusion.4), channel_id=1, source_target_pairs={{0,1},{1,0},{2,3},{3,2},{4,5},{5,4},{6,7},{7,6},{8,9},{9,8},{10,11... | collective-permute-start | bytes 1572872 | tf_op jit(solution)/shard_map/hidden_spread/hidden_gather_stage/ppermute | solution.py:46
  50.0 2.1 collective-permute-start.7
  67.6 137.3 %all-gather.3.cloned.1.call-start = ((), (), s32[]{:S(2)}) async-start(), calls=%async_computation.2 | async-start | bytes 2621440 | tf_op jit(solution)/shard_map/all_gather | solution.py:141
  145.6 12.3 %copy-start.1 = (f32[1,16,128,128]{3,2,1,0:T(8,128)S(1)}, f32[1,16,128,128]{3,2,1,0:T(8,128)}, u32[]{:S(2)}) copy-start(f32[1,16,128,128]{3,2,1,0:T(8,128)} %reduce-scatter.2.cloned.1.call-done) | copy-start | bytes 3145732
  207.6 9.9 %slice-start = ((s8[9961472]{0:T(1024)(128)(4,1)}), s8[4194304]{0:T(1024)(128)(4,1)S(1)}, s32[]{:S(2)}) async-start(s8[9961472]{0:T(1024)(128)(4,1)} %bitcast.206), calls=%async_computation.3 | async-start | bytes 8388608
  207.6 9.9 %slice-start.1 = ((s8[9961472]{0:T(1024)(128)(4,1)}), s8[4194304]{0:T(1024)(128)(4,1)S(1)}, s32[]{:S(2)}) async-start(s8[9961472]{0:T(1024)(128)(4,1)} %bitcast.206), calls=%async_computation.4 | async-start | bytes 8388608
  207.6 9.9 %slice-start.2 = ((s8[9961472]{0:T(1024)(128)(4,1)}), s8[1572864]{0:T(1024)(128)(4,1)S(1)}, s32[]{:S(2)}) async-start(s8[9961472]{0:T(1024)(128)(4,1)} %bitcast.206), calls=%async_computation.5 | async-start | bytes 3145728
  213.2 4.2 %collective-permute-start.11 = (f32[4,64,2048]{2,1,0:T(8,128)S(1)}, f32[4,64,2048]{2,1,0:T(8,128)S(1)}, u32[]{:S(2)}, u32[]{:S(2)}) collective-permute-start(f32[4,64,2048]{2,1,0:T(8,128)S(1)} %convolution_bitcast_fusion), channel_id=1, source_target_pairs={{0,1},{1,0},{2,3},{3,2},{4,5},{5,4},{6,7},{7,6},{8,9},{9,8},{10,11... | collective-permute-start | bytes 6291464 | tf_op jit(solution)/shard_map/summed_core_stage/ppermute | solution.py:27
  220.7 14.0 %collective-permute-start.14 = (f32[2,64,1024]{2,1,0:T(8,128)S(1)}, f32[2,64,1024]{2,1,0:T(8,128)S(1)}, u32[]{:S(2)}, u32[]{:S(2)}) collective-permute-start(f32[2,64,1024]{2,1,0:T(8,128)S(1)} %dynamic-slice_bitcast_fusion.2), channel_id=1, source_target_pairs={{0,4},{1,5},{2,6},{3,7},{4,0},{5,1},{6,2},{7,3},{8,12},{9,13},{10,... | collective-permute-start | bytes 1572872 | tf_op jit(solution)/shard_map/summed_chip_stage/ppermute | solution.py:18
  222.2 14.1 %collective-permute-start.12 = (f32[2,64,1024]{2,1,0:T(8,128)S(1)}, f32[2,64,1024]{2,1,0:T(8,128)S(1)}, u32[]{:S(2)}, u32[]{:S(2)}) collective-permute-start(f32[2,64,1024]{2,1,0:T(8,128)S(1)} %dynamic-slice_bitcast_fusion.3), channel_id=1, source_target_pairs={{0,2},{1,3},{2,0},{3,1},{4,6},{5,7},{6,4},{7,5},{8,10},{9,11},{10,... | collective-permute-start | bytes 1572872 | tf_op jit(solution)/shard_map/summed_chip_stage/ppermute | solution.py:18
  234.8 7.5 %collective-permute-start.15 = (f32[64,1024]{1,0:T(8,128)S(1)}, f32[64,1024]{1,0:T(8,128)S(1)}, u32[]{:S(2)}, u32[]{:S(2)}) collective-permute-start(f32[64,1024]{1,0:T(8,128)S(1)} %dynamic-slice_bitcast_fusion.4), channel_id=1, source_target_pairs={{0,2},{1,3},{2,0},{3,1},{4,6},{5,7},{6,4},{7,5},{8,10},{9,11},{10,... | collective-permute-start | bytes 786440 | tf_op jit(solution)/shard_map/summed_chip_stage/ppermute | solution.py:18
  236.5 7.3 %collective-permute-start.13 = (f32[64,1024]{1,0:T(8,128)S(1)}, f32[64,1024]{1,0:T(8,128)S(1)}, u32[]{:S(2)}, u32[]{:S(2)}) collective-permute-start(f32[64,1024]{1,0:T(8,128)S(1)} %dynamic-slice_bitcast_fusion.5), channel_id=1, source_target_pairs={{0,4},{1,5},{2,6},{3,7},{4,0},{5,1},{6,2},{7,3},{8,12},{9,13},{10,... | collective-permute-start | bytes 786440 | tf_op jit(solution)/shard_map/summed_chip_stage/ppermute | solution.py:18
  243.9 3.6 %collective-permute-start.16 = (f32[64]{0:T(128)S(1)}, f32[64]{0:T(128)S(1)}, u32[]{:S(2)}, u32[]{:S(2)}) collective-permute-start(f32[64]{0:T(128)S(1)} %multiply_reduce_fusion), channel_id=1, source_target_pairs={{0,8},{8,0},{16,24},{24,16},{1,9},{9,1},{17,25},{25,17},{2,10},{10... | collective-permute-start | bytes 776 | tf_op jit(solution)/shard_map/ppermute | solution.py:73
  247.5 4.5 %collective-permute-start.17 = (f32[64]{0:T(128)S(1)}, f32[64]{0:T(128)S(1)}, u32[]{:S(2)}, u32[]{:S(2)}) collective-permute-start(f32[64]{0:T(128)S(1)} %add.156), channel_id=1, source_target_pairs={{0,16},{8,24},{16,0},{24,8},{1,17},{9,25},{17,1},{25,9},{2,18},{10... | collective-permute-start | bytes 776 | tf_op jit(solution)/shard_map/ppermute | solution.py:73
Sparse Core Ops, SparseCore 0:
  67.7 77.8 reduce-scatter.1
  159.6 45.2 all-gather.2

commit v19 on v11

--- a/solution.py
+++ b/solution.py
@@ -23,12 +23,14 @@
     levels = n.bit_length() - 1
     _, group, cols = keep.shape
     perm = [(s, s ^ 1) for s in range(n)]
-    with jax.named_scope("summed_core_stage"):
-        x = keep + lax.ppermute(send, "vocab", perm=perm)
-    x = x.reshape([2] * (levels - 1) + [group, cols])
+    half = cols // 2
+    streams = []
+    for cut in (slice(0, half), slice(half, cols)):
+        with jax.named_scope("summed_core_stage"):
+            x = keep[:, :, cut] + lax.ppermute(send[:, :, cut], "vocab", perm=perm)
+        streams.append(x.reshape([2] * (levels - 1) + [group, half]))
+    first, second = streams
     remaining = list(range(levels - 1, 0, -1))
-    half = cols // 2
-    first, second = x[..., :half], x[..., half:]
     rest_a, rest_b = list(remaining), list(remaining)
     order_a = sorted(remaining)
     order_b = sorted(remaining, reverse=True)

time: 260 us -> 257 us (0.988)
  waiting for transfers between devices: 175 us -> 172 us
    ppermute x1 -> x2, waiting for transfers between devices: 3.21 us -> 0.01 us  [halving_reduce_scatter(): x = keep[:, :, cut] + lax.ppermute(send[:, :, cut], 'vocab', perm=perm)]
  transfers between devices with their start and end apart: 20 -> 21, of which waited for: 19 -> 18; matrix products, arithmetic and copies ran while one was open for 1% -> 2% of each run, Pallas kernels for 0% -> 0%
where the time goes in v19:
time: 257 us
  waiting for transfers between devices  172 us (67%)
  starting transfers between devices  24.2 us (9%)
  matrix products  17.9 us (7%)
  between operations  14.6 us (6%)
  local copies, waits for them, and re-layouts  11.4 us (4%)
  blocking collectives  9.06 us (4%)
  other arithmetic  8.24 us (3%)
    reduce_scatter x1, waiting for transfers between devices, per_device(): logits = lax.psum_scatter(picked, 'dp', scatter_dimension=0, tiled=True)  76.7 us
    all_gather x1, waiting for transfers between devices, per_device(): prob_part = lax.all_gather(probabilities, 'dp', axis=0, tiled=True)  45.4 us
    ppermute x4, waiting for transfers between devices, exchange_stage(): got = lax.ppermute(send, 'vocab', perm=perm)  16.5 us
    ppermute x5, waiting for transfers between devices, bruck_all_to_all(): got = lax.ppermute(send, axis_name, perm=perm)  15.5 us
    ppermute x6, waiting for transfers between devices, gather_stage(): got = lax.ppermute(x, 'vocab', perm=perm)  10.9 us
    ppermute x5, starting transfers between devices, bruck_all_to_all(): got = lax.ppermute(send, axis_name, perm=perm)  10.5 us
    all_gather x1, blocking collectives, per_device(): stats = lax.all_gather(jnp.stack([local_max, local_total]), 'vocab', axis=0)  9.06 us
    dot_general x2, matrix products, expected_half(): jnp.einsum('brkt,ktd->brd', spread, out_weight.reshape(n_tb, TB, columns_...  8.76 us
  transfers between devices with their start and end apart: 21, of which 18 were waited for; matrix products, arithmetic and copies ran while one was open for 2% of the time, Pallas kernels for 0%

profile of v19, /device:TPU:0, one launch (start us, length us, event | category | flops | bytes accessed | tf_op | source)
XLA Modules:
  0.0 257.0 jit_solution(8309426912669872888)
XLA Ops:
  7.3 1.0 constant_dynamic-slice_fusion.6
  8.3 0.6 collective-permute-start
  8.8 1.0 collective-permute-done
  9.9 2.9 %collective-permute-start.1 = (bf16[2,2,16,1024]{3,2,1,0:T(8,128)(2,1)S(1)}, bf16[2,2,16,1024]{3,2,1,0:T(8,128)(2,1)S(1)}, u32[]{:S(2)}, u32[]{:S(2)}) collective-permute-start(bf16[2,2,16,1024]{3,2,1,0:T(8,128)(2,1)S(1)} %get-tuple-element.29), channel_id=1, source_target_pairs={{0,2},{1,3},{2,0},{3,1},{4,6},{5,7},{6,4},{7,5},{8,10},{9,11},{10,... | collective-permute-start | bytes 393224 | tf_op jit(solution)/shard_map/hidden_spread/ppermute | solution.py:93
  12.8 3.8 %collective-permute-done.1 = bf16[2,2,16,1024]{3,2,1,0:T(8,128)(2,1)S(1)} collective-permute-done((bf16[2,2,16,1024]{3,2,1,0:T(8,128)(2,1)S(1)}, bf16[2,2,16,1024]{3,2,1,0:T(8,128)(2,1)S(1)}, u32[]{:S(2)}, u32[]{:S(2)}) %collective-permute-start.1) | collective-permute-done | bytes 131104 | tf_op jit(solution)/shard_map/hidden_spread/ppermute | solution.py:93
  16.6 1.8 collective-permute-start.2
  18.5 3.2 %collective-permute-done.2 = bf16[2,2,16,1024]{3,2,1,0:T(8,128)(2,1)S(1)} collective-permute-done((bf16[2,2,16,1024]{3,2,1,0:T(8,128)(2,1)S(1)}, bf16[2,2,16,1024]{3,2,1,0:T(8,128)(2,1)S(1)}, u32[]{:S(2)}, u32[]{:S(2)}) %collective-permute-start.2) | collective-permute-done | bytes 131104 | tf_op jit(solution)/shard_map/hidden_spread/ppermute | solution.py:93
  21.8 0.2 reshape.526
  22.0 0.2 copy.51
  22.2 1.9 collective-permute-start.3
  24.1 3.1 %collective-permute-done.3 = bf16[2,16,2048]{2,1,0:T(8,128)(2,1)S(1)} collective-permute-done((bf16[2,16,2048]{2,1,0:T(8,128)(2,1)S(1)}, bf16[2,16,2048]{2,1,0:T(8,128)(2,1)S(1)}, u32[]{:S(2)}, u32[]{:S(2)}) %collective-permute-start.3) | collective-permute-done | bytes 131104 | tf_op jit(solution)/shard_map/hidden_spread/ppermute | solution.py:93
  27.3 3.3 %collective-permute-start.4 = (bf16[2,16,2048]{2,1,0:T(8,128)(2,1)S(1)}, bf16[2,16,2048]{2,1,0:T(8,128)(2,1)S(1)}, u32[]{:S(2)}, u32[]{:S(2)}) collective-permute-start(bf16[2,16,2048]{2,1,0:T(8,128)(2,1)S(1)} %get-tuple-element.23), channel_id=1, source_target_pairs={{0,16},{8,24},{16,0},{24,8},{1,17},{9,25},{17,1},{25,9},{2,18},{10... | collective-permute-start | bytes 393224 | tf_op jit(solution)/shard_map/hidden_spread/ppermute | solution.py:93
  30.6 4.4 %collective-permute-done.4 = bf16[2,16,2048]{2,1,0:T(8,128)(2,1)S(1)} collective-permute-done((bf16[2,16,2048]{2,1,0:T(8,128)(2,1)S(1)}, bf16[2,16,2048]{2,1,0:T(8,128)(2,1)S(1)}, u32[]{:S(2)}, u32[]{:S(2)}) %collective-permute-start.4) | collective-permute-done | bytes 131104 | tf_op jit(solution)/shard_map/hidden_spread/ppermute | solution.py:93
  35.0 0.1 slice_bitcast_fusion.15
  35.1 1.6 collective-permute-start.5
  36.7 0.1 reshape.533
  36.8 1.5 collective-permute-start.8
  38.3 3.3 %collective-permute-done.5 = bf16[64,1024]{1,0:T(8,128)(2,1)S(1)} collective-permute-done((bf16[64,1024]{1,0:T(8,128)(2,1)S(1)}, bf16[64,1024]{1,0:T(8,128)(2,1)S(1)}, u32[]{:S(2)}, u32[]{:S(2)}) %collective-permute-start.5) | collective-permute-done | bytes 131104 | tf_op jit(solution)/shard_map/hidden_spread/hidden_gather_stage/ppermute | solution.py:48
  41.6 1.5 collective-permute-done.8
  43.2 0.6 collective-permute-start.9
  43.8 1.6 collective-permute-start.6
  45.5 4.2 %collective-permute-done.9 = bf16[2,64,1024]{2,1,0:T(8,128)(2,1)S(1)} collective-permute-done((bf16[2,64,1024]{2,1,0:T(8,128)(2,1)S(1)}, bf16[2,64,1024]{2,1,0:T(8,128)(2,1)S(1)}, u32[]{:S(2)}, u32[]{:S(2)}) %collective-permute-start.9) | collective-permute-done | bytes 262176 | tf_op jit(solution)/shard_map/hidden_spread/hidden_gather_stage/ppermute | solution.py:48
  49.8 0.5 collective-permute-done.6
  50.3 0.1 collective-permute-start.7
  50.4 0.1 pad_maximum_fusion
  50.6 1.0 collective-permute-done.10
  51.7 0.2 maximum_select_fusion.1
  51.9 0.5 collective-permute-done.7
  52.4 0.2 maximum_select_fusion
  52.7 0.2 maximum_bitcast_fusion
  52.9 0.2 copy.60
  53.1 0.9 slice-done.1
  54.1 0.4 slice-done.2
  54.5 7.3 %fusion.24 = f32[4,128,19,128]{3,1,2,0:T(8,128)} fusion(bf16[4,128,2048,1]{2,1,3,0:T(8,128)(2,1)S(1)} %bitcast.178, bf16[19,128,2048,1]{2,1,0,3:T(8,128)(2,1)S(1)} %bitcast.219), kind=kOutput, calls=%fused_computation.101 | convolution fusion | flops 5100273664 | bytes 17039360 | tf_op jit(solution)/shard_map/dense_logits/bd,vd->bv/dot_general | solution.py:126
  61.8 5.2 %gather_fusion = f32[64,128,128]{2,1,0:T(8,128)} fusion(f32[4,128,19,128]{3,1,2,0:T(8,128)} %fusion.24, s32[64]{0:T(128)S(1)} %reshape.533), kind=kCustom, calls=%fused_computation | custom fusion | bytes 8389120 | tf_op jit(solution)/shard_map/dense_logits/gather | solution.py:131
  67.1 0.6 constant_dynamic-slice_fusion.7
  67.7 0.6 iota_compare_fusion.1
  68.4 76.7 %reduce-scatter.2.cloned.1.call-done = f32[1,16,128,128]{3,2,1,0:T(8,128)} async-done(((f32[4,16,128,128]{3,2,1,0:T(8,128)}), f32[1,16,128,128]{3,2,1,0:T(8,128)}) %reduce-scatter.2.cloned.1.call-update) | async-done | bytes 1048592 | tf_op jit(solution)/shard_map/reduce_scatter | solution.py:133
  145.0 1.5 select_reduce_fusion
  146.6 1.6 exponential_reduce_fusion
  148.1 9.1 %all-gather = f32[16,1,128]{2,1,0:T(1,128)S(1)} all-gather(f32[2,1,128]{2,1,0:T(1,128)S(1)} %pad_maximum_fusion.4), channel_id=2, replica_groups=mesh['dp'=4,'vocab'=8] {'vocab'}, dimensions={0}, use_global_device_ids=true | all-gather | bytes 9216 | tf_op jit(solution)/shard_map/softmax_stats/all_gather | solution.py:141
  157.3 1.6 select_convert_fusion
  158.9 45.4 %all-gather.3.cloned.1.call-done = bf16[4,16,128,128]{3,2,1,0:T(8,128)(2,1)} async-done(((bf16[1,16,128,128]{3,2,1,0:T(8,128)(2,1)}), bf16[4,16,128,128]{3,2,1,0:T(8,128)(2,1)}) %all-gather.3.cloned.1.call-update) | async-done | bytes 2097168 | tf_op jit(solution)/shard_map/all_gather | solution.py:148
  204.3 1.7 constant_dynamic-slice_fusion.1
  206.0 0.9 fusion.1
  207.0 5.8 %convolution_bitcast_fusion = f32[4,64,2048]{2,1,0:T(8,128)S(1)} fusion(bf16[19,128,2048,1]{2,1,0,3:T(8,128)(2,1)} %bitcast.216, bf16[4,64,19,128]{3,2,1,0:T(8,128)(2,1)S(1)} %fusion.1), kind=kOutput, calls=%fused_computation.1 | convolution fusion | flops 2550136832 | bytes 13303808 | tf_op jit(solution)/shard_map/dense_expected/brkt,ktd->brd/dot_general | solution.py:165
  212.8 0.2 fusion.22
  213.2 0.5 collective-permute-start.14
  213.6 0.9 fusion
  214.6 3.0 %convolution_bitcast_fusion.1 = f32[4,64,2048]{2,1,0:T(8,128)S(1)} fusion(bf16[19,128,2048,1]{2,1,0,3:T(8,128)(2,1)S(1)} %bitcast.222, bf16[4,64,19,128]{3,2,1,0:T(8,128)(2,1)S(1)} %fusion), kind=kOutput, calls=%fused_computation.2 | convolution fusion | flops 2550136832 | bytes 13303808 | tf_op jit(solution)/shard_map/dense_expected/brkt,ktd->brd/dot_general | solution.py:165
  217.6 0.4 slice_add_fusion.1
  218.1 1.5 collective-permute-start.12
  219.6 1.5 collective-permute-start.15
  221.2 10.9 %collective-permute-done.12 = f32[2,64,1024]{2,1,0:T(8,128)S(1)} collective-permute-done((f32[2,64,1024]{2,1,0:T(8,128)S(1)}, f32[2,64,1024]{2,1,0:T(8,128)S(1)}, u32[]{:S(2)}, u32[]{:S(2)}) %collective-permute-start.12) | collective-permute-done | bytes 524320 | tf_op jit(solution)/shard_map/summed_chip_stage/ppermute | solution.py:18
  232.1 1.5 collective-permute-start.13
  233.8 1.5 collective-permute-start.16
  235.3 4.3 %collective-permute-done.13 = f32[64,1024]{1,0:T(8,128)S(1)} collective-permute-done((f32[64,1024]{1,0:T(8,128)S(1)}, f32[64,1024]{1,0:T(8,128)S(1)}, u32[]{:S(2)}, u32[]{:S(2)}) %collective-permute-start.13) | collective-permute-done | bytes 262176 | tf_op jit(solution)/shard_map/summed_chip_stage/ppermute | solution.py:18
  239.7 1.3 collective-permute-done.16
  241.1 0.1 multiply_reduce_fusion
  241.2 0.2 collective-permute-start.17
  241.4 3.4 %collective-permute-done.17 = f32[64]{0:T(128)S(1)} collective-permute-done((f32[64]{0:T(128)S(1)}, f32[64]{0:T(128)S(1)}, u32[]{:S(2)}, u32[]{:S(2)}) %collective-permute-start.17) | collective-permute-done | bytes 288 | tf_op jit(solution)/shard_map/ppermute | solution.py:75
  244.8 1.2 collective-permute-start.18
  246.0 3.2 %collective-permute-done.18 = f32[64]{0:T(128)S(1)} collective-permute-done((f32[64]{0:T(128)S(1)}, f32[64]{0:T(128)S(1)}, u32[]{:S(2)}, u32[]{:S(2)}) %collective-permute-start.18) | collective-permute-done | bytes 288 | tf_op jit(solution)/shard_map/ppermute | solution.py:75
  249.3 0.9 fusion.4
  (74 shorter events, 1.6 us)
Async XLA Ops:
  7.2 59.9 %copy-start = (s32[1,4]{1,0:T(1,128)S(1)}, s32[1,4]{1,0:T(1,128)}, u32[]{:S(2)}) copy-start(s32[1,4]{1,0:T(1,128)} %param.7) | copy-start | bytes 52
  7.2 137.9 %reduce-scatter.2.cloned.1.call-start = ((), (), s32[]{:S(2)}) async-start(), calls=%async_computation.1 | async-start | bytes 5242880 | tf_op jit(solution)/shard_map/reduce_scatter | solution.py:133
  8.3 1.5 collective-permute-start
  9.9 6.7 %collective-permute-start.1 = (bf16[2,2,16,1024]{3,2,1,0:T(8,128)(2,1)S(1)}, bf16[2,2,16,1024]{3,2,1,0:T(8,128)(2,1)S(1)}, u32[]{:S(2)}, u32[]{:S(2)}) collective-permute-start(bf16[2,2,16,1024]{3,2,1,0:T(8,128)(2,1)S(1)} %get-tuple-element.29), channel_id=1, source_target_pairs={{0,2},{1,3},{2,0},{3,1},{4,6},{5,7},{6,4},{7,5},{8,10},{9,11},{10,... | collective-permute-start | bytes 393224 | tf_op jit(solution)/shard_map/hidden_spread/ppermute | solution.py:93
  16.6 5.0 %collective-permute-start.2 = (bf16[2,2,16,1024]{3,2,1,0:T(8,128)(2,1)S(1)}, bf16[2,2,16,1024]{3,2,1,0:T(8,128)(2,1)S(1)}, u32[]{:S(2)}, u32[]{:S(2)}) collective-permute-start(bf16[2,2,16,1024]{3,2,1,0:T(8,128)(2,1)S(1)} %get-tuple-element.27), channel_id=1, source_target_pairs={{0,4},{1,5},{2,6},{3,7},{4,0},{5,1},{6,2},{7,3},{8,12},{9,13},{10,... | collective-permute-start | bytes 393224 | tf_op jit(solution)/shard_map/hidden_spread/ppermute | solution.py:93
  22.2 14.5 %copy-start.2 = (s32[1,4,16]{2,1,0:T(4,128)S(1)}, s32[1,4,16]{2,1,0:T(4,128)}, u32[]{:S(2)}) copy-start(s32[1,4,16]{2,1,0:T(4,128)} %param.6) | copy-start | bytes 772
  22.2 5.0 %collective-permute-start.3 = (bf16[2,16,2048]{2,1,0:T(8,128)(2,1)S(1)}, bf16[2,16,2048]{2,1,0:T(8,128)(2,1)S(1)}, u32[]{:S(2)}, u32[]{:S(2)}) collective-permute-start(bf16[2,16,2048]{2,1,0:T(8,128)(2,1)S(1)} %get-tuple-element.25), channel_id=1, source_target_pairs={{0,8},{8,0},{16,24},{24,16},{1,9},{9,1},{17,25},{25,17},{2,10},{10... | collective-permute-start | bytes 393224 | tf_op jit(solution)/shard_map/hidden_spread/ppermute | solution.py:93
  27.3 7.6 %collective-permute-start.4 = (bf16[2,16,2048]{2,1,0:T(8,128)(2,1)S(1)}, bf16[2,16,2048]{2,1,0:T(8,128)(2,1)S(1)}, u32[]{:S(2)}, u32[]{:S(2)}) collective-permute-start(bf16[2,16,2048]{2,1,0:T(8,128)(2,1)S(1)} %get-tuple-element.23), channel_id=1, source_target_pairs={{0,16},{8,24},{16,0},{24,8},{1,17},{9,25},{17,1},{25,9},{2,18},{10... | collective-permute-start | bytes 393224 | tf_op jit(solution)/shard_map/hidden_spread/ppermute | solution.py:93
  35.1 6.4 %collective-permute-start.5 = (bf16[64,1024]{1,0:T(8,128)(2,1)S(1)}, bf16[64,1024]{1,0:T(8,128)(2,1)S(1)}, u32[]{:S(2)}, u32[]{:S(2)}) collective-permute-start(bf16[64,1024]{1,0:T(8,128)(2,1)S(1)} %get-tuple-element.17), channel_id=1, source_target_pairs={{0,2},{1,3},{2,0},{3,1},{4,6},{5,7},{6,4},{7,5},{8,10},{9,11},{10,... | collective-permute-start | bytes 393224 | tf_op jit(solution)/shard_map/hidden_spread/hidden_gather_stage/ppermute | solution.py:48
  36.8 6.4 %collective-permute-start.8 = (bf16[64,1024]{1,0:T(8,128)(2,1)S(1)}, bf16[64,1024]{1,0:T(8,128)(2,1)S(1)}, u32[]{:S(2)}, u32[]{:S(2)}) collective-permute-start(bf16[64,1024]{1,0:T(8,128)(2,1)S(1)} %get-tuple-element.16), channel_id=1, source_target_pairs={{0,4},{1,5},{2,6},{3,7},{4,0},{5,1},{6,2},{7,3},{8,12},{9,13},{10,... | collective-permute-start | bytes 393224 | tf_op jit(solution)/shard_map/hidden_spread/hidden_gather_stage/ppermute | solution.py:48
  43.2 6.4 %collective-permute-start.9 = (bf16[2,64,1024]{2,1,0:T(8,128)(2,1)S(1)}, bf16[2,64,1024]{2,1,0:T(8,128)(2,1)S(1)}, u32[]{:S(2)}, u32[]{:S(2)}) collective-permute-start(bf16[2,64,1024]{2,1,0:T(8,128)(2,1)S(1)} %maximum_select_fusion.12), channel_id=1, source_target_pairs={{0,2},{1,3},{2,0},{3,1},{4,6},{5,7},{6,4},{7,5},{8,10},{9,11},{10,... | collective-permute-start | bytes 786440 | tf_op jit(solution)/shard_map/hidden_spread/hidden_gather_stage/ppermute | solution.py:48
  43.8 6.4 %collective-permute-start.6 = (bf16[2,64,1024]{2,1,0:T(8,128)(2,1)S(1)}, bf16[2,64,1024]{2,1,0:T(8,128)(2,1)S(1)}, u32[]{:S(2)}, u32[]{:S(2)}) collective-permute-start(bf16[2,64,1024]{2,1,0:T(8,128)(2,1)S(1)} %maximum_select_fusion.10), channel_id=1, source_target_pairs={{0,4},{1,5},{2,6},{3,7},{4,0},{5,1},{6,2},{7,3},{8,12},{9,13},{10,... | collective-permute-start | bytes 786440 | tf_op jit(solution)/shard_map/hidden_spread/hidden_gather_stage/ppermute | solution.py:48
  49.7 2.0 collective-permute-start.10
  50.2 2.9 %slice-start = ((s8[9961472]{0:T(1024)(128)(4,1)}), s8[4194304]{0:T(1024)(128)(4,1)S(1)}, s32[]{:S(2)}) async-start(s8[9961472]{0:T(1024)(128)(4,1)} %bitcast.217), calls=%async_computation.3 | async-start | bytes 8388608
  50.3 2.1 collective-permute-start.7
  51.7 2.4 slice-start.1
  52.7 1.8 slice-start.2
  67.1 137.3 %all-gather.3.cloned.1.call-start = ((), (), s32[]{:S(2)}) async-start(), calls=%async_computation.2 | async-start | bytes 2621440 | tf_op jit(solution)/shard_map/all_gather | solution.py:148
  145.0 12.2 %copy-start.1 = (f32[1,16,128,128]{3,2,1,0:T(8,128)S(1)}, f32[1,16,128,128]{3,2,1,0:T(8,128)}, u32[]{:S(2)}) copy-start(f32[1,16,128,128]{3,2,1,0:T(8,128)} %reduce-scatter.2.cloned.1.call-done) | copy-start | bytes 3145732
  206.0 8.6 %slice-start.3 = ((s8[9961472]{0:T(1024)(128)(4,1)}), s8[4194304]{0:T(1024)(128)(4,1)S(1)}, s32[]{:S(2)}) async-start(s8[9961472]{0:T(1024)(128)(4,1)} %bitcast.220), calls=%async_computation.6 | async-start | bytes 8388608
  207.0 7.6 %slice-start.4 = ((s8[9961472]{0:T(1024)(128)(4,1)}), s8[4194304]{0:T(1024)(128)(4,1)S(1)}, s32[]{:S(2)}) async-start(s8[9961472]{0:T(1024)(128)(4,1)} %bitcast.220), calls=%async_computation.7 | async-start | bytes 8388608
  207.0 7.6 %slice-start.5 = ((s8[9961472]{0:T(1024)(128)(4,1)}), s8[1572864]{0:T(1024)(128)(4,1)S(1)}, s32[]{:S(2)}) async-start(s8[9961472]{0:T(1024)(128)(4,1)} %bitcast.220), calls=%async_computation.8 | async-start | bytes 3145728
  213.1 4.5 %collective-permute-start.11 = (f32[4,64,1024]{2,1,0:T(8,128)S(1)}, f32[4,64,1024]{2,1,0:T(8,128)S(1)}, u32[]{:S(2)}, u32[]{:S(2)}) collective-permute-start(f32[4,64,1024]{2,1,0:T(8,128)S(1)} %get-tuple-element.4), channel_id=1, source_target_pairs={{0,1},{1,0},{2,3},{3,2},{4,5},{5,4},{6,7},{7,6},{8,9},{9,8},{10,11... | collective-permute-start | bytes 3145736 | tf_op jit(solution)/shard_map/summed_core_stage/ppermute | solution.py:30
  213.2 4.4 %collective-permute-start.14 = (f32[4,64,1024]{2,1,0:T(8,128)S(1)}, f32[4,64,1024]{2,1,0:T(8,128)S(1)}, u32[]{:S(2)}, u32[]{:S(2)}) collective-permute-start(f32[4,64,1024]{2,1,0:T(8,128)S(1)} %get-tuple-element.5), channel_id=1, source_target_pairs={{0,1},{1,0},{2,3},{3,2},{4,5},{5,4},{6,7},{7,6},{8,9},{9,8},{10,11... | collective-permute-start | bytes 3145736 | tf_op jit(solution)/shard_map/summed_core_stage/ppermute | solution.py:30
  218.1 14.0 %collective-permute-start.12 = (f32[2,64,1024]{2,1,0:T(8,128)S(1)}, f32[2,64,1024]{2,1,0:T(8,128)S(1)}, u32[]{:S(2)}, u32[]{:S(2)}) collective-permute-start(f32[2,64,1024]{2,1,0:T(8,128)S(1)} %dynamic-slice_bitcast_fusion.1), channel_id=1, source_target_pairs={{0,2},{1,3},{2,0},{3,1},{4,6},{5,7},{6,4},{7,5},{8,10},{9,11},{10,... | collective-permute-start | bytes 1572872 | tf_op jit(solution)/shard_map/summed_chip_stage/ppermute | solution.py:18
  219.6 14.1 %collective-permute-start.15 = (f32[2,64,1024]{2,1,0:T(8,128)S(1)}, f32[2,64,1024]{2,1,0:T(8,128)S(1)}, u32[]{:S(2)}, u32[]{:S(2)}) collective-permute-start(f32[2,64,1024]{2,1,0:T(8,128)S(1)} %dynamic-slice_bitcast_fusion), channel_id=1, source_target_pairs={{0,4},{1,5},{2,6},{3,7},{4,0},{5,1},{6,2},{7,3},{8,12},{9,13},{10,... | collective-permute-start | bytes 1572872 | tf_op jit(solution)/shard_map/summed_chip_stage/ppermute | solution.py:18
  232.1 7.5 %collective-permute-start.13 = (f32[64,1024]{1,0:T(8,128)S(1)}, f32[64,1024]{1,0:T(8,128)S(1)}, u32[]{:S(2)}, u32[]{:S(2)}) collective-permute-start(f32[64,1024]{1,0:T(8,128)S(1)} %dynamic-slice_bitcast_fusion.3), channel_id=1, source_target_pairs={{0,4},{1,5},{2,6},{3,7},{4,0},{5,1},{6,2},{7,3},{8,12},{9,13},{10,... | collective-permute-start | bytes 786440 | tf_op jit(solution)/shard_map/summed_chip_stage/ppermute | solution.py:18
  233.8 7.2 %collective-permute-start.16 = (f32[64,1024]{1,0:T(8,128)S(1)}, f32[64,1024]{1,0:T(8,128)S(1)}, u32[]{:S(2)}, u32[]{:S(2)}) collective-permute-start(f32[64,1024]{1,0:T(8,128)S(1)} %dynamic-slice_bitcast_fusion.2), channel_id=1, source_target_pairs={{0,2},{1,3},{2,0},{3,1},{4,6},{5,7},{6,4},{7,5},{8,10},{9,11},{10,... | collective-permute-start | bytes 786440 | tf_op jit(solution)/shard_map/summed_chip_stage/ppermute | solution.py:18
  241.2 3.6 %collective-permute-start.17 = (f32[64]{0:T(128)S(1)}, f32[64]{0:T(128)S(1)}, u32[]{:S(2)}, u32[]{:S(2)}) collective-permute-start(f32[64]{0:T(128)S(1)} %multiply_reduce_fusion), channel_id=1, source_target_pairs={{0,8},{8,0},{16,24},{24,16},{1,9},{9,1},{17,25},{25,17},{2,10},{10... | collective-permute-start | bytes 776 | tf_op jit(solution)/shard_map/ppermute | solution.py:75
  244.8 4.5 %collective-permute-start.18 = (f32[64]{0:T(128)S(1)}, f32[64]{0:T(128)S(1)}, u32[]{:S(2)}, u32[]{:S(2)}) collective-permute-start(f32[64]{0:T(128)S(1)} %add.160), channel_id=1, source_target_pairs={{0,16},{8,24},{16,0},{24,8},{1,17},{9,25},{17,1},{25,9},{2,18},{10... | collective-permute-start | bytes 776 | tf_op jit(solution)/shard_map/ppermute | solution.py:75
Sparse Core Ops, SparseCore 0:
  67.2 77.8 reduce-scatter.1
  159.0 45.2 all-gather.2

commit v20 on v19

--- a/solution.py
+++ b/solution.py
@@ -142,8 +142,9 @@
         beam_max = jnp.max(stats[:, 0], axis=0)
         beam_total = jnp.sum(stats[:, 1] * jnp.exp(stats[:, 0] - beam_max[None]), axis=0)
         shifted = logits - beam_max[:, None, :, None] - jnp.log(beam_total)[:, None, :, None]
-        allowed_logprob = jnp.where(live_mask, shifted, 0.0)
         probabilities = jnp.where(live_mask, jnp.exp(shifted), 0.0).astype(jnp.bfloat16)
+        later, probabilities = lax.optimization_barrier((shifted, probabilities))
+        allowed_logprob = jnp.where(live_mask, later, 0.0)
 
     prob_part = lax.all_gather(probabilities, "dp", axis=0, tiled=True)
 

time: 257 us -> 257 us (level)
  transfers between devices with their start and end apart: 21 -> 21, of which waited for: 18 -> 18; matrix products, arithmetic and copies ran while one was open for 2% -> 3% of each run, Pallas kernels for 0% -> 0%
where the time goes in v20:
time: 257 us
  waiting for transfers between devices  171 us (67%)
  starting transfers between devices  24.2 us (9%)
  matrix products  17.9 us (7%)
  between operations  14.6 us (6%)
  local copies, waits for them, and re-layouts  11.4 us (4%)
  blocking collectives  9.06 us (4%)
  other arithmetic  8.94 us (3%)
    reduce_scatter x1, waiting for transfers between devices, per_device(): logits = lax.psum_scatter(picked, 'dp', scatter_dimension=0, tiled=True)  76.7 us
    all_gather x1, waiting for transfers between devices, per_device(): prob_part = lax.all_gather(probabilities, 'dp', axis=0, tiled=True)  45.4 us
    ppermute x4, waiting for transfers between devices, exchange_stage(): got = lax.ppermute(send, 'vocab', perm=perm)  16.5 us
    ppermute x5, waiting for transfers between devices, bruck_all_to_all(): got = lax.ppermute(send, axis_name, perm=perm)  15.5 us
    ppermute x6, waiting for transfers between devices, gather_stage(): got = lax.ppermute(x, 'vocab', perm=perm)  10.9 us
    ppermute x5, starting transfers between devices, bruck_all_to_all(): got = lax.ppermute(send, axis_name, perm=perm)  10.5 us
    all_gather x1, blocking collectives, per_device(): stats = lax.all_gather(jnp.stack([local_max, local_total]), 'vocab', axis=0)  9.06 us
    dot_general x2, matrix products, expected_half(): jnp.einsum('brkt,ktd->brd', spread, out_weight.reshape(n_tb, TB, columns_...  8.76 us
  transfers between devices with their start and end apart: 21, of which 18 were waited for; matrix products, arithmetic and copies ran while one was open for 3% of the time, Pallas kernels for 0%

profile of v20, /device:TPU:0, one launch (start us, length us, event | category | flops | bytes accessed | tf_op | source)
XLA Modules:
  0.0 256.6 jit_solution(8060321489412911778)
XLA Ops:
  7.3 1.0 constant_dynamic-slice_fusion.6
  8.3 0.6 collective-permute-start
  8.8 1.0 collective-permute-done
  9.9 2.9 %collective-permute-start.1 = (bf16[2,2,16,1024]{3,2,1,0:T(8,128)(2,1)S(1)}, bf16[2,2,16,1024]{3,2,1,0:T(8,128)(2,1)S(1)}, u32[]{:S(2)}, u32[]{:S(2)}) collective-permute-start(bf16[2,2,16,1024]{3,2,1,0:T(8,128)(2,1)S(1)} %get-tuple-element.33), channel_id=1, source_target_pairs={{0,2},{1,3},{2,0},{3,1},{4,6},{5,7},{6,4},{7,5},{8,10},{9,11},{10,... | collective-permute-start | bytes 393224 | tf_op jit(solution)/shard_map/hidden_spread/ppermute | solution.py:93
  12.8 3.8 %collective-permute-done.1 = bf16[2,2,16,1024]{3,2,1,0:T(8,128)(2,1)S(1)} collective-permute-done((bf16[2,2,16,1024]{3,2,1,0:T(8,128)(2,1)S(1)}, bf16[2,2,16,1024]{3,2,1,0:T(8,128)(2,1)S(1)}, u32[]{:S(2)}, u32[]{:S(2)}) %collective-permute-start.1) | collective-permute-done | bytes 131104 | tf_op jit(solution)/shard_map/hidden_spread/ppermute | solution.py:93
  16.6 1.8 collective-permute-start.2
  18.5 3.2 %collective-permute-done.2 = bf16[2,2,16,1024]{3,2,1,0:T(8,128)(2,1)S(1)} collective-permute-done((bf16[2,2,16,1024]{3,2,1,0:T(8,128)(2,1)S(1)}, bf16[2,2,16,1024]{3,2,1,0:T(8,128)(2,1)S(1)}, u32[]{:S(2)}, u32[]{:S(2)}) %collective-permute-start.2) | collective-permute-done | bytes 131104 | tf_op jit(solution)/shard_map/hidden_spread/ppermute | solution.py:93
  21.8 0.2 reshape.526
  22.0 0.2 copy.51
  22.2 1.9 collective-permute-start.3
  24.1 3.1 %collective-permute-done.3 = bf16[2,16,2048]{2,1,0:T(8,128)(2,1)S(1)} collective-permute-done((bf16[2,16,2048]{2,1,0:T(8,128)(2,1)S(1)}, bf16[2,16,2048]{2,1,0:T(8,128)(2,1)S(1)}, u32[]{:S(2)}, u32[]{:S(2)}) %collective-permute-start.3) | collective-permute-done | bytes 131104 | tf_op jit(solution)/shard_map/hidden_spread/ppermute | solution.py:93
  27.3 3.3 %collective-permute-start.4 = (bf16[2,16,2048]{2,1,0:T(8,128)(2,1)S(1)}, bf16[2,16,2048]{2,1,0:T(8,128)(2,1)S(1)}, u32[]{:S(2)}, u32[]{:S(2)}) collective-permute-start(bf16[2,16,2048]{2,1,0:T(8,128)(2,1)S(1)} %get-tuple-element.27), channel_id=1, source_target_pairs={{0,16},{8,24},{16,0},{24,8},{1,17},{9,25},{17,1},{25,9},{2,18},{10... | collective-permute-start | bytes 393224 | tf_op jit(solution)/shard_map/hidden_spread/ppermute | solution.py:93
  30.6 4.4 %collective-permute-done.4 = bf16[2,16,2048]{2,1,0:T(8,128)(2,1)S(1)} collective-permute-done((bf16[2,16,2048]{2,1,0:T(8,128)(2,1)S(1)}, bf16[2,16,2048]{2,1,0:T(8,128)(2,1)S(1)}, u32[]{:S(2)}, u32[]{:S(2)}) %collective-permute-start.4) | collective-permute-done | bytes 131104 | tf_op jit(solution)/shard_map/hidden_spread/ppermute | solution.py:93
  35.0 0.1 slice_bitcast_fusion.15
  35.1 1.6 collective-permute-start.5
  36.7 0.1 reshape.533
  36.8 1.5 collective-permute-start.8
  38.3 3.3 %collective-permute-done.5 = bf16[64,1024]{1,0:T(8,128)(2,1)S(1)} collective-permute-done((bf16[64,1024]{1,0:T(8,128)(2,1)S(1)}, bf16[64,1024]{1,0:T(8,128)(2,1)S(1)}, u32[]{:S(2)}, u32[]{:S(2)}) %collective-permute-start.5) | collective-permute-done | bytes 131104 | tf_op jit(solution)/shard_map/hidden_spread/hidden_gather_stage/ppermute | solution.py:48
  41.6 1.5 collective-permute-done.8
  43.2 0.6 collective-permute-start.9
  43.8 1.6 collective-permute-start.6
  45.5 4.2 %collective-permute-done.9 = bf16[2,64,1024]{2,1,0:T(8,128)(2,1)S(1)} collective-permute-done((bf16[2,64,1024]{2,1,0:T(8,128)(2,1)S(1)}, bf16[2,64,1024]{2,1,0:T(8,128)(2,1)S(1)}, u32[]{:S(2)}, u32[]{:S(2)}) %collective-permute-start.9) | collective-permute-done | bytes 262176 | tf_op jit(solution)/shard_map/hidden_spread/hidden_gather_stage/ppermute | solution.py:48
  49.8 0.5 collective-permute-done.6
  50.3 0.1 collective-permute-start.7
  50.6 1.0 collective-permute-done.10
  51.7 0.2 maximum_select_fusion.1
  51.9 0.5 collective-permute-done.7
  52.4 0.2 maximum_select_fusion
  52.7 0.2 maximum_bitcast_fusion
  52.9 0.2 copy.60
  53.1 0.9 slice-done.1
  54.1 0.4 slice-done.2
  54.5 7.3 %fusion.24 = f32[4,128,19,128]{3,1,2,0:T(8,128)} fusion(bf16[4,128,2048,1]{2,1,3,0:T(8,128)(2,1)S(1)} %bitcast.178, bf16[19,128,2048,1]{2,1,0,3:T(8,128)(2,1)S(1)} %bitcast.219), kind=kOutput, calls=%fused_computation.101 | convolution fusion | flops 5100273664 | bytes 17039360 | tf_op jit(solution)/shard_map/dense_logits/bd,vd->bv/dot_general | solution.py:126
  61.8 5.2 %gather_fusion = f32[64,128,128]{2,1,0:T(8,128)} fusion(f32[4,128,19,128]{3,1,2,0:T(8,128)} %fusion.24, s32[64]{0:T(128)S(1)} %reshape.533), kind=kCustom, calls=%fused_computation | custom fusion | bytes 8389120 | tf_op jit(solution)/shard_map/dense_logits/gather | solution.py:131
  67.1 0.6 constant_dynamic-slice_fusion.7
  67.7 0.6 iota_compare_fusion.1
  68.4 76.7 %reduce-scatter.2.cloned.1.call-done = f32[1,16,128,128]{3,2,1,0:T(8,128)} async-done(((f32[4,16,128,128]{3,2,1,0:T(8,128)}), f32[1,16,128,128]{3,2,1,0:T(8,128)}) %reduce-scatter.2.cloned.1.call-update) | async-done | bytes 1048592 | tf_op jit(solution)/shard_map/reduce_scatter | solution.py:133
  145.0 1.5 select_reduce_fusion
  146.6 1.6 exponential_reduce_fusion
  148.1 9.1 %all-gather = f32[16,1,128]{2,1,0:T(1,128)S(1)} all-gather(f32[2,1,128]{2,1,0:T(1,128)S(1)} %pad_maximum_fusion.4), channel_id=2, replica_groups=mesh['dp'=4,'vocab'=8] {'vocab'}, dimensions={0}, use_global_device_ids=true | all-gather | bytes 9216 | tf_op jit(solution)/shard_map/softmax_stats/all_gather | solution.py:141
  157.3 1.2 select_convert_fusion
  158.5 45.4 %all-gather.3.cloned.1.call-done = bf16[4,16,128,128]{3,2,1,0:T(8,128)(2,1)} async-done(((bf16[1,16,128,128]{3,2,1,0:T(8,128)(2,1)}), bf16[4,16,128,128]{3,2,1,0:T(8,128)(2,1)}) %all-gather.3.cloned.1.call-update) | async-done | bytes 2097168 | tf_op jit(solution)/shard_map/all_gather | solution.py:149
  203.9 1.7 constant_dynamic-slice_fusion.1
  205.6 0.9 fusion.1
  206.6 5.8 %convolution_bitcast_fusion = f32[4,64,2048]{2,1,0:T(8,128)S(1)} fusion(bf16[19,128,2048,1]{2,1,0,3:T(8,128)(2,1)} %bitcast.216, bf16[4,64,19,128]{3,2,1,0:T(8,128)(2,1)S(1)} %fusion.1), kind=kOutput, calls=%fused_computation.1 | convolution fusion | flops 2550136832 | bytes 13303808 | tf_op jit(solution)/shard_map/dense_expected/brkt,ktd->brd/dot_general | solution.py:166
  212.4 0.2 fusion.22
  212.7 0.5 collective-permute-start.14
  213.2 0.9 fusion
  214.2 3.0 %convolution_bitcast_fusion.1 = f32[4,64,2048]{2,1,0:T(8,128)S(1)} fusion(bf16[19,128,2048,1]{2,1,0,3:T(8,128)(2,1)S(1)} %bitcast.222, bf16[4,64,19,128]{3,2,1,0:T(8,128)(2,1)S(1)} %fusion), kind=kOutput, calls=%fused_computation.2 | convolution fusion | flops 2550136832 | bytes 13303808 | tf_op jit(solution)/shard_map/dense_expected/brkt,ktd->brd/dot_general | solution.py:166
  217.2 0.4 slice_add_fusion.1
  217.6 1.5 collective-permute-start.12
  219.2 1.5 collective-permute-start.15
  220.8 10.9 %collective-permute-done.12 = f32[2,64,1024]{2,1,0:T(8,128)S(1)} collective-permute-done((f32[2,64,1024]{2,1,0:T(8,128)S(1)}, f32[2,64,1024]{2,1,0:T(8,128)S(1)}, u32[]{:S(2)}, u32[]{:S(2)}) %collective-permute-start.12) | collective-permute-done | bytes 524320 | tf_op jit(solution)/shard_map/summed_chip_stage/ppermute | solution.py:18
  231.7 1.5 collective-permute-start.13
  233.4 1.5 collective-permute-start.16
  234.9 4.3 %collective-permute-done.13 = f32[64,1024]{1,0:T(8,128)S(1)} collective-permute-done((f32[64,1024]{1,0:T(8,128)S(1)}, f32[64,1024]{1,0:T(8,128)S(1)}, u32[]{:S(2)}, u32[]{:S(2)}) %collective-permute-start.13) | collective-permute-done | bytes 262176 | tf_op jit(solution)/shard_map/summed_chip_stage/ppermute | solution.py:18
  239.3 1.4 collective-permute-done.16
  240.7 0.1 multiply_reduce_fusion
  240.8 0.2 collective-permute-start.17
  241.0 3.4 %collective-permute-done.17 = f32[64]{0:T(128)S(1)} collective-permute-done((f32[64]{0:T(128)S(1)}, f32[64]{0:T(128)S(1)}, u32[]{:S(2)}, u32[]{:S(2)}) %collective-permute-start.17) | collective-permute-done | bytes 288 | tf_op jit(solution)/shard_map/ppermute | solution.py:75
  244.4 1.2 collective-permute-start.18
  245.7 1.1 select_bitcast_fusion
  246.8 2.1 collective-permute-done.18
  248.9 0.9 fusion.4
  (75 shorter events, 1.7 us)
Async XLA Ops:
  7.2 59.9 %copy-start = (s32[1,4]{1,0:T(1,128)S(1)}, s32[1,4]{1,0:T(1,128)}, u32[]{:S(2)}) copy-start(s32[1,4]{1,0:T(1,128)} %param.7) | copy-start | bytes 52
  7.2 137.9 %reduce-scatter.2.cloned.1.call-start = ((), (), s32[]{:S(2)}) async-start(), calls=%async_computation.1 | async-start | bytes 5242880 | tf_op jit(solution)/shard_map/reduce_scatter | solution.py:133
  8.3 1.5 collective-permute-start
  9.9 6.7 %collective-permute-start.1 = (bf16[2,2,16,1024]{3,2,1,0:T(8,128)(2,1)S(1)}, bf16[2,2,16,1024]{3,2,1,0:T(8,128)(2,1)S(1)}, u32[]{:S(2)}, u32[]{:S(2)}) collective-permute-start(bf16[2,2,16,1024]{3,2,1,0:T(8,128)(2,1)S(1)} %get-tuple-element.33), channel_id=1, source_target_pairs={{0,2},{1,3},{2,0},{3,1},{4,6},{5,7},{6,4},{7,5},{8,10},{9,11},{10,... | collective-permute-start | bytes 393224 | tf_op jit(solution)/shard_map/hidden_spread/ppermute | solution.py:93
  16.6 5.0 %collective-permute-start.2 = (bf16[2,2,16,1024]{3,2,1,0:T(8,128)(2,1)S(1)}, bf16[2,2,16,1024]{3,2,1,0:T(8,128)(2,1)S(1)}, u32[]{:S(2)}, u32[]{:S(2)}) collective-permute-start(bf16[2,2,16,1024]{3,2,1,0:T(8,128)(2,1)S(1)} %get-tuple-element.31), channel_id=1, source_target_pairs={{0,4},{1,5},{2,6},{3,7},{4,0},{5,1},{6,2},{7,3},{8,12},{9,13},{10,... | collective-permute-start | bytes 393224 | tf_op jit(solution)/shard_map/hidden_spread/ppermute | solution.py:93
  22.2 14.5 %copy-start.2 = (s32[1,4,16]{2,1,0:T(4,128)S(1)}, s32[1,4,16]{2,1,0:T(4,128)}, u32[]{:S(2)}) copy-start(s32[1,4,16]{2,1,0:T(4,128)} %param.6) | copy-start | bytes 772
  22.2 5.0 %collective-permute-start.3 = (bf16[2,16,2048]{2,1,0:T(8,128)(2,1)S(1)}, bf16[2,16,2048]{2,1,0:T(8,128)(2,1)S(1)}, u32[]{:S(2)}, u32[]{:S(2)}) collective-permute-start(bf16[2,16,2048]{2,1,0:T(8,128)(2,1)S(1)} %get-tuple-element.29), channel_id=1, source_target_pairs={{0,8},{8,0},{16,24},{24,16},{1,9},{9,1},{17,25},{25,17},{2,10},{10... | collective-permute-start | bytes 393224 | tf_op jit(solution)/shard_map/hidden_spread/ppermute | solution.py:93
  27.3 7.6 %collective-permute-start.4 = (bf16[2,16,2048]{2,1,0:T(8,128)(2,1)S(1)}, bf16[2,16,2048]{2,1,0:T(8,128)(2,1)S(1)}, u32[]{:S(2)}, u32[]{:S(2)}) collective-permute-start(bf16[2,16,2048]{2,1,0:T(8,128)(2,1)S(1)} %get-tuple-element.27), channel_id=1, source_target_pairs={{0,16},{8,24},{16,0},{24,8},{1,17},{9,25},{17,1},{25,9},{2,18},{10... | collective-permute-start | bytes 393224 | tf_op jit(solution)/shard_map/hidden_spread/ppermute | solution.py:93
  35.1 6.4 %collective-permute-start.5 = (bf16[64,1024]{1,0:T(8,128)(2,1)S(1)}, bf16[64,1024]{1,0:T(8,128)(2,1)S(1)}, u32[]{:S(2)}, u32[]{:S(2)}) collective-permute-start(bf16[64,1024]{1,0:T(8,128)(2,1)S(1)} %get-tuple-element.21), channel_id=1, source_target_pairs={{0,2},{1,3},{2,0},{3,1},{4,6},{5,7},{6,4},{7,5},{8,10},{9,11},{10,... | collective-permute-start | bytes 393224 | tf_op jit(solution)/shard_map/hidden_spread/hidden_gather_stage/ppermute | solution.py:48
  36.8 6.4 %collective-permute-start.8 = (bf16[64,1024]{1,0:T(8,128)(2,1)S(1)}, bf16[64,1024]{1,0:T(8,128)(2,1)S(1)}, u32[]{:S(2)}, u32[]{:S(2)}) collective-permute-start(bf16[64,1024]{1,0:T(8,128)(2,1)S(1)} %get-tuple-element.20), channel_id=1, source_target_pairs={{0,4},{1,5},{2,6},{3,7},{4,0},{5,1},{6,2},{7,3},{8,12},{9,13},{10,... | collective-permute-start | bytes 393224 | tf_op jit(solution)/shard_map/hidden_spread/hidden_gather_stage/ppermute | solution.py:48
  43.2 6.4 %collective-permute-start.9 = (bf16[2,64,1024]{2,1,0:T(8,128)(2,1)S(1)}, bf16[2,64,1024]{2,1,0:T(8,128)(2,1)S(1)}, u32[]{:S(2)}, u32[]{:S(2)}) collective-permute-start(bf16[2,64,1024]{2,1,0:T(8,128)(2,1)S(1)} %maximum_select_fusion.12), channel_id=1, source_target_pairs={{0,2},{1,3},{2,0},{3,1},{4,6},{5,7},{6,4},{7,5},{8,10},{9,11},{10,... | collective-permute-start | bytes 786440 | tf_op jit(solution)/shard_map/hidden_spread/hidden_gather_stage/ppermute | solution.py:48
  43.8 6.4 %collective-permute-start.6 = (bf16[2,64,1024]{2,1,0:T(8,128)(2,1)S(1)}, bf16[2,64,1024]{2,1,0:T(8,128)(2,1)S(1)}, u32[]{:S(2)}, u32[]{:S(2)}) collective-permute-start(bf16[2,64,1024]{2,1,0:T(8,128)(2,1)S(1)} %maximum_select_fusion.10), channel_id=1, source_target_pairs={{0,4},{1,5},{2,6},{3,7},{4,0},{5,1},{6,2},{7,3},{8,12},{9,13},{10,... | collective-permute-start | bytes 786440 | tf_op jit(solution)/shard_map/hidden_spread/hidden_gather_stage/ppermute | solution.py:48
  49.7 2.0 collective-permute-start.10
  50.2 2.9 %slice-start = ((s8[9961472]{0:T(1024)(128)(4,1)}), s8[4194304]{0:T(1024)(128)(4,1)S(1)}, s32[]{:S(2)}) async-start(s8[9961472]{0:T(1024)(128)(4,1)} %bitcast.217), calls=%async_computation.3 | async-start | bytes 8388608
  50.3 2.1 collective-permute-start.7
  51.7 2.4 slice-start.1
  52.7 1.8 slice-start.2
  67.1 136.8 %all-gather.3.cloned.1.call-start = ((), (), s32[]{:S(2)}) async-start(), calls=%async_computation.2 | async-start | bytes 2621440 | tf_op jit(solution)/shard_map/all_gather | solution.py:149
  145.0 12.2 %copy-start.1 = (f32[1,16,128,128]{3,2,1,0:T(8,128)S(1)}, f32[1,16,128,128]{3,2,1,0:T(8,128)}, u32[]{:S(2)}) copy-start(f32[1,16,128,128]{3,2,1,0:T(8,128)} %reduce-scatter.2.cloned.1.call-done) | copy-start | bytes 3145732
  205.6 8.6 %slice-start.3 = ((s8[9961472]{0:T(1024)(128)(4,1)}), s8[4194304]{0:T(1024)(128)(4,1)S(1)}, s32[]{:S(2)}) async-start(s8[9961472]{0:T(1024)(128)(4,1)} %bitcast.220), calls=%async_computation.6 | async-start | bytes 8388608
  206.6 7.6 %slice-start.4 = ((s8[9961472]{0:T(1024)(128)(4,1)}), s8[4194304]{0:T(1024)(128)(4,1)S(1)}, s32[]{:S(2)}) async-start(s8[9961472]{0:T(1024)(128)(4,1)} %bitcast.220), calls=%async_computation.7 | async-start | bytes 8388608
  206.6 7.6 %slice-start.5 = ((s8[9961472]{0:T(1024)(128)(4,1)}), s8[1572864]{0:T(1024)(128)(4,1)S(1)}, s32[]{:S(2)}) async-start(s8[9961472]{0:T(1024)(128)(4,1)} %bitcast.220), calls=%async_computation.8 | async-start | bytes 3145728
  212.7 4.5 %collective-permute-start.11 = (f32[4,64,1024]{2,1,0:T(8,128)S(1)}, f32[4,64,1024]{2,1,0:T(8,128)S(1)}, u32[]{:S(2)}, u32[]{:S(2)}) collective-permute-start(f32[4,64,1024]{2,1,0:T(8,128)S(1)} %get-tuple-element.10), channel_id=1, source_target_pairs={{0,1},{1,0},{2,3},{3,2},{4,5},{5,4},{6,7},{7,6},{8,9},{9,8},{10,11... | collective-permute-start | bytes 3145736 | tf_op jit(solution)/shard_map/summed_core_stage/ppermute | solution.py:30
  212.7 4.4 %collective-permute-start.14 = (f32[4,64,1024]{2,1,0:T(8,128)S(1)}, f32[4,64,1024]{2,1,0:T(8,128)S(1)}, u32[]{:S(2)}, u32[]{:S(2)}) collective-permute-start(f32[4,64,1024]{2,1,0:T(8,128)S(1)} %get-tuple-element.11), channel_id=1, source_target_pairs={{0,1},{1,0},{2,3},{3,2},{4,5},{5,4},{6,7},{7,6},{8,9},{9,8},{10,11... | collective-permute-start | bytes 3145736 | tf_op jit(solution)/shard_map/summed_core_stage/ppermute | solution.py:30
  217.6 14.0 %collective-permute-start.12 = (f32[2,64,1024]{2,1,0:T(8,128)S(1)}, f32[2,64,1024]{2,1,0:T(8,128)S(1)}, u32[]{:S(2)}, u32[]{:S(2)}) collective-permute-start(f32[2,64,1024]{2,1,0:T(8,128)S(1)} %dynamic-slice_bitcast_fusion.1), channel_id=1, source_target_pairs={{0,2},{1,3},{2,0},{3,1},{4,6},{5,7},{6,4},{7,5},{8,10},{9,11},{10,... | collective-permute-start | bytes 1572872 | tf_op jit(solution)/shard_map/summed_chip_stage/ppermute | solution.py:18
  219.2 14.1 %collective-permute-start.15 = (f32[2,64,1024]{2,1,0:T(8,128)S(1)}, f32[2,64,1024]{2,1,0:T(8,128)S(1)}, u32[]{:S(2)}, u32[]{:S(2)}) collective-permute-start(f32[2,64,1024]{2,1,0:T(8,128)S(1)} %dynamic-slice_bitcast_fusion), channel_id=1, source_target_pairs={{0,4},{1,5},{2,6},{3,7},{4,0},{5,1},{6,2},{7,3},{8,12},{9,13},{10,... | collective-permute-start | bytes 1572872 | tf_op jit(solution)/shard_map/summed_chip_stage/ppermute | solution.py:18
  231.7 7.5 %collective-permute-start.13 = (f32[64,1024]{1,0:T(8,128)S(1)}, f32[64,1024]{1,0:T(8,128)S(1)}, u32[]{:S(2)}, u32[]{:S(2)}) collective-permute-start(f32[64,1024]{1,0:T(8,128)S(1)} %dynamic-slice_bitcast_fusion.3), channel_id=1, source_target_pairs={{0,4},{1,5},{2,6},{3,7},{4,0},{5,1},{6,2},{7,3},{8,12},{9,13},{10,... | collective-permute-start | bytes 786440 | tf_op jit(solution)/shard_map/summed_chip_stage/ppermute | solution.py:18
  233.4 7.2 %collective-permute-start.16 = (f32[64,1024]{1,0:T(8,128)S(1)}, f32[64,1024]{1,0:T(8,128)S(1)}, u32[]{:S(2)}, u32[]{:S(2)}) collective-permute-start(f32[64,1024]{1,0:T(8,128)S(1)} %dynamic-slice_bitcast_fusion.2), channel_id=1, source_target_pairs={{0,2},{1,3},{2,0},{3,1},{4,6},{5,7},{6,4},{7,5},{8,10},{9,11},{10,... | collective-permute-start | bytes 786440 | tf_op jit(solution)/shard_map/summed_chip_stage/ppermute | solution.py:18
  240.8 3.6 %collective-permute-start.17 = (f32[64]{0:T(128)S(1)}, f32[64]{0:T(128)S(1)}, u32[]{:S(2)}, u32[]{:S(2)}) collective-permute-start(f32[64]{0:T(128)S(1)} %multiply_reduce_fusion), channel_id=1, source_target_pairs={{0,8},{8,0},{16,24},{24,16},{1,9},{9,1},{17,25},{25,17},{2,10},{10... | collective-permute-start | bytes 776 | tf_op jit(solution)/shard_map/ppermute | solution.py:75
  244.4 4.5 %collective-permute-start.18 = (f32[64]{0:T(128)S(1)}, f32[64]{0:T(128)S(1)}, u32[]{:S(2)}, u32[]{:S(2)}) collective-permute-start(f32[64]{0:T(128)S(1)} %add.160), channel_id=1, source_target_pairs={{0,16},{8,24},{16,0},{24,8},{1,17},{9,25},{17,1},{25,9},{2,18},{10... | collective-permute-start | bytes 776 | tf_op jit(solution)/shard_map/ppermute | solution.py:75
Sparse Core Ops, SparseCore 0:
  67.2 77.8 reduce-scatter.1
  158.6 45.2 all-gather.2

commit v21 on v20

--- a/solution.py
+++ b/solution.py
@@ -146,7 +146,13 @@
         later, probabilities = lax.optimization_barrier((shifted, probabilities))
         allowed_logprob = jnp.where(live_mask, later, 0.0)
 
-    prob_part = lax.all_gather(probabilities, "dp", axis=0, tiled=True)
+    rows_per_dev = n_blk * BB // n_vocab
+    pairs = BB // rows_per_dev // 2
+    split_rows = probabilities.reshape(1, MOST, pairs, 2, rows_per_dev, TB)
+    send_first = jnp.where(
+        lax.axis_index("vocab") % 2 == 0, jnp.flip(split_rows, axis=3), split_rows
+    ).reshape(probabilities.shape)
+    prob_part = lax.all_gather(send_first, "dp", axis=0, tiled=True)
 
     rows_per_dev = n_blk * BB // n_vocab
     pairs = BB // rows_per_dev // 2
@@ -158,7 +164,7 @@
 
     def expected_half(which):
         with jax.named_scope("dense_expected"):
-            chosen = lax.dynamic_index_in_dim(halves, which, axis=3, keepdims=False)
+            chosen = halves[:, :, :, which]
             chosen = chosen.reshape(n_blk, MOST, pairs * rows_per_dev, TB)
             spread = jnp.einsum(
                 "bsk,bsrt->brkt", onehot, chosen, preferred_element_type=jnp.float32
@@ -171,8 +177,8 @@
             )
             return term.reshape(n_blk * pairs, rows_per_dev, columns_here)
 
-    send_half = expected_half(1 - low_bit)
-    keep_half = expected_half(low_bit)
+    send_half = expected_half(0)
+    keep_half = expected_half(1)
     summed = halving_reduce_scatter(keep_half, send_half, n_vocab)
     squares = butterfly_sum(jnp.sum(summed * summed, axis=1), "dp", n_dp)
     width = hidden.shape[1] * n_vocab

time: 257 us -> 257 us (level)
  no operation moved by 1% of the time
where the time goes in v21:
time: 257 us
  waiting for transfers between devices  171 us (67%)
  starting transfers between devices  24.2 us (9%)
  matrix products  17.9 us (7%)
  between operations  14.6 us (6%)
  local copies, waits for them, and re-layouts  11.4 us (4%)
  other arithmetic  9.08 us (4%)
  blocking collectives  9.06 us (4%)
    reduce_scatter x1, waiting for transfers between devices, per_device(): logits = lax.psum_scatter(picked, 'dp', scatter_dimension=0, tiled=True)  76.7 us
    all_gather x1, waiting for transfers between devices, per_device(): prob_part = lax.all_gather(send_first, 'dp', axis=0, tiled=True)  45.4 us
    ppermute x4, waiting for transfers between devices, exchange_stage(): got = lax.ppermute(send, 'vocab', perm=perm)  16.5 us
    ppermute x5, waiting for transfers between devices, bruck_all_to_all(): got = lax.ppermute(send, axis_name, perm=perm)  15.5 us
    ppermute x6, waiting for transfers between devices, gather_stage(): got = lax.ppermute(x, 'vocab', perm=perm)  10.9 us
    ppermute x5, starting transfers between devices, bruck_all_to_all(): got = lax.ppermute(send, axis_name, perm=perm)  10.5 us
    all_gather x1, blocking collectives, per_device(): stats = lax.all_gather(jnp.stack([local_max, local_total]), 'vocab', axis=0)  9.06 us
    dot_general x2, matrix products, expected_half(): jnp.einsum('brkt,ktd->brd', spread, out_weight.reshape(n_tb, TB, columns_...  8.76 us
  transfers between devices with their start and end apart: 21, of which 18 were waited for; matrix products, arithmetic and copies ran while one was open for 3% of the time, Pallas kernels for 0%

profile of v21, /device:TPU:0, one launch (start us, length us, event | category | flops | bytes accessed | tf_op | source)
XLA Modules:
  0.0 256.8 jit_solution(11396257973825878255)
XLA Ops:
  7.3 1.0 constant_dynamic-slice_fusion.4
  8.3 0.6 collective-permute-start
  8.8 1.0 collective-permute-done
  9.9 2.9 %collective-permute-start.1 = (bf16[2,2,16,1024]{3,2,1,0:T(8,128)(2,1)S(1)}, bf16[2,2,16,1024]{3,2,1,0:T(8,128)(2,1)S(1)}, u32[]{:S(2)}, u32[]{:S(2)}) collective-permute-start(bf16[2,2,16,1024]{3,2,1,0:T(8,128)(2,1)S(1)} %get-tuple-element.33), channel_id=1, source_target_pairs={{0,2},{1,3},{2,0},{3,1},{4,6},{5,7},{6,4},{7,5},{8,10},{9,11},{10,... | collective-permute-start | bytes 393224 | tf_op jit(solution)/shard_map/hidden_spread/ppermute | solution.py:93
  12.8 3.8 %collective-permute-done.1 = bf16[2,2,16,1024]{3,2,1,0:T(8,128)(2,1)S(1)} collective-permute-done((bf16[2,2,16,1024]{3,2,1,0:T(8,128)(2,1)S(1)}, bf16[2,2,16,1024]{3,2,1,0:T(8,128)(2,1)S(1)}, u32[]{:S(2)}, u32[]{:S(2)}) %collective-permute-start.1) | collective-permute-done | bytes 131104 | tf_op jit(solution)/shard_map/hidden_spread/ppermute | solution.py:93
  16.6 1.8 collective-permute-start.2
  18.5 3.2 %collective-permute-done.2 = bf16[2,2,16,1024]{3,2,1,0:T(8,128)(2,1)S(1)} collective-permute-done((bf16[2,2,16,1024]{3,2,1,0:T(8,128)(2,1)S(1)}, bf16[2,2,16,1024]{3,2,1,0:T(8,128)(2,1)S(1)}, u32[]{:S(2)}, u32[]{:S(2)}) %collective-permute-start.2) | collective-permute-done | bytes 131104 | tf_op jit(solution)/shard_map/hidden_spread/ppermute | solution.py:93
  21.8 0.2 reshape.524
  22.0 0.2 copy.49
  22.2 1.9 collective-permute-start.3
  24.1 3.1 %collective-permute-done.3 = bf16[2,16,2048]{2,1,0:T(8,128)(2,1)S(1)} collective-permute-done((bf16[2,16,2048]{2,1,0:T(8,128)(2,1)S(1)}, bf16[2,16,2048]{2,1,0:T(8,128)(2,1)S(1)}, u32[]{:S(2)}, u32[]{:S(2)}) %collective-permute-start.3) | collective-permute-done | bytes 131104 | tf_op jit(solution)/shard_map/hidden_spread/ppermute | solution.py:93
  27.3 3.3 %collective-permute-start.4 = (bf16[2,16,2048]{2,1,0:T(8,128)(2,1)S(1)}, bf16[2,16,2048]{2,1,0:T(8,128)(2,1)S(1)}, u32[]{:S(2)}, u32[]{:S(2)}) collective-permute-start(bf16[2,16,2048]{2,1,0:T(8,128)(2,1)S(1)} %get-tuple-element.27), channel_id=1, source_target_pairs={{0,16},{8,24},{16,0},{24,8},{1,17},{9,25},{17,1},{25,9},{2,18},{10... | collective-permute-start | bytes 393224 | tf_op jit(solution)/shard_map/hidden_spread/ppermute | solution.py:93
  30.6 4.4 %collective-permute-done.4 = bf16[2,16,2048]{2,1,0:T(8,128)(2,1)S(1)} collective-permute-done((bf16[2,16,2048]{2,1,0:T(8,128)(2,1)S(1)}, bf16[2,16,2048]{2,1,0:T(8,128)(2,1)S(1)}, u32[]{:S(2)}, u32[]{:S(2)}) %collective-permute-start.4) | collective-permute-done | bytes 131104 | tf_op jit(solution)/shard_map/hidden_spread/ppermute | solution.py:93
  35.0 0.1 slice_bitcast_fusion.15
  35.1 1.6 collective-permute-start.5
  36.8 1.5 collective-permute-start.8
  38.3 3.3 %collective-permute-done.5 = bf16[64,1024]{1,0:T(8,128)(2,1)S(1)} collective-permute-done((bf16[64,1024]{1,0:T(8,128)(2,1)S(1)}, bf16[64,1024]{1,0:T(8,128)(2,1)S(1)}, u32[]{:S(2)}, u32[]{:S(2)}) %collective-permute-start.5) | collective-permute-done | bytes 131104 | tf_op jit(solution)/shard_map/hidden_spread/hidden_gather_stage/ppermute | solution.py:48
  41.6 1.5 collective-permute-done.8
  43.2 0.6 collective-permute-start.9
  43.8 1.6 collective-permute-start.6
  45.5 4.2 %collective-permute-done.9 = bf16[2,64,1024]{2,1,0:T(8,128)(2,1)S(1)} collective-permute-done((bf16[2,64,1024]{2,1,0:T(8,128)(2,1)S(1)}, bf16[2,64,1024]{2,1,0:T(8,128)(2,1)S(1)}, u32[]{:S(2)}, u32[]{:S(2)}) %collective-permute-start.9) | collective-permute-done | bytes 262176 | tf_op jit(solution)/shard_map/hidden_spread/hidden_gather_stage/ppermute | solution.py:48
  49.8 0.5 collective-permute-done.6
  50.3 0.1 collective-permute-start.7
  50.6 1.0 collective-permute-done.10
  51.7 0.2 maximum_select_fusion.1
  51.9 0.5 collective-permute-done.7
  52.4 0.2 maximum_select_fusion
  52.7 0.2 maximum_bitcast_fusion
  52.9 0.2 copy.58
  53.1 0.9 slice-done.1
  54.1 0.4 slice-done.2
  54.5 7.3 %fusion.25 = f32[4,128,19,128]{3,1,2,0:T(8,128)} fusion(bf16[4,128,2048,1]{2,1,3,0:T(8,128)(2,1)S(1)} %bitcast.180, bf16[19,128,2048,1]{2,1,0,3:T(8,128)(2,1)S(1)} %bitcast.223), kind=kOutput, calls=%fused_computation.101 | convolution fusion | flops 5100273664 | bytes 17039360 | tf_op jit(solution)/shard_map/dense_logits/bd,vd->bv/dot_general | solution.py:126
  61.8 5.2 %gather_fusion = f32[64,128,128]{2,1,0:T(8,128)} fusion(f32[4,128,19,128]{3,1,2,0:T(8,128)} %fusion.25, s32[64]{0:T(128)S(1)} %reshape.531), kind=kCustom, calls=%fused_computation | custom fusion | bytes 8389120 | tf_op jit(solution)/shard_map/dense_logits/gather | solution.py:131
  67.1 0.6 constant_dynamic-slice_fusion.5
  67.7 0.6 iota_compare_fusion.1
  68.4 76.7 %reduce-scatter.2.cloned.1.call-done = f32[1,16,128,128]{3,2,1,0:T(8,128)} async-done(((f32[4,16,128,128]{3,2,1,0:T(8,128)}), f32[1,16,128,128]{3,2,1,0:T(8,128)}) %reduce-scatter.2.cloned.1.call-update) | async-done | bytes 1048592 | tf_op jit(solution)/shard_map/reduce_scatter | solution.py:133
  145.0 1.5 select_reduce_fusion
  146.6 1.6 exponential_reduce_fusion
  148.1 9.1 %all-gather = f32[16,1,128]{2,1,0:T(1,128)S(1)} all-gather(f32[2,1,128]{2,1,0:T(1,128)S(1)} %pad_maximum_fusion.4), channel_id=2, replica_groups=mesh['dp'=4,'vocab'=8] {'vocab'}, dimensions={0}, use_global_device_ids=true | all-gather | bytes 9216 | tf_op jit(solution)/shard_map/softmax_stats/all_gather | solution.py:141
  157.3 0.4 select_convert_fusion
  157.7 0.9 reverse_select_fusion
  158.6 45.4 %all-gather.3.cloned.1.call-done = bf16[4,16,128,128]{3,2,1,0:T(8,128)(2,1)} async-done(((bf16[1,16,128,128]{3,2,1,0:T(8,128)(2,1)}), bf16[4,16,128,128]{3,2,1,0:T(8,128)(2,1)}) %all-gather.3.cloned.1.call-update) | async-done | bytes 2097168 | tf_op jit(solution)/shard_map/all_gather | solution.py:155
  204.0 1.7 fusion.23
  205.8 0.9 fusion.1
  206.8 5.8 %convolution_bitcast_fusion = f32[4,64,2048]{2,1,0:T(8,128)S(1)} fusion(bf16[19,128,2048,1]{2,1,0,3:T(8,128)(2,1)} %bitcast.220, bf16[4,64,19,128]{3,2,1,0:T(8,128)(2,1)S(1)} %fusion.1), kind=kOutput, calls=%fused_computation.1 | convolution fusion | flops 2550136832 | bytes 13303808 | tf_op jit(solution)/shard_map/dense_expected/brkt,ktd->brd/dot_general | solution.py:172
  212.6 0.2 fusion.22
  212.9 0.5 collective-permute-start.14
  213.4 0.9 fusion
  214.4 3.0 %convolution_bitcast_fusion.1 = f32[4,64,2048]{2,1,0:T(8,128)S(1)} fusion(bf16[19,128,2048,1]{2,1,0,3:T(8,128)(2,1)S(1)} %bitcast.226, bf16[4,64,19,128]{3,2,1,0:T(8,128)(2,1)S(1)} %fusion), kind=kOutput, calls=%fused_computation.2 | convolution fusion | flops 2550136832 | bytes 13303808 | tf_op jit(solution)/shard_map/dense_expected/brkt,ktd->brd/dot_general | solution.py:172
  217.3 0.4 slice_add_fusion.1
  217.8 1.5 collective-permute-start.12
  219.4 1.5 collective-permute-start.15
  220.9 10.9 %collective-permute-done.12 = f32[2,64,1024]{2,1,0:T(8,128)S(1)} collective-permute-done((f32[2,64,1024]{2,1,0:T(8,128)S(1)}, f32[2,64,1024]{2,1,0:T(8,128)S(1)}, u32[]{:S(2)}, u32[]{:S(2)}) %collective-permute-start.12) | collective-permute-done | bytes 524320 | tf_op jit(solution)/shard_map/summed_chip_stage/ppermute | solution.py:18
  231.9 1.5 collective-permute-start.13
  233.5 1.5 collective-permute-start.16
  235.1 4.3 %collective-permute-done.13 = f32[64,1024]{1,0:T(8,128)S(1)} collective-permute-done((f32[64,1024]{1,0:T(8,128)S(1)}, f32[64,1024]{1,0:T(8,128)S(1)}, u32[]{:S(2)}, u32[]{:S(2)}) %collective-permute-start.13) | collective-permute-done | bytes 262176 | tf_op jit(solution)/shard_map/summed_chip_stage/ppermute | solution.py:18
  239.4 1.3 collective-permute-done.16
  240.8 0.1 multiply_reduce_fusion
  240.9 0.2 collective-permute-start.17
  241.2 3.4 %collective-permute-done.17 = f32[64]{0:T(128)S(1)} collective-permute-done((f32[64]{0:T(128)S(1)}, f32[64]{0:T(128)S(1)}, u32[]{:S(2)}, u32[]{:S(2)}) %collective-permute-start.17) | collective-permute-done | bytes 288 | tf_op jit(solution)/shard_map/ppermute | solution.py:75
  244.6 1.2 collective-permute-start.18
  245.8 1.1 select_bitcast_fusion
  246.9 2.1 collective-permute-done.18
  249.0 0.9 fusion.4
  (76 shorter events, 1.8 us)
Async XLA Ops:
  7.2 59.9 %copy-start = (s32[1,4]{1,0:T(1,128)S(1)}, s32[1,4]{1,0:T(1,128)}, u32[]{:S(2)}) copy-start(s32[1,4]{1,0:T(1,128)} %param.7) | copy-start | bytes 52
  7.2 137.9 %reduce-scatter.2.cloned.1.call-start = ((), (), s32[]{:S(2)}) async-start(), calls=%async_computation.1 | async-start | bytes 5242880 | tf_op jit(solution)/shard_map/reduce_scatter | solution.py:133
  8.3 1.5 collective-permute-start
  9.9 6.7 %collective-permute-start.1 = (bf16[2,2,16,1024]{3,2,1,0:T(8,128)(2,1)S(1)}, bf16[2,2,16,1024]{3,2,1,0:T(8,128)(2,1)S(1)}, u32[]{:S(2)}, u32[]{:S(2)}) collective-permute-start(bf16[2,2,16,1024]{3,2,1,0:T(8,128)(2,1)S(1)} %get-tuple-element.33), channel_id=1, source_target_pairs={{0,2},{1,3},{2,0},{3,1},{4,6},{5,7},{6,4},{7,5},{8,10},{9,11},{10,... | collective-permute-start | bytes 393224 | tf_op jit(solution)/shard_map/hidden_spread/ppermute | solution.py:93
  16.6 5.0 %collective-permute-start.2 = (bf16[2,2,16,1024]{3,2,1,0:T(8,128)(2,1)S(1)}, bf16[2,2,16,1024]{3,2,1,0:T(8,128)(2,1)S(1)}, u32[]{:S(2)}, u32[]{:S(2)}) collective-permute-start(bf16[2,2,16,1024]{3,2,1,0:T(8,128)(2,1)S(1)} %get-tuple-element.31), channel_id=1, source_target_pairs={{0,4},{1,5},{2,6},{3,7},{4,0},{5,1},{6,2},{7,3},{8,12},{9,13},{10,... | collective-permute-start | bytes 393224 | tf_op jit(solution)/shard_map/hidden_spread/ppermute | solution.py:93
  22.2 14.5 %copy-start.2 = (s32[1,4,16]{2,1,0:T(4,128)S(1)}, s32[1,4,16]{2,1,0:T(4,128)}, u32[]{:S(2)}) copy-start(s32[1,4,16]{2,1,0:T(4,128)} %param.6) | copy-start | bytes 772
  22.2 5.0 %collective-permute-start.3 = (bf16[2,16,2048]{2,1,0:T(8,128)(2,1)S(1)}, bf16[2,16,2048]{2,1,0:T(8,128)(2,1)S(1)}, u32[]{:S(2)}, u32[]{:S(2)}) collective-permute-start(bf16[2,16,2048]{2,1,0:T(8,128)(2,1)S(1)} %get-tuple-element.29), channel_id=1, source_target_pairs={{0,8},{8,0},{16,24},{24,16},{1,9},{9,1},{17,25},{25,17},{2,10},{10... | collective-permute-start | bytes 393224 | tf_op jit(solution)/shard_map/hidden_spread/ppermute | solution.py:93
  27.3 7.6 %collective-permute-start.4 = (bf16[2,16,2048]{2,1,0:T(8,128)(2,1)S(1)}, bf16[2,16,2048]{2,1,0:T(8,128)(2,1)S(1)}, u32[]{:S(2)}, u32[]{:S(2)}) collective-permute-start(bf16[2,16,2048]{2,1,0:T(8,128)(2,1)S(1)} %get-tuple-element.27), channel_id=1, source_target_pairs={{0,16},{8,24},{16,0},{24,8},{1,17},{9,25},{17,1},{25,9},{2,18},{10... | collective-permute-start | bytes 393224 | tf_op jit(solution)/shard_map/hidden_spread/ppermute | solution.py:93
  35.1 6.4 %collective-permute-start.5 = (bf16[64,1024]{1,0:T(8,128)(2,1)S(1)}, bf16[64,1024]{1,0:T(8,128)(2,1)S(1)}, u32[]{:S(2)}, u32[]{:S(2)}) collective-permute-start(bf16[64,1024]{1,0:T(8,128)(2,1)S(1)} %get-tuple-element.21), channel_id=1, source_target_pairs={{0,2},{1,3},{2,0},{3,1},{4,6},{5,7},{6,4},{7,5},{8,10},{9,11},{10,... | collective-permute-start | bytes 393224 | tf_op jit(solution)/shard_map/hidden_spread/hidden_gather_stage/ppermute | solution.py:48
  36.8 6.4 %collective-permute-start.8 = (bf16[64,1024]{1,0:T(8,128)(2,1)S(1)}, bf16[64,1024]{1,0:T(8,128)(2,1)S(1)}, u32[]{:S(2)}, u32[]{:S(2)}) collective-permute-start(bf16[64,1024]{1,0:T(8,128)(2,1)S(1)} %get-tuple-element.20), channel_id=1, source_target_pairs={{0,4},{1,5},{2,6},{3,7},{4,0},{5,1},{6,2},{7,3},{8,12},{9,13},{10,... | collective-permute-start | bytes 393224 | tf_op jit(solution)/shard_map/hidden_spread/hidden_gather_stage/ppermute | solution.py:48
  43.2 6.4 %collective-permute-start.9 = (bf16[2,64,1024]{2,1,0:T(8,128)(2,1)S(1)}, bf16[2,64,1024]{2,1,0:T(8,128)(2,1)S(1)}, u32[]{:S(2)}, u32[]{:S(2)}) collective-permute-start(bf16[2,64,1024]{2,1,0:T(8,128)(2,1)S(1)} %maximum_select_fusion.12), channel_id=1, source_target_pairs={{0,2},{1,3},{2,0},{3,1},{4,6},{5,7},{6,4},{7,5},{8,10},{9,11},{10,... | collective-permute-start | bytes 786440 | tf_op jit(solution)/shard_map/hidden_spread/hidden_gather_stage/ppermute | solution.py:48
  43.8 6.4 %collective-permute-start.6 = (bf16[2,64,1024]{2,1,0:T(8,128)(2,1)S(1)}, bf16[2,64,1024]{2,1,0:T(8,128)(2,1)S(1)}, u32[]{:S(2)}, u32[]{:S(2)}) collective-permute-start(bf16[2,64,1024]{2,1,0:T(8,128)(2,1)S(1)} %maximum_select_fusion.10), channel_id=1, source_target_pairs={{0,4},{1,5},{2,6},{3,7},{4,0},{5,1},{6,2},{7,3},{8,12},{9,13},{10,... | collective-permute-start | bytes 786440 | tf_op jit(solution)/shard_map/hidden_spread/hidden_gather_stage/ppermute | solution.py:48
  49.7 2.0 collective-permute-start.10
  50.2 2.9 %slice-start = ((s8[9961472]{0:T(1024)(128)(4,1)}), s8[4194304]{0:T(1024)(128)(4,1)S(1)}, s32[]{:S(2)}) async-start(s8[9961472]{0:T(1024)(128)(4,1)} %bitcast.221), calls=%async_computation.3 | async-start | bytes 8388608
  50.3 2.1 collective-permute-start.7
  51.7 2.4 slice-start.1
  52.7 1.8 slice-start.2
  67.1 137.0 %all-gather.3.cloned.1.call-start = ((), (), s32[]{:S(2)}) async-start(), calls=%async_computation.2 | async-start | bytes 2621440 | tf_op jit(solution)/shard_map/all_gather | solution.py:155
  145.0 12.2 %copy-start.1 = (f32[1,16,128,128]{3,2,1,0:T(8,128)S(1)}, f32[1,16,128,128]{3,2,1,0:T(8,128)}, u32[]{:S(2)}) copy-start(f32[1,16,128,128]{3,2,1,0:T(8,128)} %reduce-scatter.2.cloned.1.call-done) | copy-start | bytes 3145732
  205.8 8.6 %slice-start.3 = ((s8[9961472]{0:T(1024)(128)(4,1)}), s8[4194304]{0:T(1024)(128)(4,1)S(1)}, s32[]{:S(2)}) async-start(s8[9961472]{0:T(1024)(128)(4,1)} %bitcast.224), calls=%async_computation.6 | async-start | bytes 8388608
  206.7 7.6 %slice-start.4 = ((s8[9961472]{0:T(1024)(128)(4,1)}), s8[4194304]{0:T(1024)(128)(4,1)S(1)}, s32[]{:S(2)}) async-start(s8[9961472]{0:T(1024)(128)(4,1)} %bitcast.224), calls=%async_computation.7 | async-start | bytes 8388608
  206.7 7.6 %slice-start.5 = ((s8[9961472]{0:T(1024)(128)(4,1)}), s8[1572864]{0:T(1024)(128)(4,1)S(1)}, s32[]{:S(2)}) async-start(s8[9961472]{0:T(1024)(128)(4,1)} %bitcast.224), calls=%async_computation.8 | async-start | bytes 3145728
  212.8 4.5 %collective-permute-start.11 = (f32[4,64,1024]{2,1,0:T(8,128)S(1)}, f32[4,64,1024]{2,1,0:T(8,128)S(1)}, u32[]{:S(2)}, u32[]{:S(2)}) collective-permute-start(f32[4,64,1024]{2,1,0:T(8,128)S(1)} %get-tuple-element.10), channel_id=1, source_target_pairs={{0,1},{1,0},{2,3},{3,2},{4,5},{5,4},{6,7},{7,6},{8,9},{9,8},{10,11... | collective-permute-start | bytes 3145736 | tf_op jit(solution)/shard_map/summed_core_stage/ppermute | solution.py:30
  212.9 4.4 %collective-permute-start.14 = (f32[4,64,1024]{2,1,0:T(8,128)S(1)}, f32[4,64,1024]{2,1,0:T(8,128)S(1)}, u32[]{:S(2)}, u32[]{:S(2)}) collective-permute-start(f32[4,64,1024]{2,1,0:T(8,128)S(1)} %get-tuple-element.11), channel_id=1, source_target_pairs={{0,1},{1,0},{2,3},{3,2},{4,5},{5,4},{6,7},{7,6},{8,9},{9,8},{10,11... | collective-permute-start | bytes 3145736 | tf_op jit(solution)/shard_map/summed_core_stage/ppermute | solution.py:30
  217.8 14.0 %collective-permute-start.12 = (f32[2,64,1024]{2,1,0:T(8,128)S(1)}, f32[2,64,1024]{2,1,0:T(8,128)S(1)}, u32[]{:S(2)}, u32[]{:S(2)}) collective-permute-start(f32[2,64,1024]{2,1,0:T(8,128)S(1)} %dynamic-slice_bitcast_fusion.1), channel_id=1, source_target_pairs={{0,2},{1,3},{2,0},{3,1},{4,6},{5,7},{6,4},{7,5},{8,10},{9,11},{10,... | collective-permute-start | bytes 1572872 | tf_op jit(solution)/shard_map/summed_chip_stage/ppermute | solution.py:18
  219.4 14.1 %collective-permute-start.15 = (f32[2,64,1024]{2,1,0:T(8,128)S(1)}, f32[2,64,1024]{2,1,0:T(8,128)S(1)}, u32[]{:S(2)}, u32[]{:S(2)}) collective-permute-start(f32[2,64,1024]{2,1,0:T(8,128)S(1)} %dynamic-slice_bitcast_fusion), channel_id=1, source_target_pairs={{0,4},{1,5},{2,6},{3,7},{4,0},{5,1},{6,2},{7,3},{8,12},{9,13},{10,... | collective-permute-start | bytes 1572872 | tf_op jit(solution)/shard_map/summed_chip_stage/ppermute | solution.py:18
  231.9 7.5 %collective-permute-start.13 = (f32[64,1024]{1,0:T(8,128)S(1)}, f32[64,1024]{1,0:T(8,128)S(1)}, u32[]{:S(2)}, u32[]{:S(2)}) collective-permute-start(f32[64,1024]{1,0:T(8,128)S(1)} %dynamic-slice_bitcast_fusion.3), channel_id=1, source_target_pairs={{0,4},{1,5},{2,6},{3,7},{4,0},{5,1},{6,2},{7,3},{8,12},{9,13},{10,... | collective-permute-start | bytes 786440 | tf_op jit(solution)/shard_map/summed_chip_stage/ppermute | solution.py:18
  233.5 7.2 %collective-permute-start.16 = (f32[64,1024]{1,0:T(8,128)S(1)}, f32[64,1024]{1,0:T(8,128)S(1)}, u32[]{:S(2)}, u32[]{:S(2)}) collective-permute-start(f32[64,1024]{1,0:T(8,128)S(1)} %dynamic-slice_bitcast_fusion.2), channel_id=1, source_target_pairs={{0,2},{1,3},{2,0},{3,1},{4,6},{5,7},{6,4},{7,5},{8,10},{9,11},{10,... | collective-permute-start | bytes 786440 | tf_op jit(solution)/shard_map/summed_chip_stage/ppermute | solution.py:18
  240.9 3.6 %collective-permute-start.17 = (f32[64]{0:T(128)S(1)}, f32[64]{0:T(128)S(1)}, u32[]{:S(2)}, u32[]{:S(2)}) collective-permute-start(f32[64]{0:T(128)S(1)} %multiply_reduce_fusion), channel_id=1, source_target_pairs={{0,8},{8,0},{16,24},{24,16},{1,9},{9,1},{17,25},{25,17},{2,10},{10... | collective-permute-start | bytes 776 | tf_op jit(solution)/shard_map/ppermute | solution.py:75
  244.6 4.5 %collective-permute-start.18 = (f32[64]{0:T(128)S(1)}, f32[64]{0:T(128)S(1)}, u32[]{:S(2)}, u32[]{:S(2)}) collective-permute-start(f32[64]{0:T(128)S(1)} %add.156), channel_id=1, source_target_pairs={{0,16},{8,24},{16,0},{24,8},{1,17},{9,25},{17,1},{25,9},{2,18},{10... | collective-permute-start | bytes 776 | tf_op jit(solution)/shard_map/ppermute | solution.py:75
Sparse Core Ops, SparseCore 0:
  67.2 77.8 reduce-scatter.1
  158.8 45.2 all-gather.2

commit v22 on v12

--- a/solution.py
+++ b/solution.py
@@ -23,12 +23,14 @@
     levels = n.bit_length() - 1
     _, group, cols = keep.shape
     perm = [(s, s ^ 1) for s in range(n)]
-    with jax.named_scope("summed_core_stage"):
-        x = keep + lax.ppermute(send, "vocab", perm=perm)
-    x = x.reshape([2] * (levels - 1) + [group, cols])
+    half = cols // 2
+    streams = []
+    for cut in (slice(0, half), slice(half, cols)):
+        with jax.named_scope("summed_core_stage"):
+            x = keep[:, :, cut] + lax.ppermute(send[:, :, cut], "vocab", perm=perm)
+        streams.append(x.reshape([2] * (levels - 1) + [group, half]))
+    first, second = streams
     remaining = list(range(levels - 1, 0, -1))
-    half = cols // 2
-    first, second = x[..., :half], x[..., half:]
     rest_a, rest_b = list(remaining), list(remaining)
     order_a = sorted(remaining)
     order_b = sorted(remaining, reverse=True)
@@ -164,8 +166,9 @@
         beam_max = jnp.max(stats[:, 0], axis=0)
         beam_total = jnp.sum(stats[:, 1] * jnp.exp(stats[:, 0] - beam_max[None]), axis=0)
         shifted = logits - beam_max[:, None, :, None] - jnp.log(beam_total)[:, None, :, None]
-        allowed_logprob = jnp.where(live_mask, shifted, 0.0)
         probabilities = jnp.where(live_mask, jnp.exp(shifted), 0.0).astype(jnp.bfloat16)
+        later, probabilities = lax.optimization_barrier((shifted, probabilities))
+        allowed_logprob = jnp.where(live_mask, later, 0.0)
 
     prob_part = lax.all_gather(probabilities, "dp", axis=0, tiled=True)
 

time: 260 us -> 257 us (0.988)
  waiting for transfers between devices: 166 us -> 161 us
  other arithmetic: 7.82 us -> 11 us
  matrix products: 20.7 us -> 18 us
    ppermute x1 -> x2, waiting for transfers between devices: 3.33 us -> 0.01 us  [halving_reduce_scatter(): x = keep[:, :, cut] + lax.ppermute(send[:, :, cut], 'vocab', perm=perm)]
    dot_general x2, matrix products: 11.5 us -> 8.75 us  [expected_half(): jnp.einsum('brkt,ktd->brd', spread, out_weight.reshape(n_tb, TB, columns_...]
  transfers between devices with their start and end apart: 23 -> 24, of which waited for: 17 -> 15; matrix products, arithmetic and copies ran while one was open for 2% -> 4% of each run, Pallas kernels for 0% -> 0%
where the time goes in v22:
time: 257 us; the launch traced here: 256 us
  waiting for transfers between devices  161 us (63%)
  starting transfers between devices  29.3 us (11%)
  matrix products  18 us (7%)
  between operations  14.7 us (6%)
  local copies, waits for them, and re-layouts  13.3 us (5%)
  other arithmetic  11 us (4%)
  blocking collectives  9.07 us (4%)
    reduce_scatter x1, waiting for transfers between devices, per_device(): logits = lax.psum_scatter(picked, 'dp', scatter_dimension=0, tiled=True)  75.5 us
    all_gather x1, waiting for transfers between devices, per_device(): prob_part = lax.all_gather(probabilities, 'dp', axis=0, tiled=True)  45.4 us
    ppermute x8, starting transfers between devices, direct_spread(): got.append(lax.ppermute(send, ('dp', 'vocab'), perm=perm))  17.7 us
    ppermute x4, waiting for transfers between devices, exchange_stage(): got = lax.ppermute(send, 'vocab', perm=perm)  16.1 us
    ppermute x6, waiting for transfers between devices, gather_stage(): got = lax.ppermute(x, 'vocab', perm=perm)  12.2 us
    all_gather x1, blocking collectives, per_device(): stats = lax.all_gather(jnp.stack([local_max, local_total]), 'vocab', axis=0)  9.07 us
    dot_general x2, matrix products, expected_half(): jnp.einsum('brkt,ktd->brd', spread, out_weight.reshape(n_tb, TB, columns_...  8.75 us
    dot_general x1, matrix products, per_device(): jnp.einsum('bd,vd->bv', beam_columns, out_weight, preferred_element_type=...  7.37 us
  transfers between devices with their start and end apart: 24, of which 15 were waited for; matrix products, arithmetic and copies ran while one was open for 4% of the time, Pallas kernels for 0%

profile of v22, /device:TPU:0, one launch (start us, length us, event | category | flops | bytes accessed | tf_op | source)
XLA Modules:
  0.0 256.5 jit_solution(2233426413767012074)
XLA Ops:
  7.4 0.9 dynamic-slice_bitcast_fusion.4
  8.3 0.7 collective-permute-start
  8.9 0.5 collective-permute-start.1
  9.5 5.8 %collective-permute-start.2 = (bf16[16,1024]{1,0:T(8,128)(2,1)S(1)}, bf16[16,1024]{1,0:T(8,128)(2,1)S(1)}, u32[]{:S(2)}, u32[]{:S(2)}) collective-permute-start(bf16[16,1024]{1,0:T(8,128)(2,1)S(1)} %get-tuple-element.27), channel_id=1, source_target_pairs={{0,2},{1,3},{2,10},{3,11},{4,18},{5,19},{6,26},{7,27},{8,4},{9,5},... | collective-permute-start | bytes 98312 | tf_op jit(solution)/shard_map/hidden_spread/ppermute | solution.py:117
  15.3 2.9 %collective-permute-start.3 = (bf16[16,1024]{1,0:T(8,128)(2,1)S(1)}, bf16[16,1024]{1,0:T(8,128)(2,1)S(1)}, u32[]{:S(2)}, u32[]{:S(2)}) collective-permute-start(bf16[16,1024]{1,0:T(8,128)(2,1)S(1)} %get-tuple-element.26), channel_id=1, source_target_pairs={{0,3},{1,4},{2,11},{3,12},{4,19},{5,20},{6,27},{7,28},{8,5},{9,6},... | collective-permute-start | bytes 98312 | tf_op jit(solution)/shard_map/hidden_spread/ppermute | solution.py:117
  18.2 3.3 %collective-permute-start.4 = (bf16[16,1024]{1,0:T(8,128)(2,1)S(1)}, bf16[16,1024]{1,0:T(8,128)(2,1)S(1)}, u32[]{:S(2)}, u32[]{:S(2)}) collective-permute-start(bf16[16,1024]{1,0:T(8,128)(2,1)S(1)} %get-tuple-element.25), channel_id=1, source_target_pairs={{0,4},{1,5},{2,12},{3,13},{4,20},{5,21},{6,28},{7,29},{8,6},{9,7},... | collective-permute-start | bytes 98312 | tf_op jit(solution)/shard_map/hidden_spread/ppermute | solution.py:117
  21.6 1.3 collective-permute-start.5
  23.0 1.9 collective-permute-start.6
  24.9 1.2 collective-permute-start.7
  26.1 5.7 %collective-permute-done.5 = bf16[16,1024]{1,0:T(8,128)(2,1)S(1)} collective-permute-done((bf16[16,1024]{1,0:T(8,128)(2,1)S(1)}, bf16[16,1024]{1,0:T(8,128)(2,1)S(1)}, u32[]{:S(2)}, u32[]{:S(2)}) %collective-permute-start.5) | collective-permute-done | bytes 32800 | tf_op jit(solution)/shard_map/hidden_spread/ppermute | solution.py:117
  31.8 0.7 collective-permute-done.6
  32.5 0.6 gather_fusion
  33.1 0.1 select_bitcast_fusion.1
  33.2 0.3 copy.31
  33.6 2.2 collective-permute-start.8
  36.0 3.6 %collective-permute-done.8 = bf16[64,1024]{1,0:T(8,128)(2,1)S(1)} collective-permute-done((bf16[64,1024]{1,0:T(8,128)(2,1)S(1)}, bf16[64,1024]{1,0:T(8,128)(2,1)S(1)}, u32[]{:S(2)}, u32[]{:S(2)}) %collective-permute-start.8) | collective-permute-done | bytes 131104 | tf_op jit(solution)/shard_map/hidden_spread/hidden_gather_stage/ppermute | solution.py:48
  39.8 1.1 collective-permute-done.11
  41.0 0.6 collective-permute-start.12
  41.6 5.8 %collective-permute-done.9 = bf16[2,64,1024]{2,1,0:T(8,128)(2,1)S(1)} collective-permute-done((bf16[2,64,1024]{2,1,0:T(8,128)(2,1)S(1)}, bf16[2,64,1024]{2,1,0:T(8,128)(2,1)S(1)}, u32[]{:S(2)}, u32[]{:S(2)}) %collective-permute-start.9) | collective-permute-done | bytes 262176 | tf_op jit(solution)/shard_map/hidden_spread/hidden_gather_stage/ppermute | solution.py:48
  47.7 0.5 collective-permute-start.13
  48.5 1.0 collective-permute-done.10
  49.5 0.2 maximum_select_fusion
  49.7 0.5 collective-permute-done.13
  50.2 0.2 maximum_select_fusion.1
  50.5 0.2 maximum_bitcast_fusion
  50.7 0.2 copy.38
  50.9 0.8 slice-done.1
  51.7 0.5 slice-done.2
  52.3 7.4 %fusion.19 = f32[4,128,19,128]{3,1,2,0:T(8,128)} fusion(bf16[4,128,2048,1]{2,1,3,0:T(8,128)(2,1)S(1)} %bitcast.156, bf16[19,128,2048,1]{2,1,0,3:T(8,128)(2,1)S(1)} %bitcast.184), kind=kOutput, calls=%fused_computation.96 | convolution fusion | flops 5100273664 | bytes 17039360 | tf_op jit(solution)/shard_map/dense_logits/bd,vd->bv/dot_general | solution.py:150
  59.7 5.2 %gather_fusion.1 = f32[64,128,128]{2,1,0:T(8,128)} fusion(f32[4,128,19,128]{3,1,2,0:T(8,128)} %fusion.19, s32[64]{0:T(128)S(1)} %reshape.585), kind=kCustom, calls=%fused_computation.1 | custom fusion | bytes 8389120 | tf_op jit(solution)/shard_map/dense_logits/gather | solution.py:155
  65.0 0.6 constant_dynamic-slice_fusion.2
  65.6 0.6 iota_compare_fusion.1
  66.2 75.5 %reduce-scatter.2.cloned.1.call-done = f32[1,16,128,128]{3,2,1,0:T(8,128)} async-done(((f32[4,16,128,128]{3,2,1,0:T(8,128)}), f32[1,16,128,128]{3,2,1,0:T(8,128)}) %reduce-scatter.2.cloned.1.call-update) | async-done | bytes 1048592 | tf_op jit(solution)/shard_map/reduce_scatter | solution.py:157
  141.7 1.5 select_reduce_fusion
  143.2 1.6 exponential_reduce_fusion
  144.8 9.1 %all-gather = f32[16,1,128]{2,1,0:T(1,128)S(1)} all-gather(f32[2,1,128]{2,1,0:T(1,128)S(1)} %pad_maximum_fusion.3), channel_id=2, replica_groups=mesh['dp'=4,'vocab'=8] {'vocab'}, dimensions={0}, use_global_device_ids=true | all-gather | bytes 9216 | tf_op jit(solution)/shard_map/softmax_stats/all_gather | solution.py:165
  153.9 1.2 select_convert_fusion
  155.2 45.4 %all-gather.3.cloned.1.call-done = bf16[4,16,128,128]{3,2,1,0:T(8,128)(2,1)} async-done(((bf16[1,16,128,128]{3,2,1,0:T(8,128)(2,1)}), bf16[4,16,128,128]{3,2,1,0:T(8,128)(2,1)}) %all-gather.3.cloned.1.call-update) | async-done | bytes 2097168 | tf_op jit(solution)/shard_map/all_gather | solution.py:173
  200.6 1.7 constant_dynamic-slice_fusion.1
  202.3 0.9 fusion.1
  203.3 5.8 %convolution_bitcast_fusion = f32[4,64,2048]{2,1,0:T(8,128)S(1)} fusion(bf16[19,128,2048,1]{2,1,0,3:T(8,128)(2,1)} %bitcast.181, bf16[4,64,19,128]{3,2,1,0:T(8,128)(2,1)S(1)} %fusion.1), kind=kOutput, calls=%fused_computation.2 | convolution fusion | flops 2550136832 | bytes 13303808 | tf_op jit(solution)/shard_map/dense_expected/brkt,ktd->brd/dot_general | solution.py:190
  209.1 0.2 fusion.17
  209.4 0.5 collective-permute-start.17
  209.9 0.9 fusion
  210.9 2.9 %convolution_bitcast_fusion.1 = f32[4,64,2048]{2,1,0:T(8,128)S(1)} fusion(bf16[19,128,2048,1]{2,1,0,3:T(8,128)(2,1)S(1)} %bitcast.187, bf16[4,64,19,128]{3,2,1,0:T(8,128)(2,1)S(1)} %fusion), kind=kOutput, calls=%fused_computation.3 | convolution fusion | flops 2550136832 | bytes 13303808 | tf_op jit(solution)/shard_map/dense_expected/brkt,ktd->brd/dot_general | solution.py:190
  213.9 0.5 slice_add_fusion.1
  214.3 0.8 dynamic-slice_bitcast_fusion.1
  215.2 1.5 collective-permute-start.15
  216.6 0.8 dynamic-slice_bitcast_fusion
  217.5 1.5 collective-permute-start.18
  218.9 10.4 %collective-permute-done.15 = f32[2,64,1024]{2,1,0:T(8,128)} collective-permute-done((f32[2,64,1024]{2,1,0:T(8,128)}, f32[2,64,1024]{2,1,0:T(8,128)}, u32[]{:S(2)}, u32[]{:S(2)}) %collective-permute-start.15) | collective-permute-done | bytes 524320 | tf_op jit(solution)/shard_map/summed_chip_stage/ppermute | solution.py:18
  229.4 1.1 bitcast_add_fusion.1
  230.5 1.5 collective-permute-start.16
  232.1 1.1 bitcast_add_fusion
  233.2 1.5 collective-permute-start.19
  234.8 3.3 %collective-permute-done.16 = f32[64,1024]{1,0:T(8,128)S(1)} collective-permute-done((f32[64,1024]{1,0:T(8,128)S(1)}, f32[64,1024]{1,0:T(8,128)S(1)}, u32[]{:S(2)}, u32[]{:S(2)}) %collective-permute-start.16) | collective-permute-done | bytes 262176 | tf_op jit(solution)/shard_map/summed_chip_stage/ppermute | solution.py:18
  238.1 2.4 collective-permute-done.19
  240.5 0.1 multiply_reduce_fusion
  240.6 0.2 collective-permute-start.20
  240.9 3.4 %collective-permute-done.20 = f32[64]{0:T(128)S(1)} collective-permute-done((f32[64]{0:T(128)S(1)}, f32[64]{0:T(128)S(1)}, u32[]{:S(2)}, u32[]{:S(2)}) %collective-permute-start.20) | collective-permute-done | bytes 288 | tf_op jit(solution)/shard_map/ppermute | solution.py:75
  244.2 1.2 collective-permute-start.21
  245.5 1.1 select_bitcast_fusion
  246.6 2.1 collective-permute-done.21
  248.7 0.9 fusion.4
  (75 shorter events, 1.6 us)
Async XLA Ops:
  7.2 57.8 %copy-start = (s32[1,4]{1,0:T(1,128)S(1)}, s32[1,4]{1,0:T(1,128)}, u32[]{:S(2)}) copy-start(s32[1,4]{1,0:T(1,128)} %param.7) | copy-start | bytes 52
  7.2 134.5 %reduce-scatter.2.cloned.1.call-start = ((), (), s32[]{:S(2)}) async-start(), calls=%async_computation.1 | async-start | bytes 5242880 | tf_op jit(solution)/shard_map/reduce_scatter | solution.py:157
  7.3 28.5 %copy-start.2 = (s32[1,4,16]{2,1,0:T(4,128)S(1)}, s32[1,4,16]{2,1,0:T(4,128)}, u32[]{:S(2)}) copy-start(s32[1,4,16]{2,1,0:T(4,128)} %param.6) | copy-start | bytes 772
  8.3 13.3 %collective-permute-start = (bf16[16,1024]{1,0:T(8,128)(2,1)S(1)}, bf16[16,1024]{1,0:T(8,128)(2,1)S(1)}, u32[]{:S(2)}, u32[]{:S(2)}) collective-permute-start(bf16[16,1024]{1,0:T(8,128)(2,1)S(1)} %get-tuple-element.29), channel_id=1, source_target_pairs={{0,0},{1,1},{2,8},{3,9},{4,16},{5,17},{6,24},{7,25},{8,2},{9,3},{1... | collective-permute-start | bytes 98312 | tf_op jit(solution)/shard_map/hidden_spread/ppermute | solution.py:117
  8.9 14.0 %collective-permute-start.1 = (bf16[16,1024]{1,0:T(8,128)(2,1)S(1)}, bf16[16,1024]{1,0:T(8,128)(2,1)S(1)}, u32[]{:S(2)}, u32[]{:S(2)}) collective-permute-start(bf16[16,1024]{1,0:T(8,128)(2,1)S(1)} %get-tuple-element.28), channel_id=1, source_target_pairs={{0,1},{1,2},{2,9},{3,10},{4,17},{5,18},{6,25},{7,26},{8,3},{9,4},{... | collective-permute-start | bytes 98312 | tf_op jit(solution)/shard_map/hidden_spread/ppermute | solution.py:117
  9.5 15.4 %collective-permute-start.2 = (bf16[16,1024]{1,0:T(8,128)(2,1)S(1)}, bf16[16,1024]{1,0:T(8,128)(2,1)S(1)}, u32[]{:S(2)}, u32[]{:S(2)}) collective-permute-start(bf16[16,1024]{1,0:T(8,128)(2,1)S(1)} %get-tuple-element.27), channel_id=1, source_target_pairs={{0,2},{1,3},{2,10},{3,11},{4,18},{5,19},{6,26},{7,27},{8,4},{9,5},... | collective-permute-start | bytes 98312 | tf_op jit(solution)/shard_map/hidden_spread/ppermute | solution.py:117
  15.3 10.8 %collective-permute-start.3 = (bf16[16,1024]{1,0:T(8,128)(2,1)S(1)}, bf16[16,1024]{1,0:T(8,128)(2,1)S(1)}, u32[]{:S(2)}, u32[]{:S(2)}) collective-permute-start(bf16[16,1024]{1,0:T(8,128)(2,1)S(1)} %get-tuple-element.26), channel_id=1, source_target_pairs={{0,3},{1,4},{2,11},{3,12},{4,19},{5,20},{6,27},{7,28},{8,5},{9,6},... | collective-permute-start | bytes 98312 | tf_op jit(solution)/shard_map/hidden_spread/ppermute | solution.py:117
  18.2 8.0 %collective-permute-start.4 = (bf16[16,1024]{1,0:T(8,128)(2,1)S(1)}, bf16[16,1024]{1,0:T(8,128)(2,1)S(1)}, u32[]{:S(2)}, u32[]{:S(2)}) collective-permute-start(bf16[16,1024]{1,0:T(8,128)(2,1)S(1)} %get-tuple-element.25), channel_id=1, source_target_pairs={{0,4},{1,5},{2,12},{3,13},{4,20},{5,21},{6,28},{7,29},{8,6},{9,7},... | collective-permute-start | bytes 98312 | tf_op jit(solution)/shard_map/hidden_spread/ppermute | solution.py:117
  21.6 10.2 %collective-permute-start.5 = (bf16[16,1024]{1,0:T(8,128)(2,1)S(1)}, bf16[16,1024]{1,0:T(8,128)(2,1)S(1)}, u32[]{:S(2)}, u32[]{:S(2)}) collective-permute-start(bf16[16,1024]{1,0:T(8,128)(2,1)S(1)} %get-tuple-element.24), channel_id=1, source_target_pairs={{0,5},{1,6},{2,13},{3,14},{4,21},{5,22},{6,29},{7,30},{8,7},{9,0},... | collective-permute-start | bytes 98312 | tf_op jit(solution)/shard_map/hidden_spread/ppermute | solution.py:117
  23.0 9.6 %collective-permute-start.6 = (bf16[16,1024]{1,0:T(8,128)(2,1)S(1)}, bf16[16,1024]{1,0:T(8,128)(2,1)S(1)}, u32[]{:S(2)}, u32[]{:S(2)}) collective-permute-start(bf16[16,1024]{1,0:T(8,128)(2,1)S(1)} %get-tuple-element.23), channel_id=1, source_target_pairs={{0,6},{1,7},{2,14},{3,15},{4,22},{5,23},{6,30},{7,31},{8,0},{9,1},... | collective-permute-start | bytes 98312 | tf_op jit(solution)/shard_map/hidden_spread/ppermute | solution.py:117
  24.9 7.6 %collective-permute-start.7 = (bf16[16,1024]{1,0:T(8,128)(2,1)S(1)}, bf16[16,1024]{1,0:T(8,128)(2,1)S(1)}, u32[]{:S(2)}, u32[]{:S(2)}) collective-permute-start(bf16[16,1024]{1,0:T(8,128)(2,1)S(1)} %get-tuple-element.22), channel_id=1, source_target_pairs={{0,7},{1,0},{2,15},{3,8},{4,23},{5,16},{6,31},{7,24},{8,1},{9,2},{... | collective-permute-start | bytes 98312 | tf_op jit(solution)/shard_map/hidden_spread/ppermute | solution.py:117
  33.6 6.0 %collective-permute-start.8 = (bf16[64,1024]{1,0:T(8,128)(2,1)S(1)}, bf16[64,1024]{1,0:T(8,128)(2,1)S(1)}, u32[]{:S(2)}, u32[]{:S(2)}) collective-permute-start(bf16[64,1024]{1,0:T(8,128)(2,1)S(1)} %get-tuple-element.21), channel_id=1, source_target_pairs={{0,2},{1,3},{2,0},{3,1},{4,6},{5,7},{6,4},{7,5},{8,10},{9,11},{10,... | collective-permute-start | bytes 393224 | tf_op jit(solution)/shard_map/hidden_spread/hidden_gather_stage/ppermute | solution.py:48
  36.0 5.0 %collective-permute-start.11 = (bf16[64,1024]{1,0:T(8,128)(2,1)S(1)}, bf16[64,1024]{1,0:T(8,128)(2,1)S(1)}, u32[]{:S(2)}, u32[]{:S(2)}) collective-permute-start(bf16[64,1024]{1,0:T(8,128)(2,1)S(1)} %get-tuple-element.20), channel_id=1, source_target_pairs={{0,4},{1,5},{2,6},{3,7},{4,0},{5,1},{6,2},{7,3},{8,12},{9,13},{10,... | collective-permute-start | bytes 393224 | tf_op jit(solution)/shard_map/hidden_spread/hidden_gather_stage/ppermute | solution.py:48
  39.6 7.8 %collective-permute-start.9 = (bf16[2,64,1024]{2,1,0:T(8,128)(2,1)S(1)}, bf16[2,64,1024]{2,1,0:T(8,128)(2,1)S(1)}, u32[]{:S(2)}, u32[]{:S(2)}) collective-permute-start(bf16[2,64,1024]{2,1,0:T(8,128)(2,1)S(1)} %maximum_select_fusion.5), channel_id=1, source_target_pairs={{0,4},{1,5},{2,6},{3,7},{4,0},{5,1},{6,2},{7,3},{8,12},{9,13},{10,... | collective-permute-start | bytes 786440 | tf_op jit(solution)/shard_map/hidden_spread/hidden_gather_stage/ppermute | solution.py:48
  41.0 6.7 %collective-permute-start.12 = (bf16[2,64,1024]{2,1,0:T(8,128)(2,1)S(1)}, bf16[2,64,1024]{2,1,0:T(8,128)(2,1)S(1)}, u32[]{:S(2)}, u32[]{:S(2)}) collective-permute-start(bf16[2,64,1024]{2,1,0:T(8,128)(2,1)S(1)} %maximum_select_fusion.7), channel_id=1, source_target_pairs={{0,2},{1,3},{2,0},{3,1},{4,6},{5,7},{6,4},{7,5},{8,10},{9,11},{10,... | collective-permute-start | bytes 786440 | tf_op jit(solution)/shard_map/hidden_spread/hidden_gather_stage/ppermute | solution.py:48
  47.5 2.0 collective-permute-start.10
  47.6 3.3 %slice-start = ((s8[9961472]{0:T(1024)(128)(4,1)}), s8[4194304]{0:T(1024)(128)(4,1)S(1)}, s32[]{:S(2)}) async-start(s8[9961472]{0:T(1024)(128)(4,1)} %bitcast.182), calls=%async_computation.3 | async-start | bytes 8388608
  47.7 2.5 collective-permute-start.13
  49.5 2.3 slice-start.1
  50.5 1.8 slice-start.2
  64.9 135.6 %all-gather.3.cloned.1.call-start = ((), (), s32[]{:S(2)}) async-start(), calls=%async_computation.2 | async-start | bytes 2621440 | tf_op jit(solution)/shard_map/all_gather | solution.py:173
  141.7 12.2 %copy-start.1 = (f32[1,16,128,128]{3,2,1,0:T(8,128)S(1)}, f32[1,16,128,128]{3,2,1,0:T(8,128)}, u32[]{:S(2)}) copy-start(f32[1,16,128,128]{3,2,1,0:T(8,128)} %reduce-scatter.2.cloned.1.call-done) | copy-start | bytes 3145732
  202.3 8.6 %slice-start.3 = ((s8[9961472]{0:T(1024)(128)(4,1)}), s8[4194304]{0:T(1024)(128)(4,1)S(1)}, s32[]{:S(2)}) async-start(s8[9961472]{0:T(1024)(128)(4,1)} %bitcast.185), calls=%async_computation.6 | async-start | bytes 8388608
  203.2 7.6 %slice-start.4 = ((s8[9961472]{0:T(1024)(128)(4,1)}), s8[4194304]{0:T(1024)(128)(4,1)S(1)}, s32[]{:S(2)}) async-start(s8[9961472]{0:T(1024)(128)(4,1)} %bitcast.185), calls=%async_computation.7 | async-start | bytes 8388608
  203.3 7.6 %slice-start.5 = ((s8[9961472]{0:T(1024)(128)(4,1)}), s8[1572864]{0:T(1024)(128)(4,1)S(1)}, s32[]{:S(2)}) async-start(s8[9961472]{0:T(1024)(128)(4,1)} %bitcast.185), calls=%async_computation.8 | async-start | bytes 3145728
  209.3 4.5 %collective-permute-start.14 = (f32[4,64,1024]{2,1,0:T(8,128)S(1)}, f32[4,64,1024]{2,1,0:T(8,128)S(1)}, u32[]{:S(2)}, u32[]{:S(2)}) collective-permute-start(f32[4,64,1024]{2,1,0:T(8,128)S(1)} %get-tuple-element.10), channel_id=1, source_target_pairs={{0,1},{1,0},{2,3},{3,2},{4,5},{5,4},{6,7},{7,6},{8,9},{9,8},{10,11... | collective-permute-start | bytes 3145736 | tf_op jit(solution)/shard_map/summed_core_stage/ppermute | solution.py:30
  209.4 4.4 %collective-permute-start.17 = (f32[4,64,1024]{2,1,0:T(8,128)S(1)}, f32[4,64,1024]{2,1,0:T(8,128)S(1)}, u32[]{:S(2)}, u32[]{:S(2)}) collective-permute-start(f32[4,64,1024]{2,1,0:T(8,128)S(1)} %get-tuple-element.11), channel_id=1, source_target_pairs={{0,1},{1,0},{2,3},{3,2},{4,5},{5,4},{6,7},{7,6},{8,9},{9,8},{10,11... | collective-permute-start | bytes 3145736 | tf_op jit(solution)/shard_map/summed_core_stage/ppermute | solution.py:30
  215.2 14.2 %collective-permute-start.15 = (f32[2,64,1024]{2,1,0:T(8,128)}, f32[2,64,1024]{2,1,0:T(8,128)}, u32[]{:S(2)}, u32[]{:S(2)}) collective-permute-start(f32[2,64,1024]{2,1,0:T(8,128)} %dynamic-slice_bitcast_fusion.1), channel_id=1, source_target_pairs={{0,2},{1,3},{2,0},{3,1},{4,6},{5,7},{6,4},{7,5},{8,10},{9,11},{10,... | collective-permute-start | bytes 1572872 | tf_op jit(solution)/shard_map/summed_chip_stage/ppermute | solution.py:18
  217.5 14.6 %collective-permute-start.18 = (f32[2,64,1024]{2,1,0:T(8,128)}, f32[2,64,1024]{2,1,0:T(8,128)}, u32[]{:S(2)}, u32[]{:S(2)}) collective-permute-start(f32[2,64,1024]{2,1,0:T(8,128)} %dynamic-slice_bitcast_fusion), channel_id=1, source_target_pairs={{0,4},{1,5},{2,6},{3,7},{4,0},{5,1},{6,2},{7,3},{8,12},{9,13},{10,... | collective-permute-start | bytes 1572872 | tf_op jit(solution)/shard_map/summed_chip_stage/ppermute | solution.py:18
  230.5 7.5 %collective-permute-start.16 = (f32[64,1024]{1,0:T(8,128)S(1)}, f32[64,1024]{1,0:T(8,128)S(1)}, u32[]{:S(2)}, u32[]{:S(2)}) collective-permute-start(f32[64,1024]{1,0:T(8,128)S(1)} %dynamic-slice_bitcast_fusion.3), channel_id=1, source_target_pairs={{0,4},{1,5},{2,6},{3,7},{4,0},{5,1},{6,2},{7,3},{8,12},{9,13},{10,... | collective-permute-start | bytes 786440 | tf_op jit(solution)/shard_map/summed_chip_stage/ppermute | solution.py:18
  233.2 7.2 %collective-permute-start.19 = (f32[64,1024]{1,0:T(8,128)S(1)}, f32[64,1024]{1,0:T(8,128)S(1)}, u32[]{:S(2)}, u32[]{:S(2)}) collective-permute-start(f32[64,1024]{1,0:T(8,128)S(1)} %dynamic-slice_bitcast_fusion.2), channel_id=1, source_target_pairs={{0,2},{1,3},{2,0},{3,1},{4,6},{5,7},{6,4},{7,5},{8,10},{9,11},{10,... | collective-permute-start | bytes 786440 | tf_op jit(solution)/shard_map/summed_chip_stage/ppermute | solution.py:18
  240.6 3.6 %collective-permute-start.20 = (f32[64]{0:T(128)S(1)}, f32[64]{0:T(128)S(1)}, u32[]{:S(2)}, u32[]{:S(2)}) collective-permute-start(f32[64]{0:T(128)S(1)} %multiply_reduce_fusion), channel_id=1, source_target_pairs={{0,8},{8,0},{16,24},{24,16},{1,9},{9,1},{17,25},{25,17},{2,10},{10... | collective-permute-start | bytes 776 | tf_op jit(solution)/shard_map/ppermute | solution.py:75
  244.2 4.5 %collective-permute-start.21 = (f32[64]{0:T(128)S(1)}, f32[64]{0:T(128)S(1)}, u32[]{:S(2)}, u32[]{:S(2)}) collective-permute-start(f32[64]{0:T(128)S(1)} %add.268), channel_id=1, source_target_pairs={{0,16},{8,24},{16,0},{24,8},{1,17},{9,25},{17,1},{25,9},{2,18},{10... | collective-permute-start | bytes 776 | tf_op jit(solution)/shard_map/ppermute | solution.py:75
Sparse Core Ops, SparseCore 0:
  65.0 76.6 reduce-scatter.1
  155.3 45.2 all-gather.2
